TPU v7x, 256 devices: a whole 4x4x8 slice. The times are simulated.
256 devices in a mesh: feeder: 32 (over z_hi, y, core), factor: 8 (over z_lo, x).
Axes of the slice: x: 4, y: 4, z: 8 (z_hi: 4, z_lo: 2; z = z_hi * 2 + z_lo), core: 2. Of those that a mesh axis runs over, the one named last changes fastest.
Arguments:
- sensitivity: bfloat16 [32, 2048, 2048], P('feeder'), may hold values from -0.015625 to 0.015625
- headroom: float32 [32, 8, 2048], P('feeder'), may hold values from 0 to 3
- ev_power: float32 [32, 8, 256], P('feeder'), may hold values from 0.5 to 4
- ev_node: int32 [32, 8, 256], P('feeder'), may hold values from 0 to 2047
- region_map: int32 [32, 256], P('feeder'), may hold values from 0 to 511
- loadings: float32 [512, 8, 512], P('feeder', None, 'factor'), may hold values from -8 to 8
Outputs:
- margin: float32 [32, 8, 2048], P('feeder')
- new_loadings: float32 [512, 8, 512], P('feeder', None, 'factor')
All inputs are finite; a program needn't handle non-finite values.
Results may differ from a plain program's by a relative error of at most 0.0031.
Values may be sent and summed in bfloat16 or wider, within the bound.
No kernel may reach another device: no remote copies, remote signals or barrier semaphores. Data moves between devices by JAX's collectives and lax.ppermute only.
A program may use at most 64 MiB of HBM per device.

v0:
```python
import jax
import jax.numpy as jnp
from jax import lax
from jax.sharding import PartitionSpec as P

quantile = 1.645
epsilon = 1e-06
step_size = 16.0


def shards(sensitivity, headroom, ev_power, ev_node, region_map, loadings):
    members = sensitivity.shape[0]
    ev_count = ev_power.shape[2]
    reg_local, hours, columns = loadings.shape
    total_regions = reg_local * lax.axis_size("feeder")
    packed = loadings.astype(jnp.bfloat16).reshape(reg_local, hours * columns)
    regions = region_map.reshape(-1)
    shard_rows = lax.all_gather(packed, "feeder", axis=0, tiled=True)
    row_count = shard_rows.shape[0]
    matches = (regions[:, None] == lax.iota(jnp.int32, row_count)[None, :]).astype(jnp.bfloat16)
    looked = jnp.dot(matches, shard_rows, preferred_element_type=jnp.float32)
    volts_list = []
    rows_list = []
    partial_list = []
    member = 0
    for interval in range(hours):
        block = looked[
            member * ev_count : (member + 1) * ev_count,
            interval * columns : (interval + 1) * columns,
        ]
        weighted = (ev_power[member, interval][:, None] * block).astype(jnp.bfloat16)
        sens_rows = jnp.take(sensitivity[member], ev_node[member, interval], axis=0)
        factor_volts = jnp.dot(weighted.T, sens_rows, preferred_element_type=jnp.float32)
        volts_list.append(factor_volts)
        rows_list.append(sens_rows)
        partial_sum = jnp.sum(factor_volts * factor_volts, axis=0)
        partial_list.append(partial_sum)
    variance = jnp.stack(partial_list, axis=0).reshape(members, hours, -1)
    variance = lax.psum(variance, "factor")
    deviation = jnp.sqrt(variance + epsilon)
    margin = headroom - quantile * deviation
    violation = jnp.maximum(-margin, 0.0)
    var_grad = quantile * violation / deviation
    member = 0
    interval_grads = []
    for interval in range(hours):
        position = member * hours + interval
        volt_grad = (2.0 * var_grad[member, interval][None, :] * volts_list[position]).astype(
            jnp.bfloat16
        )
        weight_grad = jnp.dot(rows_list[position], volt_grad.T, preferred_element_type=jnp.float32)
        interval_grads.append(ev_power[member, interval][:, None] * weight_grad)
    member_grads = jnp.concatenate(interval_grads, axis=1)
    offset = regions - 0
    inside = jnp.logical_and(offset >= 0, offset < total_regions)
    target = jnp.where(inside, offset, total_regions)
    summed = jax.ops.segment_sum(member_grads, target, num_segments=total_regions + 1)
    whole_term = summed[:total_regions]
    reduced = lax.psum_scatter(whole_term, "feeder", scatter_dimension=0, tiled=True)
    new_loadings = loadings - step_size * reduced.reshape(reg_local, hours, columns)
    return (margin, new_loadings)


def solution(mesh):
    return jax.shard_map(
        shards,
        mesh=mesh,
        in_specs=(
            P("feeder", None, None),
            P("feeder", None, None),
            P("feeder", None, None),
            P("feeder", None, None),
            P("feeder", None),
            P("feeder", None, "factor"),
        ),
        out_specs=(P("feeder", None, None), P("feeder", None, "factor")),
        check_vma=False,
    )
```

profile of v0, /device:TPU:4, one launch (start us, length us, event | category | flops | bytes accessed | tf_op | source)
XLA Modules:
  0.0 323.9 jit_solution(15895754559689770932)
XLA Ops:
  7.2 0.0 all-reduce.2.cloned.1.call-start
  7.2 1.0 fusion.61
  8.4 1.0 fusion.60
  9.4 0.8 convert_element_type.52
  10.3 0.1 reshape.133
  10.4 49.2 %all_gather.3 = bf16[512,512]{1,0:T(8,128)(2,1)S(1)} all-gather(bf16[16,512]{1,0:T(8,128)(2,1)S(1)} %reshape.133), channel_id=1, replica_groups=mesh['feeder'=32,'factor'=8] {'feeder'}, dimensions={0}, use_global_device_ids=true | all-gather | bytes 540672 | tf_op jit(solution)/shard_map/all_gather | solution.py:18
  59.6 6.8 %gather_fusion.2 = bf16[256,2048]{1,0:T(8,128)(2,1)S(1)} fusion(bf16[2048,2048]{1,0:T(8,128)(2,1)} %bitcast.39, s32[1024]{0:T(1024)S(1)} %pad_clamp_fusion.5), kind=kCustom, calls=%fused_computation.2.clone | custom fusion | bytes 2098176 | tf_op jit(solution)/shard_map/jit(_take)/gather | solution.py:32
  66.4 6.8 %gather_fusion.3 = bf16[256,2048]{1,0:T(8,128)(2,1)S(1)} fusion(bf16[2048,2048]{1,0:T(8,128)(2,1)} %bitcast.40, s32[1024]{0:T(1024)S(1)} %pad_clamp_fusion.4), kind=kCustom, calls=%fused_computation.3.clone | custom fusion | bytes 2098176 | tf_op jit(solution)/shard_map/jit(_take)/gather | solution.py:32
  73.3 7.8 %gather_fusion.4 = bf16[256,2048]{1,0:T(8,128)(2,1)} fusion(bf16[2048,2048]{1,0:T(8,128)(2,1)} %bitcast.41, s32[1024]{0:T(1024)S(1)} %pad_clamp_fusion.3), kind=kCustom, calls=%fused_computation.4.clone | custom fusion | bytes 2098176 | tf_op jit(solution)/shard_map/jit(_take)/gather | solution.py:32
  81.1 8.0 %gather_fusion.5 = bf16[256,2048]{1,0:T(8,128)(2,1)} fusion(bf16[2048,2048]{1,0:T(8,128)(2,1)} %bitcast.42, s32[1024]{0:T(1024)S(1)} %pad_clamp_fusion.2), kind=kCustom, calls=%fused_computation.5.clone | custom fusion | bytes 2098176 | tf_op jit(solution)/shard_map/jit(_take)/gather | solution.py:32
  89.1 7.8 %gather_fusion.6 = bf16[256,2048]{1,0:T(8,128)(2,1)} fusion(bf16[2048,2048]{1,0:T(8,128)(2,1)} %bitcast.43, s32[1024]{0:T(1024)S(1)} %pad_clamp_fusion.1), kind=kCustom, calls=%fused_computation.6.clone | custom fusion | bytes 2098176 | tf_op jit(solution)/shard_map/jit(_take)/gather | solution.py:32
  96.9 7.8 %gather_fusion.7 = bf16[256,2048]{1,0:T(8,128)(2,1)} fusion(bf16[2048,2048]{1,0:T(8,128)(2,1)} %bitcast.44, s32[1024]{0:T(1024)S(1)} %pad_clamp_fusion), kind=kCustom, calls=%fused_computation.7.clone | custom fusion | bytes 2098176 | tf_op jit(solution)/shard_map/jit(_take)/gather | solution.py:32
  104.7 0.0 copy-start.7
  104.7 7.9 %gather_fusion.1 = bf16[256,2048]{1,0:T(8,128)(2,1)} fusion(bf16[2048,2048]{1,0:T(8,128)(2,1)} %bitcast.45, s32[1024]{0:T(1024)S(1)} %pad_clamp_fusion.6), kind=kCustom, calls=%fused_computation.1.clone | custom fusion | bytes 2098176 | tf_op jit(solution)/shard_map/jit(_take)/gather | solution.py:32
  112.6 8.0 %gather_fusion = bf16[256,2048]{1,0:T(8,128)(2,1)} fusion(bf16[2048,2048]{1,0:T(8,128)(2,1)} %bitcast.46, s32[1024]{0:T(1024)S(1)} %pad_clamp_fusion.7), kind=kCustom, calls=%fused_computation.clone | custom fusion | bytes 2098176 | tf_op jit(solution)/shard_map/jit(_take)/gather | solution.py:32
  120.6 0.0 copy-start.4
  120.6 0.0 copy-start.2
  120.6 0.0 copy-start
  120.6 0.0 copy-start.6
  120.6 0.0 copy-done.7
  120.7 0.3 fusion.2
  121.0 1.2 multiply_reduce_fusion.5
  122.2 1.2 multiply_reduce_fusion.4
  123.5 2.5 multiply_reduce_fusion.3
  126.0 2.6 multiply_reduce_fusion.2
  128.5 2.4 multiply_reduce_fusion.1
  131.0 0.0 copy-done.4
  131.0 1.3 multiply_reduce_fusion
  132.2 0.0 copy-done.2
  132.2 1.3 multiply_reduce_fusion.6
  133.5 0.0 copy-done
  133.5 1.2 multiply_reduce_fusion.7
  134.8 0.7 stack.35
  135.5 0.0 all-reduce.2.cloned.1.call-update
  135.5 0.0 reduce-scatter.2.cloned.1.call-start
  135.6 71.2 %all-reduce.2.cloned.1.call-done = f32[1,8,2048]{2,1,0:T(8,128)} async-done(((f32[1,8,2048]{2,1,0:T(8,128)}), f32[1,8,2048]{2,1,0:T(8,128)}) %all-reduce.2.cloned.1.call-update) | async-done | bytes 65552 | tf_op jit(solution)/shard_map/psum | solution.py:39
  206.7 0.0 copy-done.6
  206.8 1.6 multiply_divide_fusion
  208.4 0.1 slice_multiply_fusion.8
  208.4 0.0 copy-start.1
  208.4 0.0 copy-start.9
  208.5 2.0 convolution_multiply_fusion
  210.4 1.8 convolution_multiply_fusion.1
  212.3 2.5 convolution_multiply_fusion.2
  214.7 2.5 convolution_multiply_fusion.3
  217.3 0.0 copy-done.10
  217.3 1.1 convolution_multiply_fusion.4
  218.4 0.0 copy-done.8
  218.4 0.5 convolution_multiply_fusion.5
  218.9 0.0 copy-done.3
  218.9 0.0 copy-done.11
  218.9 0.5 convolution_multiply_fusion.6
  219.4 0.0 copy-done.1
  219.4 0.0 copy-done.9
  219.5 0.5 convolution_multiply_fusion.7
  219.9 1.3 concatenate.3
  221.3 2.3 scatter_custom_fusion
  223.6 1.1 slice.172
  224.7 0.0 reduce-scatter.2.cloned.1.call-update
  224.7 90.9 %reduce-scatter.2.cloned.1.call-done = f32[16,512]{1,0:T(8,128)} async-done(((f32[512,512]{1,0:T(8,128)}), f32[16,512]{1,0:T(8,128)}) %reduce-scatter.2.cloned.1.call-update) | async-done | bytes 32784 | tf_op jit(solution)/shard_map/reduce_scatter | solution.py:59
  315.6 0.8 broadcast_multiply_fusion
  316.4 0.1 mul.395
  316.5 0.0 copy-done.5
  316.5 0.6 sub.7
  (30 shorter events, 0.2 us)
Async XLA Ops:
  7.2 199.6 %all-reduce.2.cloned.1.call-start = ((), (), s32[]{:S(2)}) async-start(), calls=%async_computation.1 | async-start | bytes 131072 | tf_op jit(solution)/shard_map/psum | solution.py:39
  104.7 15.9 %copy-start.7 = (s32[1,256]{1,0:T(1,128)S(1)}, s32[1,256]{1,0:T(1,128)}, u32[]{:S(2)}) copy-start(s32[1,256]{1,0:T(1,128)} %param.12) | copy-start | bytes 3076
  120.6 10.4 %copy-start.4 = (bf16[256,2048]{1,0:T(8,128)(2,1)S(1)}, bf16[256,2048]{1,0:T(8,128)(2,1)}, u32[]{:S(2)}) copy-start(bf16[256,2048]{1,0:T(8,128)(2,1)} %gather_fusion.7) | copy-start | bytes 3145732
  120.6 11.6 %copy-start.2 = (bf16[256,2048]{1,0:T(8,128)(2,1)S(1)}, bf16[256,2048]{1,0:T(8,128)(2,1)}, u32[]{:S(2)}) copy-start(bf16[256,2048]{1,0:T(8,128)(2,1)} %gather_fusion.1) | copy-start | bytes 3145732
  120.6 12.9 %copy-start = (bf16[256,2048]{1,0:T(8,128)(2,1)S(1)}, bf16[256,2048]{1,0:T(8,128)(2,1)}, u32[]{:S(2)}) copy-start(bf16[256,2048]{1,0:T(8,128)(2,1)} %gather_fusion) | copy-start | bytes 3145732
  120.6 86.1 %copy-start.6 = (f32[1,8,2048]{2,1,0:T(8,128)S(1)}, f32[1,8,2048]{2,1,0:T(8,128)}, u32[]{:S(2)}) copy-start(f32[1,8,2048]{2,1,0:T(8,128)} %param.9) | copy-start | bytes 196612
  133.5 85.4 %copy-start.3 = (bf16[256,2048]{1,0:T(8,128)(2,1)S(1)}, bf16[256,2048]{1,0:T(8,128)(2,1)}, u32[]{:S(2)}) copy-start(bf16[256,2048]{1,0:T(8,128)(2,1)} %gather_fusion.1) | copy-start | bytes 3145732
  135.5 180.1 %reduce-scatter.2.cloned.1.call-start = ((), (), s32[]{:S(2)}) async-start(), calls=%async_computation.2 | async-start | bytes 1081344 | tf_op jit(solution)/shard_map/reduce_scatter | solution.py:59
  206.7 10.5 %copy-start.10 = (f32[64,2048]{1,0:T(8,128)S(1)}, f32[64,2048]{1,0:T(8,128)}, u32[]{:S(2)}) copy-start(f32[64,2048]{1,0:T(8,128)} %get-tuple-element.36) | copy-start | bytes 1572868
  206.7 11.7 %copy-start.8 = (f32[64,2048]{1,0:T(8,128)S(1)}, f32[64,2048]{1,0:T(8,128)}, u32[]{:S(2)}) copy-start(f32[64,2048]{1,0:T(8,128)} %get-tuple-element.34) | copy-start | bytes 1572868
  206.7 12.2 %copy-start.11 = (f32[64,2048]{1,0:T(8,128)S(1)}, f32[64,2048]{1,0:T(8,128)}, u32[]{:S(2)}) copy-start(f32[64,2048]{1,0:T(8,128)} %get-tuple-element.32) | copy-start | bytes 1572868
  208.4 11.0 %copy-start.1 = (bf16[256,2048]{1,0:T(8,128)(2,1)S(1)}, bf16[256,2048]{1,0:T(8,128)(2,1)}, u32[]{:S(2)}) copy-start(bf16[256,2048]{1,0:T(8,128)(2,1)} %gather_fusion) | copy-start | bytes 3145732
  208.4 11.0 %copy-start.9 = (f32[64,2048]{1,0:T(8,128)S(1)}, f32[64,2048]{1,0:T(8,128)}, u32[]{:S(2)}) copy-start(f32[64,2048]{1,0:T(8,128)} %get-tuple-element.30) | copy-start | bytes 1572868
  214.7 101.7 %copy-start.5 = (f32[16,8,64]{2,1,0:T(8,128)S(1)}, f32[16,8,64]{2,1,0:T(8,128)}, u32[]{:S(2)}) copy-start(f32[16,8,64]{2,1,0:T(8,128)} %param.13) | copy-start | bytes 98308
Sparse Core Ops, SparseCore 0:
  135.6 71.0 all-reduce.1
  224.8 90.7 reduce-scatter.1
where the time goes:
time: 325 us; the launch traced here: 324 us
  waiting for transfers between devices  162 us (50%)
  local copies, waits for them, and re-layouts  66.3 us (20%)
  blocking collectives  49.2 us (15%)
  matrix products  25.5 us (8%)
  between operations  14.3 us (4%)
  other arithmetic  6.4 us (2%)
    reduce_scatter x1, waiting for transfers between devices, shards(): lax.psum_scatter(whole_term, 'feeder', scatter_dimension=0, tiled=True)  90.9 us
    psum x1, waiting for transfers between devices, shards(): variance = lax.psum(variance, 'factor')  71.2 us
    gather x8, local copies, waits for them, and re-layouts, shards(): sens_rows = jnp.take(sensitivity[member], ev_node[member, interval], axis=0)  61 us
    all_gather x1, blocking collectives, shards(): shard_rows = lax.all_gather(packed, 'feeder', axis=0, tiled=True)  49.2 us
    dot_general x8, matrix products, shards(): jnp.dot(weighted.T, sens_rows, preferred_element_type=jnp.float32)  13.7 us
    dot_general x8, matrix products, shards(): jnp.dot(rows_list[position], volt_grad.T, preferred_element_type=jnp.floa...  11.4 us
  transfers between devices with their start and end apart: 2, of which 2 were waited for; matrix products, arithmetic and copies ran while one was open for 0% of the time, Pallas kernels for 0%

commit v1 on v0

v1 whole, which is shorter than its diff:
```python
import jax
import jax.numpy as jnp
from jax import lax
from jax.sharding import PartitionSpec as P

quantile = 1.645
epsilon = 1e-06
step_size = 16.0


def _bit_count(size):
    bits = size.bit_length() - 1
    assert (1 << bits) == size
    return bits


def _exchange(x, axis, bit, size):
    perm = [(i, i ^ (1 << bit)) for i in range(size)]
    return lax.ppermute(x, axis, perm)


def gather_blocks(x, axis):
    size = lax.axis_size(axis)
    bits = _bit_count(size)
    me = lax.axis_index(axis)
    buf = x
    for step, bit in enumerate(reversed(range(bits))):
        other = _exchange(buf, axis, bit, size)
        mine = (me >> bit) & 1
        low = jnp.where(mine == 0, buf, other)
        high = jnp.where(mine == 0, other, buf)
        buf = jnp.stack([low, high], axis=step)
    return buf.reshape((size * x.shape[0],) + x.shape[1:])


def scatter_blocks(x, axis):
    size = lax.axis_size(axis)
    bits = _bit_count(size)
    me = lax.axis_index(axis)
    block = x.shape[0] // size
    buf = x.reshape((2,) * bits + (block,) + x.shape[1:])
    for bit in range(bits):
        at = bits - 1 - bit
        mine = (me >> bit) & 1
        keep = lax.dynamic_index_in_dim(buf, mine, at, keepdims=False)
        send = lax.dynamic_index_in_dim(buf, 1 - mine, at, keepdims=False)
        buf = keep + _exchange(send, axis, bit, size)
    return buf


def sum_all(x, axis):
    size = lax.axis_size(axis)
    for bit in range(_bit_count(size)):
        x = x + _exchange(x, axis, bit, size)
    return x


def shards(sensitivity, headroom, ev_power, ev_node, region_map, loadings):
    reg_local, hours, columns = loadings.shape
    nodes = sensitivity.shape[2]
    ev_count = ev_power.shape[2]
    total_regions = reg_local * lax.axis_size("feeder")
    packed = loadings.astype(jnp.bfloat16).reshape(reg_local, hours * columns)
    shard_rows = gather_blocks(packed, "feeder")
    regions = region_map.reshape(-1)
    matches = (regions[:, None] == lax.iota(jnp.int32, total_regions)[None, :]).astype(jnp.bfloat16)
    looked = jnp.dot(matches, shard_rows, preferred_element_type=jnp.float32)
    looked = looked.reshape(ev_count, hours, columns)
    power = ev_power[0].T
    weighted = (power[:, :, None] * looked).astype(jnp.bfloat16)
    node_hot = (ev_node[0][:, :, None] == lax.iota(jnp.int32, nodes)[None, None, :]).astype(jnp.bfloat16)
    spread = jnp.einsum("hkm,khr->mhr", node_hot, weighted, preferred_element_type=jnp.float32)
    spread_hi = spread.astype(jnp.bfloat16)
    spread_lo = (spread - spread_hi.astype(jnp.float32)).astype(jnp.bfloat16)
    both = jnp.concatenate([spread_hi, spread_lo], axis=2)
    sens = sensitivity[0]
    volts_both = jnp.einsum("mhr,mn->hrn", both, sens, preferred_element_type=jnp.float32)
    factor_volts = volts_both[:, :columns] + volts_both[:, columns:]
    partial_sum = jnp.sum(factor_volts * factor_volts, axis=1)
    variance = sum_all(partial_sum, "factor")[None]
    deviation = jnp.sqrt(variance + epsilon)
    margin = headroom - quantile * deviation
    violation = jnp.maximum(-margin, 0.0)
    var_grad = quantile * violation / deviation
    volt_grad = (2.0 * var_grad[0][:, None, :] * factor_volts).astype(jnp.bfloat16)
    node_grads = jnp.einsum("mn,hrn->mhr", sens, volt_grad, preferred_element_type=jnp.float32)
    picked = jnp.einsum(
        "hkm,mhr->khr",
        node_hot,
        node_grads,
        precision=lax.Precision.HIGHEST,
        preferred_element_type=jnp.float32,
    )
    member_grads = (power[:, :, None] * picked).reshape(ev_count, hours * columns)
    summed = jax.ops.segment_sum(member_grads, regions, num_segments=total_regions)
    reduced = scatter_blocks(summed, "feeder")
    new_loadings = loadings - step_size * reduced.reshape(reg_local, hours, columns)
    return (margin, new_loadings)


def solution(mesh):
    return jax.shard_map(
        shards,
        mesh=mesh,
        in_specs=(
            P("feeder", None, None),
            P("feeder", None, None),
            P("feeder", None, None),
            P("feeder", None, None),
            P("feeder", None),
            P("feeder", None, "factor"),
        ),
        out_specs=(P("feeder", None, None), P("feeder", None, "factor")),
        check_vma=False,
    )
```

time: 325 us -> 118 us (0.36)
  waiting for transfers between devices: 162 us -> 40.5 us
  local copies, waits for them, and re-layouts: 66.3 us -> 2.9 us
  blocking collectives: 49.2 us -> 0 us
  starting transfers between devices: 0.08 us -> 32.1 us
  between operations: 14.3 us -> 0.9 us
  matrix products: 25.5 us -> 35.6 us
    reduce_scatter x1 -> x0, waiting for transfers between devices: 90.9 us -> none  [shards(): lax.psum_scatter(whole_term, 'feeder', scatter_dimension=0, tiled=True)]
    psum x1 -> x0, waiting for transfers between devices: 71.2 us -> none  [shards(): variance = lax.psum(variance, 'factor')]
    gather x8 -> x0, local copies, waits for them, and re-layouts: 61 us -> none  [shards(): sens_rows = jnp.take(sensitivity[member], ev_node[member, interval], axis=0)]
    all_gather x1 -> x0, blocking collectives: 49.2 us -> none  [shards(): shard_rows = lax.all_gather(packed, 'feeder', axis=0, tiled=True)]
    ppermute x0 -> x13, waiting for transfers between devices: none -> 40.5 us  [_exchange(): return lax.ppermute(x, axis, perm)]
    ppermute x0 -> x13, starting transfers between devices: none -> 32.1 us  [_exchange(): return lax.ppermute(x, axis, perm)]
    dot_general x17 -> x4, matrix products: 25.5 us -> 35.6 us  [the longest x1 12.1 us: shards(): jnp.einsum('mhr,mn->hrn', both, sens, preferred_element_type=jnp.float32)]
  transfers between devices with their start and end apart: 2 -> 13, of which waited for: 2 -> 13; matrix products, arithmetic and copies ran while one was open for 0% -> 0% of each run, Pallas kernels for 0% -> 0%
where the time goes in v1:
time: 118 us
  waiting for transfers between devices  40.5 us (34%)
  matrix products  35.6 us (30%)
  starting transfers between devices  32.1 us (27%)
  other arithmetic  5.99 us (5%)
  local copies, waits for them, and re-layouts  2.9 us (2%)
    ppermute x13, waiting for transfers between devices, _exchange(): return lax.ppermute(x, axis, perm)  40.5 us
    ppermute x13, starting transfers between devices, _exchange(): return lax.ppermute(x, axis, perm)  32.1 us
    dot_general x1, matrix products, shards(): jnp.einsum('mhr,mn->hrn', both, sens, preferred_element_type=jnp.float32)  12.1 us
    dot_general x1, matrix products, shards(): jnp.einsum('mn,hrn->mhr', sens, volt_grad, preferred_element_type=jnp.flo...  9.49 us
    dot_general x1, matrix products, shards(): jnp.einsum('hkm,mhr->khr', node_hot, node_grads, precision=lax.Precision....  8.9 us
    dot_general x1, matrix products, shards(): jnp.einsum('hkm,khr->mhr', node_hot, weighted, preferred_element_type=jnp...  5.1 us
  transfers between devices with their start and end apart: 13, of which 13 were waited for; matrix products, arithmetic and copies ran while one was open for 0% of the time, Pallas kernels for 0%

profile of v1, /device:TPU:4, one launch (start us, length us, event | category | flops | bytes accessed | tf_op | source)
XLA Modules:
  0.0 118.0 jit_solution(10293701249887338660)
XLA Ops:
  0.6 0.0 copy-start.3
  0.6 0.0 copy-start.5
  0.7 0.0 copy-start.4
  0.7 0.9 convert_element_type.20
  1.5 0.1 reshape.36
  1.6 7.3 %collective-permute-start = (bf16[16,512]{1,0:T(8,128)(2,1)S(1)}, bf16[16,512]{1,0:T(8,128)(2,1)S(1)}, u32[]{:S(2)}, u32[]{:S(2)}) collective-permute-start(bf16[16,512]{1,0:T(8,128)(2,1)S(1)} %reshape.36), channel_id=1, source_target_pairs={{0,128},{8,136},{16,144},{24,152},{32,160},{40,168},{48,176},{56,1... | collective-permute-start | bytes 49160 | tf_op jit(solution)/shard_map/ppermute | solution.py:19
  8.9 1.7 %collective-permute-done = bf16[16,512]{1,0:T(8,128)(2,1)S(1)} collective-permute-done((bf16[16,512]{1,0:T(8,128)(2,1)S(1)}, bf16[16,512]{1,0:T(8,128)(2,1)S(1)}, u32[]{:S(2)}, u32[]{:S(2)}) %collective-permute-start) | collective-permute-done | bytes 16416 | tf_op jit(solution)/shard_map/ppermute | solution.py:19
  10.6 2.1 %collective-permute-start.1 = (bf16[2,16,512]{2,1,0:T(8,128)(2,1)S(1)}, bf16[2,16,512]{2,1,0:T(8,128)(2,1)S(1)}, u32[]{:S(2)}, u32[]{:S(2)}) collective-permute-start(bf16[2,16,512]{2,1,0:T(8,128)(2,1)S(1)} %pad_maximum_fusion.4), channel_id=1, source_target_pairs={{0,64},{8,72},{16,80},{24,88},{32,96},{40,104},{48,112},{56,120},{... | collective-permute-start | bytes 98312 | tf_op jit(solution)/shard_map/ppermute | solution.py:19
  12.7 2.8 %collective-permute-done.1 = bf16[2,16,512]{2,1,0:T(8,128)(2,1)S(1)} collective-permute-done((bf16[2,16,512]{2,1,0:T(8,128)(2,1)S(1)}, bf16[2,16,512]{2,1,0:T(8,128)(2,1)S(1)}, u32[]{:S(2)}, u32[]{:S(2)}) %collective-permute-start.1) | collective-permute-done | bytes 32800 | tf_op jit(solution)/shard_map/ppermute | solution.py:19
  15.6 3.3 %collective-permute-start.2 = (bf16[2,2,16,512]{3,2,1,0:T(8,128)(2,1)S(1)}, bf16[2,2,16,512]{3,2,1,0:T(8,128)(2,1)S(1)}, u32[]{:S(2)}, u32[]{:S(2)}) collective-permute-start(bf16[2,2,16,512]{3,2,1,0:T(8,128)(2,1)S(1)} %pad_maximum_fusion.3), channel_id=1, source_target_pairs={{0,32},{8,40},{16,48},{24,56},{32,0},{40,8},{48,16},{56,24},{64,96... | collective-permute-start | bytes 196616 | tf_op jit(solution)/shard_map/ppermute | solution.py:19
  18.8 2.6 %collective-permute-done.2 = bf16[2,2,16,512]{3,2,1,0:T(8,128)(2,1)S(1)} collective-permute-done((bf16[2,2,16,512]{3,2,1,0:T(8,128)(2,1)S(1)}, bf16[2,2,16,512]{3,2,1,0:T(8,128)(2,1)S(1)}, u32[]{:S(2)}, u32[]{:S(2)}) %collective-permute-start.2) | collective-permute-done | bytes 65568 | tf_op jit(solution)/shard_map/ppermute | solution.py:19
  21.5 1.7 %collective-permute-start.3 = (bf16[2,2,2,16,512]{4,3,2,1,0:T(8,128)(2,1)S(1)}, bf16[2,2,2,16,512]{4,3,2,1,0:T(8,128)(2,1)S(1)}, u32[]{:S(2)}, u32[]{:S(2)}) collective-permute-start(bf16[2,2,2,16,512]{4,3,2,1,0:T(8,128)(2,1)S(1)} %pad_maximum_fusion.2), channel_id=1, source_target_pairs={{0,16},{8,24},{16,0},{24,8},{32,48},{40,56},{48,32},{56,40},{64,80... | collective-permute-start | bytes 393224 | tf_op jit(solution)/shard_map/ppermute | solution.py:19
  23.1 3.4 %collective-permute-done.3 = bf16[2,2,2,16,512]{4,3,2,1,0:T(8,128)(2,1)S(1)} collective-permute-done((bf16[2,2,2,16,512]{4,3,2,1,0:T(8,128)(2,1)S(1)}, bf16[2,2,2,16,512]{4,3,2,1,0:T(8,128)(2,1)S(1)}, u32[]{:S(2)}, u32[]{:S(2)}) %collective-permute-start.3) | collective-permute-done | bytes 131104 | tf_op jit(solution)/shard_map/ppermute | solution.py:19
  26.6 0.1 collective-permute-start.4
  26.7 1.5 %collective-permute-done.4 = bf16[2,2,2,2,16,512]{5,4,3,2,1,0:T(8,128)(2,1)S(1)} collective-permute-done((bf16[2,2,2,2,16,512]{5,4,3,2,1,0:T(8,128)(2,1)S(1)}, bf16[2,2,2,2,16,512]{5,4,3,2,1,0:T(8,128)(2,1)S(1)}, u32[]{:S(2)}, u32[]{:S(2)}) %collective-permute-start.4) | collective-permute-done | bytes 262176 | tf_op jit(solution)/shard_map/ppermute | solution.py:19
  28.2 0.1 pad_maximum_fusion
  28.3 0.2 copy.18
  28.5 0.0 copy-done.3
  28.5 0.0 copy-done.5
  28.5 0.0 copy-done.4
  28.6 5.1 %fusion.12 = (bf16[2048,8,64]{0,2,1:T(8,128)(2,1)S(1)}, bf16[2048,8,64]{0,2,1:T(8,128)(2,1)}) fusion(s32[8,256]{1,0:T(8,128)S(1)} %bitcast.109, bf16[8,64,512]{2,1,0:T(8,128)(2,1)S(1)} %bitcast.106, s32[256]{0:T(256)S(1)} %bitcast.113, f32[256,8]{0,1:T(8,128)S(1)} %bitcast.111), kind=kOutput, calls=%fused_computation.17 | convolution fusion | flops 679870464 | bytes 4736000 | tf_op jit(solution)/shard_map/hkm,khr->mhr/dot_general | solution.py:72
  33.6 12.1 %fusion.4 = f32[8,128,2048]{2,1,0:T(8,128)S(1)} fusion(bf16[1,2048,2048]{2,1,0:T(8,128)(2,1)} %param.6, bf16[2048,8,64]{0,2,1:T(8,128)(2,1)S(1)} %get-tuple-element.4, bf16[2048,8,64]{0,2,1:T(8,128)(2,1)} %get-tuple-element.5), kind=kOutput, calls=%fused_computation.6 | convolution fusion | flops 8598323200 | bytes 20971520 | tf_op jit(solution)/shard_map/mhr,mn->hrn/dot_general | solution.py:77
  45.7 0.0 copy-start
  45.7 0.0 copy-start.2
  45.8 1.1 multiply_reduce_fusion
  46.9 2.1 %copy-done = f32[8,128,2048]{2,1,0:T(8,128)} copy-done((f32[8,128,2048]{2,1,0:T(8,128)}, f32[8,128,2048]{2,1,0:T(8,128)S(1)}, u32[]{:S(2)}) %copy-start) | copy-done | bytes 8388632
  49.0 1.2 %collective-permute-start.5 = (f32[8,2048]{1,0:T(8,128)S(1)}, f32[8,2048]{1,0:T(8,128)S(1)}, u32[]{:S(2)}, u32[]{:S(2)}) collective-permute-start(f32[8,2048]{1,0:T(8,128)S(1)} %multiply_reduce_fusion), channel_id=1, source_target_pairs={{0,1},{1,0},{2,3},{3,2},{4,5},{5,4},{6,7},{7,6},{8,9},{9,8},{10,11... | collective-permute-start | bytes 196616 | tf_op jit(solution)/shard_map/ppermute | solution.py:19
  50.2 3.1 %collective-permute-done.5 = f32[8,2048]{1,0:T(8,128)S(1)} collective-permute-done((f32[8,2048]{1,0:T(8,128)S(1)}, f32[8,2048]{1,0:T(8,128)S(1)}, u32[]{:S(2)}, u32[]{:S(2)}) %collective-permute-start.5) | collective-permute-done | bytes 65568 | tf_op jit(solution)/shard_map/ppermute | solution.py:19
  53.3 1.6 %collective-permute-start.6 = (f32[8,2048]{1,0:T(8,128)S(1)}, f32[8,2048]{1,0:T(8,128)S(1)}, u32[]{:S(2)}, u32[]{:S(2)}) collective-permute-start(f32[8,2048]{1,0:T(8,128)S(1)} %add.77), channel_id=1, source_target_pairs={{0,2},{1,3},{2,0},{3,1},{4,6},{5,7},{6,4},{7,5},{8,10},{9,11},{10,... | collective-permute-start | bytes 196616 | tf_op jit(solution)/shard_map/ppermute | solution.py:19
  54.8 4.5 %collective-permute-done.6 = f32[8,2048]{1,0:T(8,128)S(1)} collective-permute-done((f32[8,2048]{1,0:T(8,128)S(1)}, f32[8,2048]{1,0:T(8,128)S(1)}, u32[]{:S(2)}, u32[]{:S(2)}) %collective-permute-start.6) | collective-permute-done | bytes 65568 | tf_op jit(solution)/shard_map/ppermute | solution.py:19
  59.3 1.1 collective-permute-start.7
  60.4 3.2 %collective-permute-done.7 = f32[8,2048]{1,0:T(8,128)S(1)} collective-permute-done((f32[8,2048]{1,0:T(8,128)S(1)}, f32[8,2048]{1,0:T(8,128)S(1)}, u32[]{:S(2)}, u32[]{:S(2)}) %collective-permute-start.7) | collective-permute-done | bytes 65568 | tf_op jit(solution)/shard_map/ppermute | solution.py:19
  63.7 0.0 copy-done.2
  63.7 0.7 fusion.30
  64.3 9.5 %fusion.2 = f32[8,64,2048]{2,1,0:T(8,128)S(1)} fusion(bf16[1,2048,2048]{2,1,0:T(8,128)(2,1)} %param.6, f32[8,2048]{1,0:T(8,128)S(1)} %get-tuple-element.2, f32[8,128,2048]{2,1,0:T(8,128)} %copy-done), kind=kOutput, calls=%fused_computation.4 | convolution fusion | flops 4298113024 | bytes 21037056 | tf_op jit(solution)/shard_map/mn,hrn->mhr/dot_general | solution.py:86
  73.8 8.9 %fusion.17 = f32[256,8,64]{0,2,1:T(8,128)S(1)} fusion(s32[8,256]{1,0:T(8,128)S(1)} %bitcast.110, f32[8,64,2048]{2,1,0:T(8,128)S(1)} %fusion.2, f32[256,8]{0,1:T(8,128)S(1)} %bitcast.112), kind=kOutput, calls=%fused_computation.23 | convolution fusion | flops 3225550848 | bytes 4734976 | tf_op jit(solution)/shard_map/hkm,mhr->khr/dot_general | solution.py:87
  82.7 0.0 copy-start.1
  82.7 0.2 copy.19
  82.9 2.3 %scatter_custom_fusion = f32[512,512]{1,0:T(8,128)S(1)} fusion(s32[256]{0:T(256)S(1)} %bitcast.114, f32[256,512]{1,0:T(8,128)S(1)} %copy.19, f32[]{:T(128)} %constant.58.clone.1), kind=kCustom, calls=%fused_computation.28 | custom fusion | flops 131072 | bytes 1048580 | tf_op jit(solution)/shard_map/scatter-add | solution.py:95
  85.3 0.1 collective-permute-start.8
  85.5 1.9 %collective-permute-done.8 = f32[2,2,2,2,16,512]{5,4,3,2,1,0:T(8,128)S(1)} collective-permute-done((f32[2,2,2,2,16,512]{5,4,3,2,1,0:T(8,128)S(1)}, f32[2,2,2,2,16,512]{5,4,3,2,1,0:T(8,128)S(1)}, u32[]{:S(2)}, u32[]{:S(2)}) %collective-permute-start.8) | collective-permute-done | bytes 524320 | tf_op jit(solution)/shard_map/ppermute | solution.py:19
  87.3 0.1 bitcast_add_fusion
  87.4 0.1 constant_dynamic-slice_fusion.1
  87.5 1.7 %collective-permute-start.9 = (f32[2,2,2,16,512]{4,3,1,0,2:T(8,128)S(1)}, f32[2,2,2,16,512]{4,3,1,0,2:T(8,128)S(1)}, u32[]{:S(2)}, u32[]{:S(2)}) collective-permute-start(f32[2,2,2,16,512]{4,3,1,0,2:T(8,128)S(1)} %bitcast.108), channel_id=1, source_target_pairs={{0,16},{8,24},{16,0},{24,8},{32,48},{40,56},{48,32},{56,40},{64,80... | collective-permute-start | bytes 786440 | tf_op jit(solution)/shard_map/ppermute | solution.py:19
  89.2 6.8 %collective-permute-done.9 = f32[2,2,2,16,512]{4,3,1,0,2:T(8,128)S(1)} collective-permute-done((f32[2,2,2,16,512]{4,3,1,0,2:T(8,128)S(1)}, f32[2,2,2,16,512]{4,3,1,0,2:T(8,128)S(1)}, u32[]{:S(2)}, u32[]{:S(2)}) %collective-permute-start.9) | collective-permute-done | bytes 262176 | tf_op jit(solution)/shard_map/ppermute | solution.py:19
  96.0 4.0 %collective-permute-start.10 = (f32[2,2,16,512]{3,2,1,0:T(8,128)S(1)}, f32[2,2,16,512]{3,2,1,0:T(8,128)S(1)}, u32[]{:S(2)}, u32[]{:S(2)}) collective-permute-start(f32[2,2,16,512]{3,2,1,0:T(8,128)S(1)} %dynamic-slice_bitcast_fusion.1), channel_id=1, source_target_pairs={{0,32},{8,40},{16,48},{24,56},{32,0},{40,8},{48,16},{56,24},{64,96... | collective-permute-start | bytes 393224 | tf_op jit(solution)/shard_map/ppermute | solution.py:19
  100.0 2.9 %collective-permute-done.10 = f32[2,2,16,512]{3,2,1,0:T(8,128)S(1)} collective-permute-done((f32[2,2,16,512]{3,2,1,0:T(8,128)S(1)}, f32[2,2,16,512]{3,2,1,0:T(8,128)S(1)}, u32[]{:S(2)}, u32[]{:S(2)}) %collective-permute-start.10) | collective-permute-done | bytes 131104 | tf_op jit(solution)/shard_map/ppermute | solution.py:19
  103.0 2.1 %collective-permute-start.11 = (f32[2,16,512]{2,1,0:T(8,128)S(1)}, f32[2,16,512]{2,1,0:T(8,128)S(1)}, u32[]{:S(2)}, u32[]{:S(2)}) collective-permute-start(f32[2,16,512]{2,1,0:T(8,128)S(1)} %dynamic-slice_bitcast_fusion.2), channel_id=1, source_target_pairs={{0,64},{8,72},{16,80},{24,88},{32,96},{40,104},{48,112},{56,120},{... | collective-permute-start | bytes 196616 | tf_op jit(solution)/shard_map/ppermute | solution.py:19
  105.1 3.9 %collective-permute-done.11 = f32[2,16,512]{2,1,0:T(8,128)S(1)} collective-permute-done((f32[2,16,512]{2,1,0:T(8,128)S(1)}, f32[2,16,512]{2,1,0:T(8,128)S(1)}, u32[]{:S(2)}, u32[]{:S(2)}) %collective-permute-start.11) | collective-permute-done | bytes 65568 | tf_op jit(solution)/shard_map/ppermute | solution.py:19
  109.0 6.0 %collective-permute-start.12 = (f32[16,512]{1,0:T(8,128)S(1)}, f32[16,512]{1,0:T(8,128)S(1)}, u32[]{:S(2)}, u32[]{:S(2)}) collective-permute-start(f32[16,512]{1,0:T(8,128)S(1)} %dynamic-slice_bitcast_fusion.3), channel_id=1, source_target_pairs={{0,128},{8,136},{16,144},{24,152},{32,160},{40,168},{48,176},{56,1... | collective-permute-start | bytes 98312 | tf_op jit(solution)/shard_map/ppermute | solution.py:19
  115.0 2.2 %collective-permute-done.12 = f32[16,512]{1,0:T(8,128)S(1)} collective-permute-done((f32[16,512]{1,0:T(8,128)S(1)}, f32[16,512]{1,0:T(8,128)S(1)}, u32[]{:S(2)}, u32[]{:S(2)}) %collective-permute-start.12) | collective-permute-done | bytes 32800 | tf_op jit(solution)/shard_map/ppermute | solution.py:19
  117.3 0.1 mul.71
  117.4 0.0 copy-done.1
  117.4 0.6 sub.31
  (20 shorter events, 0.4 us)
Async XLA Ops:
  0.6 27.9 %copy-start.3 = (s32[1,8,256]{2,1,0:T(8,128)S(1)}, s32[1,8,256]{2,1,0:T(8,128)}, u32[]{:S(2)}) copy-start(s32[1,8,256]{2,1,0:T(8,128)} %param.9) | copy-start | bytes 24580
  0.6 27.9 %copy-start.5 = (s32[1,256]{1,0:T(1,128)S(1)}, s32[1,256]{1,0:T(1,128)}, u32[]{:S(2)}) copy-start(s32[1,256]{1,0:T(1,128)} %param.10) | copy-start | bytes 3076
  0.7 27.9 %copy-start.4 = (f32[1,8,256]{2,1,0:T(8,128)S(1)}, f32[1,8,256]{2,1,0:T(8,128)}, u32[]{:S(2)}) copy-start(f32[1,8,256]{2,1,0:T(8,128)} %param.8) | copy-start | bytes 24580
  1.6 9.0 %collective-permute-start = (bf16[16,512]{1,0:T(8,128)(2,1)S(1)}, bf16[16,512]{1,0:T(8,128)(2,1)S(1)}, u32[]{:S(2)}, u32[]{:S(2)}) collective-permute-start(bf16[16,512]{1,0:T(8,128)(2,1)S(1)} %reshape.36), channel_id=1, source_target_pairs={{0,128},{8,136},{16,144},{24,152},{32,160},{40,168},{48,176},{56,1... | collective-permute-start | bytes 49160 | tf_op jit(solution)/shard_map/ppermute | solution.py:19
  10.6 4.9 %collective-permute-start.1 = (bf16[2,16,512]{2,1,0:T(8,128)(2,1)S(1)}, bf16[2,16,512]{2,1,0:T(8,128)(2,1)S(1)}, u32[]{:S(2)}, u32[]{:S(2)}) collective-permute-start(bf16[2,16,512]{2,1,0:T(8,128)(2,1)S(1)} %pad_maximum_fusion.4), channel_id=1, source_target_pairs={{0,64},{8,72},{16,80},{24,88},{32,96},{40,104},{48,112},{56,120},{... | collective-permute-start | bytes 98312 | tf_op jit(solution)/shard_map/ppermute | solution.py:19
  15.6 5.9 %collective-permute-start.2 = (bf16[2,2,16,512]{3,2,1,0:T(8,128)(2,1)S(1)}, bf16[2,2,16,512]{3,2,1,0:T(8,128)(2,1)S(1)}, u32[]{:S(2)}, u32[]{:S(2)}) collective-permute-start(bf16[2,2,16,512]{3,2,1,0:T(8,128)(2,1)S(1)} %pad_maximum_fusion.3), channel_id=1, source_target_pairs={{0,32},{8,40},{16,48},{24,56},{32,0},{40,8},{48,16},{56,24},{64,96... | collective-permute-start | bytes 196616 | tf_op jit(solution)/shard_map/ppermute | solution.py:19
  21.5 5.1 %collective-permute-start.3 = (bf16[2,2,2,16,512]{4,3,2,1,0:T(8,128)(2,1)S(1)}, bf16[2,2,2,16,512]{4,3,2,1,0:T(8,128)(2,1)S(1)}, u32[]{:S(2)}, u32[]{:S(2)}) collective-permute-start(bf16[2,2,2,16,512]{4,3,2,1,0:T(8,128)(2,1)S(1)} %pad_maximum_fusion.2), channel_id=1, source_target_pairs={{0,16},{8,24},{16,0},{24,8},{32,48},{40,56},{48,32},{56,40},{64,80... | collective-permute-start | bytes 393224 | tf_op jit(solution)/shard_map/ppermute | solution.py:19
  26.6 1.6 %collective-permute-start.4 = (bf16[2,2,2,2,16,512]{5,4,3,2,1,0:T(8,128)(2,1)S(1)}, bf16[2,2,2,2,16,512]{5,4,3,2,1,0:T(8,128)(2,1)S(1)}, u32[]{:S(2)}, u32[]{:S(2)}) collective-permute-start(bf16[2,2,2,2,16,512]{5,4,3,2,1,0:T(8,128)(2,1)S(1)} %pad_maximum_fusion.1), channel_id=1, source_target_pairs={{0,8},{8,0},{16,24},{24,16},{32,40},{40,32},{48,56},{56,48},{64,72... | collective-permute-start | bytes 786440 | tf_op jit(solution)/shard_map/ppermute | solution.py:19
  45.7 3.2 %copy-start = (f32[8,128,2048]{2,1,0:T(8,128)}, f32[8,128,2048]{2,1,0:T(8,128)S(1)}, u32[]{:S(2)}) copy-start(f32[8,128,2048]{2,1,0:T(8,128)S(1)} %fusion.4) | copy-start | bytes 25165828
  45.7 17.9 %copy-start.2 = (f32[1,8,2048]{2,1,0:T(8,128)S(1)}, f32[1,8,2048]{2,1,0:T(8,128)}, u32[]{:S(2)}) copy-start(f32[1,8,2048]{2,1,0:T(8,128)} %param.7) | copy-start | bytes 196612
  49.0 4.3 %collective-permute-start.5 = (f32[8,2048]{1,0:T(8,128)S(1)}, f32[8,2048]{1,0:T(8,128)S(1)}, u32[]{:S(2)}, u32[]{:S(2)}) collective-permute-start(f32[8,2048]{1,0:T(8,128)S(1)} %multiply_reduce_fusion), channel_id=1, source_target_pairs={{0,1},{1,0},{2,3},{3,2},{4,5},{5,4},{6,7},{7,6},{8,9},{9,8},{10,11... | collective-permute-start | bytes 196616 | tf_op jit(solution)/shard_map/ppermute | solution.py:19
  53.3 6.0 %collective-permute-start.6 = (f32[8,2048]{1,0:T(8,128)S(1)}, f32[8,2048]{1,0:T(8,128)S(1)}, u32[]{:S(2)}, u32[]{:S(2)}) collective-permute-start(f32[8,2048]{1,0:T(8,128)S(1)} %add.77), channel_id=1, source_target_pairs={{0,2},{1,3},{2,0},{3,1},{4,6},{5,7},{6,4},{7,5},{8,10},{9,11},{10,... | collective-permute-start | bytes 196616 | tf_op jit(solution)/shard_map/ppermute | solution.py:19
  59.3 4.4 %collective-permute-start.7 = (f32[8,2048]{1,0:T(8,128)S(1)}, f32[8,2048]{1,0:T(8,128)S(1)}, u32[]{:S(2)}, u32[]{:S(2)}) collective-permute-start(f32[8,2048]{1,0:T(8,128)S(1)} %add.78), channel_id=1, source_target_pairs={{0,4},{1,5},{2,6},{3,7},{4,0},{5,1},{6,2},{7,3},{8,12},{9,13},{10,... | collective-permute-start | bytes 196616 | tf_op jit(solution)/shard_map/ppermute | solution.py:19
  82.7 34.6 %copy-start.1 = (f32[16,8,64]{2,1,0:T(8,128)S(1)}, f32[16,8,64]{2,1,0:T(8,128)}, u32[]{:S(2)}) copy-start(f32[16,8,64]{2,1,0:T(8,128)} %param.11) | copy-start | bytes 98308
  85.3 2.0 %collective-permute-start.8 = (f32[2,2,2,2,16,512]{5,4,3,2,1,0:T(8,128)S(1)}, f32[2,2,2,2,16,512]{5,4,3,2,1,0:T(8,128)S(1)}, u32[]{:S(2)}, u32[]{:S(2)}) collective-permute-start(f32[2,2,2,2,16,512]{5,4,3,2,1,0:T(8,128)S(1)} %dynamic-slice_bitcast_fusion), channel_id=1, source_target_pairs={{0,8},{8,0},{16,24},{24,16},{32,40},{40,32},{48,56},{56,48},{64,72... | collective-permute-start | bytes 1572872 | tf_op jit(solution)/shard_map/ppermute | solution.py:19
  87.5 8.4 %collective-permute-start.9 = (f32[2,2,2,16,512]{4,3,1,0,2:T(8,128)S(1)}, f32[2,2,2,16,512]{4,3,1,0,2:T(8,128)S(1)}, u32[]{:S(2)}, u32[]{:S(2)}) collective-permute-start(f32[2,2,2,16,512]{4,3,1,0,2:T(8,128)S(1)} %bitcast.108), channel_id=1, source_target_pairs={{0,16},{8,24},{16,0},{24,8},{32,48},{40,56},{48,32},{56,40},{64,80... | collective-permute-start | bytes 786440 | tf_op jit(solution)/shard_map/ppermute | solution.py:19
  96.0 6.9 %collective-permute-start.10 = (f32[2,2,16,512]{3,2,1,0:T(8,128)S(1)}, f32[2,2,16,512]{3,2,1,0:T(8,128)S(1)}, u32[]{:S(2)}, u32[]{:S(2)}) collective-permute-start(f32[2,2,16,512]{3,2,1,0:T(8,128)S(1)} %dynamic-slice_bitcast_fusion.1), channel_id=1, source_target_pairs={{0,32},{8,40},{16,48},{24,56},{32,0},{40,8},{48,16},{56,24},{64,96... | collective-permute-start | bytes 393224 | tf_op jit(solution)/shard_map/ppermute | solution.py:19
  103.0 6.0 %collective-permute-start.11 = (f32[2,16,512]{2,1,0:T(8,128)S(1)}, f32[2,16,512]{2,1,0:T(8,128)S(1)}, u32[]{:S(2)}, u32[]{:S(2)}) collective-permute-start(f32[2,16,512]{2,1,0:T(8,128)S(1)} %dynamic-slice_bitcast_fusion.2), channel_id=1, source_target_pairs={{0,64},{8,72},{16,80},{24,88},{32,96},{40,104},{48,112},{56,120},{... | collective-permute-start | bytes 196616 | tf_op jit(solution)/shard_map/ppermute | solution.py:19
  109.0 8.3 %collective-permute-start.12 = (f32[16,512]{1,0:T(8,128)S(1)}, f32[16,512]{1,0:T(8,128)S(1)}, u32[]{:S(2)}, u32[]{:S(2)}) collective-permute-start(f32[16,512]{1,0:T(8,128)S(1)} %dynamic-slice_bitcast_fusion.3), channel_id=1, source_target_pairs={{0,128},{8,136},{16,144},{24,152},{32,160},{40,168},{48,176},{56,1... | collective-permute-start | bytes 98312 | tf_op jit(solution)/shard_map/ppermute | solution.py:19

commit v2 on v1

--- a/solution.py
+++ b/solution.py
@@ -55,6 +55,15 @@
     return x
 
 
+CHUNKS = 2
+
+
+def _split_bf16(x):
+    high = x.astype(jnp.bfloat16)
+    low = (x - high.astype(jnp.float32)).astype(jnp.bfloat16)
+    return high, low
+
+
 def shards(sensitivity, headroom, ev_power, ev_node, region_map, loadings):
     reg_local, hours, columns = loadings.shape
     nodes = sensitivity.shape[2]
@@ -68,33 +77,35 @@
     looked = looked.reshape(ev_count, hours, columns)
     power = ev_power[0].T
     weighted = (power[:, :, None] * looked).astype(jnp.bfloat16)
-    node_hot = (ev_node[0][:, :, None] == lax.iota(jnp.int32, nodes)[None, None, :]).astype(jnp.bfloat16)
-    spread = jnp.einsum("hkm,khr->mhr", node_hot, weighted, preferred_element_type=jnp.float32)
-    spread_hi = spread.astype(jnp.bfloat16)
-    spread_lo = (spread - spread_hi.astype(jnp.float32)).astype(jnp.bfloat16)
-    both = jnp.concatenate([spread_hi, spread_lo], axis=2)
     sens = sensitivity[0]
-    volts_both = jnp.einsum("mhr,mn->hrn", both, sens, preferred_element_type=jnp.float32)
-    factor_volts = volts_both[:, :columns] + volts_both[:, columns:]
-    partial_sum = jnp.sum(factor_volts * factor_volts, axis=1)
-    variance = sum_all(partial_sum, "factor")[None]
-    deviation = jnp.sqrt(variance + epsilon)
-    margin = headroom - quantile * deviation
-    violation = jnp.maximum(-margin, 0.0)
-    var_grad = quantile * violation / deviation
-    volt_grad = (2.0 * var_grad[0][:, None, :] * factor_volts).astype(jnp.bfloat16)
-    node_grads = jnp.einsum("mn,hrn->mhr", sens, volt_grad, preferred_element_type=jnp.float32)
-    picked = jnp.einsum(
-        "hkm,mhr->khr",
-        node_hot,
-        node_grads,
-        precision=lax.Precision.HIGHEST,
-        preferred_element_type=jnp.float32,
-    )
-    member_grads = (power[:, :, None] * picked).reshape(ev_count, hours * columns)
-    summed = jax.ops.segment_sum(member_grads, regions, num_segments=total_regions)
-    reduced = scatter_blocks(summed, "feeder")
-    new_loadings = loadings - step_size * reduced.reshape(reg_local, hours, columns)
+    span = hours // CHUNKS
+    margins = []
+    steps = []
+    for chunk in range(CHUNKS):
+        at = slice(chunk * span, (chunk + 1) * span)
+        node_hot = (ev_node[0, at][:, :, None] == lax.iota(jnp.int32, nodes)[None, None, :]).astype(jnp.bfloat16)
+        spread = jnp.einsum("hkm,khr->mhr", node_hot, weighted[:, at], preferred_element_type=jnp.float32)
+        both = jnp.concatenate(_split_bf16(spread), axis=2)
+        volts_both = jnp.einsum("mhr,mn->hrn", both, sens, preferred_element_type=jnp.float32)
+        factor_volts = volts_both[:, :columns] + volts_both[:, columns:]
+        partial_sum = jnp.sum(factor_volts * factor_volts, axis=1)
+        variance = sum_all(partial_sum, "factor")
+        deviation = jnp.sqrt(variance + epsilon)
+        margin = headroom[0, at] - quantile * deviation
+        violation = jnp.maximum(-margin, 0.0)
+        var_grad = quantile * violation / deviation
+        volt_grad = (2.0 * var_grad[:, None, :] * factor_volts).astype(jnp.bfloat16)
+        node_grads = jnp.einsum("mn,hrn->mhr", sens, volt_grad, preferred_element_type=jnp.float32)
+        grads_hi, grads_lo = _split_bf16(node_grads)
+        picked = jnp.einsum("hkm,mhr->khr", node_hot, grads_hi, preferred_element_type=jnp.float32)
+        picked = picked + jnp.einsum("hkm,mhr->khr", node_hot, grads_lo, preferred_element_type=jnp.float32)
+        member_grads = (power[:, at, None] * picked).reshape(ev_count, span * columns)
+        summed = jax.ops.segment_sum(member_grads, regions, num_segments=total_regions)
+        reduced = scatter_blocks(summed, "feeder")
+        margins.append(margin)
+        steps.append(reduced.reshape(reg_local, span, columns))
+    margin = jnp.concatenate(margins, axis=0)[None]
+    new_loadings = loadings - step_size * jnp.concatenate(steps, axis=1)
     return (margin, new_loadings)
 
 

time: 118 us -> 125 us (1.059)
  starting transfers between devices: 32.1 us -> 43.7 us
  waiting for transfers between devices: 40.5 us -> 31.6 us
  local copies, waits for them, and re-layouts: 2.9 us -> 5.01 us
  other arithmetic: 5.99 us -> 7.7 us
    ppermute x13 -> x21, starting transfers between devices: 32.1 us -> 43.7 us  [_exchange(): return lax.ppermute(x, axis, perm)]
    ppermute x13 -> x21, waiting for transfers between devices: 40.5 us -> 31.6 us  [_exchange(): return lax.ppermute(x, axis, perm)]
    dot_general x1 -> x2, matrix products: 9.49 us -> 14.1 us  [shards(): jnp.einsum('mn,hrn->mhr', sens, volt_grad, preferred_element_type=jnp.flo...]
    dot_general x1 -> x2, matrix products: 12.1 us -> 9.12 us  [shards(): jnp.einsum('mhr,mn->hrn', both, sens, preferred_element_type=jnp.float32)]
    unnamed x12 -> x16, local copies, waits for them, and re-layouts: 2.14 us -> 4.06 us
    scatter-add x1 -> x2, other arithmetic: 2.34 us -> 4.15 us  [shards(): jax.ops.segment_sum(member_grads, regions, num_segments=total_regions)]
    dot_general x2 -> x7, matrix products: 14 us -> 12.3 us  [the longest x2 4.03 us: shards(): jnp.einsum('hkm,mhr->khr', node_hot, grads_lo, preferred_element_type=jnp...]
  transfers between devices with their start and end apart: 13 -> 21, of which waited for: 13 -> 13; matrix products, arithmetic and copies ran while one was open for 0% -> 17% of each run, Pallas kernels for 0% -> 0%
where the time goes in v2:
time: 125 us
  starting transfers between devices  43.7 us (35%)
  matrix products  35.5 us (28%)
  waiting for transfers between devices  31.6 us (25%)
  other arithmetic  7.7 us (6%)
  local copies, waits for them, and re-layouts  5.01 us (4%)
    ppermute x21, starting transfers between devices, _exchange(): return lax.ppermute(x, axis, perm)  43.7 us
    ppermute x21, waiting for transfers between devices, _exchange(): return lax.ppermute(x, axis, perm)  31.6 us
    dot_general x2, matrix products, shards(): jnp.einsum('mn,hrn->mhr', sens, volt_grad, preferred_element_type=jnp.flo...  14.1 us
    dot_general x2, matrix products, shards(): jnp.einsum('mhr,mn->hrn', both, sens, preferred_element_type=jnp.float32)  9.12 us
    scatter-add x2, other arithmetic, shards(): jax.ops.segment_sum(member_grads, regions, num_segments=total_regions)  4.15 us
    unnamed x16, local copies, waits for them, and re-layouts  4.06 us
    dot_general x2, matrix products, shards(): jnp.einsum('hkm,mhr->khr', node_hot, grads_lo, preferred_element_type=jnp...  4.03 us
    dot_general x2, matrix products, shards(): jnp.einsum('hkm,mhr->khr', node_hot, grads_hi, preferred_element_type=jnp...  3.96 us
  transfers between devices with their start and end apart: 21, of which 13 were waited for; matrix products, arithmetic and copies ran while one was open for 17% of the time, Pallas kernels for 0%

profile of v2, /device:TPU:4, one launch (start us, length us, event | category | flops | bytes accessed | tf_op | source)
XLA Modules:
  0.0 124.6 jit_solution(2917525206548119826)
XLA Ops:
  0.6 0.9 convert_element_type.51
  1.5 0.1 reshape.40
  1.6 7.3 %collective-permute-start = (bf16[16,512]{1,0:T(8,128)(2,1)S(1)}, bf16[16,512]{1,0:T(8,128)(2,1)S(1)}, u32[]{:S(2)}, u32[]{:S(2)}) collective-permute-start(bf16[16,512]{1,0:T(8,128)(2,1)S(1)} %reshape.40), channel_id=1, source_target_pairs={{0,128},{8,136},{16,144},{24,152},{32,160},{40,168},{48,176},{56,1... | collective-permute-start | bytes 49160 | tf_op jit(solution)/shard_map/ppermute | solution.py:19
  8.9 1.7 %collective-permute-done = bf16[16,512]{1,0:T(8,128)(2,1)S(1)} collective-permute-done((bf16[16,512]{1,0:T(8,128)(2,1)S(1)}, bf16[16,512]{1,0:T(8,128)(2,1)S(1)}, u32[]{:S(2)}, u32[]{:S(2)}) %collective-permute-start) | collective-permute-done | bytes 16416 | tf_op jit(solution)/shard_map/ppermute | solution.py:19
  10.6 2.1 %collective-permute-start.1 = (bf16[2,16,512]{2,1,0:T(8,128)(2,1)S(1)}, bf16[2,16,512]{2,1,0:T(8,128)(2,1)S(1)}, u32[]{:S(2)}, u32[]{:S(2)}) collective-permute-start(bf16[2,16,512]{2,1,0:T(8,128)(2,1)S(1)} %pad_maximum_fusion.4), channel_id=1, source_target_pairs={{0,64},{8,72},{16,80},{24,88},{32,96},{40,104},{48,112},{56,120},{... | collective-permute-start | bytes 98312 | tf_op jit(solution)/shard_map/ppermute | solution.py:19
  12.7 2.8 %collective-permute-done.1 = bf16[2,16,512]{2,1,0:T(8,128)(2,1)S(1)} collective-permute-done((bf16[2,16,512]{2,1,0:T(8,128)(2,1)S(1)}, bf16[2,16,512]{2,1,0:T(8,128)(2,1)S(1)}, u32[]{:S(2)}, u32[]{:S(2)}) %collective-permute-start.1) | collective-permute-done | bytes 32800 | tf_op jit(solution)/shard_map/ppermute | solution.py:19
  15.5 3.3 %collective-permute-start.2 = (bf16[2,2,16,512]{3,2,1,0:T(8,128)(2,1)S(1)}, bf16[2,2,16,512]{3,2,1,0:T(8,128)(2,1)S(1)}, u32[]{:S(2)}, u32[]{:S(2)}) collective-permute-start(bf16[2,2,16,512]{3,2,1,0:T(8,128)(2,1)S(1)} %pad_maximum_fusion.3), channel_id=1, source_target_pairs={{0,32},{8,40},{16,48},{24,56},{32,0},{40,8},{48,16},{56,24},{64,96... | collective-permute-start | bytes 196616 | tf_op jit(solution)/shard_map/ppermute | solution.py:19
  18.8 2.6 %collective-permute-done.2 = bf16[2,2,16,512]{3,2,1,0:T(8,128)(2,1)S(1)} collective-permute-done((bf16[2,2,16,512]{3,2,1,0:T(8,128)(2,1)S(1)}, bf16[2,2,16,512]{3,2,1,0:T(8,128)(2,1)S(1)}, u32[]{:S(2)}, u32[]{:S(2)}) %collective-permute-start.2) | collective-permute-done | bytes 65568 | tf_op jit(solution)/shard_map/ppermute | solution.py:19
  21.4 1.7 %collective-permute-start.3 = (bf16[2,2,2,16,512]{4,3,2,1,0:T(8,128)(2,1)S(1)}, bf16[2,2,2,16,512]{4,3,2,1,0:T(8,128)(2,1)S(1)}, u32[]{:S(2)}, u32[]{:S(2)}) collective-permute-start(bf16[2,2,2,16,512]{4,3,2,1,0:T(8,128)(2,1)S(1)} %pad_maximum_fusion.2), channel_id=1, source_target_pairs={{0,16},{8,24},{16,0},{24,8},{32,48},{40,56},{48,32},{56,40},{64,80... | collective-permute-start | bytes 393224 | tf_op jit(solution)/shard_map/ppermute | solution.py:19
  23.1 3.4 %collective-permute-done.3 = bf16[2,2,2,16,512]{4,3,2,1,0:T(8,128)(2,1)S(1)} collective-permute-done((bf16[2,2,2,16,512]{4,3,2,1,0:T(8,128)(2,1)S(1)}, bf16[2,2,2,16,512]{4,3,2,1,0:T(8,128)(2,1)S(1)}, u32[]{:S(2)}, u32[]{:S(2)}) %collective-permute-start.3) | collective-permute-done | bytes 131104 | tf_op jit(solution)/shard_map/ppermute | solution.py:19
  26.5 0.1 collective-permute-start.4
  26.7 1.5 %collective-permute-done.4 = bf16[2,2,2,2,16,512]{5,4,3,2,1,0:T(8,128)(2,1)S(1)} collective-permute-done((bf16[2,2,2,2,16,512]{5,4,3,2,1,0:T(8,128)(2,1)S(1)}, bf16[2,2,2,2,16,512]{5,4,3,2,1,0:T(8,128)(2,1)S(1)}, u32[]{:S(2)}, u32[]{:S(2)}) %collective-permute-start.4) | collective-permute-done | bytes 262176 | tf_op jit(solution)/shard_map/ppermute | solution.py:19
  28.2 0.1 pad_maximum_fusion
  28.3 0.2 copy.20
  28.5 0.0 copy-start.6
  28.5 0.4 fusion.34
  28.9 1.9 %subtract_convert_fusion.2 = (bf16[2048,4,64]{0,2,1:T(8,128)(2,1)S(1)}, bf16[2048,4,64]{0,2,1:T(8,128)(2,1)S(1)}) fusion(bf16[256,8,64]{0,2,1:T(8,128)(2,1)S(1)} %fusion.34, s32[4,256]{1,0:T(4,128)S(1)} %get-tuple-element.29), kind=kOutput, calls=%fused_computation.41 | convolution fusion | flops 272629760 | bytes 2363392 | tf_op jit(solution)/shard_map/hkm,khr->mhr/dot_general | solution.py:87
  30.9 1.0 copy-done.6
  31.9 4.6 %fusion.4 = f32[4,128,2048]{2,1,0:T(8,128)S(1)} fusion(bf16[1,2048,2048]{2,1,0:T(8,128)(2,1)S(1)} %copy-done.6, bf16[2048,4,64]{0,2,1:T(8,128)(2,1)S(1)} %get-tuple-element.4, bf16[2048,4,64]{0,2,1:T(8,128)(2,1)S(1)} %get-tuple-element.5), kind=kOutput, calls=%fused_computation.6 | convolution fusion | flops 4299161600 | bytes 14680064 | tf_op jit(solution)/shard_map/mhr,mn->hrn/dot_general | solution.py:89
  36.5 0.5 multiply_reduce_fusion
  36.9 1.5 %copy-done = f32[4,128,2048]{2,1,0:T(8,128)} copy-done((f32[4,128,2048]{2,1,0:T(8,128)}, f32[4,128,2048]{2,1,0:T(8,128)S(1)}, u32[]{:S(2)}) %copy-start) | copy-done | bytes 4194328
  38.4 1.2 collective-permute-start.8
  39.6 1.9 %subtract_convert_fusion.3 = (bf16[2048,4,64]{0,2,1:T(8,128)(2,1)S(1)}, bf16[2048,4,64]{0,2,1:T(8,128)(2,1)S(1)}) fusion(bf16[256,8,64]{0,2,1:T(8,128)(2,1)S(1)} %fusion.34, s32[4,256]{1,0:T(4,128)S(1)} %get-tuple-element.28), kind=kOutput, calls=%fused_computation.43 | convolution fusion | flops 272629760 | bytes 2363392 | tf_op jit(solution)/shard_map/hkm,khr->mhr/dot_general | solution.py:87
  41.5 4.6 %fusion.6 = f32[4,128,2048]{2,1,0:T(8,128)S(1)} fusion(bf16[1,2048,2048]{2,1,0:T(8,128)(2,1)S(1)} %copy-done.6, bf16[2048,4,64]{0,2,1:T(8,128)(2,1)S(1)} %get-tuple-element.2, bf16[2048,4,64]{0,2,1:T(8,128)(2,1)S(1)} %get-tuple-element.3), kind=kOutput, calls=%fused_computation.8 | convolution fusion | flops 4299161600 | bytes 14680064 | tf_op jit(solution)/shard_map/mhr,mn->hrn/dot_general | solution.py:89
  46.1 0.5 multiply_reduce_fusion.1
  46.6 1.5 %copy-done.1 = f32[4,128,2048]{2,1,0:T(8,128)} copy-done((f32[4,128,2048]{2,1,0:T(8,128)}, f32[4,128,2048]{2,1,0:T(8,128)S(1)}, u32[]{:S(2)}) %copy-start.1) | copy-done | bytes 4194328
  48.1 0.8 collective-permute-start.5
  49.0 1.4 %collective-permute-start.9 = (f32[4,2048]{1,0:T(4,128)S(1)}, f32[4,2048]{1,0:T(4,128)S(1)}, u32[]{:S(2)}, u32[]{:S(2)}) collective-permute-start(f32[4,2048]{1,0:T(4,128)S(1)} %add.132), channel_id=1, source_target_pairs={{0,2},{1,3},{2,0},{3,1},{4,6},{5,7},{6,4},{7,5},{8,10},{9,11},{10,... | collective-permute-start | bytes 98312 | tf_op jit(solution)/shard_map/ppermute | solution.py:19
  50.4 1.9 %collective-permute-done.5 = f32[4,2048]{1,0:T(4,128)S(1)} collective-permute-done((f32[4,2048]{1,0:T(4,128)S(1)}, f32[4,2048]{1,0:T(4,128)S(1)}, u32[]{:S(2)}, u32[]{:S(2)}) %collective-permute-start.5) | collective-permute-done | bytes 32800 | tf_op jit(solution)/shard_map/ppermute | solution.py:19
  52.3 0.7 collective-permute-start.6
  53.0 1.5 %collective-permute-done.9 = f32[4,2048]{1,0:T(4,128)S(1)} collective-permute-done((f32[4,2048]{1,0:T(4,128)S(1)}, f32[4,2048]{1,0:T(4,128)S(1)}, u32[]{:S(2)}, u32[]{:S(2)}) %collective-permute-start.9) | collective-permute-done | bytes 32800 | tf_op jit(solution)/shard_map/ppermute | solution.py:19
  54.5 1.1 collective-permute-start.10
  55.6 2.2 %collective-permute-done.6 = f32[4,2048]{1,0:T(4,128)S(1)} collective-permute-done((f32[4,2048]{1,0:T(4,128)S(1)}, f32[4,2048]{1,0:T(4,128)S(1)}, u32[]{:S(2)}, u32[]{:S(2)}) %collective-permute-start.6) | collective-permute-done | bytes 32800 | tf_op jit(solution)/shard_map/ppermute | solution.py:19
  57.8 1.3 %collective-permute-start.7 = (f32[4,2048]{1,0:T(4,128)S(1)}, f32[4,2048]{1,0:T(4,128)S(1)}, u32[]{:S(2)}, u32[]{:S(2)}) collective-permute-start(f32[4,2048]{1,0:T(4,128)S(1)} %add.128), channel_id=1, source_target_pairs={{0,4},{1,5},{2,6},{3,7},{4,0},{5,1},{6,2},{7,3},{8,12},{9,13},{10,... | collective-permute-start | bytes 98312 | tf_op jit(solution)/shard_map/ppermute | solution.py:19
  59.2 2.9 %collective-permute-done.7 = f32[4,2048]{1,0:T(4,128)S(1)} collective-permute-done((f32[4,2048]{1,0:T(4,128)S(1)}, f32[4,2048]{1,0:T(4,128)S(1)}, u32[]{:S(2)}, u32[]{:S(2)}) %collective-permute-start.7) | collective-permute-done | bytes 32800 | tf_op jit(solution)/shard_map/ppermute | solution.py:19
  62.0 0.1 fusion.55
  62.1 7.0 %fusion.22 = f32[2048,4,64]{0,2,1:T(8,128)S(1)} fusion(bf16[1,2048,2048]{2,1,0:T(8,128)(2,1)} %param.6, f32[4,2048]{1,0:T(4,128)S(1)} %get-tuple-element.14, f32[4,128,2048]{2,1,0:T(8,128)} %copy-done.1), kind=kOutput, calls=%fused_computation.26 | convolution fusion | flops 2149056512 | bytes 14712832 | tf_op jit(solution)/shard_map/mn,hrn->mhr/dot_general | solution.py:98
  69.2 2.0 %fusion.11 = f32[4,64,256]{2,1,0:T(8,128)S(1)} fusion(s32[4,256]{1,0:T(4,128)S(1)} %get-tuple-element.28, f32[2048,4,64]{0,2,1:T(8,128)S(1)} %fusion.22), kind=kOutput, calls=%fused_computation.15 | convolution fusion | flops 272629760 | bytes 2363392 | tf_op jit(solution)/shard_map/hkm,mhr->khr/dot_general | solution.py:101
  71.2 2.0 %fusion.40 = f32[256,4,64]{0,2,1:T(8,128)S(1)} fusion(f32[4,64,256]{2,1,0:T(8,128)S(1)} %fusion.11, s32[4,256]{1,0:T(4,128)S(1)} %get-tuple-element.28, f32[2048,4,64]{0,2,1:T(8,128)S(1)} %fusion.22, f32[256,4]{0,1:T(4,128)S(1)} %get-tuple-element.26), kind=kOutput, calls=%fused_computation.51 | convolution fusion | flops 271187968 | bytes 2629632 | tf_op jit(solution)/shard_map/hkm,mhr->khr/dot_general | solution.py:100
  73.2 0.1 copy.21
  73.3 2.1 %scatter_custom_fusion = f32[512,256]{1,0:T(8,128)S(1)} fusion(s32[256]{0:T(256)S(1)} %bitcast.145, f32[256,256]{1,0:T(8,128)S(1)} %copy.21, f32[]{:T(128)} %constant.78.clone.1), kind=kCustom, calls=%fused_computation.68 | custom fusion | flops 65536 | bytes 524292 | tf_op jit(solution)/shard_map/scatter-add | solution.py:103
  75.4 0.1 collective-permute-start.11
  75.5 7.0 %fusion.25 = f32[2048,4,64]{0,2,1:T(8,128)S(1)} fusion(bf16[1,2048,2048]{2,1,0:T(8,128)(2,1)} %param.6, f32[4,2048]{1,0:T(4,128)S(1)} %get-tuple-element.21, f32[4,128,2048]{2,1,0:T(8,128)} %copy-done), kind=kOutput, calls=%fused_computation.27 | convolution fusion | flops 2149056512 | bytes 14712832 | tf_op jit(solution)/shard_map/mn,hrn->mhr/dot_general | solution.py:98
  82.6 2.0 %fusion.8 = f32[4,64,256]{2,1,0:T(8,128)S(1)} fusion(s32[4,256]{1,0:T(4,128)S(1)} %get-tuple-element.29, f32[2048,4,64]{0,2,1:T(8,128)S(1)} %fusion.25), kind=kOutput, calls=%fused_computation.11 | convolution fusion | flops 272629760 | bytes 2363392 | tf_op jit(solution)/shard_map/hkm,mhr->khr/dot_general | solution.py:101
  84.6 2.0 %fusion.39 = f32[256,4,64]{0,2,1:T(8,128)S(1)} fusion(f32[4,64,256]{2,1,0:T(8,128)S(1)} %fusion.8, s32[4,256]{1,0:T(4,128)S(1)} %get-tuple-element.29, f32[2048,4,64]{0,2,1:T(8,128)S(1)} %fusion.25, f32[256,4]{0,1:T(4,128)S(1)} %get-tuple-element.27), kind=kOutput, calls=%fused_computation.50 | convolution fusion | flops 271187968 | bytes 2629632 | tf_op jit(solution)/shard_map/hkm,mhr->khr/dot_general | solution.py:100
  86.6 0.1 copy.24
  86.7 2.1 %scatter_custom_fusion.1 = f32[512,256]{1,0:T(8,128)S(1)} fusion(s32[256]{0:T(256)S(1)} %bitcast.146, f32[256,256]{1,0:T(8,128)S(1)} %copy.24, f32[]{:T(128)} %constant.78.clone.1), kind=kCustom, calls=%fused_computation.66 | custom fusion | flops 65536 | bytes 524292 | tf_op jit(solution)/shard_map/scatter-add | solution.py:103
  88.8 0.8 collective-permute-start.16
  89.7 1.1 collective-permute-done.16
  90.9 1.7 %collective-permute-start.12 = (f32[2,2,2,16,256]{4,3,1,0,2:T(8,128)S(1)}, f32[2,2,2,16,256]{4,3,1,0,2:T(8,128)S(1)}, u32[]{:S(2)}, u32[]{:S(2)}) collective-permute-start(f32[2,2,2,16,256]{4,3,1,0,2:T(8,128)S(1)} %bitcast.141), channel_id=1, source_target_pairs={{0,16},{8,24},{16,0},{24,8},{32,48},{40,56},{48,32},{56,40},{64,80... | collective-permute-start | bytes 393224 | tf_op jit(solution)/shard_map/ppermute | solution.py:19
  92.6 0.6 maximum_bitcast_fusion
  93.3 0.5 collective-permute-start.17
  93.8 3.6 %collective-permute-done.12 = f32[2,2,2,16,256]{4,3,1,0,2:T(8,128)S(1)} collective-permute-done((f32[2,2,2,16,256]{4,3,1,0,2:T(8,128)S(1)}, f32[2,2,2,16,256]{4,3,1,0,2:T(8,128)S(1)}, u32[]{:S(2)}, u32[]{:S(2)}) %collective-permute-start.12) | collective-permute-done | bytes 131104 | tf_op jit(solution)/shard_map/ppermute | solution.py:19
  97.4 4.0 %collective-permute-start.13 = (f32[2,2,16,256]{3,2,1,0:T(8,128)S(1)}, f32[2,2,16,256]{3,2,1,0:T(8,128)S(1)}, u32[]{:S(2)}, u32[]{:S(2)}) collective-permute-start(f32[2,2,16,256]{3,2,1,0:T(8,128)S(1)} %dynamic-slice_bitcast_fusion.3), channel_id=1, source_target_pairs={{0,32},{8,40},{16,48},{24,56},{32,0},{40,8},{48,16},{56,24},{64,96... | collective-permute-start | bytes 196616 | tf_op jit(solution)/shard_map/ppermute | solution.py:19
  101.5 2.8 %collective-permute-start.18 = (f32[2,2,16,256]{3,2,1,0:T(8,128)S(1)}, f32[2,2,16,256]{3,2,1,0:T(8,128)S(1)}, u32[]{:S(2)}, u32[]{:S(2)}) collective-permute-start(f32[2,2,16,256]{3,2,1,0:T(8,128)S(1)} %dynamic-slice_bitcast_fusion.2), channel_id=1, source_target_pairs={{0,32},{8,40},{16,48},{24,56},{32,0},{40,8},{48,16},{56,24},{64,96... | collective-permute-start | bytes 196616 | tf_op jit(solution)/shard_map/ppermute | solution.py:19
  104.3 2.1 %collective-permute-start.14 = (f32[2,16,256]{2,1,0:T(8,128)S(1)}, f32[2,16,256]{2,1,0:T(8,128)S(1)}, u32[]{:S(2)}, u32[]{:S(2)}) collective-permute-start(f32[2,16,256]{2,1,0:T(8,128)S(1)} %dynamic-slice_bitcast_fusion.5), channel_id=1, source_target_pairs={{0,64},{8,72},{16,80},{24,88},{32,96},{40,104},{48,112},{56,120},{... | collective-permute-start | bytes 98312 | tf_op jit(solution)/shard_map/ppermute | solution.py:19
  106.4 1.0 collective-permute-done.18
  107.4 2.1 %collective-permute-start.19 = (f32[2,16,256]{2,1,0:T(8,128)S(1)}, f32[2,16,256]{2,1,0:T(8,128)S(1)}, u32[]{:S(2)}, u32[]{:S(2)}) collective-permute-start(f32[2,16,256]{2,1,0:T(8,128)S(1)} %dynamic-slice_bitcast_fusion.4), channel_id=1, source_target_pairs={{0,64},{8,72},{16,80},{24,88},{32,96},{40,104},{48,112},{56,120},{... | collective-permute-start | bytes 98312 | tf_op jit(solution)/shard_map/ppermute | solution.py:19
  109.5 6.6 %collective-permute-start.15 = (f32[16,256]{1,0:T(8,128)S(1)}, f32[16,256]{1,0:T(8,128)S(1)}, u32[]{:S(2)}, u32[]{:S(2)}) collective-permute-start(f32[16,256]{1,0:T(8,128)S(1)} %dynamic-slice_bitcast_fusion.7), channel_id=1, source_target_pairs={{0,128},{8,136},{16,144},{24,152},{32,160},{40,168},{48,176},{56,1... | collective-permute-start | bytes 49160 | tf_op jit(solution)/shard_map/ppermute | solution.py:19
  116.1 2.2 %collective-permute-start.20 = (f32[16,256]{1,0:T(8,128)S(1)}, f32[16,256]{1,0:T(8,128)S(1)}, u32[]{:S(2)}, u32[]{:S(2)}) collective-permute-start(f32[16,256]{1,0:T(8,128)S(1)} %dynamic-slice_bitcast_fusion.6), channel_id=1, source_target_pairs={{0,128},{8,136},{16,144},{24,152},{32,160},{40,168},{48,176},{56,1... | collective-permute-start | bytes 49160 | tf_op jit(solution)/shard_map/ppermute | solution.py:19
  118.3 0.1 reshape.44
  118.4 5.4 %collective-permute-done.20 = f32[16,256]{1,0:T(8,128)S(1)} collective-permute-done((f32[16,256]{1,0:T(8,128)S(1)}, f32[16,256]{1,0:T(8,128)S(1)}, u32[]{:S(2)}, u32[]{:S(2)}) %collective-permute-start.20) | collective-permute-done | bytes 16416 | tf_op jit(solution)/shard_map/ppermute | solution.py:19
  123.8 0.1 reshape.47
  123.9 0.7 fusion.54
  (56 shorter events, 0.6 us)
Async XLA Ops:
  0.6 26.0 %copy-start.4 = (s32[1,8,256]{2,1,0:T(8,128)S(1)}, s32[1,8,256]{2,1,0:T(8,128)}, u32[]{:S(2)}) copy-start(s32[1,8,256]{2,1,0:T(8,128)} %param.9) | copy-start | bytes 24580
  1.6 9.0 %collective-permute-start = (bf16[16,512]{1,0:T(8,128)(2,1)S(1)}, bf16[16,512]{1,0:T(8,128)(2,1)S(1)}, u32[]{:S(2)}, u32[]{:S(2)}) collective-permute-start(bf16[16,512]{1,0:T(8,128)(2,1)S(1)} %reshape.40), channel_id=1, source_target_pairs={{0,128},{8,136},{16,144},{24,152},{32,160},{40,168},{48,176},{56,1... | collective-permute-start | bytes 49160 | tf_op jit(solution)/shard_map/ppermute | solution.py:19
  10.6 4.9 %collective-permute-start.1 = (bf16[2,16,512]{2,1,0:T(8,128)(2,1)S(1)}, bf16[2,16,512]{2,1,0:T(8,128)(2,1)S(1)}, u32[]{:S(2)}, u32[]{:S(2)}) collective-permute-start(bf16[2,16,512]{2,1,0:T(8,128)(2,1)S(1)} %pad_maximum_fusion.4), channel_id=1, source_target_pairs={{0,64},{8,72},{16,80},{24,88},{32,96},{40,104},{48,112},{56,120},{... | collective-permute-start | bytes 98312 | tf_op jit(solution)/shard_map/ppermute | solution.py:19
  15.5 5.9 %collective-permute-start.2 = (bf16[2,2,16,512]{3,2,1,0:T(8,128)(2,1)S(1)}, bf16[2,2,16,512]{3,2,1,0:T(8,128)(2,1)S(1)}, u32[]{:S(2)}, u32[]{:S(2)}) collective-permute-start(bf16[2,2,16,512]{3,2,1,0:T(8,128)(2,1)S(1)} %pad_maximum_fusion.3), channel_id=1, source_target_pairs={{0,32},{8,40},{16,48},{24,56},{32,0},{40,8},{48,16},{56,24},{64,96... | collective-permute-start | bytes 196616 | tf_op jit(solution)/shard_map/ppermute | solution.py:19
  21.4 5.1 %collective-permute-start.3 = (bf16[2,2,2,16,512]{4,3,2,1,0:T(8,128)(2,1)S(1)}, bf16[2,2,2,16,512]{4,3,2,1,0:T(8,128)(2,1)S(1)}, u32[]{:S(2)}, u32[]{:S(2)}) collective-permute-start(bf16[2,2,2,16,512]{4,3,2,1,0:T(8,128)(2,1)S(1)} %pad_maximum_fusion.2), channel_id=1, source_target_pairs={{0,16},{8,24},{16,0},{24,8},{32,48},{40,56},{48,32},{56,40},{64,80... | collective-permute-start | bytes 393224 | tf_op jit(solution)/shard_map/ppermute | solution.py:19
  23.1 5.4 %copy-start.5 = (f32[1,8,256]{2,1,0:T(8,128)S(1)}, f32[1,8,256]{2,1,0:T(8,128)}, u32[]{:S(2)}) copy-start(f32[1,8,256]{2,1,0:T(8,128)} %param.8) | copy-start | bytes 24580
  23.1 5.4 %copy-start.7 = (s32[1,256]{1,0:T(1,128)S(1)}, s32[1,256]{1,0:T(1,128)}, u32[]{:S(2)}) copy-start(s32[1,256]{1,0:T(1,128)} %param.10) | copy-start | bytes 3076
  26.5 1.6 %collective-permute-start.4 = (bf16[2,2,2,2,16,512]{5,4,3,2,1,0:T(8,128)(2,1)S(1)}, bf16[2,2,2,2,16,512]{5,4,3,2,1,0:T(8,128)(2,1)S(1)}, u32[]{:S(2)}, u32[]{:S(2)}) collective-permute-start(bf16[2,2,2,2,16,512]{5,4,3,2,1,0:T(8,128)(2,1)S(1)} %pad_maximum_fusion.1), channel_id=1, source_target_pairs={{0,8},{8,0},{16,24},{24,16},{32,40},{40,32},{48,56},{56,48},{64,72... | collective-permute-start | bytes 786440 | tf_op jit(solution)/shard_map/ppermute | solution.py:19
  28.5 3.4 %copy-start.6 = (bf16[1,2048,2048]{2,1,0:T(8,128)(2,1)S(1)}, bf16[1,2048,2048]{2,1,0:T(8,128)(2,1)}, u32[]{:S(2)}) copy-start(bf16[1,2048,2048]{2,1,0:T(8,128)(2,1)} %param.6) | copy-start | bytes 25165828
  36.5 1.9 %copy-start = (f32[4,128,2048]{2,1,0:T(8,128)}, f32[4,128,2048]{2,1,0:T(8,128)S(1)}, u32[]{:S(2)}) copy-start(f32[4,128,2048]{2,1,0:T(8,128)S(1)} %fusion.4) | copy-start | bytes 12582916
  38.4 10.6 %collective-permute-start.8 = (f32[4,2048]{1,0:T(4,128)S(1)}, f32[4,2048]{1,0:T(4,128)S(1)}, u32[]{:S(2)}, u32[]{:S(2)}) collective-permute-start(f32[4,2048]{1,0:T(4,128)S(1)} %multiply_reduce_fusion), channel_id=1, source_target_pairs={{0,1},{1,0},{2,3},{3,2},{4,5},{5,4},{6,7},{7,6},{8,9},{9,8},{10,11... | collective-permute-start | bytes 98312 | tf_op jit(solution)/shard_map/ppermute | solution.py:19
  46.1 2.0 %copy-start.1 = (f32[4,128,2048]{2,1,0:T(8,128)}, f32[4,128,2048]{2,1,0:T(8,128)S(1)}, u32[]{:S(2)}) copy-start(f32[4,128,2048]{2,1,0:T(8,128)S(1)} %fusion.6) | copy-start | bytes 12582916
  46.1 15.9 %copy-start.3 = (f32[1,8,2048]{2,1,0:T(8,128)S(1)}, f32[1,8,2048]{2,1,0:T(8,128)}, u32[]{:S(2)}) copy-start(f32[1,8,2048]{2,1,0:T(8,128)} %param.7) | copy-start | bytes 196612
  48.1 4.1 %collective-permute-start.5 = (f32[4,2048]{1,0:T(4,128)S(1)}, f32[4,2048]{1,0:T(4,128)S(1)}, u32[]{:S(2)}, u32[]{:S(2)}) collective-permute-start(f32[4,2048]{1,0:T(4,128)S(1)} %multiply_reduce_fusion.1), channel_id=1, source_target_pairs={{0,1},{1,0},{2,3},{3,2},{4,5},{5,4},{6,7},{7,6},{8,9},{9,8},{10,11... | collective-permute-start | bytes 98312 | tf_op jit(solution)/shard_map/ppermute | solution.py:19
  49.0 5.5 %collective-permute-start.9 = (f32[4,2048]{1,0:T(4,128)S(1)}, f32[4,2048]{1,0:T(4,128)S(1)}, u32[]{:S(2)}, u32[]{:S(2)}) collective-permute-start(f32[4,2048]{1,0:T(4,128)S(1)} %add.132), channel_id=1, source_target_pairs={{0,2},{1,3},{2,0},{3,1},{4,6},{5,7},{6,4},{7,5},{8,10},{9,11},{10,... | collective-permute-start | bytes 98312 | tf_op jit(solution)/shard_map/ppermute | solution.py:19
  52.3 5.5 %collective-permute-start.6 = (f32[4,2048]{1,0:T(4,128)S(1)}, f32[4,2048]{1,0:T(4,128)S(1)}, u32[]{:S(2)}, u32[]{:S(2)}) collective-permute-start(f32[4,2048]{1,0:T(4,128)S(1)} %add.127), channel_id=1, source_target_pairs={{0,2},{1,3},{2,0},{3,1},{4,6},{5,7},{6,4},{7,5},{8,10},{9,11},{10,... | collective-permute-start | bytes 98312 | tf_op jit(solution)/shard_map/ppermute | solution.py:19
  54.5 4.6 %collective-permute-start.10 = (f32[4,2048]{1,0:T(4,128)S(1)}, f32[4,2048]{1,0:T(4,128)S(1)}, u32[]{:S(2)}, u32[]{:S(2)}) collective-permute-start(f32[4,2048]{1,0:T(4,128)S(1)} %add.133), channel_id=1, source_target_pairs={{0,4},{1,5},{2,6},{3,7},{4,0},{5,1},{6,2},{7,3},{8,12},{9,13},{10,... | collective-permute-start | bytes 98312 | tf_op jit(solution)/shard_map/ppermute | solution.py:19
  57.8 4.2 %collective-permute-start.7 = (f32[4,2048]{1,0:T(4,128)S(1)}, f32[4,2048]{1,0:T(4,128)S(1)}, u32[]{:S(2)}, u32[]{:S(2)}) collective-permute-start(f32[4,2048]{1,0:T(4,128)S(1)} %add.128), channel_id=1, source_target_pairs={{0,4},{1,5},{2,6},{3,7},{4,0},{5,1},{6,2},{7,3},{8,12},{9,13},{10,... | collective-permute-start | bytes 98312 | tf_op jit(solution)/shard_map/ppermute | solution.py:19
  75.4 14.2 %collective-permute-start.11 = (f32[2,2,2,2,16,256]{5,4,3,2,1,0:T(8,128)S(1)}, f32[2,2,2,2,16,256]{5,4,3,2,1,0:T(8,128)S(1)}, u32[]{:S(2)}, u32[]{:S(2)}) collective-permute-start(f32[2,2,2,2,16,256]{5,4,3,2,1,0:T(8,128)S(1)} %dynamic-slice_bitcast_fusion.1), channel_id=1, source_target_pairs={{0,8},{8,0},{16,24},{24,16},{32,40},{40,32},{48,56},{56,48},{64,72... | collective-permute-start | bytes 786440 | tf_op jit(solution)/shard_map/ppermute | solution.py:19
  88.8 2.0 %collective-permute-start.16 = (f32[2,2,2,2,16,256]{5,4,3,2,1,0:T(8,128)S(1)}, f32[2,2,2,2,16,256]{5,4,3,2,1,0:T(8,128)S(1)}, u32[]{:S(2)}, u32[]{:S(2)}) collective-permute-start(f32[2,2,2,2,16,256]{5,4,3,2,1,0:T(8,128)S(1)} %dynamic-slice_bitcast_fusion), channel_id=1, source_target_pairs={{0,8},{8,0},{16,24},{24,16},{32,40},{40,32},{48,56},{56,48},{64,72... | collective-permute-start | bytes 786440 | tf_op jit(solution)/shard_map/ppermute | solution.py:19
  89.7 34.2 %copy-start.2 = (f32[16,8,64]{2,1,0:T(8,128)S(1)}, f32[16,8,64]{2,1,0:T(8,128)}, u32[]{:S(2)}) copy-start(f32[16,8,64]{2,1,0:T(8,128)} %param.11) | copy-start | bytes 98308
  90.9 6.5 %collective-permute-start.12 = (f32[2,2,2,16,256]{4,3,1,0,2:T(8,128)S(1)}, f32[2,2,2,16,256]{4,3,1,0,2:T(8,128)S(1)}, u32[]{:S(2)}, u32[]{:S(2)}) collective-permute-start(f32[2,2,2,16,256]{4,3,1,0,2:T(8,128)S(1)} %bitcast.141), channel_id=1, source_target_pairs={{0,16},{8,24},{16,0},{24,8},{32,48},{40,56},{48,32},{56,40},{64,80... | collective-permute-start | bytes 393224 | tf_op jit(solution)/shard_map/ppermute | solution.py:19
  93.3 8.2 %collective-permute-start.17 = (f32[2,2,2,16,256]{4,3,1,0,2:T(8,128)S(1)}, f32[2,2,2,16,256]{4,3,1,0,2:T(8,128)S(1)}, u32[]{:S(2)}, u32[]{:S(2)}) collective-permute-start(f32[2,2,2,16,256]{4,3,1,0,2:T(8,128)S(1)} %bitcast.140), channel_id=1, source_target_pairs={{0,16},{8,24},{16,0},{24,8},{32,48},{40,56},{48,32},{56,40},{64,80... | collective-permute-start | bytes 393224 | tf_op jit(solution)/shard_map/ppermute | solution.py:19
  97.4 6.8 %collective-permute-start.13 = (f32[2,2,16,256]{3,2,1,0:T(8,128)S(1)}, f32[2,2,16,256]{3,2,1,0:T(8,128)S(1)}, u32[]{:S(2)}, u32[]{:S(2)}) collective-permute-start(f32[2,2,16,256]{3,2,1,0:T(8,128)S(1)} %dynamic-slice_bitcast_fusion.3), channel_id=1, source_target_pairs={{0,32},{8,40},{16,48},{24,56},{32,0},{40,8},{48,16},{56,24},{64,96... | collective-permute-start | bytes 196616 | tf_op jit(solution)/shard_map/ppermute | solution.py:19
  101.5 5.9 %collective-permute-start.18 = (f32[2,2,16,256]{3,2,1,0:T(8,128)S(1)}, f32[2,2,16,256]{3,2,1,0:T(8,128)S(1)}, u32[]{:S(2)}, u32[]{:S(2)}) collective-permute-start(f32[2,2,16,256]{3,2,1,0:T(8,128)S(1)} %dynamic-slice_bitcast_fusion.2), channel_id=1, source_target_pairs={{0,32},{8,40},{16,48},{24,56},{32,0},{40,8},{48,16},{56,24},{64,96... | collective-permute-start | bytes 196616 | tf_op jit(solution)/shard_map/ppermute | solution.py:19
  104.3 5.2 %collective-permute-start.14 = (f32[2,16,256]{2,1,0:T(8,128)S(1)}, f32[2,16,256]{2,1,0:T(8,128)S(1)}, u32[]{:S(2)}, u32[]{:S(2)}) collective-permute-start(f32[2,16,256]{2,1,0:T(8,128)S(1)} %dynamic-slice_bitcast_fusion.5), channel_id=1, source_target_pairs={{0,64},{8,72},{16,80},{24,88},{32,96},{40,104},{48,112},{56,120},{... | collective-permute-start | bytes 98312 | tf_op jit(solution)/shard_map/ppermute | solution.py:19
  107.4 8.7 %collective-permute-start.19 = (f32[2,16,256]{2,1,0:T(8,128)S(1)}, f32[2,16,256]{2,1,0:T(8,128)S(1)}, u32[]{:S(2)}, u32[]{:S(2)}) collective-permute-start(f32[2,16,256]{2,1,0:T(8,128)S(1)} %dynamic-slice_bitcast_fusion.4), channel_id=1, source_target_pairs={{0,64},{8,72},{16,80},{24,88},{32,96},{40,104},{48,112},{56,120},{... | collective-permute-start | bytes 98312 | tf_op jit(solution)/shard_map/ppermute | solution.py:19
  109.5 8.8 %collective-permute-start.15 = (f32[16,256]{1,0:T(8,128)S(1)}, f32[16,256]{1,0:T(8,128)S(1)}, u32[]{:S(2)}, u32[]{:S(2)}) collective-permute-start(f32[16,256]{1,0:T(8,128)S(1)} %dynamic-slice_bitcast_fusion.7), channel_id=1, source_target_pairs={{0,128},{8,136},{16,144},{24,152},{32,160},{40,168},{48,176},{56,1... | collective-permute-start | bytes 49160 | tf_op jit(solution)/shard_map/ppermute | solution.py:19
  116.1 7.7 %collective-permute-start.20 = (f32[16,256]{1,0:T(8,128)S(1)}, f32[16,256]{1,0:T(8,128)S(1)}, u32[]{:S(2)}, u32[]{:S(2)}) collective-permute-start(f32[16,256]{1,0:T(8,128)S(1)} %dynamic-slice_bitcast_fusion.6), channel_id=1, source_target_pairs={{0,128},{8,136},{16,144},{24,152},{32,160},{40,168},{48,176},{56,1... | collective-permute-start | bytes 49160 | tf_op jit(solution)/shard_map/ppermute | solution.py:19

commit v3 on v1

--- a/solution.py
+++ b/solution.py
@@ -55,13 +55,103 @@
     return x
 
 
+def _mask(j, bits):
+    m = 0
+    for pos, b in enumerate(bits):
+        if (j >> pos) & 1:
+            m |= 1 << b
+    return m
+
+def _sub(me, bits):
+    s = 0
+    for pos, b in enumerate(bits):
+        s = s + ((me >> b) & 1) * (1 << pos)
+    return s
+
+def _send_all(x_for, axis, bits, size):
+    out = {}
+    for j in range(1, 1 << len(bits)):
+        m = _mask(j, bits)
+        out[j] = lax.ppermute(x_for(j), axis, [(i, i ^ m) for i in range(size)])
+    return out
+
+def _ordered(own, got, s, count):
+    cand = jnp.stack([own] + [got[j] for j in range(1, count)])
+    idx = jnp.arange(count, dtype=jnp.int32) ^ s
+    return jnp.take(cand, idx, axis=0)
+
+def gather_groups(x, axis, groups):
+    size = lax.axis_size(axis)
+    me = lax.axis_index(axis)
+    buf = x[None]
+    done = []
+    for bits in groups:
+        count = 1 << len(bits)
+        s = _sub(me, bits)
+        got = _send_all(lambda j: buf, axis, bits, size)
+        stacked = _ordered(buf, got, s, count)
+        buf = stacked
+        done.append(bits)
+    buf = buf.reshape(buf.shape[:len(groups)] + x.shape)
+    order = sorted(range(len(groups)), key=lambda g: -max(groups[len(groups) - 1 - g]))
+    buf = jnp.transpose(buf, order + list(range(len(groups), buf.ndim)))
+    return buf.reshape((size * x.shape[0],) + x.shape[1:])
+
+def scatter_groups(x, axis, groups):
+    size = lax.axis_size(axis)
+    me = lax.axis_index(axis)
+    block = x.shape[0] // size
+    total = sum(len(b) for b in groups)
+    buf = x.reshape((2,) * total + (block,) + x.shape[1:])
+    remaining = list(reversed(range(total)))
+    for bits in groups:
+        count = 1 << len(bits)
+        s = _sub(me, bits)
+        axes = [remaining.index(b) for b in reversed(bits)]
+        rest = [a for a in range(len(remaining)) if a not in axes]
+        buf = jnp.transpose(buf, axes + rest + list(range(len(remaining), buf.ndim)))
+        buf = buf.reshape((count,) + buf.shape[len(bits):])
+        remaining = [b for b in remaining if b not in bits]
+        own = lax.dynamic_index_in_dim(buf, s, 0, keepdims=False)
+        got = _send_all(lambda j: lax.dynamic_index_in_dim(buf, s ^ j, 0, keepdims=False), axis, bits, size)
+        acc = own
+        for j in range(1, count):
+            acc = acc + got[j]
+        buf = acc
+    return buf
+
+def sum_groups(x, axis, groups):
+    size = lax.axis_size(axis)
+    me = lax.axis_index(axis)
+    for bits in groups:
+        count = 1 << len(bits)
+        s = _sub(me, bits)
+        got = _send_all(lambda j: x, axis, bits, size)
+        vals = _ordered(x, got, s, count)
+        while vals.shape[0] > 1:
+            vals = vals[0::2] + vals[1::2]
+        x = vals[0]
+    return x
+
+
+def _bit_groups(axis):
+    rest = list(range(1, _bit_count(lax.axis_size(axis))))
+    pairs = [tuple(rest[max(0, i - 1) : i + 1]) for i in range(len(rest) - 1, -1, -2)]
+    return pairs + [(0,)]
+
+
+def _split_bf16(x):
+    high = lax.reduce_precision(x, exponent_bits=8, mantissa_bits=7)
+    return high.astype(jnp.bfloat16), (x - high).astype(jnp.bfloat16)
+
+
 def shards(sensitivity, headroom, ev_power, ev_node, region_map, loadings):
     reg_local, hours, columns = loadings.shape
     nodes = sensitivity.shape[2]
     ev_count = ev_power.shape[2]
     total_regions = reg_local * lax.axis_size("feeder")
     packed = loadings.astype(jnp.bfloat16).reshape(reg_local, hours * columns)
-    shard_rows = gather_blocks(packed, "feeder")
+    shard_rows = gather_groups(packed, "feeder", _bit_groups("feeder"))
     regions = region_map.reshape(-1)
     matches = (regions[:, None] == lax.iota(jnp.int32, total_regions)[None, :]).astype(jnp.bfloat16)
     looked = jnp.dot(matches, shard_rows, preferred_element_type=jnp.float32)
@@ -70,9 +160,7 @@
     weighted = (power[:, :, None] * looked).astype(jnp.bfloat16)
     node_hot = (ev_node[0][:, :, None] == lax.iota(jnp.int32, nodes)[None, None, :]).astype(jnp.bfloat16)
     spread = jnp.einsum("hkm,khr->mhr", node_hot, weighted, preferred_element_type=jnp.float32)
-    spread_hi = spread.astype(jnp.bfloat16)
-    spread_lo = (spread - spread_hi.astype(jnp.float32)).astype(jnp.bfloat16)
-    both = jnp.concatenate([spread_hi, spread_lo], axis=2)
+    both = jnp.concatenate(_split_bf16(spread), axis=2)
     sens = sensitivity[0]
     volts_both = jnp.einsum("mhr,mn->hrn", both, sens, preferred_element_type=jnp.float32)
     factor_volts = volts_both[:, :columns] + volts_both[:, columns:]
@@ -93,7 +181,7 @@
     )
     member_grads = (power[:, :, None] * picked).reshape(ev_count, hours * columns)
     summed = jax.ops.segment_sum(member_grads, regions, num_segments=total_regions)
-    reduced = scatter_blocks(summed, "feeder")
+    reduced = scatter_groups(summed, "feeder", _bit_groups("feeder")[::-1])
     new_loadings = loadings - step_size * reduced.reshape(reg_local, hours, columns)
     return (margin, new_loadings)
 

time: 118 us -> 109 us (0.924)
  waiting for transfers between devices: 40.5 us -> 33.9 us
  starting transfers between devices: 32.1 us -> 27.2 us
  local copies, waits for them, and re-layouts: 2.9 us -> 4.68 us
    ppermute x13 -> x3, starting transfers between devices: 32.1 us -> 3.12 us  [_exchange(): return lax.ppermute(x, axis, perm)]
    ppermute x13 -> x3, waiting for transfers between devices: 40.5 us -> 11.6 us  [_exchange(): return lax.ppermute(x, axis, perm)]
    ppermute x0 -> x14, starting transfers between devices: none -> 24.1 us  [_send_all(): out[j] = lax.ppermute(x_for(j), axis, [(i, i ^ m) for i in range(size)])]
    ppermute x0 -> x14, waiting for transfers between devices: none -> 22.3 us  [_send_all(): out[j] = lax.ppermute(x_for(j), axis, [(i, i ^ m) for i in range(size)])]
    gather x0 -> x3, local copies, waits for them, and re-layouts: none -> 1.7 us  [_ordered(): return jnp.take(cand, idx, axis=0)]
  transfers between devices with their start and end apart: 13 -> 17, of which waited for: 13 -> 11; matrix products, arithmetic and copies ran while one was open for 0% -> 0% of each run, Pallas kernels for 0% -> 0%
where the time goes in v3:
time: 109 us
  matrix products  35.7 us (33%)
  waiting for transfers between devices  33.9 us (31%)
  starting transfers between devices  27.2 us (25%)
  other arithmetic  6.37 us (6%)
  local copies, waits for them, and re-layouts  4.68 us (4%)
    ppermute x14, starting transfers between devices, _send_all(): out[j] = lax.ppermute(x_for(j), axis, [(i, i ^ m) for i in range(size)])  24.1 us
    ppermute x14, waiting for transfers between devices, _send_all(): out[j] = lax.ppermute(x_for(j), axis, [(i, i ^ m) for i in range(size)])  22.3 us
    dot_general x1, matrix products, shards(): jnp.einsum('mhr,mn->hrn', both, sens, preferred_element_type=jnp.float32)  12.1 us
    ppermute x3, waiting for transfers between devices, _exchange(): return lax.ppermute(x, axis, perm)  11.6 us
    dot_general x1, matrix products, shards(): jnp.einsum('mn,hrn->mhr', sens, volt_grad, preferred_element_type=jnp.flo...  9.49 us
    dot_general x1, matrix products, shards(): jnp.einsum('hkm,mhr->khr', node_hot, node_grads, precision=lax.Precision....  8.9 us
    dot_general x1, matrix products, shards(): jnp.einsum('hkm,khr->mhr', node_hot, weighted, preferred_element_type=jnp...  5.26 us
    ppermute x3, starting transfers between devices, _exchange(): return lax.ppermute(x, axis, perm)  3.12 us
  transfers between devices with their start and end apart: 17, of which 11 were waited for; matrix products, arithmetic and copies ran while one was open for 0% of the time, Pallas kernels for 0%

profile of v3, /device:TPU:4, one launch (start us, length us, event | category | flops | bytes accessed | tf_op | source)
XLA Modules:
  0.0 108.8 jit_solution(11518283738105907566)
XLA Ops:
  0.6 0.0 copy-start.3
  0.6 0.0 copy-start.5
  0.7 0.0 copy-start.4
  0.7 0.9 convert_element_type.17
  1.5 0.1 broadcast_in_dim_reshape.7
  1.6 6.4 %collective-permute-start.2 = (bf16[1,16,512]{2,1,0:T(8,128)(2,1)S(1)}, bf16[1,16,512]{2,1,0:T(8,128)(2,1)S(1)}, u32[]{:S(2)}, u32[]{:S(2)}) collective-permute-start(bf16[1,16,512]{2,1,0:T(8,128)(2,1)S(1)} %broadcast_in_dim_reshape.7), channel_id=1, source_target_pairs={{0,192},{8,200},{16,208},{24,216},{32,224},{40,232},{48,240},{56,2... | collective-permute-start | bytes 49160 | tf_op jit(solution)/shard_map/ppermute | solution.py:75
  8.0 1.0 collective-permute-start.1
  9.0 1.5 %collective-permute-start = (bf16[1,16,512]{2,1,0:T(8,128)(2,1)S(1)}, bf16[1,16,512]{2,1,0:T(8,128)(2,1)S(1)}, u32[]{:S(2)}, u32[]{:S(2)}) collective-permute-start(bf16[1,16,512]{2,1,0:T(8,128)(2,1)S(1)} %broadcast_in_dim_reshape.7), channel_id=1, source_target_pairs={{0,64},{8,72},{16,80},{24,88},{32,96},{40,104},{48,112},{56,120},{... | collective-permute-start | bytes 49160 | tf_op jit(solution)/shard_map/ppermute | solution.py:75
  10.6 0.1 stack_broadcast_in_dim_reshape.3
  10.7 0.0 collective-permute-done.2
  10.7 5.0 %collective-permute-done.1 = bf16[1,16,512]{2,1,0:T(8,128)(2,1)S(1)} collective-permute-done((bf16[1,16,512]{2,1,0:T(8,128)(2,1)S(1)}, bf16[1,16,512]{2,1,0:T(8,128)(2,1)S(1)}, u32[]{:S(2)}, u32[]{:S(2)}) %collective-permute-start.1) | collective-permute-done | bytes 16416 | tf_op jit(solution)/shard_map/ppermute | solution.py:75
  15.7 0.0 collective-permute-done
  15.7 0.6 gather_fusion
  16.2 0.1 bitcast_select_fusion.2
  16.3 3.0 %collective-permute-start.5 = (bf16[4,1,16,512]{3,2,0,1:T(8,128)(2,1)S(1)}, bf16[4,1,16,512]{3,2,0,1:T(8,128)(2,1)S(1)}, u32[]{:S(2)}, u32[]{:S(2)}) collective-permute-start(bf16[4,1,16,512]{3,2,0,1:T(8,128)(2,1)S(1)} %bitcast_select_fusion.2), channel_id=1, source_target_pairs={{0,48},{8,56},{16,32},{24,40},{32,16},{40,24},{48,0},{56,8},{64,11... | collective-permute-start | bytes 196616 | tf_op jit(solution)/shard_map/ppermute | solution.py:75
  19.4 0.6 collective-permute-start.4
  20.0 0.5 collective-permute-start.3
  20.4 0.1 bitcast_select_fusion.3
  20.5 2.0 %collective-permute-done.5 = bf16[4,1,16,512]{3,2,0,1:T(8,128)(2,1)S(1)} collective-permute-done((bf16[4,1,16,512]{3,2,0,1:T(8,128)(2,1)S(1)}, bf16[4,1,16,512]{3,2,0,1:T(8,128)(2,1)S(1)}, u32[]{:S(2)}, u32[]{:S(2)}) %collective-permute-start.5) | collective-permute-done | bytes 65568 | tf_op jit(solution)/shard_map/ppermute | solution.py:75
  22.5 2.6 %collective-permute-done.4 = bf16[4,1,16,512]{3,2,0,1:T(8,128)(2,1)S(1)} collective-permute-done((bf16[4,1,16,512]{3,2,0,1:T(8,128)(2,1)S(1)}, bf16[4,1,16,512]{3,2,0,1:T(8,128)(2,1)S(1)}, u32[]{:S(2)}, u32[]{:S(2)}) %collective-permute-start.4) | collective-permute-done | bytes 65568 | tf_op jit(solution)/shard_map/ppermute | solution.py:75
  25.1 0.0 collective-permute-done.3
  25.2 0.6 gather_fusion.1
  25.7 0.1 bitcast_select_fusion
  25.8 0.3 collective-permute-start.6
  26.1 0.1 fusion.26
  26.2 1.4 %collective-permute-done.6 = bf16[4,4,1,16,512]{4,3,1,0,2:T(8,128)(2,1)S(1)} collective-permute-done((bf16[4,4,1,16,512]{4,3,1,0,2:T(8,128)(2,1)S(1)}, bf16[4,4,1,16,512]{4,3,1,0,2:T(8,128)(2,1)S(1)}, u32[]{:S(2)}, u32[]{:S(2)}) %collective-permute-start.6) | collective-permute-done | bytes 262176 | tf_op jit(solution)/shard_map/ppermute | solution.py:75
  27.6 0.1 maximum_bitcast_fusion
  27.7 0.6 gather_fusion.2
  28.3 0.1 select_bitcast_fusion
  28.4 0.2 copy.12
  28.7 5.3 %reduce-precision_convert_fusion = (bf16[2048,8,64]{0,2,1:T(8,128)(2,1)S(1)}, bf16[2048,8,64]{0,2,1:T(8,128)(2,1)}) fusion(s32[8,256]{1,0:T(8,128)S(1)} %bitcast.132, bf16[8,64,512]{2,1,0:T(8,128)(2,1)S(1)} %bitcast.121, s32[256]{0:T(256)S(1)} %bitcast.136, f32[256,8]{0,1:T(8,128)S(1)} %bitcast.134), kind=kOutput, calls=%fused_computation.14 | convolution fusion | flops 679870464 | bytes 4736000 | tf_op jit(solution)/shard_map/hkm,khr->mhr/dot_general | solution.py:162
  34.0 12.1 %fusion.4 = f32[8,128,2048]{2,1,0:T(8,128)S(1)} fusion(bf16[1,2048,2048]{2,1,0:T(8,128)(2,1)} %param.6, bf16[2048,8,64]{0,2,1:T(8,128)(2,1)} %get-tuple-element.5, bf16[2048,8,64]{0,2,1:T(8,128)(2,1)S(1)} %get-tuple-element.4), kind=kOutput, calls=%fused_computation.9 | convolution fusion | flops 8598323200 | bytes 20971520 | tf_op jit(solution)/shard_map/mhr,mn->hrn/dot_general | solution.py:165
  46.1 0.0 copy-start.2
  46.1 1.1 %multiply_reduce_fusion = f32[8,2048]{1,0:T(8,128)S(1)} fusion(f32[8,128,2048]{2,1,0:T(8,128)S(1)} %fusion.4), kind=kLoop, calls=%fused_computation.22 | loop fusion | flops 3129344 | bytes 8454144 | tf_op jit(solution)/shard_map/reduce_sum | solution.py:167
  47.2 2.1 %copy-done = f32[8,128,2048]{2,1,0:T(8,128)} copy-done((f32[8,128,2048]{2,1,0:T(8,128)}, f32[8,128,2048]{2,1,0:T(8,128)S(1)}, u32[]{:S(2)}) %copy-start) | copy-done | bytes 8388632
  49.3 1.2 %collective-permute-start.7 = (f32[8,2048]{1,0:T(8,128)S(1)}, f32[8,2048]{1,0:T(8,128)S(1)}, u32[]{:S(2)}, u32[]{:S(2)}) collective-permute-start(f32[8,2048]{1,0:T(8,128)S(1)} %multiply_reduce_fusion), channel_id=1, source_target_pairs={{0,1},{1,0},{2,3},{3,2},{4,5},{5,4},{6,7},{7,6},{8,9},{9,8},{10,11... | collective-permute-start | bytes 196616 | tf_op jit(solution)/shard_map/ppermute | solution.py:19
  50.5 3.1 %collective-permute-done.7 = f32[8,2048]{1,0:T(8,128)S(1)} collective-permute-done((f32[8,2048]{1,0:T(8,128)S(1)}, f32[8,2048]{1,0:T(8,128)S(1)}, u32[]{:S(2)}, u32[]{:S(2)}) %collective-permute-start.7) | collective-permute-done | bytes 65568 | tf_op jit(solution)/shard_map/ppermute | solution.py:19
  53.6 0.6 collective-permute-start.8
  54.2 5.3 %collective-permute-done.8 = f32[8,2048]{1,0:T(8,128)S(1)} collective-permute-done((f32[8,2048]{1,0:T(8,128)S(1)}, f32[8,2048]{1,0:T(8,128)S(1)}, u32[]{:S(2)}, u32[]{:S(2)}) %collective-permute-start.8) | collective-permute-done | bytes 65568 | tf_op jit(solution)/shard_map/ppermute | solution.py:19
  59.5 1.3 %collective-permute-start.9 = (f32[8,2048]{1,0:T(8,128)S(1)}, f32[8,2048]{1,0:T(8,128)S(1)}, u32[]{:S(2)}, u32[]{:S(2)}) collective-permute-start(f32[8,2048]{1,0:T(8,128)S(1)} %add.138), channel_id=1, source_target_pairs={{0,4},{1,5},{2,6},{3,7},{4,0},{5,1},{6,2},{7,3},{8,12},{9,13},{10,... | collective-permute-start | bytes 196616 | tf_op jit(solution)/shard_map/ppermute | solution.py:19
  60.8 3.2 %collective-permute-done.9 = f32[8,2048]{1,0:T(8,128)S(1)} collective-permute-done((f32[8,2048]{1,0:T(8,128)S(1)}, f32[8,2048]{1,0:T(8,128)S(1)}, u32[]{:S(2)}, u32[]{:S(2)}) %collective-permute-start.9) | collective-permute-done | bytes 65568 | tf_op jit(solution)/shard_map/ppermute | solution.py:19
  64.0 0.0 copy-done.2
  64.0 0.7 fusion.33
  64.7 9.5 %fusion.2 = f32[8,64,2048]{2,1,0:T(8,128)S(1)} fusion(bf16[1,2048,2048]{2,1,0:T(8,128)(2,1)} %param.6, f32[8,2048]{1,0:T(8,128)S(1)} %get-tuple-element.2, f32[8,128,2048]{2,1,0:T(8,128)} %copy-done), kind=kOutput, calls=%fused_computation.7 | convolution fusion | flops 4298113024 | bytes 21037056 | tf_op jit(solution)/shard_map/mn,hrn->mhr/dot_general | solution.py:174
  74.2 8.9 %fusion.17 = f32[256,8,64]{0,2,1:T(8,128)S(1)} fusion(s32[8,256]{1,0:T(8,128)S(1)} %bitcast.133, f32[8,64,2048]{2,1,0:T(8,128)S(1)} %fusion.2, f32[256,8]{0,1:T(8,128)S(1)} %bitcast.135), kind=kOutput, calls=%fused_computation.26 | convolution fusion | flops 3225550848 | bytes 4734976 | tf_op jit(solution)/shard_map/hkm,mhr->khr/dot_general | solution.py:175
  83.1 0.2 copy.13
  83.3 2.3 %scatter_custom_fusion = f32[512,512]{1,0:T(8,128)S(1)} fusion(s32[256]{0:T(256)S(1)} %bitcast.137, f32[256,512]{1,0:T(8,128)S(1)} %copy.13, f32[]{:T(128)} %constant.86.clone.1), kind=kCustom, calls=%fused_computation.31 | custom fusion | flops 131072 | bytes 1048580 | tf_op jit(solution)/shard_map/scatter-add | solution.py:183
  85.7 0.1 collective-permute-start.10
  85.8 1.9 %collective-permute-done.10 = f32[2,2,2,2,16,512]{5,4,3,2,1,0:T(8,128)S(1)} collective-permute-done((f32[2,2,2,2,16,512]{5,4,3,2,1,0:T(8,128)S(1)}, f32[2,2,2,2,16,512]{5,4,3,2,1,0:T(8,128)S(1)}, u32[]{:S(2)}, u32[]{:S(2)}) %collective-permute-start.10) | collective-permute-done | bytes 524320 | tf_op jit(solution)/shard_map/ppermute | solution.py:75
  87.7 0.1 bitcast_add_fusion
  87.9 1.4 %collective-permute-start.13 = (f32[2,2,16,512]{3,2,1,0:T(8,128)S(1)}, f32[2,2,16,512]{3,2,1,0:T(8,128)S(1)}, u32[]{:S(2)}, u32[]{:S(2)}) collective-permute-start(f32[2,2,16,512]{3,2,1,0:T(8,128)S(1)} %get-tuple-element.7), channel_id=1, source_target_pairs={{0,48},{8,56},{16,32},{24,40},{32,16},{40,24},{48,0},{56,8},{64,11... | collective-permute-start | bytes 393224 | tf_op jit(solution)/shard_map/ppermute | solution.py:75
  89.2 0.9 collective-permute-start.12
  90.1 1.9 %collective-permute-start.11 = (f32[2,2,16,512]{3,2,1,0:T(8,128)S(1)}, f32[2,2,16,512]{3,2,1,0:T(8,128)S(1)}, u32[]{:S(2)}, u32[]{:S(2)}) collective-permute-start(f32[2,2,16,512]{3,2,1,0:T(8,128)S(1)} %get-tuple-element.6), channel_id=1, source_target_pairs={{0,16},{8,24},{16,0},{24,8},{32,48},{40,56},{48,32},{56,40},{64,80... | collective-permute-start | bytes 393224 | tf_op jit(solution)/shard_map/ppermute | solution.py:75
  92.0 5.5 %collective-permute-done.13 = f32[2,2,16,512]{3,2,1,0:T(8,128)S(1)} collective-permute-done((f32[2,2,16,512]{3,2,1,0:T(8,128)S(1)}, f32[2,2,16,512]{3,2,1,0:T(8,128)S(1)}, u32[]{:S(2)}, u32[]{:S(2)}) %collective-permute-start.13) | collective-permute-done | bytes 131104 | tf_op jit(solution)/shard_map/ppermute | solution.py:75
  97.5 0.0 collective-permute-done.12
  97.5 0.6 collective-permute-done.11
  98.2 2.1 %collective-permute-start.16 = (f32[16,512]{1,0:T(8,128)S(1)}, f32[16,512]{1,0:T(8,128)S(1)}, u32[]{:S(2)}, u32[]{:S(2)}) collective-permute-start(f32[16,512]{1,0:T(8,128)S(1)} %get-tuple-element.10), channel_id=1, source_target_pairs={{0,192},{8,200},{16,208},{24,216},{32,224},{40,232},{48,240},{56,2... | collective-permute-start | bytes 98312 | tf_op jit(solution)/shard_map/ppermute | solution.py:75
  100.3 3.0 %collective-permute-start.15 = (f32[16,512]{1,0:T(8,128)S(1)}, f32[16,512]{1,0:T(8,128)S(1)}, u32[]{:S(2)}, u32[]{:S(2)}) collective-permute-start(f32[16,512]{1,0:T(8,128)S(1)} %get-tuple-element.11), channel_id=1, source_target_pairs={{0,128},{8,136},{16,144},{24,152},{32,160},{40,168},{48,176},{56,1... | collective-permute-start | bytes 98312 | tf_op jit(solution)/shard_map/ppermute | solution.py:75
  103.3 1.5 %collective-permute-start.14 = (f32[16,512]{1,0:T(8,128)S(1)}, f32[16,512]{1,0:T(8,128)S(1)}, u32[]{:S(2)}, u32[]{:S(2)}) collective-permute-start(f32[16,512]{1,0:T(8,128)S(1)} %get-tuple-element.9), channel_id=1, source_target_pairs={{0,64},{8,72},{16,80},{24,88},{32,96},{40,104},{48,112},{56,120},{... | collective-permute-start | bytes 98312 | tf_op jit(solution)/shard_map/ppermute | solution.py:75
  104.8 0.0 collective-permute-done.16
  104.8 3.3 %collective-permute-done.15 = f32[16,512]{1,0:T(8,128)S(1)} collective-permute-done((f32[16,512]{1,0:T(8,128)S(1)}, f32[16,512]{1,0:T(8,128)S(1)}, u32[]{:S(2)}, u32[]{:S(2)}) %collective-permute-start.15) | collective-permute-done | bytes 32800 | tf_op jit(solution)/shard_map/ppermute | solution.py:75
  108.1 0.0 collective-permute-done.14
  108.1 0.1 mul.81
  108.2 0.6 sub.11
  (24 shorter events, 0.3 us)
Async XLA Ops:
  0.6 28.0 %copy-start.3 = (s32[1,8,256]{2,1,0:T(8,128)S(1)}, s32[1,8,256]{2,1,0:T(8,128)}, u32[]{:S(2)}) copy-start(s32[1,8,256]{2,1,0:T(8,128)} %param.9) | copy-start | bytes 24580
  0.6 28.0 %copy-start.5 = (s32[1,256]{1,0:T(1,128)S(1)}, s32[1,256]{1,0:T(1,128)}, u32[]{:S(2)}) copy-start(s32[1,256]{1,0:T(1,128)} %param.10) | copy-start | bytes 3076
  0.7 28.0 %copy-start.4 = (f32[1,8,256]{2,1,0:T(8,128)S(1)}, f32[1,8,256]{2,1,0:T(8,128)}, u32[]{:S(2)}) copy-start(f32[1,8,256]{2,1,0:T(8,128)} %param.8) | copy-start | bytes 24580
  1.6 9.0 %collective-permute-start.2 = (bf16[1,16,512]{2,1,0:T(8,128)(2,1)S(1)}, bf16[1,16,512]{2,1,0:T(8,128)(2,1)S(1)}, u32[]{:S(2)}, u32[]{:S(2)}) collective-permute-start(bf16[1,16,512]{2,1,0:T(8,128)(2,1)S(1)} %broadcast_in_dim_reshape.7), channel_id=1, source_target_pairs={{0,192},{8,200},{16,208},{24,216},{32,224},{40,232},{48,240},{56,2... | collective-permute-start | bytes 49160 | tf_op jit(solution)/shard_map/ppermute | solution.py:75
  8.0 7.6 %collective-permute-start.1 = (bf16[1,16,512]{2,1,0:T(8,128)(2,1)S(1)}, bf16[1,16,512]{2,1,0:T(8,128)(2,1)S(1)}, u32[]{:S(2)}, u32[]{:S(2)}) collective-permute-start(bf16[1,16,512]{2,1,0:T(8,128)(2,1)S(1)} %broadcast_in_dim_reshape.7), channel_id=1, source_target_pairs={{0,128},{8,136},{16,144},{24,152},{32,160},{40,168},{48,176},{56,1... | collective-permute-start | bytes 49160 | tf_op jit(solution)/shard_map/ppermute | solution.py:75
  9.0 6.7 %collective-permute-start = (bf16[1,16,512]{2,1,0:T(8,128)(2,1)S(1)}, bf16[1,16,512]{2,1,0:T(8,128)(2,1)S(1)}, u32[]{:S(2)}, u32[]{:S(2)}) collective-permute-start(bf16[1,16,512]{2,1,0:T(8,128)(2,1)S(1)} %broadcast_in_dim_reshape.7), channel_id=1, source_target_pairs={{0,64},{8,72},{16,80},{24,88},{32,96},{40,104},{48,112},{56,120},{... | collective-permute-start | bytes 49160 | tf_op jit(solution)/shard_map/ppermute | solution.py:75
  16.3 6.2 %collective-permute-start.5 = (bf16[4,1,16,512]{3,2,0,1:T(8,128)(2,1)S(1)}, bf16[4,1,16,512]{3,2,0,1:T(8,128)(2,1)S(1)}, u32[]{:S(2)}, u32[]{:S(2)}) collective-permute-start(bf16[4,1,16,512]{3,2,0,1:T(8,128)(2,1)S(1)} %bitcast_select_fusion.2), channel_id=1, source_target_pairs={{0,48},{8,56},{16,32},{24,40},{32,16},{40,24},{48,0},{56,8},{64,11... | collective-permute-start | bytes 196616 | tf_op jit(solution)/shard_map/ppermute | solution.py:75
  19.4 5.8 %collective-permute-start.4 = (bf16[4,1,16,512]{3,2,0,1:T(8,128)(2,1)S(1)}, bf16[4,1,16,512]{3,2,0,1:T(8,128)(2,1)S(1)}, u32[]{:S(2)}, u32[]{:S(2)}) collective-permute-start(bf16[4,1,16,512]{3,2,0,1:T(8,128)(2,1)S(1)} %bitcast_select_fusion.2), channel_id=1, source_target_pairs={{0,32},{8,40},{16,48},{24,56},{32,0},{40,8},{48,16},{56,24},{64,96... | collective-permute-start | bytes 196616 | tf_op jit(solution)/shard_map/ppermute | solution.py:75
  20.0 5.1 %collective-permute-start.3 = (bf16[4,1,16,512]{3,2,0,1:T(8,128)(2,1)S(1)}, bf16[4,1,16,512]{3,2,0,1:T(8,128)(2,1)S(1)}, u32[]{:S(2)}, u32[]{:S(2)}) collective-permute-start(bf16[4,1,16,512]{3,2,0,1:T(8,128)(2,1)S(1)} %bitcast_select_fusion.2), channel_id=1, source_target_pairs={{0,16},{8,24},{16,0},{24,8},{32,48},{40,56},{48,32},{56,40},{64,80... | collective-permute-start | bytes 196616 | tf_op jit(solution)/shard_map/ppermute | solution.py:75
  25.8 1.8 %collective-permute-start.6 = (bf16[4,4,1,16,512]{4,3,1,0,2:T(8,128)(2,1)S(1)}, bf16[4,4,1,16,512]{4,3,1,0,2:T(8,128)(2,1)S(1)}, u32[]{:S(2)}, u32[]{:S(2)}) collective-permute-start(bf16[4,4,1,16,512]{4,3,1,0,2:T(8,128)(2,1)S(1)} %bitcast_select_fusion), channel_id=1, source_target_pairs={{0,8},{8,0},{16,24},{24,16},{32,40},{40,32},{48,56},{56,48},{64,72... | collective-permute-start | bytes 786440 | tf_op jit(solution)/shard_map/ppermute | solution.py:75
  46.1 3.3 %copy-start = (f32[8,128,2048]{2,1,0:T(8,128)}, f32[8,128,2048]{2,1,0:T(8,128)S(1)}, u32[]{:S(2)}) copy-start(f32[8,128,2048]{2,1,0:T(8,128)S(1)} %fusion.4) | copy-start | bytes 25165828
  46.1 18.0 %copy-start.2 = (f32[1,8,2048]{2,1,0:T(8,128)S(1)}, f32[1,8,2048]{2,1,0:T(8,128)}, u32[]{:S(2)}) copy-start(f32[1,8,2048]{2,1,0:T(8,128)} %param.7) | copy-start | bytes 196612
  49.3 4.3 %collective-permute-start.7 = (f32[8,2048]{1,0:T(8,128)S(1)}, f32[8,2048]{1,0:T(8,128)S(1)}, u32[]{:S(2)}, u32[]{:S(2)}) collective-permute-start(f32[8,2048]{1,0:T(8,128)S(1)} %multiply_reduce_fusion), channel_id=1, source_target_pairs={{0,1},{1,0},{2,3},{3,2},{4,5},{5,4},{6,7},{7,6},{8,9},{9,8},{10,11... | collective-permute-start | bytes 196616 | tf_op jit(solution)/shard_map/ppermute | solution.py:19
  53.6 5.9 %collective-permute-start.8 = (f32[8,2048]{1,0:T(8,128)S(1)}, f32[8,2048]{1,0:T(8,128)S(1)}, u32[]{:S(2)}, u32[]{:S(2)}) collective-permute-start(f32[8,2048]{1,0:T(8,128)S(1)} %add.137), channel_id=1, source_target_pairs={{0,2},{1,3},{2,0},{3,1},{4,6},{5,7},{6,4},{7,5},{8,10},{9,11},{10,... | collective-permute-start | bytes 196616 | tf_op jit(solution)/shard_map/ppermute | solution.py:19
  59.5 4.6 %collective-permute-start.9 = (f32[8,2048]{1,0:T(8,128)S(1)}, f32[8,2048]{1,0:T(8,128)S(1)}, u32[]{:S(2)}, u32[]{:S(2)}) collective-permute-start(f32[8,2048]{1,0:T(8,128)S(1)} %add.138), channel_id=1, source_target_pairs={{0,4},{1,5},{2,6},{3,7},{4,0},{5,1},{6,2},{7,3},{8,12},{9,13},{10,... | collective-permute-start | bytes 196616 | tf_op jit(solution)/shard_map/ppermute | solution.py:19
  83.1 25.1 %copy-start.1 = (f32[16,8,64]{2,1,0:T(8,128)S(1)}, f32[16,8,64]{2,1,0:T(8,128)}, u32[]{:S(2)}) copy-start(f32[16,8,64]{2,1,0:T(8,128)} %param.11) | copy-start | bytes 98308
  85.7 2.0 %collective-permute-start.10 = (f32[2,2,2,2,16,512]{5,4,3,2,1,0:T(8,128)S(1)}, f32[2,2,2,2,16,512]{5,4,3,2,1,0:T(8,128)S(1)}, u32[]{:S(2)}, u32[]{:S(2)}) collective-permute-start(f32[2,2,2,2,16,512]{5,4,3,2,1,0:T(8,128)S(1)} %dynamic-slice_bitcast_fusion), channel_id=1, source_target_pairs={{0,8},{8,0},{16,24},{24,16},{32,40},{40,32},{48,56},{56,48},{64,72... | collective-permute-start | bytes 1572872 | tf_op jit(solution)/shard_map/ppermute | solution.py:75
  87.9 9.6 %collective-permute-start.13 = (f32[2,2,16,512]{3,2,1,0:T(8,128)S(1)}, f32[2,2,16,512]{3,2,1,0:T(8,128)S(1)}, u32[]{:S(2)}, u32[]{:S(2)}) collective-permute-start(f32[2,2,16,512]{3,2,1,0:T(8,128)S(1)} %get-tuple-element.7), channel_id=1, source_target_pairs={{0,48},{8,56},{16,32},{24,40},{32,16},{40,24},{48,0},{56,8},{64,11... | collective-permute-start | bytes 393224 | tf_op jit(solution)/shard_map/ppermute | solution.py:75
  89.2 8.3 %collective-permute-start.12 = (f32[2,2,16,512]{3,2,1,0:T(8,128)S(1)}, f32[2,2,16,512]{3,2,1,0:T(8,128)S(1)}, u32[]{:S(2)}, u32[]{:S(2)}) collective-permute-start(f32[2,2,16,512]{3,2,1,0:T(8,128)S(1)} %get-tuple-element.8), channel_id=1, source_target_pairs={{0,32},{8,40},{16,48},{24,56},{32,0},{40,8},{48,16},{56,24},{64,96... | collective-permute-start | bytes 393224 | tf_op jit(solution)/shard_map/ppermute | solution.py:75
  90.1 8.0 %collective-permute-start.11 = (f32[2,2,16,512]{3,2,1,0:T(8,128)S(1)}, f32[2,2,16,512]{3,2,1,0:T(8,128)S(1)}, u32[]{:S(2)}, u32[]{:S(2)}) collective-permute-start(f32[2,2,16,512]{3,2,1,0:T(8,128)S(1)} %get-tuple-element.6), channel_id=1, source_target_pairs={{0,16},{8,24},{16,0},{24,8},{32,48},{40,56},{48,32},{56,40},{64,80... | collective-permute-start | bytes 393224 | tf_op jit(solution)/shard_map/ppermute | solution.py:75
  98.2 6.6 %collective-permute-start.16 = (f32[16,512]{1,0:T(8,128)S(1)}, f32[16,512]{1,0:T(8,128)S(1)}, u32[]{:S(2)}, u32[]{:S(2)}) collective-permute-start(f32[16,512]{1,0:T(8,128)S(1)} %get-tuple-element.10), channel_id=1, source_target_pairs={{0,192},{8,200},{16,208},{24,216},{32,224},{40,232},{48,240},{56,2... | collective-permute-start | bytes 98312 | tf_op jit(solution)/shard_map/ppermute | solution.py:75
  100.3 7.8 %collective-permute-start.15 = (f32[16,512]{1,0:T(8,128)S(1)}, f32[16,512]{1,0:T(8,128)S(1)}, u32[]{:S(2)}, u32[]{:S(2)}) collective-permute-start(f32[16,512]{1,0:T(8,128)S(1)} %get-tuple-element.11), channel_id=1, source_target_pairs={{0,128},{8,136},{16,144},{24,152},{32,160},{40,168},{48,176},{56,1... | collective-permute-start | bytes 98312 | tf_op jit(solution)/shard_map/ppermute | solution.py:75
  103.3 4.8 %collective-permute-start.14 = (f32[16,512]{1,0:T(8,128)S(1)}, f32[16,512]{1,0:T(8,128)S(1)}, u32[]{:S(2)}, u32[]{:S(2)}) collective-permute-start(f32[16,512]{1,0:T(8,128)S(1)} %get-tuple-element.9), channel_id=1, source_target_pairs={{0,64},{8,72},{16,80},{24,88},{32,96},{40,104},{48,112},{56,120},{... | collective-permute-start | bytes 98312 | tf_op jit(solution)/shard_map/ppermute | solution.py:75

commit v4 on v3

--- a/solution.py
+++ b/solution.py
@@ -159,11 +159,11 @@
     power = ev_power[0].T
     weighted = (power[:, :, None] * looked).astype(jnp.bfloat16)
     node_hot = (ev_node[0][:, :, None] == lax.iota(jnp.int32, nodes)[None, None, :]).astype(jnp.bfloat16)
-    spread = jnp.einsum("hkm,khr->mhr", node_hot, weighted, preferred_element_type=jnp.float32)
-    both = jnp.concatenate(_split_bf16(spread), axis=2)
+    spread = jnp.einsum("khr,hkm->hrm", weighted, node_hot, preferred_element_type=jnp.float32)
+    spread_hi, spread_lo = _split_bf16(spread)
     sens = sensitivity[0]
-    volts_both = jnp.einsum("mhr,mn->hrn", both, sens, preferred_element_type=jnp.float32)
-    factor_volts = volts_both[:, :columns] + volts_both[:, columns:]
+    factor_volts = jnp.einsum("hrm,mn->hrn", spread_hi, sens, preferred_element_type=jnp.float32)
+    factor_volts = factor_volts + jnp.einsum("hrm,mn->hrn", spread_lo, sens, preferred_element_type=jnp.float32)
     partial_sum = jnp.sum(factor_volts * factor_volts, axis=1)
     variance = sum_all(partial_sum, "factor")[None]
     deviation = jnp.sqrt(variance + epsilon)
@@ -171,16 +171,14 @@
     violation = jnp.maximum(-margin, 0.0)
     var_grad = quantile * violation / deviation
     volt_grad = (2.0 * var_grad[0][:, None, :] * factor_volts).astype(jnp.bfloat16)
-    node_grads = jnp.einsum("mn,hrn->mhr", sens, volt_grad, preferred_element_type=jnp.float32)
-    picked = jnp.einsum(
-        "hkm,mhr->khr",
-        node_hot,
-        node_grads,
-        precision=lax.Precision.HIGHEST,
-        preferred_element_type=jnp.float32,
-    )
+    node_grads = jnp.einsum("hrn,mn->hrm", volt_grad, sens, preferred_element_type=jnp.float32)
+    both = jnp.concatenate(_split_bf16(node_grads), axis=1)
+    picked_both = jnp.einsum("hkm,hrm->khr", node_hot, both, preferred_element_type=jnp.float32)
+    picked = picked_both[:, :, :columns] + picked_both[:, :, columns:]
     member_grads = (power[:, :, None] * picked).reshape(ev_count, hours * columns)
-    summed = jax.ops.segment_sum(member_grads, regions, num_segments=total_regions)
+    grads_hi, grads_lo = _split_bf16(member_grads)
+    summed = jnp.einsum("kg,kc->gc", matches, grads_hi, preferred_element_type=jnp.float32)
+    summed = summed + jnp.einsum("kg,kc->gc", matches, grads_lo, preferred_element_type=jnp.float32)
     reduced = scatter_groups(summed, "feeder", _bit_groups("feeder")[::-1])
     new_loadings = loadings - step_size * reduced.reshape(reg_local, hours, columns)
     return (margin, new_loadings)

time: 109 us -> 106 us (0.972)
  other arithmetic: 6.37 us -> 3.08 us
  matrix products: 35.7 us -> 38.4 us
  local copies, waits for them, and re-layouts: 4.68 us -> 2.36 us
    dot_general x4 -> x7, matrix products: 35.7 us -> 38.4 us  [the longest x1 9.63 us: shards(): jnp.einsum('hrm,mn->hrn', spread_hi, sens, preferred_element_type=jnp.flo...]
    scatter-add x1 -> x0, other arithmetic: 2.34 us -> none  [shards(): jax.ops.segment_sum(member_grads, regions, num_segments=total_regions)]
    unnamed x12, local copies, waits for them, and re-layouts: 2.15 us -> 0.03 us
    reduce_sum x1 -> x0, other arithmetic: 1.1 us -> none  [shards(): partial_sum = jnp.sum(factor_volts * factor_volts, axis=1)]
where the time goes in v4:
time: 106 us
  matrix products  38.4 us (36%)
  waiting for transfers between devices  33.9 us (32%)
  starting transfers between devices  27.2 us (26%)
  other arithmetic  3.08 us (3%)
  local copies, waits for them, and re-layouts  2.36 us (2%)
    ppermute x14, starting transfers between devices, _send_all(): out[j] = lax.ppermute(x_for(j), axis, [(i, i ^ m) for i in range(size)])  24.1 us
    ppermute x14, waiting for transfers between devices, _send_all(): out[j] = lax.ppermute(x_for(j), axis, [(i, i ^ m) for i in range(size)])  22.3 us
    ppermute x3, waiting for transfers between devices, _exchange(): return lax.ppermute(x, axis, perm)  11.6 us
    dot_general x1, matrix products, shards(): jnp.einsum('hrm,mn->hrn', spread_hi, sens, preferred_element_type=jnp.flo...  9.63 us
    dot_general x1, matrix products, shards(): jnp.einsum('hrn,mn->hrm', volt_grad, sens, preferred_element_type=jnp.flo...  9.21 us
    dot_general x1, matrix products, shards(): jnp.einsum('hrm,mn->hrn', spread_lo, sens, preferred_element_type=jnp.flo...  9.08 us
    dot_general x1, matrix products, shards(): jnp.einsum('khr,hkm->hrm', weighted, node_hot, preferred_element_type=jnp...  5.48 us
    dot_general x1, matrix products, shards(): jnp.einsum('hkm,hrm->khr', node_hot, both, preferred_element_type=jnp.flo...  4.17 us
  transfers between devices with their start and end apart: 17, of which 11 were waited for; matrix products, arithmetic and copies ran while one was open for 0% of the time, Pallas kernels for 0%

profile of v4, /device:TPU:4, one launch (start us, length us, event | category | flops | bytes accessed | tf_op | source)
XLA Modules:
  0.0 105.9 jit_solution(13022612264635493787)
XLA Ops:
  0.7 0.9 convert_element_type.29
  1.5 0.1 broadcast_in_dim_reshape.4
  1.6 6.4 %collective-permute-start.2 = (bf16[1,16,512]{2,1,0:T(8,128)(2,1)S(1)}, bf16[1,16,512]{2,1,0:T(8,128)(2,1)S(1)}, u32[]{:S(2)}, u32[]{:S(2)}) collective-permute-start(bf16[1,16,512]{2,1,0:T(8,128)(2,1)S(1)} %broadcast_in_dim_reshape.4), channel_id=1, source_target_pairs={{0,192},{8,200},{16,208},{24,216},{32,224},{40,232},{48,240},{56,2... | collective-permute-start | bytes 49160 | tf_op jit(solution)/shard_map/ppermute | solution.py:75
  8.0 1.0 collective-permute-start.1
  9.0 1.5 %collective-permute-start = (bf16[1,16,512]{2,1,0:T(8,128)(2,1)S(1)}, bf16[1,16,512]{2,1,0:T(8,128)(2,1)S(1)}, u32[]{:S(2)}, u32[]{:S(2)}) collective-permute-start(bf16[1,16,512]{2,1,0:T(8,128)(2,1)S(1)} %broadcast_in_dim_reshape.4), channel_id=1, source_target_pairs={{0,64},{8,72},{16,80},{24,88},{32,96},{40,104},{48,112},{56,120},{... | collective-permute-start | bytes 49160 | tf_op jit(solution)/shard_map/ppermute | solution.py:75
  10.6 0.1 stack_broadcast_in_dim_reshape.3
  10.7 0.0 collective-permute-done.2
  10.7 5.0 %collective-permute-done.1 = bf16[1,16,512]{2,1,0:T(8,128)(2,1)S(1)} collective-permute-done((bf16[1,16,512]{2,1,0:T(8,128)(2,1)S(1)}, bf16[1,16,512]{2,1,0:T(8,128)(2,1)S(1)}, u32[]{:S(2)}, u32[]{:S(2)}) %collective-permute-start.1) | collective-permute-done | bytes 16416 | tf_op jit(solution)/shard_map/ppermute | solution.py:75
  15.7 0.0 collective-permute-done
  15.7 0.6 gather_fusion
  16.2 0.1 bitcast_select_fusion.2
  16.3 3.0 %collective-permute-start.5 = (bf16[4,1,16,512]{3,2,0,1:T(8,128)(2,1)S(1)}, bf16[4,1,16,512]{3,2,0,1:T(8,128)(2,1)S(1)}, u32[]{:S(2)}, u32[]{:S(2)}) collective-permute-start(bf16[4,1,16,512]{3,2,0,1:T(8,128)(2,1)S(1)} %bitcast_select_fusion.2), channel_id=1, source_target_pairs={{0,48},{8,56},{16,32},{24,40},{32,16},{40,24},{48,0},{56,8},{64,11... | collective-permute-start | bytes 196616 | tf_op jit(solution)/shard_map/ppermute | solution.py:75
  19.4 0.6 collective-permute-start.4
  20.0 0.5 collective-permute-start.3
  20.4 0.1 bitcast_select_fusion.3
  20.5 2.0 %collective-permute-done.5 = bf16[4,1,16,512]{3,2,0,1:T(8,128)(2,1)S(1)} collective-permute-done((bf16[4,1,16,512]{3,2,0,1:T(8,128)(2,1)S(1)}, bf16[4,1,16,512]{3,2,0,1:T(8,128)(2,1)S(1)}, u32[]{:S(2)}, u32[]{:S(2)}) %collective-permute-start.5) | collective-permute-done | bytes 65568 | tf_op jit(solution)/shard_map/ppermute | solution.py:75
  22.5 2.6 %collective-permute-done.4 = bf16[4,1,16,512]{3,2,0,1:T(8,128)(2,1)S(1)} collective-permute-done((bf16[4,1,16,512]{3,2,0,1:T(8,128)(2,1)S(1)}, bf16[4,1,16,512]{3,2,0,1:T(8,128)(2,1)S(1)}, u32[]{:S(2)}, u32[]{:S(2)}) %collective-permute-start.4) | collective-permute-done | bytes 65568 | tf_op jit(solution)/shard_map/ppermute | solution.py:75
  25.1 0.0 collective-permute-done.3
  25.2 0.6 gather_fusion.1
  25.7 0.1 bitcast_select_fusion
  25.8 0.3 collective-permute-start.6
  26.1 0.1 fusion.33
  26.2 1.4 %collective-permute-done.6 = bf16[4,4,1,16,512]{4,3,1,0,2:T(8,128)(2,1)S(1)} collective-permute-done((bf16[4,4,1,16,512]{4,3,1,0,2:T(8,128)(2,1)S(1)}, bf16[4,4,1,16,512]{4,3,1,0,2:T(8,128)(2,1)S(1)}, u32[]{:S(2)}, u32[]{:S(2)}) %collective-permute-start.6) | collective-permute-done | bytes 262176 | tf_op jit(solution)/shard_map/ppermute | solution.py:75
  27.6 0.1 maximum_bitcast_fusion
  27.7 0.6 gather_fusion.2
  28.3 0.1 select_bitcast_fusion
  28.4 0.2 copy.11
  28.7 0.0 copy-done.4
  28.7 0.0 copy-done.3
  28.7 5.5 %fusion.1 = f32[8,64,2048]{2,1,0:T(8,128)} fusion(s32[8,256]{1,0:T(8,128)S(1)} %bitcast.134, bf16[8,64,512]{2,1,0:T(8,128)(2,1)S(1)} %bitcast.119, s32[256]{0:T(256)S(1)} %bitcast.131, f32[256,8]{0,1:T(8,128)S(1)} %bitcast.129), kind=kOutput, calls=%fused_computation.5 | convolution fusion | flops 675676160 | bytes 4736000 | tf_op jit(solution)/shard_map/khr,hkm->hrm/dot_general | solution.py:162
  34.2 9.1 %fusion.4 = f32[8,64,2048]{2,1,0:T(8,128)S(1)} fusion(bf16[1,2048,2048]{2,1,0:T(8,128)(2,1)} %param.6, f32[8,64,2048]{2,1,0:T(8,128)} %fusion.1), kind=kOutput, calls=%fused_computation.8 | convolution fusion | flops 4298113024 | bytes 16777216 | tf_op jit(solution)/shard_map/hrm,mn->hrn/dot_general | solution.py:166
  43.3 0.0 copy-start.1
  43.3 9.6 %multiply_reduce_fusion = (f32[8,2048]{1,0:T(8,128)S(1)}, f32[8,64,2048]{2,1,0:T(8,128)}) fusion(f32[8,64,2048]{2,1,0:T(8,128)S(1)} %fusion.4, bf16[1,2048,2048]{2,1,0:T(8,128)(2,1)} %param.6, f32[8,64,2048]{2,1,0:T(8,128)S(1)} %copy-done.5), kind=kOutput, calls=%fused_computation.24 | convolution fusion | flops 4300193792 | bytes 21037056 | tf_op jit(solution)/shard_map/hrm,mn->hrn/dot_general | solution.py:165
  52.9 1.2 %collective-permute-start.7 = (f32[8,2048]{1,0:T(8,128)S(1)}, f32[8,2048]{1,0:T(8,128)S(1)}, u32[]{:S(2)}, u32[]{:S(2)}) collective-permute-start(f32[8,2048]{1,0:T(8,128)S(1)} %get-tuple-element.14), channel_id=1, source_target_pairs={{0,1},{1,0},{2,3},{3,2},{4,5},{5,4},{6,7},{7,6},{8,9},{9,8},{10,11... | collective-permute-start | bytes 196616 | tf_op jit(solution)/shard_map/ppermute | solution.py:19
  54.1 3.1 %collective-permute-done.7 = f32[8,2048]{1,0:T(8,128)S(1)} collective-permute-done((f32[8,2048]{1,0:T(8,128)S(1)}, f32[8,2048]{1,0:T(8,128)S(1)}, u32[]{:S(2)}, u32[]{:S(2)}) %collective-permute-start.7) | collective-permute-done | bytes 65568 | tf_op jit(solution)/shard_map/ppermute | solution.py:19
  57.2 0.6 collective-permute-start.8
  57.8 5.3 %collective-permute-done.8 = f32[8,2048]{1,0:T(8,128)S(1)} collective-permute-done((f32[8,2048]{1,0:T(8,128)S(1)}, f32[8,2048]{1,0:T(8,128)S(1)}, u32[]{:S(2)}, u32[]{:S(2)}) %collective-permute-start.8) | collective-permute-done | bytes 65568 | tf_op jit(solution)/shard_map/ppermute | solution.py:19
  63.1 1.3 %collective-permute-start.9 = (f32[8,2048]{1,0:T(8,128)S(1)}, f32[8,2048]{1,0:T(8,128)S(1)}, u32[]{:S(2)}, u32[]{:S(2)}) collective-permute-start(f32[8,2048]{1,0:T(8,128)S(1)} %add.142), channel_id=1, source_target_pairs={{0,4},{1,5},{2,6},{3,7},{4,0},{5,1},{6,2},{7,3},{8,12},{9,13},{10,... | collective-permute-start | bytes 196616 | tf_op jit(solution)/shard_map/ppermute | solution.py:19
  64.4 3.2 %collective-permute-done.9 = f32[8,2048]{1,0:T(8,128)S(1)} collective-permute-done((f32[8,2048]{1,0:T(8,128)S(1)}, f32[8,2048]{1,0:T(8,128)S(1)}, u32[]{:S(2)}, u32[]{:S(2)}) %collective-permute-start.9) | collective-permute-done | bytes 65568 | tf_op jit(solution)/shard_map/ppermute | solution.py:19
  67.6 0.7 fusion.42
  68.3 9.2 %reduce-precision_convert_fusion = (bf16[8,64,2048]{2,1,0:T(8,128)(2,1)S(1)}, bf16[8,64,2048]{2,1,0:T(8,128)(2,1)S(1)}) fusion(bf16[1,2048,2048]{2,1,0:T(8,128)(2,1)} %param.6, f32[8,64,2048]{2,1,0:T(8,128)} %get-tuple-element.15, f32[8,2048]{1,0:T(8,128)S(1)} %get-tuple-element.2), kind=kOutput, calls=%fused_computation.15 | convolution fusion | flops 4301258752 | bytes 16842752 | tf_op jit(solution)/shard_map/hrn,mn->hrm/dot_general | solution.py:174
  77.5 4.2 %fusion.20 = f32[256,8,128]{0,2,1:T(8,128)S(1)} fusion(s32[8,256]{1,0:T(8,128)S(1)} %bitcast.135, bf16[8,64,2048]{2,1,0:T(8,128)(2,1)S(1)} %get-tuple-element.5, bf16[8,64,2048]{2,1,0:T(8,128)(2,1)S(1)} %get-tuple-element.4), kind=kOutput, calls=%fused_computation.27 | convolution fusion | flops 1086324736 | bytes 5251072 | tf_op jit(solution)/shard_map/hkm,hrm->khr/dot_general | solution.py:176
  81.7 0.1 fusion.25
  81.8 0.1 fusion.24
  81.9 0.0 copy-start
  81.9 0.4 fusion.31
  82.3 0.4 convolution_add_fusion
  82.8 0.1 collective-permute-start.10
  82.9 1.9 %collective-permute-done.10 = f32[2,2,2,2,16,512]{5,4,3,2,1,0:T(8,128)S(1)} collective-permute-done((f32[2,2,2,2,16,512]{5,4,3,2,1,0:T(8,128)S(1)}, f32[2,2,2,2,16,512]{5,4,3,2,1,0:T(8,128)S(1)}, u32[]{:S(2)}, u32[]{:S(2)}) %collective-permute-start.10) | collective-permute-done | bytes 524320 | tf_op jit(solution)/shard_map/ppermute | solution.py:75
  84.8 0.1 bitcast_add_fusion
  84.9 1.4 %collective-permute-start.13 = (f32[2,2,16,512]{3,2,1,0:T(8,128)S(1)}, f32[2,2,16,512]{3,2,1,0:T(8,128)S(1)}, u32[]{:S(2)}, u32[]{:S(2)}) collective-permute-start(f32[2,2,16,512]{3,2,1,0:T(8,128)S(1)} %get-tuple-element.7), channel_id=1, source_target_pairs={{0,48},{8,56},{16,32},{24,40},{32,16},{40,24},{48,0},{56,8},{64,11... | collective-permute-start | bytes 393224 | tf_op jit(solution)/shard_map/ppermute | solution.py:75
  86.3 0.9 collective-permute-start.12
  87.2 1.9 %collective-permute-start.11 = (f32[2,2,16,512]{3,2,1,0:T(8,128)S(1)}, f32[2,2,16,512]{3,2,1,0:T(8,128)S(1)}, u32[]{:S(2)}, u32[]{:S(2)}) collective-permute-start(f32[2,2,16,512]{3,2,1,0:T(8,128)S(1)} %get-tuple-element.6), channel_id=1, source_target_pairs={{0,16},{8,24},{16,0},{24,8},{32,48},{40,56},{48,32},{56,40},{64,80... | collective-permute-start | bytes 393224 | tf_op jit(solution)/shard_map/ppermute | solution.py:75
  89.1 5.5 %collective-permute-done.13 = f32[2,2,16,512]{3,2,1,0:T(8,128)S(1)} collective-permute-done((f32[2,2,16,512]{3,2,1,0:T(8,128)S(1)}, f32[2,2,16,512]{3,2,1,0:T(8,128)S(1)}, u32[]{:S(2)}, u32[]{:S(2)}) %collective-permute-start.13) | collective-permute-done | bytes 131104 | tf_op jit(solution)/shard_map/ppermute | solution.py:75
  94.6 0.0 collective-permute-done.12
  94.6 0.6 collective-permute-done.11
  95.3 2.1 %collective-permute-start.16 = (f32[16,512]{1,0:T(8,128)S(1)}, f32[16,512]{1,0:T(8,128)S(1)}, u32[]{:S(2)}, u32[]{:S(2)}) collective-permute-start(f32[16,512]{1,0:T(8,128)S(1)} %get-tuple-element.12), channel_id=1, source_target_pairs={{0,192},{8,200},{16,208},{24,216},{32,224},{40,232},{48,240},{56,2... | collective-permute-start | bytes 98312 | tf_op jit(solution)/shard_map/ppermute | solution.py:75
  97.4 3.0 %collective-permute-start.15 = (f32[16,512]{1,0:T(8,128)S(1)}, f32[16,512]{1,0:T(8,128)S(1)}, u32[]{:S(2)}, u32[]{:S(2)}) collective-permute-start(f32[16,512]{1,0:T(8,128)S(1)} %get-tuple-element.13), channel_id=1, source_target_pairs={{0,128},{8,136},{16,144},{24,152},{32,160},{40,168},{48,176},{56,1... | collective-permute-start | bytes 98312 | tf_op jit(solution)/shard_map/ppermute | solution.py:75
  100.4 1.5 %collective-permute-start.14 = (f32[16,512]{1,0:T(8,128)S(1)}, f32[16,512]{1,0:T(8,128)S(1)}, u32[]{:S(2)}, u32[]{:S(2)}) collective-permute-start(f32[16,512]{1,0:T(8,128)S(1)} %get-tuple-element.11), channel_id=1, source_target_pairs={{0,64},{8,72},{16,80},{24,88},{32,96},{40,104},{48,112},{56,120},{... | collective-permute-start | bytes 98312 | tf_op jit(solution)/shard_map/ppermute | solution.py:75
  101.9 0.0 collective-permute-done.16
  101.9 3.3 %collective-permute-done.15 = f32[16,512]{1,0:T(8,128)S(1)} collective-permute-done((f32[16,512]{1,0:T(8,128)S(1)}, f32[16,512]{1,0:T(8,128)S(1)}, u32[]{:S(2)}, u32[]{:S(2)}) %collective-permute-start.15) | collective-permute-done | bytes 32800 | tf_op jit(solution)/shard_map/ppermute | solution.py:75
  105.2 0.0 collective-permute-done.14
  105.2 0.1 mul.81
  105.3 0.6 sub.19
  (26 shorter events, 0.3 us)
Async XLA Ops:
  0.6 28.0 %copy-start.4 = (s32[1,8,256]{2,1,0:T(8,128)S(1)}, s32[1,8,256]{2,1,0:T(8,128)}, u32[]{:S(2)}) copy-start(s32[1,8,256]{2,1,0:T(8,128)} %param.9) | copy-start | bytes 24580
  0.6 28.0 %copy-start.3 = (s32[1,256]{1,0:T(1,128)S(1)}, s32[1,256]{1,0:T(1,128)}, u32[]{:S(2)}) copy-start(s32[1,256]{1,0:T(1,128)} %param.10) | copy-start | bytes 3076
  0.7 28.0 %copy-start.2 = (f32[1,8,256]{2,1,0:T(8,128)S(1)}, f32[1,8,256]{2,1,0:T(8,128)}, u32[]{:S(2)}) copy-start(f32[1,8,256]{2,1,0:T(8,128)} %param.8) | copy-start | bytes 24580
  1.6 9.0 %collective-permute-start.2 = (bf16[1,16,512]{2,1,0:T(8,128)(2,1)S(1)}, bf16[1,16,512]{2,1,0:T(8,128)(2,1)S(1)}, u32[]{:S(2)}, u32[]{:S(2)}) collective-permute-start(bf16[1,16,512]{2,1,0:T(8,128)(2,1)S(1)} %broadcast_in_dim_reshape.4), channel_id=1, source_target_pairs={{0,192},{8,200},{16,208},{24,216},{32,224},{40,232},{48,240},{56,2... | collective-permute-start | bytes 49160 | tf_op jit(solution)/shard_map/ppermute | solution.py:75
  8.0 7.6 %collective-permute-start.1 = (bf16[1,16,512]{2,1,0:T(8,128)(2,1)S(1)}, bf16[1,16,512]{2,1,0:T(8,128)(2,1)S(1)}, u32[]{:S(2)}, u32[]{:S(2)}) collective-permute-start(bf16[1,16,512]{2,1,0:T(8,128)(2,1)S(1)} %broadcast_in_dim_reshape.4), channel_id=1, source_target_pairs={{0,128},{8,136},{16,144},{24,152},{32,160},{40,168},{48,176},{56,1... | collective-permute-start | bytes 49160 | tf_op jit(solution)/shard_map/ppermute | solution.py:75
  9.0 6.7 %collective-permute-start = (bf16[1,16,512]{2,1,0:T(8,128)(2,1)S(1)}, bf16[1,16,512]{2,1,0:T(8,128)(2,1)S(1)}, u32[]{:S(2)}, u32[]{:S(2)}) collective-permute-start(bf16[1,16,512]{2,1,0:T(8,128)(2,1)S(1)} %broadcast_in_dim_reshape.4), channel_id=1, source_target_pairs={{0,64},{8,72},{16,80},{24,88},{32,96},{40,104},{48,112},{56,120},{... | collective-permute-start | bytes 49160 | tf_op jit(solution)/shard_map/ppermute | solution.py:75
  16.3 6.2 %collective-permute-start.5 = (bf16[4,1,16,512]{3,2,0,1:T(8,128)(2,1)S(1)}, bf16[4,1,16,512]{3,2,0,1:T(8,128)(2,1)S(1)}, u32[]{:S(2)}, u32[]{:S(2)}) collective-permute-start(bf16[4,1,16,512]{3,2,0,1:T(8,128)(2,1)S(1)} %bitcast_select_fusion.2), channel_id=1, source_target_pairs={{0,48},{8,56},{16,32},{24,40},{32,16},{40,24},{48,0},{56,8},{64,11... | collective-permute-start | bytes 196616 | tf_op jit(solution)/shard_map/ppermute | solution.py:75
  19.4 5.8 %collective-permute-start.4 = (bf16[4,1,16,512]{3,2,0,1:T(8,128)(2,1)S(1)}, bf16[4,1,16,512]{3,2,0,1:T(8,128)(2,1)S(1)}, u32[]{:S(2)}, u32[]{:S(2)}) collective-permute-start(bf16[4,1,16,512]{3,2,0,1:T(8,128)(2,1)S(1)} %bitcast_select_fusion.2), channel_id=1, source_target_pairs={{0,32},{8,40},{16,48},{24,56},{32,0},{40,8},{48,16},{56,24},{64,96... | collective-permute-start | bytes 196616 | tf_op jit(solution)/shard_map/ppermute | solution.py:75
  20.0 5.1 %collective-permute-start.3 = (bf16[4,1,16,512]{3,2,0,1:T(8,128)(2,1)S(1)}, bf16[4,1,16,512]{3,2,0,1:T(8,128)(2,1)S(1)}, u32[]{:S(2)}, u32[]{:S(2)}) collective-permute-start(bf16[4,1,16,512]{3,2,0,1:T(8,128)(2,1)S(1)} %bitcast_select_fusion.2), channel_id=1, source_target_pairs={{0,16},{8,24},{16,0},{24,8},{32,48},{40,56},{48,32},{56,40},{64,80... | collective-permute-start | bytes 196616 | tf_op jit(solution)/shard_map/ppermute | solution.py:75
  25.8 1.8 %collective-permute-start.6 = (bf16[4,4,1,16,512]{4,3,1,0,2:T(8,128)(2,1)S(1)}, bf16[4,4,1,16,512]{4,3,1,0,2:T(8,128)(2,1)S(1)}, u32[]{:S(2)}, u32[]{:S(2)}) collective-permute-start(bf16[4,4,1,16,512]{4,3,1,0,2:T(8,128)(2,1)S(1)} %bitcast_select_fusion), channel_id=1, source_target_pairs={{0,8},{8,0},{16,24},{24,16},{32,40},{40,32},{48,56},{56,48},{64,72... | collective-permute-start | bytes 786440 | tf_op jit(solution)/shard_map/ppermute | solution.py:75
  34.2 9.1 %copy-start.5 = (f32[8,64,2048]{2,1,0:T(8,128)S(1)}, f32[8,64,2048]{2,1,0:T(8,128)}, u32[]{:S(2)}) copy-start(f32[8,64,2048]{2,1,0:T(8,128)} %fusion.1) | copy-start | bytes 12582916
  43.3 24.4 %copy-start.1 = (f32[1,8,2048]{2,1,0:T(8,128)S(1)}, f32[1,8,2048]{2,1,0:T(8,128)}, u32[]{:S(2)}) copy-start(f32[1,8,2048]{2,1,0:T(8,128)} %param.7) | copy-start | bytes 196612
  52.9 4.3 %collective-permute-start.7 = (f32[8,2048]{1,0:T(8,128)S(1)}, f32[8,2048]{1,0:T(8,128)S(1)}, u32[]{:S(2)}, u32[]{:S(2)}) collective-permute-start(f32[8,2048]{1,0:T(8,128)S(1)} %get-tuple-element.14), channel_id=1, source_target_pairs={{0,1},{1,0},{2,3},{3,2},{4,5},{5,4},{6,7},{7,6},{8,9},{9,8},{10,11... | collective-permute-start | bytes 196616 | tf_op jit(solution)/shard_map/ppermute | solution.py:19
  57.2 5.9 %collective-permute-start.8 = (f32[8,2048]{1,0:T(8,128)S(1)}, f32[8,2048]{1,0:T(8,128)S(1)}, u32[]{:S(2)}, u32[]{:S(2)}) collective-permute-start(f32[8,2048]{1,0:T(8,128)S(1)} %add.141), channel_id=1, source_target_pairs={{0,2},{1,3},{2,0},{3,1},{4,6},{5,7},{6,4},{7,5},{8,10},{9,11},{10,... | collective-permute-start | bytes 196616 | tf_op jit(solution)/shard_map/ppermute | solution.py:19
  63.1 4.6 %collective-permute-start.9 = (f32[8,2048]{1,0:T(8,128)S(1)}, f32[8,2048]{1,0:T(8,128)S(1)}, u32[]{:S(2)}, u32[]{:S(2)}) collective-permute-start(f32[8,2048]{1,0:T(8,128)S(1)} %add.142), channel_id=1, source_target_pairs={{0,4},{1,5},{2,6},{3,7},{4,0},{5,1},{6,2},{7,3},{8,12},{9,13},{10,... | collective-permute-start | bytes 196616 | tf_op jit(solution)/shard_map/ppermute | solution.py:19
  81.9 23.4 %copy-start = (f32[16,8,64]{2,1,0:T(8,128)S(1)}, f32[16,8,64]{2,1,0:T(8,128)}, u32[]{:S(2)}) copy-start(f32[16,8,64]{2,1,0:T(8,128)} %param.11) | copy-start | bytes 98308
  82.8 2.0 %collective-permute-start.10 = (f32[2,2,2,2,16,512]{5,4,3,2,1,0:T(8,128)S(1)}, f32[2,2,2,2,16,512]{5,4,3,2,1,0:T(8,128)S(1)}, u32[]{:S(2)}, u32[]{:S(2)}) collective-permute-start(f32[2,2,2,2,16,512]{5,4,3,2,1,0:T(8,128)S(1)} %dynamic-slice_bitcast_fusion), channel_id=1, source_target_pairs={{0,8},{8,0},{16,24},{24,16},{32,40},{40,32},{48,56},{56,48},{64,72... | collective-permute-start | bytes 1572872 | tf_op jit(solution)/shard_map/ppermute | solution.py:75
  84.9 9.6 %collective-permute-start.13 = (f32[2,2,16,512]{3,2,1,0:T(8,128)S(1)}, f32[2,2,16,512]{3,2,1,0:T(8,128)S(1)}, u32[]{:S(2)}, u32[]{:S(2)}) collective-permute-start(f32[2,2,16,512]{3,2,1,0:T(8,128)S(1)} %get-tuple-element.7), channel_id=1, source_target_pairs={{0,48},{8,56},{16,32},{24,40},{32,16},{40,24},{48,0},{56,8},{64,11... | collective-permute-start | bytes 393224 | tf_op jit(solution)/shard_map/ppermute | solution.py:75
  86.3 8.3 %collective-permute-start.12 = (f32[2,2,16,512]{3,2,1,0:T(8,128)S(1)}, f32[2,2,16,512]{3,2,1,0:T(8,128)S(1)}, u32[]{:S(2)}, u32[]{:S(2)}) collective-permute-start(f32[2,2,16,512]{3,2,1,0:T(8,128)S(1)} %get-tuple-element.8), channel_id=1, source_target_pairs={{0,32},{8,40},{16,48},{24,56},{32,0},{40,8},{48,16},{56,24},{64,96... | collective-permute-start | bytes 393224 | tf_op jit(solution)/shard_map/ppermute | solution.py:75
  87.2 8.0 %collective-permute-start.11 = (f32[2,2,16,512]{3,2,1,0:T(8,128)S(1)}, f32[2,2,16,512]{3,2,1,0:T(8,128)S(1)}, u32[]{:S(2)}, u32[]{:S(2)}) collective-permute-start(f32[2,2,16,512]{3,2,1,0:T(8,128)S(1)} %get-tuple-element.6), channel_id=1, source_target_pairs={{0,16},{8,24},{16,0},{24,8},{32,48},{40,56},{48,32},{56,40},{64,80... | collective-permute-start | bytes 393224 | tf_op jit(solution)/shard_map/ppermute | solution.py:75
  95.3 6.6 %collective-permute-start.16 = (f32[16,512]{1,0:T(8,128)S(1)}, f32[16,512]{1,0:T(8,128)S(1)}, u32[]{:S(2)}, u32[]{:S(2)}) collective-permute-start(f32[16,512]{1,0:T(8,128)S(1)} %get-tuple-element.12), channel_id=1, source_target_pairs={{0,192},{8,200},{16,208},{24,216},{32,224},{40,232},{48,240},{56,2... | collective-permute-start | bytes 98312 | tf_op jit(solution)/shard_map/ppermute | solution.py:75
  97.4 7.8 %collective-permute-start.15 = (f32[16,512]{1,0:T(8,128)S(1)}, f32[16,512]{1,0:T(8,128)S(1)}, u32[]{:S(2)}, u32[]{:S(2)}) collective-permute-start(f32[16,512]{1,0:T(8,128)S(1)} %get-tuple-element.13), channel_id=1, source_target_pairs={{0,128},{8,136},{16,144},{24,152},{32,160},{40,168},{48,176},{56,1... | collective-permute-start | bytes 98312 | tf_op jit(solution)/shard_map/ppermute | solution.py:75
  100.4 4.8 %collective-permute-start.14 = (f32[16,512]{1,0:T(8,128)S(1)}, f32[16,512]{1,0:T(8,128)S(1)}, u32[]{:S(2)}, u32[]{:S(2)}) collective-permute-start(f32[16,512]{1,0:T(8,128)S(1)} %get-tuple-element.11), channel_id=1, source_target_pairs={{0,64},{8,72},{16,80},{24,88},{32,96},{40,104},{48,112},{56,120},{... | collective-permute-start | bytes 98312 | tf_op jit(solution)/shard_map/ppermute | solution.py:75

commit v5 on v4

--- a/solution.py
+++ b/solution.py
@@ -160,10 +160,10 @@
     weighted = (power[:, :, None] * looked).astype(jnp.bfloat16)
     node_hot = (ev_node[0][:, :, None] == lax.iota(jnp.int32, nodes)[None, None, :]).astype(jnp.bfloat16)
     spread = jnp.einsum("khr,hkm->hrm", weighted, node_hot, preferred_element_type=jnp.float32)
-    spread_hi, spread_lo = _split_bf16(spread)
+    spread_both = jnp.concatenate(_split_bf16(spread), axis=1)
     sens = sensitivity[0]
-    factor_volts = jnp.einsum("hrm,mn->hrn", spread_hi, sens, preferred_element_type=jnp.float32)
-    factor_volts = factor_volts + jnp.einsum("hrm,mn->hrn", spread_lo, sens, preferred_element_type=jnp.float32)
+    volts_both = jnp.einsum("hrm,mn->hrn", spread_both, sens, preferred_element_type=jnp.float32)
+    factor_volts = volts_both[:, :columns] + volts_both[:, columns:]
     partial_sum = jnp.sum(factor_volts * factor_volts, axis=1)
     variance = sum_all(partial_sum, "factor")[None]
     deviation = jnp.sqrt(variance + epsilon)

time: 106 us -> 104 us (0.981)
  matrix products: 38.4 us -> 32.8 us
  local copies, waits for them, and re-layouts: 2.36 us -> 4.5 us
  other arithmetic: 3.08 us -> 4.18 us
    dot_general x2 -> x1, matrix products: 18.7 us -> 12.1 us  [shards(): jnp.einsum('hrm,mn->hrn', spread_both, sens, preferred_element_type=jnp.f...]
    unnamed x12, local copies, waits for them, and re-layouts: 0.03 us -> 2.17 us
    dot_general x1, matrix products: 9.21 us -> 10.4 us  [shards(): jnp.einsum('hrn,mn->hrm', volt_grad, sens, preferred_element_type=jnp.flo...]
    reduce_sum x0 -> x1, other arithmetic: none -> 1.1 us  [shards(): partial_sum = jnp.sum(factor_volts * factor_volts, axis=1)]
where the time goes in v5:
time: 104 us
  waiting for transfers between devices  33.9 us (33%)
  matrix products  32.8 us (32%)
  starting transfers between devices  27.2 us (26%)
  local copies, waits for them, and re-layouts  4.5 us (4%)
  other arithmetic  4.18 us (4%)
    ppermute x14, starting transfers between devices, _send_all(): out[j] = lax.ppermute(x_for(j), axis, [(i, i ^ m) for i in range(size)])  24.1 us
    ppermute x14, waiting for transfers between devices, _send_all(): out[j] = lax.ppermute(x_for(j), axis, [(i, i ^ m) for i in range(size)])  22.3 us
    dot_general x1, matrix products, shards(): jnp.einsum('hrm,mn->hrn', spread_both, sens, preferred_element_type=jnp.f...  12.1 us
    ppermute x3, waiting for transfers between devices, _exchange(): return lax.ppermute(x, axis, perm)  11.6 us
    dot_general x1, matrix products, shards(): jnp.einsum('hrn,mn->hrm', volt_grad, sens, preferred_element_type=jnp.flo...  10.4 us
    dot_general x1, matrix products, shards(): jnp.einsum('khr,hkm->hrm', weighted, node_hot, preferred_element_type=jnp...  5.26 us
    dot_general x1, matrix products, shards(): jnp.einsum('hkm,hrm->khr', node_hot, both, preferred_element_type=jnp.flo...  4.15 us
    ppermute x3, starting transfers between devices, _exchange(): return lax.ppermute(x, axis, perm)  3.12 us
  transfers between devices with their start and end apart: 17, of which 11 were waited for; matrix products, arithmetic and copies ran while one was open for 0% of the time, Pallas kernels for 0%

profile of v5, /device:TPU:4, one launch (start us, length us, event | category | flops | bytes accessed | tf_op | source)
XLA Modules:
  0.0 103.5 jit_solution(3176947124526752413)
XLA Ops:
  0.6 0.0 copy-start.5
  0.7 0.9 convert_element_type.29
  1.5 0.1 broadcast_in_dim_reshape.4
  1.6 6.4 %collective-permute-start.2 = (bf16[1,16,512]{2,1,0:T(8,128)(2,1)S(1)}, bf16[1,16,512]{2,1,0:T(8,128)(2,1)S(1)}, u32[]{:S(2)}, u32[]{:S(2)}) collective-permute-start(bf16[1,16,512]{2,1,0:T(8,128)(2,1)S(1)} %broadcast_in_dim_reshape.4), channel_id=1, source_target_pairs={{0,192},{8,200},{16,208},{24,216},{32,224},{40,232},{48,240},{56,2... | collective-permute-start | bytes 49160 | tf_op jit(solution)/shard_map/ppermute | solution.py:75
  8.0 1.0 collective-permute-start.1
  9.0 1.5 %collective-permute-start = (bf16[1,16,512]{2,1,0:T(8,128)(2,1)S(1)}, bf16[1,16,512]{2,1,0:T(8,128)(2,1)S(1)}, u32[]{:S(2)}, u32[]{:S(2)}) collective-permute-start(bf16[1,16,512]{2,1,0:T(8,128)(2,1)S(1)} %broadcast_in_dim_reshape.4), channel_id=1, source_target_pairs={{0,64},{8,72},{16,80},{24,88},{32,96},{40,104},{48,112},{56,120},{... | collective-permute-start | bytes 49160 | tf_op jit(solution)/shard_map/ppermute | solution.py:75
  10.6 0.1 stack_broadcast_in_dim_reshape.3
  10.7 0.0 collective-permute-done.2
  10.7 5.0 %collective-permute-done.1 = bf16[1,16,512]{2,1,0:T(8,128)(2,1)S(1)} collective-permute-done((bf16[1,16,512]{2,1,0:T(8,128)(2,1)S(1)}, bf16[1,16,512]{2,1,0:T(8,128)(2,1)S(1)}, u32[]{:S(2)}, u32[]{:S(2)}) %collective-permute-start.1) | collective-permute-done | bytes 16416 | tf_op jit(solution)/shard_map/ppermute | solution.py:75
  15.7 0.0 collective-permute-done
  15.7 0.6 gather_fusion
  16.2 0.1 bitcast_select_fusion.2
  16.3 3.0 %collective-permute-start.5 = (bf16[4,1,16,512]{3,2,0,1:T(8,128)(2,1)S(1)}, bf16[4,1,16,512]{3,2,0,1:T(8,128)(2,1)S(1)}, u32[]{:S(2)}, u32[]{:S(2)}) collective-permute-start(bf16[4,1,16,512]{3,2,0,1:T(8,128)(2,1)S(1)} %bitcast_select_fusion.2), channel_id=1, source_target_pairs={{0,48},{8,56},{16,32},{24,40},{32,16},{40,24},{48,0},{56,8},{64,11... | collective-permute-start | bytes 196616 | tf_op jit(solution)/shard_map/ppermute | solution.py:75
  19.4 0.6 collective-permute-start.4
  20.0 0.5 collective-permute-start.3
  20.4 0.1 bitcast_select_fusion.3
  20.5 2.0 %collective-permute-done.5 = bf16[4,1,16,512]{3,2,0,1:T(8,128)(2,1)S(1)} collective-permute-done((bf16[4,1,16,512]{3,2,0,1:T(8,128)(2,1)S(1)}, bf16[4,1,16,512]{3,2,0,1:T(8,128)(2,1)S(1)}, u32[]{:S(2)}, u32[]{:S(2)}) %collective-permute-start.5) | collective-permute-done | bytes 65568 | tf_op jit(solution)/shard_map/ppermute | solution.py:75
  22.5 2.6 %collective-permute-done.4 = bf16[4,1,16,512]{3,2,0,1:T(8,128)(2,1)S(1)} collective-permute-done((bf16[4,1,16,512]{3,2,0,1:T(8,128)(2,1)S(1)}, bf16[4,1,16,512]{3,2,0,1:T(8,128)(2,1)S(1)}, u32[]{:S(2)}, u32[]{:S(2)}) %collective-permute-start.4) | collective-permute-done | bytes 65568 | tf_op jit(solution)/shard_map/ppermute | solution.py:75
  25.1 0.0 collective-permute-done.3
  25.2 0.6 gather_fusion.1
  25.7 0.1 bitcast_select_fusion
  25.8 0.3 collective-permute-start.6
  26.1 0.1 fusion.30
  26.2 1.4 %collective-permute-done.6 = bf16[4,4,1,16,512]{4,3,1,0,2:T(8,128)(2,1)S(1)} collective-permute-done((bf16[4,4,1,16,512]{4,3,1,0,2:T(8,128)(2,1)S(1)}, bf16[4,4,1,16,512]{4,3,1,0,2:T(8,128)(2,1)S(1)}, u32[]{:S(2)}, u32[]{:S(2)}) %collective-permute-start.6) | collective-permute-done | bytes 262176 | tf_op jit(solution)/shard_map/ppermute | solution.py:75
  27.6 0.1 maximum_bitcast_fusion
  27.7 0.6 gather_fusion.2
  28.3 0.1 select_bitcast_fusion
  28.4 0.2 copy.11
  28.7 5.3 %reduce-precision_convert_fusion.1 = (bf16[8,64,2048]{2,1,0:T(8,128)(2,1)S(1)}, bf16[8,64,2048]{2,1,0:T(8,128)(2,1)}) fusion(s32[8,256]{1,0:T(8,128)S(1)} %bitcast.130, bf16[8,64,512]{2,1,0:T(8,128)(2,1)S(1)} %bitcast.115, s32[256]{0:T(256)S(1)} %bitcast.127, f32[256,8]{0,1:T(8,128)S(1)} %bitcast.125), kind=kOutput, calls=%fused_computation.15 | convolution fusion | flops 679870464 | bytes 4736000 | tf_op jit(solution)/shard_map/khr,hkm->hrm/dot_general | solution.py:162
  34.0 12.1 %fusion.4 = f32[8,128,2048]{2,1,0:T(8,128)S(1)} fusion(bf16[1,2048,2048]{2,1,0:T(8,128)(2,1)} %param.6, bf16[8,64,2048]{2,1,0:T(8,128)(2,1)} %get-tuple-element.7, bf16[8,64,2048]{2,1,0:T(8,128)(2,1)S(1)} %get-tuple-element.6), kind=kOutput, calls=%fused_computation.8 | convolution fusion | flops 8598323200 | bytes 20971520 | tf_op jit(solution)/shard_map/hrm,mn->hrn/dot_general | solution.py:165
  46.1 0.0 copy-start.2
  46.1 1.1 %multiply_reduce_fusion = f32[8,2048]{1,0:T(8,128)S(1)} fusion(f32[8,128,2048]{2,1,0:T(8,128)S(1)} %fusion.4), kind=kLoop, calls=%fused_computation.26 | loop fusion | flops 3129344 | bytes 8454144 | tf_op jit(solution)/shard_map/reduce_sum | solution.py:167
  47.2 2.1 %copy-done = f32[8,128,2048]{2,1,0:T(8,128)} copy-done((f32[8,128,2048]{2,1,0:T(8,128)}, f32[8,128,2048]{2,1,0:T(8,128)S(1)}, u32[]{:S(2)}) %copy-start) | copy-done | bytes 8388632
  49.3 1.2 %collective-permute-start.7 = (f32[8,2048]{1,0:T(8,128)S(1)}, f32[8,2048]{1,0:T(8,128)S(1)}, u32[]{:S(2)}, u32[]{:S(2)}) collective-permute-start(f32[8,2048]{1,0:T(8,128)S(1)} %multiply_reduce_fusion), channel_id=1, source_target_pairs={{0,1},{1,0},{2,3},{3,2},{4,5},{5,4},{6,7},{7,6},{8,9},{9,8},{10,11... | collective-permute-start | bytes 196616 | tf_op jit(solution)/shard_map/ppermute | solution.py:19
  50.5 3.1 %collective-permute-done.7 = f32[8,2048]{1,0:T(8,128)S(1)} collective-permute-done((f32[8,2048]{1,0:T(8,128)S(1)}, f32[8,2048]{1,0:T(8,128)S(1)}, u32[]{:S(2)}, u32[]{:S(2)}) %collective-permute-start.7) | collective-permute-done | bytes 65568 | tf_op jit(solution)/shard_map/ppermute | solution.py:19
  53.6 0.6 collective-permute-start.8
  54.2 5.3 %collective-permute-done.8 = f32[8,2048]{1,0:T(8,128)S(1)} collective-permute-done((f32[8,2048]{1,0:T(8,128)S(1)}, f32[8,2048]{1,0:T(8,128)S(1)}, u32[]{:S(2)}, u32[]{:S(2)}) %collective-permute-start.8) | collective-permute-done | bytes 65568 | tf_op jit(solution)/shard_map/ppermute | solution.py:19
  59.5 1.3 %collective-permute-start.9 = (f32[8,2048]{1,0:T(8,128)S(1)}, f32[8,2048]{1,0:T(8,128)S(1)}, u32[]{:S(2)}, u32[]{:S(2)}) collective-permute-start(f32[8,2048]{1,0:T(8,128)S(1)} %add.142), channel_id=1, source_target_pairs={{0,4},{1,5},{2,6},{3,7},{4,0},{5,1},{6,2},{7,3},{8,12},{9,13},{10,... | collective-permute-start | bytes 196616 | tf_op jit(solution)/shard_map/ppermute | solution.py:19
  60.8 3.2 %collective-permute-done.9 = f32[8,2048]{1,0:T(8,128)S(1)} collective-permute-done((f32[8,2048]{1,0:T(8,128)S(1)}, f32[8,2048]{1,0:T(8,128)S(1)}, u32[]{:S(2)}, u32[]{:S(2)}) %collective-permute-start.9) | collective-permute-done | bytes 65568 | tf_op jit(solution)/shard_map/ppermute | solution.py:19
  64.1 0.7 fusion.39
  64.7 10.4 %reduce-precision_convert_fusion = (bf16[8,64,2048]{2,1,0:T(8,128)(2,1)S(1)}, bf16[8,64,2048]{2,1,0:T(8,128)(2,1)S(1)}) fusion(bf16[1,2048,2048]{2,1,0:T(8,128)(2,1)} %param.6, f32[8,2048]{1,0:T(8,128)S(1)} %get-tuple-element.2, f32[8,128,2048]{2,1,0:T(8,128)} %copy-done), kind=kOutput, calls=%fused_computation.13 | convolution fusion | flops 4302307328 | bytes 21037056 | tf_op jit(solution)/shard_map/hrn,mn->hrm/dot_general | solution.py:174
  75.1 4.1 %fusion.17 = f32[256,8,128]{0,2,1:T(8,128)S(1)} fusion(s32[8,256]{1,0:T(8,128)S(1)} %bitcast.131, bf16[8,64,2048]{2,1,0:T(8,128)(2,1)S(1)} %get-tuple-element.5, bf16[8,64,2048]{2,1,0:T(8,128)(2,1)S(1)} %get-tuple-element.4), kind=kOutput, calls=%fused_computation.28 | convolution fusion | flops 1086324736 | bytes 5251072 | tf_op jit(solution)/shard_map/hkm,hrm->khr/dot_general | solution.py:176
  79.3 0.1 fusion.22
  79.4 0.1 fusion.21
  79.4 0.0 copy-start.1
  79.5 0.4 fusion.28
  79.9 0.4 convolution_add_fusion
  80.4 0.1 collective-permute-start.10
  80.5 1.9 %collective-permute-done.10 = f32[2,2,2,2,16,512]{5,4,3,2,1,0:T(8,128)S(1)} collective-permute-done((f32[2,2,2,2,16,512]{5,4,3,2,1,0:T(8,128)S(1)}, f32[2,2,2,2,16,512]{5,4,3,2,1,0:T(8,128)S(1)}, u32[]{:S(2)}, u32[]{:S(2)}) %collective-permute-start.10) | collective-permute-done | bytes 524320 | tf_op jit(solution)/shard_map/ppermute | solution.py:75
  82.4 0.1 bitcast_add_fusion
  82.5 1.4 %collective-permute-start.13 = (f32[2,2,16,512]{3,2,1,0:T(8,128)S(1)}, f32[2,2,16,512]{3,2,1,0:T(8,128)S(1)}, u32[]{:S(2)}, u32[]{:S(2)}) collective-permute-start(f32[2,2,16,512]{3,2,1,0:T(8,128)S(1)} %get-tuple-element.9), channel_id=1, source_target_pairs={{0,48},{8,56},{16,32},{24,40},{32,16},{40,24},{48,0},{56,8},{64,11... | collective-permute-start | bytes 393224 | tf_op jit(solution)/shard_map/ppermute | solution.py:75
  83.9 0.9 collective-permute-start.12
  84.8 1.9 %collective-permute-start.11 = (f32[2,2,16,512]{3,2,1,0:T(8,128)S(1)}, f32[2,2,16,512]{3,2,1,0:T(8,128)S(1)}, u32[]{:S(2)}, u32[]{:S(2)}) collective-permute-start(f32[2,2,16,512]{3,2,1,0:T(8,128)S(1)} %get-tuple-element.8), channel_id=1, source_target_pairs={{0,16},{8,24},{16,0},{24,8},{32,48},{40,56},{48,32},{56,40},{64,80... | collective-permute-start | bytes 393224 | tf_op jit(solution)/shard_map/ppermute | solution.py:75
  86.7 5.5 %collective-permute-done.13 = f32[2,2,16,512]{3,2,1,0:T(8,128)S(1)} collective-permute-done((f32[2,2,16,512]{3,2,1,0:T(8,128)S(1)}, f32[2,2,16,512]{3,2,1,0:T(8,128)S(1)}, u32[]{:S(2)}, u32[]{:S(2)}) %collective-permute-start.13) | collective-permute-done | bytes 131104 | tf_op jit(solution)/shard_map/ppermute | solution.py:75
  92.2 0.0 collective-permute-done.12
  92.2 0.6 collective-permute-done.11
  92.9 2.1 %collective-permute-start.16 = (f32[16,512]{1,0:T(8,128)S(1)}, f32[16,512]{1,0:T(8,128)S(1)}, u32[]{:S(2)}, u32[]{:S(2)}) collective-permute-start(f32[16,512]{1,0:T(8,128)S(1)} %get-tuple-element.14), channel_id=1, source_target_pairs={{0,192},{8,200},{16,208},{24,216},{32,224},{40,232},{48,240},{56,2... | collective-permute-start | bytes 98312 | tf_op jit(solution)/shard_map/ppermute | solution.py:75
  95.0 3.0 %collective-permute-start.15 = (f32[16,512]{1,0:T(8,128)S(1)}, f32[16,512]{1,0:T(8,128)S(1)}, u32[]{:S(2)}, u32[]{:S(2)}) collective-permute-start(f32[16,512]{1,0:T(8,128)S(1)} %get-tuple-element.15), channel_id=1, source_target_pairs={{0,128},{8,136},{16,144},{24,152},{32,160},{40,168},{48,176},{56,1... | collective-permute-start | bytes 98312 | tf_op jit(solution)/shard_map/ppermute | solution.py:75
  98.0 1.5 %collective-permute-start.14 = (f32[16,512]{1,0:T(8,128)S(1)}, f32[16,512]{1,0:T(8,128)S(1)}, u32[]{:S(2)}, u32[]{:S(2)}) collective-permute-start(f32[16,512]{1,0:T(8,128)S(1)} %get-tuple-element.13), channel_id=1, source_target_pairs={{0,64},{8,72},{16,80},{24,88},{32,96},{40,104},{48,112},{56,120},{... | collective-permute-start | bytes 98312 | tf_op jit(solution)/shard_map/ppermute | solution.py:75
  99.4 0.0 collective-permute-done.16
  99.4 3.3 %collective-permute-done.15 = f32[16,512]{1,0:T(8,128)S(1)} collective-permute-done((f32[16,512]{1,0:T(8,128)S(1)}, f32[16,512]{1,0:T(8,128)S(1)}, u32[]{:S(2)}, u32[]{:S(2)}) %collective-permute-start.15) | collective-permute-done | bytes 32800 | tf_op jit(solution)/shard_map/ppermute | solution.py:75
  102.8 0.0 collective-permute-done.14
  102.8 0.1 mul.81
  102.9 0.6 sub.19
  (26 shorter events, 0.3 us)
Async XLA Ops:
  0.6 28.0 %copy-start.5 = (s32[1,8,256]{2,1,0:T(8,128)S(1)}, s32[1,8,256]{2,1,0:T(8,128)}, u32[]{:S(2)}) copy-start(s32[1,8,256]{2,1,0:T(8,128)} %param.9) | copy-start | bytes 24580
  0.6 28.0 %copy-start.4 = (s32[1,256]{1,0:T(1,128)S(1)}, s32[1,256]{1,0:T(1,128)}, u32[]{:S(2)}) copy-start(s32[1,256]{1,0:T(1,128)} %param.10) | copy-start | bytes 3076
  0.7 28.0 %copy-start.3 = (f32[1,8,256]{2,1,0:T(8,128)S(1)}, f32[1,8,256]{2,1,0:T(8,128)}, u32[]{:S(2)}) copy-start(f32[1,8,256]{2,1,0:T(8,128)} %param.8) | copy-start | bytes 24580
  1.6 9.0 %collective-permute-start.2 = (bf16[1,16,512]{2,1,0:T(8,128)(2,1)S(1)}, bf16[1,16,512]{2,1,0:T(8,128)(2,1)S(1)}, u32[]{:S(2)}, u32[]{:S(2)}) collective-permute-start(bf16[1,16,512]{2,1,0:T(8,128)(2,1)S(1)} %broadcast_in_dim_reshape.4), channel_id=1, source_target_pairs={{0,192},{8,200},{16,208},{24,216},{32,224},{40,232},{48,240},{56,2... | collective-permute-start | bytes 49160 | tf_op jit(solution)/shard_map/ppermute | solution.py:75
  8.0 7.6 %collective-permute-start.1 = (bf16[1,16,512]{2,1,0:T(8,128)(2,1)S(1)}, bf16[1,16,512]{2,1,0:T(8,128)(2,1)S(1)}, u32[]{:S(2)}, u32[]{:S(2)}) collective-permute-start(bf16[1,16,512]{2,1,0:T(8,128)(2,1)S(1)} %broadcast_in_dim_reshape.4), channel_id=1, source_target_pairs={{0,128},{8,136},{16,144},{24,152},{32,160},{40,168},{48,176},{56,1... | collective-permute-start | bytes 49160 | tf_op jit(solution)/shard_map/ppermute | solution.py:75
  9.0 6.7 %collective-permute-start = (bf16[1,16,512]{2,1,0:T(8,128)(2,1)S(1)}, bf16[1,16,512]{2,1,0:T(8,128)(2,1)S(1)}, u32[]{:S(2)}, u32[]{:S(2)}) collective-permute-start(bf16[1,16,512]{2,1,0:T(8,128)(2,1)S(1)} %broadcast_in_dim_reshape.4), channel_id=1, source_target_pairs={{0,64},{8,72},{16,80},{24,88},{32,96},{40,104},{48,112},{56,120},{... | collective-permute-start | bytes 49160 | tf_op jit(solution)/shard_map/ppermute | solution.py:75
  16.3 6.2 %collective-permute-start.5 = (bf16[4,1,16,512]{3,2,0,1:T(8,128)(2,1)S(1)}, bf16[4,1,16,512]{3,2,0,1:T(8,128)(2,1)S(1)}, u32[]{:S(2)}, u32[]{:S(2)}) collective-permute-start(bf16[4,1,16,512]{3,2,0,1:T(8,128)(2,1)S(1)} %bitcast_select_fusion.2), channel_id=1, source_target_pairs={{0,48},{8,56},{16,32},{24,40},{32,16},{40,24},{48,0},{56,8},{64,11... | collective-permute-start | bytes 196616 | tf_op jit(solution)/shard_map/ppermute | solution.py:75
  19.4 5.8 %collective-permute-start.4 = (bf16[4,1,16,512]{3,2,0,1:T(8,128)(2,1)S(1)}, bf16[4,1,16,512]{3,2,0,1:T(8,128)(2,1)S(1)}, u32[]{:S(2)}, u32[]{:S(2)}) collective-permute-start(bf16[4,1,16,512]{3,2,0,1:T(8,128)(2,1)S(1)} %bitcast_select_fusion.2), channel_id=1, source_target_pairs={{0,32},{8,40},{16,48},{24,56},{32,0},{40,8},{48,16},{56,24},{64,96... | collective-permute-start | bytes 196616 | tf_op jit(solution)/shard_map/ppermute | solution.py:75
  20.0 5.1 %collective-permute-start.3 = (bf16[4,1,16,512]{3,2,0,1:T(8,128)(2,1)S(1)}, bf16[4,1,16,512]{3,2,0,1:T(8,128)(2,1)S(1)}, u32[]{:S(2)}, u32[]{:S(2)}) collective-permute-start(bf16[4,1,16,512]{3,2,0,1:T(8,128)(2,1)S(1)} %bitcast_select_fusion.2), channel_id=1, source_target_pairs={{0,16},{8,24},{16,0},{24,8},{32,48},{40,56},{48,32},{56,40},{64,80... | collective-permute-start | bytes 196616 | tf_op jit(solution)/shard_map/ppermute | solution.py:75
  25.8 1.8 %collective-permute-start.6 = (bf16[4,4,1,16,512]{4,3,1,0,2:T(8,128)(2,1)S(1)}, bf16[4,4,1,16,512]{4,3,1,0,2:T(8,128)(2,1)S(1)}, u32[]{:S(2)}, u32[]{:S(2)}) collective-permute-start(bf16[4,4,1,16,512]{4,3,1,0,2:T(8,128)(2,1)S(1)} %bitcast_select_fusion), channel_id=1, source_target_pairs={{0,8},{8,0},{16,24},{24,16},{32,40},{40,32},{48,56},{56,48},{64,72... | collective-permute-start | bytes 786440 | tf_op jit(solution)/shard_map/ppermute | solution.py:75
  46.1 3.3 %copy-start = (f32[8,128,2048]{2,1,0:T(8,128)}, f32[8,128,2048]{2,1,0:T(8,128)S(1)}, u32[]{:S(2)}) copy-start(f32[8,128,2048]{2,1,0:T(8,128)S(1)} %fusion.4) | copy-start | bytes 25165828
  46.1 18.0 %copy-start.2 = (f32[1,8,2048]{2,1,0:T(8,128)S(1)}, f32[1,8,2048]{2,1,0:T(8,128)}, u32[]{:S(2)}) copy-start(f32[1,8,2048]{2,1,0:T(8,128)} %param.7) | copy-start | bytes 196612
  49.3 4.3 %collective-permute-start.7 = (f32[8,2048]{1,0:T(8,128)S(1)}, f32[8,2048]{1,0:T(8,128)S(1)}, u32[]{:S(2)}, u32[]{:S(2)}) collective-permute-start(f32[8,2048]{1,0:T(8,128)S(1)} %multiply_reduce_fusion), channel_id=1, source_target_pairs={{0,1},{1,0},{2,3},{3,2},{4,5},{5,4},{6,7},{7,6},{8,9},{9,8},{10,11... | collective-permute-start | bytes 196616 | tf_op jit(solution)/shard_map/ppermute | solution.py:19
  53.6 5.9 %collective-permute-start.8 = (f32[8,2048]{1,0:T(8,128)S(1)}, f32[8,2048]{1,0:T(8,128)S(1)}, u32[]{:S(2)}, u32[]{:S(2)}) collective-permute-start(f32[8,2048]{1,0:T(8,128)S(1)} %add.141), channel_id=1, source_target_pairs={{0,2},{1,3},{2,0},{3,1},{4,6},{5,7},{6,4},{7,5},{8,10},{9,11},{10,... | collective-permute-start | bytes 196616 | tf_op jit(solution)/shard_map/ppermute | solution.py:19
  59.5 4.6 %collective-permute-start.9 = (f32[8,2048]{1,0:T(8,128)S(1)}, f32[8,2048]{1,0:T(8,128)S(1)}, u32[]{:S(2)}, u32[]{:S(2)}) collective-permute-start(f32[8,2048]{1,0:T(8,128)S(1)} %add.142), channel_id=1, source_target_pairs={{0,4},{1,5},{2,6},{3,7},{4,0},{5,1},{6,2},{7,3},{8,12},{9,13},{10,... | collective-permute-start | bytes 196616 | tf_op jit(solution)/shard_map/ppermute | solution.py:19
  79.4 23.4 %copy-start.1 = (f32[16,8,64]{2,1,0:T(8,128)S(1)}, f32[16,8,64]{2,1,0:T(8,128)}, u32[]{:S(2)}) copy-start(f32[16,8,64]{2,1,0:T(8,128)} %param.11) | copy-start | bytes 98308
  80.4 2.0 %collective-permute-start.10 = (f32[2,2,2,2,16,512]{5,4,3,2,1,0:T(8,128)S(1)}, f32[2,2,2,2,16,512]{5,4,3,2,1,0:T(8,128)S(1)}, u32[]{:S(2)}, u32[]{:S(2)}) collective-permute-start(f32[2,2,2,2,16,512]{5,4,3,2,1,0:T(8,128)S(1)} %dynamic-slice_bitcast_fusion), channel_id=1, source_target_pairs={{0,8},{8,0},{16,24},{24,16},{32,40},{40,32},{48,56},{56,48},{64,72... | collective-permute-start | bytes 1572872 | tf_op jit(solution)/shard_map/ppermute | solution.py:75
  82.5 9.6 %collective-permute-start.13 = (f32[2,2,16,512]{3,2,1,0:T(8,128)S(1)}, f32[2,2,16,512]{3,2,1,0:T(8,128)S(1)}, u32[]{:S(2)}, u32[]{:S(2)}) collective-permute-start(f32[2,2,16,512]{3,2,1,0:T(8,128)S(1)} %get-tuple-element.9), channel_id=1, source_target_pairs={{0,48},{8,56},{16,32},{24,40},{32,16},{40,24},{48,0},{56,8},{64,11... | collective-permute-start | bytes 393224 | tf_op jit(solution)/shard_map/ppermute | solution.py:75
  83.9 8.3 %collective-permute-start.12 = (f32[2,2,16,512]{3,2,1,0:T(8,128)S(1)}, f32[2,2,16,512]{3,2,1,0:T(8,128)S(1)}, u32[]{:S(2)}, u32[]{:S(2)}) collective-permute-start(f32[2,2,16,512]{3,2,1,0:T(8,128)S(1)} %get-tuple-element.10), channel_id=1, source_target_pairs={{0,32},{8,40},{16,48},{24,56},{32,0},{40,8},{48,16},{56,24},{64,96... | collective-permute-start | bytes 393224 | tf_op jit(solution)/shard_map/ppermute | solution.py:75
  84.8 8.0 %collective-permute-start.11 = (f32[2,2,16,512]{3,2,1,0:T(8,128)S(1)}, f32[2,2,16,512]{3,2,1,0:T(8,128)S(1)}, u32[]{:S(2)}, u32[]{:S(2)}) collective-permute-start(f32[2,2,16,512]{3,2,1,0:T(8,128)S(1)} %get-tuple-element.8), channel_id=1, source_target_pairs={{0,16},{8,24},{16,0},{24,8},{32,48},{40,56},{48,32},{56,40},{64,80... | collective-permute-start | bytes 393224 | tf_op jit(solution)/shard_map/ppermute | solution.py:75
  92.9 6.6 %collective-permute-start.16 = (f32[16,512]{1,0:T(8,128)S(1)}, f32[16,512]{1,0:T(8,128)S(1)}, u32[]{:S(2)}, u32[]{:S(2)}) collective-permute-start(f32[16,512]{1,0:T(8,128)S(1)} %get-tuple-element.14), channel_id=1, source_target_pairs={{0,192},{8,200},{16,208},{24,216},{32,224},{40,232},{48,240},{56,2... | collective-permute-start | bytes 98312 | tf_op jit(solution)/shard_map/ppermute | solution.py:75
  95.0 7.8 %collective-permute-start.15 = (f32[16,512]{1,0:T(8,128)S(1)}, f32[16,512]{1,0:T(8,128)S(1)}, u32[]{:S(2)}, u32[]{:S(2)}) collective-permute-start(f32[16,512]{1,0:T(8,128)S(1)} %get-tuple-element.15), channel_id=1, source_target_pairs={{0,128},{8,136},{16,144},{24,152},{32,160},{40,168},{48,176},{56,1... | collective-permute-start | bytes 98312 | tf_op jit(solution)/shard_map/ppermute | solution.py:75
  98.0 4.8 %collective-permute-start.14 = (f32[16,512]{1,0:T(8,128)S(1)}, f32[16,512]{1,0:T(8,128)S(1)}, u32[]{:S(2)}, u32[]{:S(2)}) collective-permute-start(f32[16,512]{1,0:T(8,128)S(1)} %get-tuple-element.13), channel_id=1, source_target_pairs={{0,64},{8,72},{16,80},{24,88},{32,96},{40,104},{48,112},{56,120},{... | collective-permute-start | bytes 98312 | tf_op jit(solution)/shard_map/ppermute | solution.py:75

commit v6 on v5

--- a/solution.py
+++ b/solution.py
@@ -134,6 +134,9 @@
     return x
 
 
+CHUNKS = 2
+
+
 def _bit_groups(axis):
     rest = list(range(1, _bit_count(lax.axis_size(axis))))
     pairs = [tuple(rest[max(0, i - 1) : i + 1]) for i in range(len(rest) - 1, -1, -2)]
@@ -159,13 +162,20 @@
     power = ev_power[0].T
     weighted = (power[:, :, None] * looked).astype(jnp.bfloat16)
     node_hot = (ev_node[0][:, :, None] == lax.iota(jnp.int32, nodes)[None, None, :]).astype(jnp.bfloat16)
-    spread = jnp.einsum("khr,hkm->hrm", weighted, node_hot, preferred_element_type=jnp.float32)
-    spread_both = jnp.concatenate(_split_bf16(spread), axis=1)
     sens = sensitivity[0]
-    volts_both = jnp.einsum("hrm,mn->hrn", spread_both, sens, preferred_element_type=jnp.float32)
-    factor_volts = volts_both[:, :columns] + volts_both[:, columns:]
-    partial_sum = jnp.sum(factor_volts * factor_volts, axis=1)
-    variance = sum_all(partial_sum, "factor")[None]
+    span = hours // CHUNKS
+    volts_parts = []
+    variance_parts = []
+    for chunk in range(CHUNKS):
+        at = slice(chunk * span, (chunk + 1) * span)
+        spread = jnp.einsum("khr,hkm->hrm", weighted[:, at], node_hot[at], preferred_element_type=jnp.float32)
+        spread_both = jnp.concatenate(_split_bf16(spread), axis=1)
+        volts_both = jnp.einsum("hrm,mn->hrn", spread_both, sens, preferred_element_type=jnp.float32)
+        part = volts_both[:, :columns] + volts_both[:, columns:]
+        volts_parts.append(part)
+        variance_parts.append(sum_all(jnp.sum(part * part, axis=1), "factor"))
+    factor_volts = jnp.concatenate(volts_parts, axis=0)
+    variance = jnp.concatenate(variance_parts, axis=0)[None]
     deviation = jnp.sqrt(variance + epsilon)
     margin = headroom - quantile * deviation
     violation = jnp.maximum(-margin, 0.0)

time: 104 us -> 101 us (0.971)
  other arithmetic: 4.18 us -> 10.1 us
  matrix products: 32.8 us -> 27.8 us
  waiting for transfers between devices: 33.9 us -> 29.1 us
  starting transfers between devices: 27.2 us -> 30.1 us
  local copies, waits for them, and re-layouts: 4.5 us -> 3.14 us
    eq x0 -> x1, other arithmetic: none -> 4.72 us  [shards(): ev_node[0][:, :, None] == lax.iota(jnp.int32, nodes)[None, None, :]]
    dot_general x1 -> x2, matrix products: 12.1 us -> 9.11 us  [shards(): jnp.einsum('hrm,mn->hrn', spread_both, sens, preferred_element_type=jnp.f...]
    ppermute x3 -> x6, waiting for transfers between devices: 11.6 us -> 8.67 us  [_exchange(): return lax.ppermute(x, axis, perm)]
    ppermute x3 -> x6, starting transfers between devices: 3.12 us -> 6.01 us  [_exchange(): return lax.ppermute(x, axis, perm)]
    ppermute x14, waiting for transfers between devices: 22.3 us -> 20.4 us  [_send_all(): out[j] = lax.ppermute(x_for(j), axis, [(i, i ^ m) for i in range(size)])]
    dot_general x1, matrix products: 10.4 us -> 8.59 us  [shards(): jnp.einsum('hrn,mn->hrm', volt_grad, sens, preferred_element_type=jnp.flo...]
    unnamed x12 -> x16, local copies, waits for them, and re-layouts: 2.17 us -> 0.81 us
    reduce_sum x1 -> x2, other arithmetic: 1.1 us -> 2.23 us  [shards(): variance_parts.append(sum_all(jnp.sum(part * part, axis=1), 'factor'))]
  transfers between devices with their start and end apart: 17 -> 20, of which waited for: 11 -> 13; matrix products, arithmetic and copies ran while one was open for 0% -> 11% of each run, Pallas kernels for 0% -> 0%
where the time goes in v6:
time: 101 us
  starting transfers between devices  30.1 us (30%)
  waiting for transfers between devices  29.1 us (29%)
  matrix products  27.8 us (28%)
  other arithmetic  10.1 us (10%)
  local copies, waits for them, and re-layouts  3.14 us (3%)
    ppermute x14, starting transfers between devices, _send_all(): out[j] = lax.ppermute(x_for(j), axis, [(i, i ^ m) for i in range(size)])  24.1 us
    ppermute x14, waiting for transfers between devices, _send_all(): out[j] = lax.ppermute(x_for(j), axis, [(i, i ^ m) for i in range(size)])  20.4 us
    dot_general x2, matrix products, shards(): jnp.einsum('hrm,mn->hrn', spread_both, sens, preferred_element_type=jnp.f...  9.11 us
    ppermute x6, waiting for transfers between devices, _exchange(): return lax.ppermute(x, axis, perm)  8.67 us
    dot_general x1, matrix products, shards(): jnp.einsum('hrn,mn->hrm', volt_grad, sens, preferred_element_type=jnp.flo...  8.59 us
    ppermute x6, starting transfers between devices, _exchange(): return lax.ppermute(x, axis, perm)  6.01 us
    eq x1, other arithmetic, shards(): ev_node[0][:, :, None] == lax.iota(jnp.int32, nodes)[None, None, :]  4.72 us
    dot_general x2, matrix products, shards(): jnp.einsum('khr,hkm->hrm', weighted[:, at], node_hot[at], preferred_eleme...  4.7 us
  transfers between devices with their start and end apart: 20, of which 13 were waited for; matrix products, arithmetic and copies ran while one was open for 11% of the time, Pallas kernels for 0%

profile of v6, /device:TPU:4, one launch (start us, length us, event | category | flops | bytes accessed | tf_op | source)
XLA Modules:
  0.0 101.2 jit_solution(8282624806577976376)
XLA Ops:
  0.6 0.8 convert_element_type.35
  1.5 0.1 broadcast_in_dim_reshape.4
  1.6 6.4 %collective-permute-start.2 = (bf16[1,16,512]{2,1,0:T(8,128)(2,1)S(1)}, bf16[1,16,512]{2,1,0:T(8,128)(2,1)S(1)}, u32[]{:S(2)}, u32[]{:S(2)}) collective-permute-start(bf16[1,16,512]{2,1,0:T(8,128)(2,1)S(1)} %broadcast_in_dim_reshape.4), channel_id=1, source_target_pairs={{0,192},{8,200},{16,208},{24,216},{32,224},{40,232},{48,240},{56,2... | collective-permute-start | bytes 49160 | tf_op jit(solution)/shard_map/ppermute | solution.py:75
  8.0 1.0 collective-permute-start.1
  9.0 1.5 %collective-permute-start = (bf16[1,16,512]{2,1,0:T(8,128)(2,1)S(1)}, bf16[1,16,512]{2,1,0:T(8,128)(2,1)S(1)}, u32[]{:S(2)}, u32[]{:S(2)}) collective-permute-start(bf16[1,16,512]{2,1,0:T(8,128)(2,1)S(1)} %broadcast_in_dim_reshape.4), channel_id=1, source_target_pairs={{0,64},{8,72},{16,80},{24,88},{32,96},{40,104},{48,112},{56,120},{... | collective-permute-start | bytes 49160 | tf_op jit(solution)/shard_map/ppermute | solution.py:75
  10.5 4.7 %iota_compare_fusion = pred[8,256,2048]{2,1,0:T(32,128)(4,1)} fusion(s32[8,256]{1,0:T(8,128)} %bitcast.121), kind=kLoop, calls=%fused_computation.3 | loop fusion | flops 4194304 | bytes 4202496 | tf_op jit(solution)/shard_map/eq | solution.py:164
  15.2 0.1 stack_broadcast_in_dim_reshape.3
  15.3 0.3 collective-permute-done.1
  15.6 0.6 gather_fusion
  16.2 0.1 bitcast_select_fusion.2
  16.3 3.0 %collective-permute-start.5 = (bf16[4,1,16,512]{3,2,0,1:T(8,128)(2,1)S(1)}, bf16[4,1,16,512]{3,2,0,1:T(8,128)(2,1)S(1)}, u32[]{:S(2)}, u32[]{:S(2)}) collective-permute-start(bf16[4,1,16,512]{3,2,0,1:T(8,128)(2,1)S(1)} %bitcast_select_fusion.2), channel_id=1, source_target_pairs={{0,48},{8,56},{16,32},{24,40},{32,16},{40,24},{48,0},{56,8},{64,11... | collective-permute-start | bytes 196616 | tf_op jit(solution)/shard_map/ppermute | solution.py:75
  19.3 0.6 collective-permute-start.4
  19.9 0.5 collective-permute-start.3
  20.4 0.1 bitcast_select_fusion.3
  20.5 1.3 %collective-permute-done.5 = bf16[4,1,16,512]{3,2,0,1:T(8,128)(2,1)S(1)} collective-permute-done((bf16[4,1,16,512]{3,2,0,1:T(8,128)(2,1)S(1)}, bf16[4,1,16,512]{3,2,0,1:T(8,128)(2,1)S(1)}, u32[]{:S(2)}, u32[]{:S(2)}) %collective-permute-start.5) | collective-permute-done | bytes 65568 | tf_op jit(solution)/shard_map/ppermute | solution.py:75
  21.8 3.3 %collective-permute-done.4 = bf16[4,1,16,512]{3,2,0,1:T(8,128)(2,1)S(1)} collective-permute-done((bf16[4,1,16,512]{3,2,0,1:T(8,128)(2,1)S(1)}, bf16[4,1,16,512]{3,2,0,1:T(8,128)(2,1)S(1)}, u32[]{:S(2)}, u32[]{:S(2)}) %collective-permute-start.4) | collective-permute-done | bytes 65568 | tf_op jit(solution)/shard_map/ppermute | solution.py:75
  25.1 0.6 gather_fusion.1
  25.7 0.1 bitcast_select_fusion
  25.8 0.3 collective-permute-start.6
  26.1 0.1 fusion.38
  26.2 1.4 %collective-permute-done.6 = bf16[4,4,1,16,512]{4,3,1,0,2:T(8,128)(2,1)S(1)} collective-permute-done((bf16[4,4,1,16,512]{4,3,1,0,2:T(8,128)(2,1)S(1)}, bf16[4,4,1,16,512]{4,3,1,0,2:T(8,128)(2,1)S(1)}, u32[]{:S(2)}, u32[]{:S(2)}) %collective-permute-start.6) | collective-permute-done | bytes 262176 | tf_op jit(solution)/shard_map/ppermute | solution.py:75
  27.6 0.6 gather_fusion.2
  28.2 0.1 select_bitcast_fusion
  28.4 0.2 copy.11
  28.6 0.4 fusion.29
  29.1 3.1 %reduce-precision_convert_fusion.1 = (bf16[4,64,2048]{2,1,0:T(8,128)(2,1)S(1)}, bf16[4,64,2048]{2,1,0:T(8,128)(2,1)S(1)}) fusion(bf16[256,8,64]{0,2,1:T(8,128)(2,1)S(1)} %fusion.29, pred[8,256,2048]{2,1,0:T(32,128)(4,1)} %iota_compare_fusion), kind=kOutput, calls=%fused_computation.24 | convolution fusion | flops 270532608 | bytes 4456448 | tf_op jit(solution)/shard_map/khr,hkm->hrm/dot_general | solution.py:171
  32.2 1.6 %reduce-precision_convert_fusion.2 = (bf16[4,64,2048]{2,1,0:T(8,128)(2,1)S(1)}, bf16[4,64,2048]{2,1,0:T(8,128)(2,1)S(1)}) fusion(bf16[256,8,64]{0,2,1:T(8,128)(2,1)S(1)} %fusion.29, pred[8,256,2048]{2,1,0:T(32,128)(4,1)S(1)} %copy-done), kind=kOutput, calls=%fused_computation.26 | convolution fusion | flops 270532608 | bytes 4456448 | tf_op jit(solution)/shard_map/khr,hkm->hrm/dot_general | solution.py:171
  33.8 0.8 slice-done.1
  34.6 4.6 %fusion.2 = f32[4,128,2048]{2,1,0:T(8,128)S(1)} fusion(bf16[1,2048,2048]{2,1,0:T(8,128)(2,1)S(1)} %bitcast.129, bf16[4,64,2048]{2,1,0:T(8,128)(2,1)S(1)} %get-tuple-element.13, bf16[4,64,2048]{2,1,0:T(8,128)(2,1)S(1)} %get-tuple-element.12), kind=kOutput, calls=%fused_computation.6 | convolution fusion | flops 4299161600 | bytes 14680064 | tf_op jit(solution)/shard_map/hrm,mn->hrn/dot_general | solution.py:173
  39.1 0.5 multiply_reduce_fusion
  39.6 1.3 %collective-permute-start.10 = (f32[4,2048]{1,0:T(4,128)S(1)}, f32[4,2048]{1,0:T(4,128)S(1)}, u32[]{:S(2)}, u32[]{:S(2)}) collective-permute-start(f32[4,2048]{1,0:T(4,128)S(1)} %get-tuple-element.6), channel_id=1, source_target_pairs={{0,1},{1,0},{2,3},{3,2},{4,5},{5,4},{6,7},{7,6},{8,9},{9,8},{10,11... | collective-permute-start | bytes 98312 | tf_op jit(solution)/shard_map/ppermute | solution.py:19
  40.9 4.6 %fusion.4 = f32[4,128,2048]{2,1,0:T(8,128)S(1)} fusion(bf16[1,2048,2048]{2,1,0:T(8,128)(2,1)S(1)} %bitcast.129, bf16[4,64,2048]{2,1,0:T(8,128)(2,1)S(1)} %get-tuple-element.11, bf16[4,64,2048]{2,1,0:T(8,128)(2,1)S(1)} %get-tuple-element.10), kind=kOutput, calls=%fused_computation.8 | convolution fusion | flops 4299161600 | bytes 14680064 | tf_op jit(solution)/shard_map/hrm,mn->hrn/dot_general | solution.py:173
  45.5 1.8 %multiply_reduce_fusion.1 = (f32[4,2048]{1,0:T(4,128)S(1)}, f32[4,64,2048]{2,1,0:T(8,128)}) fusion(f32[4,128,2048]{2,1,0:T(8,128)S(1)} %fusion.4), kind=kLoop, calls=%fused_computation.39 | loop fusion | flops 1564672 | bytes 6324224 | tf_op jit(solution)/shard_map/reduce_sum | solution.py:176
  47.2 0.8 collective-permute-start.7
  48.1 0.8 collective-permute-start.11
  48.9 2.3 %collective-permute-done.7 = f32[4,2048]{1,0:T(4,128)S(1)} collective-permute-done((f32[4,2048]{1,0:T(4,128)S(1)}, f32[4,2048]{1,0:T(4,128)S(1)}, u32[]{:S(2)}, u32[]{:S(2)}) %collective-permute-start.7) | collective-permute-done | bytes 32800 | tf_op jit(solution)/shard_map/ppermute | solution.py:19
  51.2 0.9 collective-permute-start.8
  52.1 1.8 %collective-permute-done.11 = f32[4,2048]{1,0:T(4,128)S(1)} collective-permute-done((f32[4,2048]{1,0:T(4,128)S(1)}, f32[4,2048]{1,0:T(4,128)S(1)}, u32[]{:S(2)}, u32[]{:S(2)}) %collective-permute-start.11) | collective-permute-done | bytes 32800 | tf_op jit(solution)/shard_map/ppermute | solution.py:19
  53.8 1.1 %collective-permute-start.12 = (f32[4,2048]{1,0:T(4,128)S(1)}, f32[4,2048]{1,0:T(4,128)S(1)}, u32[]{:S(2)}, u32[]{:S(2)}) collective-permute-start(f32[4,2048]{1,0:T(4,128)S(1)} %add.169), channel_id=1, source_target_pairs={{0,4},{1,5},{2,6},{3,7},{4,0},{5,1},{6,2},{7,3},{8,12},{9,13},{10,... | collective-permute-start | bytes 98312 | tf_op jit(solution)/shard_map/ppermute | solution.py:19
  54.9 1.8 %collective-permute-done.8 = f32[4,2048]{1,0:T(4,128)S(1)} collective-permute-done((f32[4,2048]{1,0:T(4,128)S(1)}, f32[4,2048]{1,0:T(4,128)S(1)}, u32[]{:S(2)}, u32[]{:S(2)}) %collective-permute-start.8) | collective-permute-done | bytes 32800 | tf_op jit(solution)/shard_map/ppermute | solution.py:19
  56.7 1.1 %collective-permute-start.9 = (f32[4,2048]{1,0:T(4,128)S(1)}, f32[4,2048]{1,0:T(4,128)S(1)}, u32[]{:S(2)}, u32[]{:S(2)}) collective-permute-start(f32[4,2048]{1,0:T(4,128)S(1)} %add.165), channel_id=1, source_target_pairs={{0,4},{1,5},{2,6},{3,7},{4,0},{5,1},{6,2},{7,3},{8,12},{9,13},{10,... | collective-permute-start | bytes 98312 | tf_op jit(solution)/shard_map/ppermute | solution.py:19
  57.8 2.9 %collective-permute-done.9 = f32[4,2048]{1,0:T(4,128)S(1)} collective-permute-done((f32[4,2048]{1,0:T(4,128)S(1)}, f32[4,2048]{1,0:T(4,128)S(1)}, u32[]{:S(2)}, u32[]{:S(2)}) %collective-permute-start.9) | collective-permute-done | bytes 32800 | tf_op jit(solution)/shard_map/ppermute | solution.py:19
  60.7 0.7 multiply_bitcast_fusion
  61.4 8.6 %reduce-precision_convert_fusion = (bf16[8,64,2048]{2,1,0:T(8,128)(2,1)S(1)}, bf16[8,64,2048]{2,1,0:T(8,128)(2,1)S(1)}) fusion(bf16[1,2048,2048]{2,1,0:T(8,128)(2,1)} %param.6, f32[4,64,2048]{2,1,0:T(8,128)S(1)} %get-tuple-element.7, f32[4,64,2048]{2,1,0:T(8,128)} %get-tuple-element.5, f32[8,2048]{1,0:T(8,128)S(1)} %get-tuple-element.2), kind=kOutput, calls=%fused_computation.15 | convolution fusion | flops 4302307328 | bytes 16842752 | tf_op jit(solution)/shard_map/hrn,mn->hrm/dot_general | solution.py:184
  70.0 4.1 %fusion.26 = f32[256,8,128]{0,2,1:T(8,128)S(1)} fusion(bf16[8,64,2048]{2,1,0:T(8,128)(2,1)S(1)} %get-tuple-element.9, bf16[8,64,2048]{2,1,0:T(8,128)(2,1)S(1)} %get-tuple-element.8, s32[8,256]{1,0:T(8,128)S(1)} %bitcast.122), kind=kOutput, calls=%fused_computation.40 | convolution fusion | flops 1086324736 | bytes 5251072 | tf_op jit(solution)/shard_map/hkm,hrm->khr/dot_general | solution.py:186
  74.2 0.1 fusion.31
  74.2 0.1 fusion.30
  74.3 0.4 fusion.36
  74.8 0.4 convolution_add_fusion
  75.3 0.1 collective-permute-start.13
  75.4 1.9 %collective-permute-done.13 = f32[2,2,2,2,16,512]{5,4,3,2,1,0:T(8,128)S(1)} collective-permute-done((f32[2,2,2,2,16,512]{5,4,3,2,1,0:T(8,128)S(1)}, f32[2,2,2,2,16,512]{5,4,3,2,1,0:T(8,128)S(1)}, u32[]{:S(2)}, u32[]{:S(2)}) %collective-permute-start.13) | collective-permute-done | bytes 524320 | tf_op jit(solution)/shard_map/ppermute | solution.py:75
  77.3 0.1 bitcast_add_fusion
  77.4 0.2 collective-permute-start.14
  77.6 2.4 %collective-permute-start.16 = (f32[2,2,16,512]{3,2,1,0:T(8,128)S(1)}, f32[2,2,16,512]{3,2,1,0:T(8,128)S(1)}, u32[]{:S(2)}, u32[]{:S(2)}) collective-permute-start(f32[2,2,16,512]{3,2,1,0:T(8,128)S(1)} %get-tuple-element.15), channel_id=1, source_target_pairs={{0,48},{8,56},{16,32},{24,40},{32,16},{40,24},{48,0},{56,8},{64,11... | collective-permute-start | bytes 393224 | tf_op jit(solution)/shard_map/ppermute | solution.py:75
  80.1 1.5 %collective-permute-start.15 = (f32[2,2,16,512]{3,2,1,0:T(8,128)S(1)}, f32[2,2,16,512]{3,2,1,0:T(8,128)S(1)}, u32[]{:S(2)}, u32[]{:S(2)}) collective-permute-start(f32[2,2,16,512]{3,2,1,0:T(8,128)S(1)} %get-tuple-element.16), channel_id=1, source_target_pairs={{0,32},{8,40},{16,48},{24,56},{32,0},{40,8},{48,16},{56,24},{64,96... | collective-permute-start | bytes 393224 | tf_op jit(solution)/shard_map/ppermute | solution.py:75
  81.6 2.3 %collective-permute-done.14 = f32[2,2,16,512]{3,2,1,0:T(8,128)S(1)} collective-permute-done((f32[2,2,16,512]{3,2,1,0:T(8,128)S(1)}, f32[2,2,16,512]{3,2,1,0:T(8,128)S(1)}, u32[]{:S(2)}, u32[]{:S(2)}) %collective-permute-start.14) | collective-permute-done | bytes 131104 | tf_op jit(solution)/shard_map/ppermute | solution.py:75
  83.9 3.3 %collective-permute-done.16 = f32[2,2,16,512]{3,2,1,0:T(8,128)S(1)} collective-permute-done((f32[2,2,16,512]{3,2,1,0:T(8,128)S(1)}, f32[2,2,16,512]{3,2,1,0:T(8,128)S(1)}, u32[]{:S(2)}, u32[]{:S(2)}) %collective-permute-start.16) | collective-permute-done | bytes 131104 | tf_op jit(solution)/shard_map/ppermute | solution.py:75
  87.2 1.5 %collective-permute-start.17 = (f32[16,512]{1,0:T(8,128)S(1)}, f32[16,512]{1,0:T(8,128)S(1)}, u32[]{:S(2)}, u32[]{:S(2)}) collective-permute-start(f32[16,512]{1,0:T(8,128)S(1)} %get-tuple-element.19), channel_id=1, source_target_pairs={{0,64},{8,72},{16,80},{24,88},{32,96},{40,104},{48,112},{56,120},{... | collective-permute-start | bytes 98312 | tf_op jit(solution)/shard_map/ppermute | solution.py:75
  88.8 3.8 %collective-permute-start.19 = (f32[16,512]{1,0:T(8,128)S(1)}, f32[16,512]{1,0:T(8,128)S(1)}, u32[]{:S(2)}, u32[]{:S(2)}) collective-permute-start(f32[16,512]{1,0:T(8,128)S(1)} %get-tuple-element.20), channel_id=1, source_target_pairs={{0,192},{8,200},{16,208},{24,216},{32,224},{40,232},{48,240},{56,2... | collective-permute-start | bytes 98312 | tf_op jit(solution)/shard_map/ppermute | solution.py:75
  92.5 1.3 %collective-permute-start.18 = (f32[16,512]{1,0:T(8,128)S(1)}, f32[16,512]{1,0:T(8,128)S(1)}, u32[]{:S(2)}, u32[]{:S(2)}) collective-permute-start(f32[16,512]{1,0:T(8,128)S(1)} %get-tuple-element.21), channel_id=1, source_target_pairs={{0,128},{8,136},{16,144},{24,152},{32,160},{40,168},{48,176},{56,1... | collective-permute-start | bytes 98312 | tf_op jit(solution)/shard_map/ppermute | solution.py:75
  93.8 1.3 %collective-permute-done.19 = f32[16,512]{1,0:T(8,128)S(1)} collective-permute-done((f32[16,512]{1,0:T(8,128)S(1)}, f32[16,512]{1,0:T(8,128)S(1)}, u32[]{:S(2)}, u32[]{:S(2)}) %collective-permute-start.19) | collective-permute-done | bytes 32800 | tf_op jit(solution)/shard_map/ppermute | solution.py:75
  95.1 5.4 %collective-permute-done.18 = f32[16,512]{1,0:T(8,128)S(1)} collective-permute-done((f32[16,512]{1,0:T(8,128)S(1)}, f32[16,512]{1,0:T(8,128)S(1)}, u32[]{:S(2)}, u32[]{:S(2)}) %collective-permute-start.18) | collective-permute-done | bytes 32800 | tf_op jit(solution)/shard_map/ppermute | solution.py:75
  100.5 0.1 mul.89
  100.6 0.6 sub.23
  (46 shorter events, 0.5 us)
Async XLA Ops:
  1.6 13.8 %collective-permute-start.2 = (bf16[1,16,512]{2,1,0:T(8,128)(2,1)S(1)}, bf16[1,16,512]{2,1,0:T(8,128)(2,1)S(1)}, u32[]{:S(2)}, u32[]{:S(2)}) collective-permute-start(bf16[1,16,512]{2,1,0:T(8,128)(2,1)S(1)} %broadcast_in_dim_reshape.4), channel_id=1, source_target_pairs={{0,192},{8,200},{16,208},{24,216},{32,224},{40,232},{48,240},{56,2... | collective-permute-start | bytes 49160 | tf_op jit(solution)/shard_map/ppermute | solution.py:75
  8.0 7.6 %collective-permute-start.1 = (bf16[1,16,512]{2,1,0:T(8,128)(2,1)S(1)}, bf16[1,16,512]{2,1,0:T(8,128)(2,1)S(1)}, u32[]{:S(2)}, u32[]{:S(2)}) collective-permute-start(bf16[1,16,512]{2,1,0:T(8,128)(2,1)S(1)} %broadcast_in_dim_reshape.4), channel_id=1, source_target_pairs={{0,128},{8,136},{16,144},{24,152},{32,160},{40,168},{48,176},{56,1... | collective-permute-start | bytes 49160 | tf_op jit(solution)/shard_map/ppermute | solution.py:75
  9.0 6.7 %collective-permute-start = (bf16[1,16,512]{2,1,0:T(8,128)(2,1)S(1)}, bf16[1,16,512]{2,1,0:T(8,128)(2,1)S(1)}, u32[]{:S(2)}, u32[]{:S(2)}) collective-permute-start(bf16[1,16,512]{2,1,0:T(8,128)(2,1)S(1)} %broadcast_in_dim_reshape.4), channel_id=1, source_target_pairs={{0,64},{8,72},{16,80},{24,88},{32,96},{40,104},{48,112},{56,120},{... | collective-permute-start | bytes 49160 | tf_op jit(solution)/shard_map/ppermute | solution.py:75
  15.2 13.4 %copy-start.4 = (f32[1,8,256]{2,1,0:T(8,128)S(1)}, f32[1,8,256]{2,1,0:T(8,128)}, u32[]{:S(2)}) copy-start(f32[1,8,256]{2,1,0:T(8,128)} %param.8) | copy-start | bytes 24580
  15.2 13.4 %copy-start.5 = (s32[1,256]{1,0:T(1,128)S(1)}, s32[1,256]{1,0:T(1,128)}, u32[]{:S(2)}) copy-start(s32[1,256]{1,0:T(1,128)} %param.10) | copy-start | bytes 3076
  16.3 5.5 %collective-permute-start.5 = (bf16[4,1,16,512]{3,2,0,1:T(8,128)(2,1)S(1)}, bf16[4,1,16,512]{3,2,0,1:T(8,128)(2,1)S(1)}, u32[]{:S(2)}, u32[]{:S(2)}) collective-permute-start(bf16[4,1,16,512]{3,2,0,1:T(8,128)(2,1)S(1)} %bitcast_select_fusion.2), channel_id=1, source_target_pairs={{0,48},{8,56},{16,32},{24,40},{32,16},{40,24},{48,0},{56,8},{64,11... | collective-permute-start | bytes 196616 | tf_op jit(solution)/shard_map/ppermute | solution.py:75
  19.3 5.8 %collective-permute-start.4 = (bf16[4,1,16,512]{3,2,0,1:T(8,128)(2,1)S(1)}, bf16[4,1,16,512]{3,2,0,1:T(8,128)(2,1)S(1)}, u32[]{:S(2)}, u32[]{:S(2)}) collective-permute-start(bf16[4,1,16,512]{3,2,0,1:T(8,128)(2,1)S(1)} %bitcast_select_fusion.2), channel_id=1, source_target_pairs={{0,32},{8,40},{16,48},{24,56},{32,0},{40,8},{48,16},{56,24},{64,96... | collective-permute-start | bytes 196616 | tf_op jit(solution)/shard_map/ppermute | solution.py:75
  19.9 5.1 %collective-permute-start.3 = (bf16[4,1,16,512]{3,2,0,1:T(8,128)(2,1)S(1)}, bf16[4,1,16,512]{3,2,0,1:T(8,128)(2,1)S(1)}, u32[]{:S(2)}, u32[]{:S(2)}) collective-permute-start(bf16[4,1,16,512]{3,2,0,1:T(8,128)(2,1)S(1)} %bitcast_select_fusion.2), channel_id=1, source_target_pairs={{0,16},{8,24},{16,0},{24,8},{32,48},{40,56},{48,32},{56,40},{64,80... | collective-permute-start | bytes 196616 | tf_op jit(solution)/shard_map/ppermute | solution.py:75
  25.8 1.8 %collective-permute-start.6 = (bf16[4,4,1,16,512]{4,3,1,0,2:T(8,128)(2,1)S(1)}, bf16[4,4,1,16,512]{4,3,1,0,2:T(8,128)(2,1)S(1)}, u32[]{:S(2)}, u32[]{:S(2)}) collective-permute-start(bf16[4,4,1,16,512]{4,3,1,0,2:T(8,128)(2,1)S(1)} %bitcast_select_fusion), channel_id=1, source_target_pairs={{0,8},{8,0},{16,24},{24,16},{32,40},{40,32},{48,56},{56,48},{64,72... | collective-permute-start | bytes 786440 | tf_op jit(solution)/shard_map/ppermute | solution.py:75
  29.1 3.1 %copy-start = (pred[8,256,2048]{2,1,0:T(32,128)(4,1)S(1)}, pred[8,256,2048]{2,1,0:T(32,128)(4,1)}, u32[]{:S(2)}) copy-start(pred[8,256,2048]{2,1,0:T(32,128)(4,1)} %iota_compare_fusion) | copy-start | bytes 12582916
  29.1 4.7 %slice-start = ((s8[8388608]{0:T(1024)(128)(4,1)}), s8[4194304]{0:T(1024)(128)(4,1)S(1)}, s32[]{:S(2)}) async-start(s8[8388608]{0:T(1024)(128)(4,1)} %bitcast.128), calls=%async_computation | async-start | bytes 8388608
  32.1 2.4 %slice-start.1 = ((s8[8388608]{0:T(1024)(128)(4,1)}), s8[4194304]{0:T(1024)(128)(4,1)S(1)}, s32[]{:S(2)}) async-start(s8[8388608]{0:T(1024)(128)(4,1)} %bitcast.128), calls=%async_computation.1 | async-start | bytes 8388608
  39.6 8.5 %collective-permute-start.10 = (f32[4,2048]{1,0:T(4,128)S(1)}, f32[4,2048]{1,0:T(4,128)S(1)}, u32[]{:S(2)}, u32[]{:S(2)}) collective-permute-start(f32[4,2048]{1,0:T(4,128)S(1)} %get-tuple-element.6), channel_id=1, source_target_pairs={{0,1},{1,0},{2,3},{3,2},{4,5},{5,4},{6,7},{7,6},{8,9},{9,8},{10,11... | collective-permute-start | bytes 98312 | tf_op jit(solution)/shard_map/ppermute | solution.py:19
  45.5 15.3 %copy-start.2 = (f32[1,8,2048]{2,1,0:T(8,128)S(1)}, f32[1,8,2048]{2,1,0:T(8,128)}, u32[]{:S(2)}) copy-start(f32[1,8,2048]{2,1,0:T(8,128)} %param.7) | copy-start | bytes 196612
  47.2 3.9 %collective-permute-start.7 = (f32[4,2048]{1,0:T(4,128)S(1)}, f32[4,2048]{1,0:T(4,128)S(1)}, u32[]{:S(2)}, u32[]{:S(2)}) collective-permute-start(f32[4,2048]{1,0:T(4,128)S(1)} %get-tuple-element.4), channel_id=1, source_target_pairs={{0,1},{1,0},{2,3},{3,2},{4,5},{5,4},{6,7},{7,6},{8,9},{9,8},{10,11... | collective-permute-start | bytes 98312 | tf_op jit(solution)/shard_map/ppermute | solution.py:19
  48.1 5.7 %collective-permute-start.11 = (f32[4,2048]{1,0:T(4,128)S(1)}, f32[4,2048]{1,0:T(4,128)S(1)}, u32[]{:S(2)}, u32[]{:S(2)}) collective-permute-start(f32[4,2048]{1,0:T(4,128)S(1)} %add.168), channel_id=1, source_target_pairs={{0,2},{1,3},{2,0},{3,1},{4,6},{5,7},{6,4},{7,5},{8,10},{9,11},{10,... | collective-permute-start | bytes 98312 | tf_op jit(solution)/shard_map/ppermute | solution.py:19
  51.2 5.5 %collective-permute-start.8 = (f32[4,2048]{1,0:T(4,128)S(1)}, f32[4,2048]{1,0:T(4,128)S(1)}, u32[]{:S(2)}, u32[]{:S(2)}) collective-permute-start(f32[4,2048]{1,0:T(4,128)S(1)} %add.164), channel_id=1, source_target_pairs={{0,2},{1,3},{2,0},{3,1},{4,6},{5,7},{6,4},{7,5},{8,10},{9,11},{10,... | collective-permute-start | bytes 98312 | tf_op jit(solution)/shard_map/ppermute | solution.py:19
  53.8 4.0 %collective-permute-start.12 = (f32[4,2048]{1,0:T(4,128)S(1)}, f32[4,2048]{1,0:T(4,128)S(1)}, u32[]{:S(2)}, u32[]{:S(2)}) collective-permute-start(f32[4,2048]{1,0:T(4,128)S(1)} %add.169), channel_id=1, source_target_pairs={{0,4},{1,5},{2,6},{3,7},{4,0},{5,1},{6,2},{7,3},{8,12},{9,13},{10,... | collective-permute-start | bytes 98312 | tf_op jit(solution)/shard_map/ppermute | solution.py:19
  56.7 4.0 %collective-permute-start.9 = (f32[4,2048]{1,0:T(4,128)S(1)}, f32[4,2048]{1,0:T(4,128)S(1)}, u32[]{:S(2)}, u32[]{:S(2)}) collective-permute-start(f32[4,2048]{1,0:T(4,128)S(1)} %add.165), channel_id=1, source_target_pairs={{0,4},{1,5},{2,6},{3,7},{4,0},{5,1},{6,2},{7,3},{8,12},{9,13},{10,... | collective-permute-start | bytes 98312 | tf_op jit(solution)/shard_map/ppermute | solution.py:19
  61.4 8.6 %copy-start.3 = (s32[1,8,256]{2,1,0:T(8,128)S(1)}, s32[1,8,256]{2,1,0:T(8,128)}, u32[]{:S(2)}) copy-start(s32[1,8,256]{2,1,0:T(8,128)} %param.9) | copy-start | bytes 24580
  74.3 26.3 %copy-start.1 = (f32[16,8,64]{2,1,0:T(8,128)S(1)}, f32[16,8,64]{2,1,0:T(8,128)}, u32[]{:S(2)}) copy-start(f32[16,8,64]{2,1,0:T(8,128)} %param.11) | copy-start | bytes 98308
  75.3 2.0 %collective-permute-start.13 = (f32[2,2,2,2,16,512]{5,4,3,2,1,0:T(8,128)S(1)}, f32[2,2,2,2,16,512]{5,4,3,2,1,0:T(8,128)S(1)}, u32[]{:S(2)}, u32[]{:S(2)}) collective-permute-start(f32[2,2,2,2,16,512]{5,4,3,2,1,0:T(8,128)S(1)} %dynamic-slice_bitcast_fusion), channel_id=1, source_target_pairs={{0,8},{8,0},{16,24},{24,16},{32,40},{40,32},{48,56},{56,48},{64,72... | collective-permute-start | bytes 1572872 | tf_op jit(solution)/shard_map/ppermute | solution.py:75
  77.4 6.5 %collective-permute-start.14 = (f32[2,2,16,512]{3,2,1,0:T(8,128)S(1)}, f32[2,2,16,512]{3,2,1,0:T(8,128)S(1)}, u32[]{:S(2)}, u32[]{:S(2)}) collective-permute-start(f32[2,2,16,512]{3,2,1,0:T(8,128)S(1)} %get-tuple-element.14), channel_id=1, source_target_pairs={{0,16},{8,24},{16,0},{24,8},{32,48},{40,56},{48,32},{56,40},{64,80... | collective-permute-start | bytes 393224 | tf_op jit(solution)/shard_map/ppermute | solution.py:75
  77.6 9.5 %collective-permute-start.16 = (f32[2,2,16,512]{3,2,1,0:T(8,128)S(1)}, f32[2,2,16,512]{3,2,1,0:T(8,128)S(1)}, u32[]{:S(2)}, u32[]{:S(2)}) collective-permute-start(f32[2,2,16,512]{3,2,1,0:T(8,128)S(1)} %get-tuple-element.15), channel_id=1, source_target_pairs={{0,48},{8,56},{16,32},{24,40},{32,16},{40,24},{48,0},{56,8},{64,11... | collective-permute-start | bytes 393224 | tf_op jit(solution)/shard_map/ppermute | solution.py:75
  80.1 7.1 %collective-permute-start.15 = (f32[2,2,16,512]{3,2,1,0:T(8,128)S(1)}, f32[2,2,16,512]{3,2,1,0:T(8,128)S(1)}, u32[]{:S(2)}, u32[]{:S(2)}) collective-permute-start(f32[2,2,16,512]{3,2,1,0:T(8,128)S(1)} %get-tuple-element.16), channel_id=1, source_target_pairs={{0,32},{8,40},{16,48},{24,56},{32,0},{40,8},{48,16},{56,24},{64,96... | collective-permute-start | bytes 393224 | tf_op jit(solution)/shard_map/ppermute | solution.py:75
  87.2 6.6 %collective-permute-start.17 = (f32[16,512]{1,0:T(8,128)S(1)}, f32[16,512]{1,0:T(8,128)S(1)}, u32[]{:S(2)}, u32[]{:S(2)}) collective-permute-start(f32[16,512]{1,0:T(8,128)S(1)} %get-tuple-element.19), channel_id=1, source_target_pairs={{0,64},{8,72},{16,80},{24,88},{32,96},{40,104},{48,112},{56,120},{... | collective-permute-start | bytes 98312 | tf_op jit(solution)/shard_map/ppermute | solution.py:75
  88.8 6.4 %collective-permute-start.19 = (f32[16,512]{1,0:T(8,128)S(1)}, f32[16,512]{1,0:T(8,128)S(1)}, u32[]{:S(2)}, u32[]{:S(2)}) collective-permute-start(f32[16,512]{1,0:T(8,128)S(1)} %get-tuple-element.20), channel_id=1, source_target_pairs={{0,192},{8,200},{16,208},{24,216},{32,224},{40,232},{48,240},{56,2... | collective-permute-start | bytes 98312 | tf_op jit(solution)/shard_map/ppermute | solution.py:75
  92.5 8.0 %collective-permute-start.18 = (f32[16,512]{1,0:T(8,128)S(1)}, f32[16,512]{1,0:T(8,128)S(1)}, u32[]{:S(2)}, u32[]{:S(2)}) collective-permute-start(f32[16,512]{1,0:T(8,128)S(1)} %get-tuple-element.21), channel_id=1, source_target_pairs={{0,128},{8,136},{16,144},{24,152},{32,160},{40,168},{48,176},{56,1... | collective-permute-start | bytes 98312 | tf_op jit(solution)/shard_map/ppermute | solution.py:75

commit v7 on v6

--- a/solution.py
+++ b/solution.py
@@ -164,27 +164,26 @@
     node_hot = (ev_node[0][:, :, None] == lax.iota(jnp.int32, nodes)[None, None, :]).astype(jnp.bfloat16)
     sens = sensitivity[0]
     span = hours // CHUNKS
+    row_parts = []
     volts_parts = []
     variance_parts = []
     for chunk in range(CHUNKS):
         at = slice(chunk * span, (chunk + 1) * span)
-        spread = jnp.einsum("khr,hkm->hrm", weighted[:, at], node_hot[at], preferred_element_type=jnp.float32)
-        spread_both = jnp.concatenate(_split_bf16(spread), axis=1)
-        volts_both = jnp.einsum("hrm,mn->hrn", spread_both, sens, preferred_element_type=jnp.float32)
-        part = volts_both[:, :columns] + volts_both[:, columns:]
+        rows = jnp.einsum("hkm,mn->hkn", node_hot[at], sens, preferred_element_type=jnp.float32)
+        rows = rows.astype(jnp.bfloat16)
+        part = jnp.einsum("khr,hkn->hrn", weighted[:, at], rows, preferred_element_type=jnp.float32)
+        row_parts.append(rows)
         volts_parts.append(part)
         variance_parts.append(sum_all(jnp.sum(part * part, axis=1), "factor"))
     factor_volts = jnp.concatenate(volts_parts, axis=0)
+    sens_rows = jnp.concatenate(row_parts, axis=0)
     variance = jnp.concatenate(variance_parts, axis=0)[None]
     deviation = jnp.sqrt(variance + epsilon)
     margin = headroom - quantile * deviation
     violation = jnp.maximum(-margin, 0.0)
     var_grad = quantile * violation / deviation
     volt_grad = (2.0 * var_grad[0][:, None, :] * factor_volts).astype(jnp.bfloat16)
-    node_grads = jnp.einsum("hrn,mn->hrm", volt_grad, sens, preferred_element_type=jnp.float32)
-    both = jnp.concatenate(_split_bf16(node_grads), axis=1)
-    picked_both = jnp.einsum("hkm,hrm->khr", node_hot, both, preferred_element_type=jnp.float32)
-    picked = picked_both[:, :, :columns] + picked_both[:, :, columns:]
+    picked = jnp.einsum("hkn,hrn->khr", sens_rows, volt_grad, preferred_element_type=jnp.float32)
     member_grads = (power[:, :, None] * picked).reshape(ev_count, hours * columns)
     grads_hi, grads_lo = _split_bf16(member_grads)
     summed = jnp.einsum("kg,kc->gc", matches, grads_hi, preferred_element_type=jnp.float32)

time: 101 us -> 101 us (level)
  matrix products: 27.8 us -> 36.1 us
  other arithmetic: 10.1 us -> 3.05 us
    dot_general x6 -> x5, matrix products: 26.5 us -> 34.8 us  [the longest x2 23.3 us: shards(): jnp.einsum('hkm,mn->hkn', node_hot[at], sens, preferred_element_type=jnp....]
    eq x1 -> x0, other arithmetic: 4.72 us -> none  [shards(): ev_node[0][:, :, None] == lax.iota(jnp.int32, nodes)[None, None, :]]
    reduce_sum x2 -> x0, other arithmetic: 2.23 us -> none  [shards(): variance_parts.append(sum_all(jnp.sum(part * part, axis=1), 'factor'))]
    ppermute x14, waiting for transfers between devices: 20.4 us -> 19.3 us  [_send_all(): out[j] = lax.ppermute(x_for(j), axis, [(i, i ^ m) for i in range(size)])]
  transfers between devices with their start and end apart: 20 -> 20, of which waited for: 13 -> 11; matrix products, arithmetic and copies ran while one was open for 11% -> 26% of each run, Pallas kernels for 0% -> 0%
where the time goes in v7:
time: 101 us
  matrix products  36.1 us (36%)
  starting transfers between devices  29.7 us (29%)
  waiting for transfers between devices  28.7 us (28%)
  other arithmetic  3.05 us (3%)
  local copies, waits for them, and re-layouts  2.36 us (2%)
    ppermute x14, starting transfers between devices, _send_all(): out[j] = lax.ppermute(x_for(j), axis, [(i, i ^ m) for i in range(size)])  24.1 us
    dot_general x2, matrix products, shards(): jnp.einsum('hkm,mn->hkn', node_hot[at], sens, preferred_element_type=jnp....  23.3 us
    ppermute x14, waiting for transfers between devices, _send_all(): out[j] = lax.ppermute(x_for(j), axis, [(i, i ^ m) for i in range(size)])  19.3 us
    ppermute x6, waiting for transfers between devices, _exchange(): return lax.ppermute(x, axis, perm)  9.34 us
    dot_general x1, matrix products, shards(): jnp.einsum('hkn,hrn->khr', sens_rows, volt_grad, preferred_element_type=j...  6.06 us
    ppermute x6, starting transfers between devices, _exchange(): return lax.ppermute(x, axis, perm)  5.56 us
    dot_general x2, matrix products, shards(): jnp.einsum('khr,hkn->hrn', weighted[:, at], rows, preferred_element_type=...  5.48 us
  transfers between devices with their start and end apart: 20, of which 11 were waited for; matrix products, arithmetic and copies ran while one was open for 26% of the time, Pallas kernels for 0%

profile of v7, /device:TPU:4, one launch (start us, length us, event | category | flops | bytes accessed | tf_op | source)
XLA Modules:
  0.0 100.8 jit_solution(3371550869356392911)
XLA Ops:
  0.6 0.8 convert_element_type.23
  1.5 0.1 broadcast_in_dim_reshape.4
  1.6 6.4 %collective-permute-start.2 = (bf16[1,16,512]{2,1,0:T(8,128)(2,1)S(1)}, bf16[1,16,512]{2,1,0:T(8,128)(2,1)S(1)}, u32[]{:S(2)}, u32[]{:S(2)}) collective-permute-start(bf16[1,16,512]{2,1,0:T(8,128)(2,1)S(1)} %broadcast_in_dim_reshape.4), channel_id=1, source_target_pairs={{0,192},{8,200},{16,208},{24,216},{32,224},{40,232},{48,240},{56,2... | collective-permute-start | bytes 49160 | tf_op jit(solution)/shard_map/ppermute | solution.py:75
  8.0 1.0 collective-permute-start.1
  9.0 1.5 %collective-permute-start = (bf16[1,16,512]{2,1,0:T(8,128)(2,1)S(1)}, bf16[1,16,512]{2,1,0:T(8,128)(2,1)S(1)}, u32[]{:S(2)}, u32[]{:S(2)}) collective-permute-start(bf16[1,16,512]{2,1,0:T(8,128)(2,1)S(1)} %broadcast_in_dim_reshape.4), channel_id=1, source_target_pairs={{0,64},{8,72},{16,80},{24,88},{32,96},{40,104},{48,112},{56,120},{... | collective-permute-start | bytes 49160 | tf_op jit(solution)/shard_map/ppermute | solution.py:75
  10.4 12.8 %fusion.14 = bf16[4,256,2048]{2,1,0:T(8,128)(2,1)} fusion(bf16[1,2048,2048]{2,1,0:T(8,128)(2,1)} %param.6, s32[8,256]{1,0:T(8,128)} %bitcast.128), kind=kOutput, calls=%fused_computation.17 | convolution fusion | flops 8596226048 | bytes 12591104 | tf_op jit(solution)/shard_map/hkm,mn->hkn/dot_general | solution.py:172
  23.2 10.5 %fusion.11 = bf16[4,256,2048]{2,1,0:T(8,128)(2,1)} fusion(bf16[1,2048,2048]{2,1,0:T(8,128)(2,1)S(1)} %copy-done.3, s32[8,256]{1,0:T(8,128)S(1)} %bitcast.129), kind=kOutput, calls=%fused_computation.16 | convolution fusion | flops 8596226048 | bytes 12591104 | tf_op jit(solution)/shard_map/hkm,mn->hkn/dot_general | solution.py:172
  33.8 0.1 stack_broadcast_in_dim_reshape.3
  33.9 0.0 collective-permute-done.2
  33.9 0.0 collective-permute-done.1
  33.9 0.0 collective-permute-done
  34.0 0.6 gather_fusion
  34.5 0.1 bitcast_select_fusion.2
  34.6 3.0 %collective-permute-start.5 = (bf16[4,1,16,512]{3,2,0,1:T(8,128)(2,1)S(1)}, bf16[4,1,16,512]{3,2,0,1:T(8,128)(2,1)S(1)}, u32[]{:S(2)}, u32[]{:S(2)}) collective-permute-start(bf16[4,1,16,512]{3,2,0,1:T(8,128)(2,1)S(1)} %bitcast_select_fusion.2), channel_id=1, source_target_pairs={{0,48},{8,56},{16,32},{24,40},{32,16},{40,24},{48,0},{56,8},{64,11... | collective-permute-start | bytes 196616 | tf_op jit(solution)/shard_map/ppermute | solution.py:75
  37.6 0.6 collective-permute-start.4
  38.3 0.5 collective-permute-start.3
  38.7 0.1 bitcast_select_fusion.3
  38.8 1.3 %collective-permute-done.5 = bf16[4,1,16,512]{3,2,0,1:T(8,128)(2,1)S(1)} collective-permute-done((bf16[4,1,16,512]{3,2,0,1:T(8,128)(2,1)S(1)}, bf16[4,1,16,512]{3,2,0,1:T(8,128)(2,1)S(1)}, u32[]{:S(2)}, u32[]{:S(2)}) %collective-permute-start.5) | collective-permute-done | bytes 65568 | tf_op jit(solution)/shard_map/ppermute | solution.py:75
  40.1 3.3 %collective-permute-done.4 = bf16[4,1,16,512]{3,2,0,1:T(8,128)(2,1)S(1)} collective-permute-done((bf16[4,1,16,512]{3,2,0,1:T(8,128)(2,1)S(1)}, bf16[4,1,16,512]{3,2,0,1:T(8,128)(2,1)S(1)}, u32[]{:S(2)}, u32[]{:S(2)}) %collective-permute-start.4) | collective-permute-done | bytes 65568 | tf_op jit(solution)/shard_map/ppermute | solution.py:75
  43.4 0.0 collective-permute-done.3
  43.4 0.6 gather_fusion.1
  44.0 0.1 bitcast_select_fusion
  44.1 0.3 collective-permute-start.6
  44.4 0.1 fusion.37
  44.5 1.4 %collective-permute-done.6 = bf16[4,4,1,16,512]{4,3,1,0,2:T(8,128)(2,1)S(1)} collective-permute-done((bf16[4,4,1,16,512]{4,3,1,0,2:T(8,128)(2,1)S(1)}, bf16[4,4,1,16,512]{4,3,1,0,2:T(8,128)(2,1)S(1)}, u32[]{:S(2)}, u32[]{:S(2)}) %collective-permute-start.6) | collective-permute-done | bytes 262176 | tf_op jit(solution)/shard_map/ppermute | solution.py:75
  45.9 0.1 maximum_bitcast_fusion
  46.0 0.6 gather_fusion.2
  46.6 0.1 select_bitcast_fusion
  46.7 0.2 copy.11
  47.0 0.4 fusion.29
  47.4 3.2 %multiply_reduce_fusion = (f32[4,2048]{1,0:T(4,128)S(1)}, f32[4,64,2048]{2,1,0:T(8,128)S(1)}) fusion(bf16[256,8,64]{0,2,1:T(8,128)(2,1)S(1)} %fusion.29, bf16[4,256,2048]{2,1,0:T(8,128)(2,1)} %fusion.14), kind=kOutput, calls=%fused_computation.19 | convolution fusion | flops 269475840 | bytes 6586368 | tf_op jit(solution)/shard_map/khr,hkn->hrn/dot_general | solution.py:174
  50.6 0.0 copy-start.1
  50.6 1.3 %collective-permute-start.10 = (f32[4,2048]{1,0:T(4,128)S(1)}, f32[4,2048]{1,0:T(4,128)S(1)}, u32[]{:S(2)}, u32[]{:S(2)}) collective-permute-start(f32[4,2048]{1,0:T(4,128)S(1)} %get-tuple-element.12), channel_id=1, source_target_pairs={{0,1},{1,0},{2,3},{3,2},{4,5},{5,4},{6,7},{7,6},{8,9},{9,8},{10,11... | collective-permute-start | bytes 98312 | tf_op jit(solution)/shard_map/ppermute | solution.py:19
  51.9 2.3 %multiply_reduce_fusion.1 = (f32[4,2048]{1,0:T(4,128)S(1)}, f32[4,64,2048]{2,1,0:T(8,128)}) fusion(bf16[256,8,64]{0,2,1:T(8,128)(2,1)S(1)} %fusion.29, bf16[4,256,2048]{2,1,0:T(8,128)(2,1)S(1)} %copy-done.6), kind=kOutput, calls=%fused_computation.20 | convolution fusion | flops 269475840 | bytes 6586368 | tf_op jit(solution)/shard_map/khr,hkn->hrn/dot_general | solution.py:174
  54.2 0.8 collective-permute-start.7
  55.0 0.0 collective-permute-done.10
  55.0 0.6 collective-permute-start.11
  55.6 2.7 %collective-permute-done.7 = f32[4,2048]{1,0:T(4,128)S(1)} collective-permute-done((f32[4,2048]{1,0:T(4,128)S(1)}, f32[4,2048]{1,0:T(4,128)S(1)}, u32[]{:S(2)}, u32[]{:S(2)}) %collective-permute-start.7) | collective-permute-done | bytes 32800 | tf_op jit(solution)/shard_map/ppermute | solution.py:19
  58.3 0.6 collective-permute-start.8
  59.0 1.5 %collective-permute-done.11 = f32[4,2048]{1,0:T(4,128)S(1)} collective-permute-done((f32[4,2048]{1,0:T(4,128)S(1)}, f32[4,2048]{1,0:T(4,128)S(1)}, u32[]{:S(2)}, u32[]{:S(2)}) %collective-permute-start.11) | collective-permute-done | bytes 32800 | tf_op jit(solution)/shard_map/ppermute | solution.py:19
  60.5 1.1 %collective-permute-start.12 = (f32[4,2048]{1,0:T(4,128)S(1)}, f32[4,2048]{1,0:T(4,128)S(1)}, u32[]{:S(2)}, u32[]{:S(2)}) collective-permute-start(f32[4,2048]{1,0:T(4,128)S(1)} %add.158), channel_id=1, source_target_pairs={{0,4},{1,5},{2,6},{3,7},{4,0},{5,1},{6,2},{7,3},{8,12},{9,13},{10,... | collective-permute-start | bytes 98312 | tf_op jit(solution)/shard_map/ppermute | solution.py:19
  61.7 2.2 %collective-permute-done.8 = f32[4,2048]{1,0:T(4,128)S(1)} collective-permute-done((f32[4,2048]{1,0:T(4,128)S(1)}, f32[4,2048]{1,0:T(4,128)S(1)}, u32[]{:S(2)}, u32[]{:S(2)}) %collective-permute-start.8) | collective-permute-done | bytes 32800 | tf_op jit(solution)/shard_map/ppermute | solution.py:19
  63.9 1.1 %collective-permute-start.9 = (f32[4,2048]{1,0:T(4,128)S(1)}, f32[4,2048]{1,0:T(4,128)S(1)}, u32[]{:S(2)}, u32[]{:S(2)}) collective-permute-start(f32[4,2048]{1,0:T(4,128)S(1)} %add.155), channel_id=1, source_target_pairs={{0,4},{1,5},{2,6},{3,7},{4,0},{5,1},{6,2},{7,3},{8,12},{9,13},{10,... | collective-permute-start | bytes 98312 | tf_op jit(solution)/shard_map/ppermute | solution.py:19
  65.0 2.9 %collective-permute-done.9 = f32[4,2048]{1,0:T(4,128)S(1)} collective-permute-done((f32[4,2048]{1,0:T(4,128)S(1)}, f32[4,2048]{1,0:T(4,128)S(1)}, u32[]{:S(2)}, u32[]{:S(2)}) %collective-permute-start.9) | collective-permute-done | bytes 32800 | tf_op jit(solution)/shard_map/ppermute | solution.py:19
  67.9 0.7 multiply_bitcast_fusion
  68.6 6.1 %fusion.24 = f32[256,8,64]{0,2,1:T(8,128)S(1)} fusion(bf16[4,256,2048]{2,1,0:T(8,128)(2,1)} %fusion.14, bf16[4,256,2048]{2,1,0:T(8,128)(2,1)} %fusion.11, f32[4,64,2048]{2,1,0:T(8,128)S(1)} %get-tuple-element.13, f32[4,64,2048]{2,1,0:T(8,128)} %get-tuple-element.15, f32[8,2048]{1,0:T(8,128)S(1)} %get-tuple-element.2, f32[256,8]{0,1:T(8,128)S(1)} %bitcast.131), kind=kOutput, calls=%fused_computation.24 | convolution fusion | flops 544342016 | bytes 13180928 | tf_op jit(solution)/shard_map/hkn,hrn->khr/dot_general | solution.py:186
  74.6 0.1 fusion.30
  74.7 0.0 copy-start
  74.7 0.4 fusion.35
  75.2 0.4 convolution_add_fusion
  75.7 0.1 collective-permute-start.13
  75.8 1.9 %collective-permute-done.13 = f32[2,2,2,2,16,512]{5,4,3,2,1,0:T(8,128)S(1)} collective-permute-done((f32[2,2,2,2,16,512]{5,4,3,2,1,0:T(8,128)S(1)}, f32[2,2,2,2,16,512]{5,4,3,2,1,0:T(8,128)S(1)}, u32[]{:S(2)}, u32[]{:S(2)}) %collective-permute-start.13) | collective-permute-done | bytes 524320 | tf_op jit(solution)/shard_map/ppermute | solution.py:75
  77.7 0.1 bitcast_add_fusion
  77.8 1.4 %collective-permute-start.16 = (f32[2,2,16,512]{3,2,1,0:T(8,128)S(1)}, f32[2,2,16,512]{3,2,1,0:T(8,128)S(1)}, u32[]{:S(2)}, u32[]{:S(2)}) collective-permute-start(f32[2,2,16,512]{3,2,1,0:T(8,128)S(1)} %get-tuple-element.5), channel_id=1, source_target_pairs={{0,48},{8,56},{16,32},{24,40},{32,16},{40,24},{48,0},{56,8},{64,11... | collective-permute-start | bytes 393224 | tf_op jit(solution)/shard_map/ppermute | solution.py:75
  79.2 0.9 collective-permute-start.15
  80.1 1.9 %collective-permute-start.14 = (f32[2,2,16,512]{3,2,1,0:T(8,128)S(1)}, f32[2,2,16,512]{3,2,1,0:T(8,128)S(1)}, u32[]{:S(2)}, u32[]{:S(2)}) collective-permute-start(f32[2,2,16,512]{3,2,1,0:T(8,128)S(1)} %get-tuple-element.4), channel_id=1, source_target_pairs={{0,16},{8,24},{16,0},{24,8},{32,48},{40,56},{48,32},{56,40},{64,80... | collective-permute-start | bytes 393224 | tf_op jit(solution)/shard_map/ppermute | solution.py:75
  82.0 5.5 %collective-permute-done.16 = f32[2,2,16,512]{3,2,1,0:T(8,128)S(1)} collective-permute-done((f32[2,2,16,512]{3,2,1,0:T(8,128)S(1)}, f32[2,2,16,512]{3,2,1,0:T(8,128)S(1)}, u32[]{:S(2)}, u32[]{:S(2)}) %collective-permute-start.16) | collective-permute-done | bytes 131104 | tf_op jit(solution)/shard_map/ppermute | solution.py:75
  87.4 0.6 collective-permute-done.14
  88.1 4.1 %collective-permute-start.19 = (f32[16,512]{1,0:T(8,128)S(1)}, f32[16,512]{1,0:T(8,128)S(1)}, u32[]{:S(2)}, u32[]{:S(2)}) collective-permute-start(f32[16,512]{1,0:T(8,128)S(1)} %get-tuple-element.10), channel_id=1, source_target_pairs={{0,192},{8,200},{16,208},{24,216},{32,224},{40,232},{48,240},{56,2... | collective-permute-start | bytes 98312 | tf_op jit(solution)/shard_map/ppermute | solution.py:75
  92.2 1.0 collective-permute-start.18
  93.2 1.5 %collective-permute-start.17 = (f32[16,512]{1,0:T(8,128)S(1)}, f32[16,512]{1,0:T(8,128)S(1)}, u32[]{:S(2)}, u32[]{:S(2)}) collective-permute-start(f32[16,512]{1,0:T(8,128)S(1)} %get-tuple-element.9), channel_id=1, source_target_pairs={{0,64},{8,72},{16,80},{24,88},{32,96},{40,104},{48,112},{56,120},{... | collective-permute-start | bytes 98312 | tf_op jit(solution)/shard_map/ppermute | solution.py:75
  94.7 5.3 %collective-permute-done.18 = f32[16,512]{1,0:T(8,128)S(1)} collective-permute-done((f32[16,512]{1,0:T(8,128)S(1)}, f32[16,512]{1,0:T(8,128)S(1)}, u32[]{:S(2)}, u32[]{:S(2)}) %collective-permute-start.18) | collective-permute-done | bytes 32800 | tf_op jit(solution)/shard_map/ppermute | solution.py:75
  100.1 0.1 mul.89
  100.2 0.6 sub.11
  (38 shorter events, 0.4 us)
Async XLA Ops:
  1.6 32.3 %collective-permute-start.2 = (bf16[1,16,512]{2,1,0:T(8,128)(2,1)S(1)}, bf16[1,16,512]{2,1,0:T(8,128)(2,1)S(1)}, u32[]{:S(2)}, u32[]{:S(2)}) collective-permute-start(bf16[1,16,512]{2,1,0:T(8,128)(2,1)S(1)} %broadcast_in_dim_reshape.4), channel_id=1, source_target_pairs={{0,192},{8,200},{16,208},{24,216},{32,224},{40,232},{48,240},{56,2... | collective-permute-start | bytes 49160 | tf_op jit(solution)/shard_map/ppermute | solution.py:75
  8.0 26.0 %collective-permute-start.1 = (bf16[1,16,512]{2,1,0:T(8,128)(2,1)S(1)}, bf16[1,16,512]{2,1,0:T(8,128)(2,1)S(1)}, u32[]{:S(2)}, u32[]{:S(2)}) collective-permute-start(bf16[1,16,512]{2,1,0:T(8,128)(2,1)S(1)} %broadcast_in_dim_reshape.4), channel_id=1, source_target_pairs={{0,128},{8,136},{16,144},{24,152},{32,160},{40,168},{48,176},{56,1... | collective-permute-start | bytes 49160 | tf_op jit(solution)/shard_map/ppermute | solution.py:75
  9.0 25.0 %collective-permute-start = (bf16[1,16,512]{2,1,0:T(8,128)(2,1)S(1)}, bf16[1,16,512]{2,1,0:T(8,128)(2,1)S(1)}, u32[]{:S(2)}, u32[]{:S(2)}) collective-permute-start(bf16[1,16,512]{2,1,0:T(8,128)(2,1)S(1)} %broadcast_in_dim_reshape.4), channel_id=1, source_target_pairs={{0,64},{8,72},{16,80},{24,88},{32,96},{40,104},{48,112},{56,120},{... | collective-permute-start | bytes 49160 | tf_op jit(solution)/shard_map/ppermute | solution.py:75
  10.4 12.8 %copy-start.3 = (bf16[1,2048,2048]{2,1,0:T(8,128)(2,1)S(1)}, bf16[1,2048,2048]{2,1,0:T(8,128)(2,1)}, u32[]{:S(2)}) copy-start(bf16[1,2048,2048]{2,1,0:T(8,128)(2,1)} %param.6) | copy-start | bytes 25165828
  10.4 12.8 %copy-start.4 = (s32[1,8,256]{2,1,0:T(8,128)S(1)}, s32[1,8,256]{2,1,0:T(8,128)}, u32[]{:S(2)}) copy-start(s32[1,8,256]{2,1,0:T(8,128)} %param.9) | copy-start | bytes 24580
  33.7 13.2 %copy-start.2 = (s32[1,256]{1,0:T(1,128)S(1)}, s32[1,256]{1,0:T(1,128)}, u32[]{:S(2)}) copy-start(s32[1,256]{1,0:T(1,128)} %param.10) | copy-start | bytes 3076
  33.7 13.3 %copy-start.5 = (f32[1,8,256]{2,1,0:T(8,128)S(1)}, f32[1,8,256]{2,1,0:T(8,128)}, u32[]{:S(2)}) copy-start(f32[1,8,256]{2,1,0:T(8,128)} %param.8) | copy-start | bytes 24580
  34.6 5.5 %collective-permute-start.5 = (bf16[4,1,16,512]{3,2,0,1:T(8,128)(2,1)S(1)}, bf16[4,1,16,512]{3,2,0,1:T(8,128)(2,1)S(1)}, u32[]{:S(2)}, u32[]{:S(2)}) collective-permute-start(bf16[4,1,16,512]{3,2,0,1:T(8,128)(2,1)S(1)} %bitcast_select_fusion.2), channel_id=1, source_target_pairs={{0,48},{8,56},{16,32},{24,40},{32,16},{40,24},{48,0},{56,8},{64,11... | collective-permute-start | bytes 196616 | tf_op jit(solution)/shard_map/ppermute | solution.py:75
  37.6 5.8 %collective-permute-start.4 = (bf16[4,1,16,512]{3,2,0,1:T(8,128)(2,1)S(1)}, bf16[4,1,16,512]{3,2,0,1:T(8,128)(2,1)S(1)}, u32[]{:S(2)}, u32[]{:S(2)}) collective-permute-start(bf16[4,1,16,512]{3,2,0,1:T(8,128)(2,1)S(1)} %bitcast_select_fusion.2), channel_id=1, source_target_pairs={{0,32},{8,40},{16,48},{24,56},{32,0},{40,8},{48,16},{56,24},{64,96... | collective-permute-start | bytes 196616 | tf_op jit(solution)/shard_map/ppermute | solution.py:75
  38.3 5.1 %collective-permute-start.3 = (bf16[4,1,16,512]{3,2,0,1:T(8,128)(2,1)S(1)}, bf16[4,1,16,512]{3,2,0,1:T(8,128)(2,1)S(1)}, u32[]{:S(2)}, u32[]{:S(2)}) collective-permute-start(bf16[4,1,16,512]{3,2,0,1:T(8,128)(2,1)S(1)} %bitcast_select_fusion.2), channel_id=1, source_target_pairs={{0,16},{8,24},{16,0},{24,8},{32,48},{40,56},{48,32},{56,40},{64,80... | collective-permute-start | bytes 196616 | tf_op jit(solution)/shard_map/ppermute | solution.py:75
  44.1 1.8 %collective-permute-start.6 = (bf16[4,4,1,16,512]{4,3,1,0,2:T(8,128)(2,1)S(1)}, bf16[4,4,1,16,512]{4,3,1,0,2:T(8,128)(2,1)S(1)}, u32[]{:S(2)}, u32[]{:S(2)}) collective-permute-start(bf16[4,4,1,16,512]{4,3,1,0,2:T(8,128)(2,1)S(1)} %bitcast_select_fusion), channel_id=1, source_target_pairs={{0,8},{8,0},{16,24},{24,16},{32,40},{40,32},{48,56},{56,48},{64,72... | collective-permute-start | bytes 786440 | tf_op jit(solution)/shard_map/ppermute | solution.py:75
  47.4 4.5 %copy-start.6 = (bf16[4,256,2048]{2,1,0:T(8,128)(2,1)S(1)}, bf16[4,256,2048]{2,1,0:T(8,128)(2,1)}, u32[]{:S(2)}) copy-start(bf16[4,256,2048]{2,1,0:T(8,128)(2,1)} %fusion.11) | copy-start | bytes 12582916
  50.6 17.3 %copy-start.1 = (f32[1,8,2048]{2,1,0:T(8,128)S(1)}, f32[1,8,2048]{2,1,0:T(8,128)}, u32[]{:S(2)}) copy-start(f32[1,8,2048]{2,1,0:T(8,128)} %param.7) | copy-start | bytes 196612
  50.6 4.4 %collective-permute-start.10 = (f32[4,2048]{1,0:T(4,128)S(1)}, f32[4,2048]{1,0:T(4,128)S(1)}, u32[]{:S(2)}, u32[]{:S(2)}) collective-permute-start(f32[4,2048]{1,0:T(4,128)S(1)} %get-tuple-element.12), channel_id=1, source_target_pairs={{0,1},{1,0},{2,3},{3,2},{4,5},{5,4},{6,7},{7,6},{8,9},{9,8},{10,11... | collective-permute-start | bytes 98312 | tf_op jit(solution)/shard_map/ppermute | solution.py:19
  54.2 4.2 %collective-permute-start.7 = (f32[4,2048]{1,0:T(4,128)S(1)}, f32[4,2048]{1,0:T(4,128)S(1)}, u32[]{:S(2)}, u32[]{:S(2)}) collective-permute-start(f32[4,2048]{1,0:T(4,128)S(1)} %get-tuple-element.14), channel_id=1, source_target_pairs={{0,1},{1,0},{2,3},{3,2},{4,5},{5,4},{6,7},{7,6},{8,9},{9,8},{10,11... | collective-permute-start | bytes 98312 | tf_op jit(solution)/shard_map/ppermute | solution.py:19
  55.0 5.5 %collective-permute-start.11 = (f32[4,2048]{1,0:T(4,128)S(1)}, f32[4,2048]{1,0:T(4,128)S(1)}, u32[]{:S(2)}, u32[]{:S(2)}) collective-permute-start(f32[4,2048]{1,0:T(4,128)S(1)} %add.157), channel_id=1, source_target_pairs={{0,2},{1,3},{2,0},{3,1},{4,6},{5,7},{6,4},{7,5},{8,10},{9,11},{10,... | collective-permute-start | bytes 98312 | tf_op jit(solution)/shard_map/ppermute | solution.py:19
  58.3 5.5 %collective-permute-start.8 = (f32[4,2048]{1,0:T(4,128)S(1)}, f32[4,2048]{1,0:T(4,128)S(1)}, u32[]{:S(2)}, u32[]{:S(2)}) collective-permute-start(f32[4,2048]{1,0:T(4,128)S(1)} %add.154), channel_id=1, source_target_pairs={{0,2},{1,3},{2,0},{3,1},{4,6},{5,7},{6,4},{7,5},{8,10},{9,11},{10,... | collective-permute-start | bytes 98312 | tf_op jit(solution)/shard_map/ppermute | solution.py:19
  60.5 4.4 %collective-permute-start.12 = (f32[4,2048]{1,0:T(4,128)S(1)}, f32[4,2048]{1,0:T(4,128)S(1)}, u32[]{:S(2)}, u32[]{:S(2)}) collective-permute-start(f32[4,2048]{1,0:T(4,128)S(1)} %add.158), channel_id=1, source_target_pairs={{0,4},{1,5},{2,6},{3,7},{4,0},{5,1},{6,2},{7,3},{8,12},{9,13},{10,... | collective-permute-start | bytes 98312 | tf_op jit(solution)/shard_map/ppermute | solution.py:19
  63.9 4.0 %collective-permute-start.9 = (f32[4,2048]{1,0:T(4,128)S(1)}, f32[4,2048]{1,0:T(4,128)S(1)}, u32[]{:S(2)}, u32[]{:S(2)}) collective-permute-start(f32[4,2048]{1,0:T(4,128)S(1)} %add.155), channel_id=1, source_target_pairs={{0,4},{1,5},{2,6},{3,7},{4,0},{5,1},{6,2},{7,3},{8,12},{9,13},{10,... | collective-permute-start | bytes 98312 | tf_op jit(solution)/shard_map/ppermute | solution.py:19
  74.7 25.4 %copy-start = (f32[16,8,64]{2,1,0:T(8,128)S(1)}, f32[16,8,64]{2,1,0:T(8,128)}, u32[]{:S(2)}) copy-start(f32[16,8,64]{2,1,0:T(8,128)} %param.11) | copy-start | bytes 98308
  75.7 2.0 %collective-permute-start.13 = (f32[2,2,2,2,16,512]{5,4,3,2,1,0:T(8,128)S(1)}, f32[2,2,2,2,16,512]{5,4,3,2,1,0:T(8,128)S(1)}, u32[]{:S(2)}, u32[]{:S(2)}) collective-permute-start(f32[2,2,2,2,16,512]{5,4,3,2,1,0:T(8,128)S(1)} %dynamic-slice_bitcast_fusion), channel_id=1, source_target_pairs={{0,8},{8,0},{16,24},{24,16},{32,40},{40,32},{48,56},{56,48},{64,72... | collective-permute-start | bytes 1572872 | tf_op jit(solution)/shard_map/ppermute | solution.py:75
  77.8 9.6 %collective-permute-start.16 = (f32[2,2,16,512]{3,2,1,0:T(8,128)S(1)}, f32[2,2,16,512]{3,2,1,0:T(8,128)S(1)}, u32[]{:S(2)}, u32[]{:S(2)}) collective-permute-start(f32[2,2,16,512]{3,2,1,0:T(8,128)S(1)} %get-tuple-element.5), channel_id=1, source_target_pairs={{0,48},{8,56},{16,32},{24,40},{32,16},{40,24},{48,0},{56,8},{64,11... | collective-permute-start | bytes 393224 | tf_op jit(solution)/shard_map/ppermute | solution.py:75
  79.2 8.3 %collective-permute-start.15 = (f32[2,2,16,512]{3,2,1,0:T(8,128)S(1)}, f32[2,2,16,512]{3,2,1,0:T(8,128)S(1)}, u32[]{:S(2)}, u32[]{:S(2)}) collective-permute-start(f32[2,2,16,512]{3,2,1,0:T(8,128)S(1)} %get-tuple-element.6), channel_id=1, source_target_pairs={{0,32},{8,40},{16,48},{24,56},{32,0},{40,8},{48,16},{56,24},{64,96... | collective-permute-start | bytes 393224 | tf_op jit(solution)/shard_map/ppermute | solution.py:75
  80.1 8.0 %collective-permute-start.14 = (f32[2,2,16,512]{3,2,1,0:T(8,128)S(1)}, f32[2,2,16,512]{3,2,1,0:T(8,128)S(1)}, u32[]{:S(2)}, u32[]{:S(2)}) collective-permute-start(f32[2,2,16,512]{3,2,1,0:T(8,128)S(1)} %get-tuple-element.4), channel_id=1, source_target_pairs={{0,16},{8,24},{16,0},{24,8},{32,48},{40,56},{48,32},{56,40},{64,80... | collective-permute-start | bytes 393224 | tf_op jit(solution)/shard_map/ppermute | solution.py:75
  88.1 6.6 %collective-permute-start.19 = (f32[16,512]{1,0:T(8,128)S(1)}, f32[16,512]{1,0:T(8,128)S(1)}, u32[]{:S(2)}, u32[]{:S(2)}) collective-permute-start(f32[16,512]{1,0:T(8,128)S(1)} %get-tuple-element.10), channel_id=1, source_target_pairs={{0,192},{8,200},{16,208},{24,216},{32,224},{40,232},{48,240},{56,2... | collective-permute-start | bytes 98312 | tf_op jit(solution)/shard_map/ppermute | solution.py:75
  92.2 7.8 %collective-permute-start.18 = (f32[16,512]{1,0:T(8,128)S(1)}, f32[16,512]{1,0:T(8,128)S(1)}, u32[]{:S(2)}, u32[]{:S(2)}) collective-permute-start(f32[16,512]{1,0:T(8,128)S(1)} %get-tuple-element.11), channel_id=1, source_target_pairs={{0,128},{8,136},{16,144},{24,152},{32,160},{40,168},{48,176},{56,1... | collective-permute-start | bytes 98312 | tf_op jit(solution)/shard_map/ppermute | solution.py:75
  93.2 6.8 %collective-permute-start.17 = (f32[16,512]{1,0:T(8,128)S(1)}, f32[16,512]{1,0:T(8,128)S(1)}, u32[]{:S(2)}, u32[]{:S(2)}) collective-permute-start(f32[16,512]{1,0:T(8,128)S(1)} %get-tuple-element.9), channel_id=1, source_target_pairs={{0,64},{8,72},{16,80},{24,88},{32,96},{40,104},{48,112},{56,120},{... | collective-permute-start | bytes 98312 | tf_op jit(solution)/shard_map/ppermute | solution.py:75

commit v8 on v7

--- a/solution.py
+++ b/solution.py
@@ -80,7 +80,7 @@
     idx = jnp.arange(count, dtype=jnp.int32) ^ s
     return jnp.take(cand, idx, axis=0)
 
-def gather_groups(x, axis, groups):
+def gather_groups(x, axis, groups, hooks=()):
     size = lax.axis_size(axis)
     me = lax.axis_index(axis)
     buf = x[None]
@@ -91,6 +91,8 @@
         got = _send_all(lambda j: buf, axis, bits, size)
         stacked = _ordered(buf, got, s, count)
         buf = stacked
+        if len(done) < len(hooks):
+            buf = hooks[len(done)](buf)
         done.append(bits)
     buf = buf.reshape(buf.shape[:len(groups)] + x.shape)
     order = sorted(range(len(groups)), key=lambda g: -max(groups[len(groups) - 1 - g]))
@@ -154,23 +156,41 @@
     ev_count = ev_power.shape[2]
     total_regions = reg_local * lax.axis_size("feeder")
     packed = loadings.astype(jnp.bfloat16).reshape(reg_local, hours * columns)
-    shard_rows = gather_groups(packed, "feeder", _bit_groups("feeder"))
+    node_hot = (ev_node[0][:, :, None] == lax.iota(jnp.int32, nodes)[None, None, :]).astype(jnp.bfloat16)
+    span = hours // CHUNKS
+    hot_parts = [node_hot[chunk * span : (chunk + 1) * span] for chunk in range(CHUNKS)]
+    sens = sensitivity[0]
+
+    def rows_of(hot):
+        rows = jnp.einsum("hkm,mn->hkn", hot, sens, preferred_element_type=jnp.float32)
+        return rows.astype(jnp.bfloat16)
+
+    later = {}
+
+    def after_first(buf):
+        buf, hot = lax.optimization_barrier((buf, hot_parts[1]))
+        later["rows"] = rows_of(hot)
+        return buf
+
+    def after_second(buf):
+        buf, later["rows"] = lax.optimization_barrier((buf, later["rows"]))
+        return buf
+
+    hooks = (after_first, after_second) if CHUNKS == 2 else ()
+    shard_rows = gather_groups(packed, "feeder", _bit_groups("feeder"), hooks)
+    row_list = [rows_of(hot_parts[0]), later["rows"]] if CHUNKS == 2 else [rows_of(h) for h in hot_parts]
     regions = region_map.reshape(-1)
     matches = (regions[:, None] == lax.iota(jnp.int32, total_regions)[None, :]).astype(jnp.bfloat16)
     looked = jnp.dot(matches, shard_rows, preferred_element_type=jnp.float32)
     looked = looked.reshape(ev_count, hours, columns)
     power = ev_power[0].T
     weighted = (power[:, :, None] * looked).astype(jnp.bfloat16)
-    node_hot = (ev_node[0][:, :, None] == lax.iota(jnp.int32, nodes)[None, None, :]).astype(jnp.bfloat16)
-    sens = sensitivity[0]
-    span = hours // CHUNKS
     row_parts = []
     volts_parts = []
     variance_parts = []
     for chunk in range(CHUNKS):
         at = slice(chunk * span, (chunk + 1) * span)
-        rows = jnp.einsum("hkm,mn->hkn", node_hot[at], sens, preferred_element_type=jnp.float32)
-        rows = rows.astype(jnp.bfloat16)
+        rows = row_list[chunk]
         part = jnp.einsum("khr,hkn->hrn", weighted[:, at], rows, preferred_element_type=jnp.float32)
         row_parts.append(rows)
         volts_parts.append(part)

time: 101 us -> 107 us (1.059)
  other arithmetic: 3.05 us -> 9.34 us
  waiting for transfers between devices: 28.7 us -> 24.9 us
  matrix products: 36.1 us -> 39.4 us
    ppermute x14, waiting for transfers between devices: 19.3 us -> 15.5 us  [_send_all(): out[j] = lax.ppermute(x_for(j), axis, [(i, i ^ m) for i in range(size)])]
    eq x0 -> x1, other arithmetic: none -> 3.43 us  [shards(): ev_node[0][:, :, None] == lax.iota(jnp.int32, nodes)[None, None, :]]
    dot_general x2, matrix products: 23.3 us -> 26.5 us  [rows_of(): jnp.einsum('hkm,mn->hkn', hot, sens, preferred_element_type=jnp.float32)]
    slice x0 -> x1, other arithmetic: none -> 3.03 us  [shards(): node_hot[chunk * span:(chunk + 1) * span]]
  transfers between devices with their start and end apart: 20 -> 20, of which waited for: 11 -> 9; matrix products, arithmetic and copies ran while one was open for 26% -> 33% of each run, Pallas kernels for 0% -> 0%
where the time goes in v8:
time: 107 us
  matrix products  39.4 us (37%)
  starting transfers between devices  29.7 us (28%)
  waiting for transfers between devices  24.9 us (23%)
  other arithmetic  9.34 us (9%)
  local copies, waits for them, and re-layouts  2.36 us (2%)
    dot_general x2, matrix products, rows_of(): jnp.einsum('hkm,mn->hkn', hot, sens, preferred_element_type=jnp.float32)  26.5 us
    ppermute x14, starting transfers between devices, _send_all(): out[j] = lax.ppermute(x_for(j), axis, [(i, i ^ m) for i in range(size)])  24.1 us
    ppermute x14, waiting for transfers between devices, _send_all(): out[j] = lax.ppermute(x_for(j), axis, [(i, i ^ m) for i in range(size)])  15.5 us
    ppermute x6, waiting for transfers between devices, _exchange(): return lax.ppermute(x, axis, perm)  9.33 us
    dot_general x1, matrix products, shards(): jnp.einsum('hkn,hrn->khr', sens_rows, volt_grad, preferred_element_type=j...  6.06 us
    ppermute x6, starting transfers between devices, _exchange(): return lax.ppermute(x, axis, perm)  5.57 us
    dot_general x2, matrix products, shards(): jnp.einsum('khr,hkn->hrn', weighted[:, at], rows, preferred_element_type=...  5.52 us
    eq x1, other arithmetic, shards(): ev_node[0][:, :, None] == lax.iota(jnp.int32, nodes)[None, None, :]  3.43 us
  transfers between devices with their start and end apart: 20, of which 9 were waited for; matrix products, arithmetic and copies ran while one was open for 33% of the time, Pallas kernels for 0%

profile of v8, /device:TPU:4, one launch (start us, length us, event | category | flops | bytes accessed | tf_op | source)
XLA Modules:
  0.0 106.6 jit_solution(930201342382708178)
XLA Ops:
  0.6 0.8 convert_element_type.23
  1.5 0.1 broadcast_in_dim_reshape.4
  1.6 6.4 %collective-permute-start.2 = (bf16[1,16,512]{2,1,0:T(8,128)(2,1)S(1)}, bf16[1,16,512]{2,1,0:T(8,128)(2,1)S(1)}, u32[]{:S(2)}, u32[]{:S(2)}) collective-permute-start(bf16[1,16,512]{2,1,0:T(8,128)(2,1)S(1)} %broadcast_in_dim_reshape.4), channel_id=1, source_target_pairs={{0,192},{8,200},{16,208},{24,216},{32,224},{40,232},{48,240},{56,2... | collective-permute-start | bytes 49160 | tf_op jit(solution)/shard_map/ppermute | solution.py:75
  8.0 1.0 collective-permute-start.1
  9.0 1.5 %collective-permute-start = (bf16[1,16,512]{2,1,0:T(8,128)(2,1)S(1)}, bf16[1,16,512]{2,1,0:T(8,128)(2,1)S(1)}, u32[]{:S(2)}, u32[]{:S(2)}) collective-permute-start(bf16[1,16,512]{2,1,0:T(8,128)(2,1)S(1)} %broadcast_in_dim_reshape.4), channel_id=1, source_target_pairs={{0,64},{8,72},{16,80},{24,88},{32,96},{40,104},{48,112},{56,120},{... | collective-permute-start | bytes 49160 | tf_op jit(solution)/shard_map/ppermute | solution.py:75
  10.4 3.4 %iota_compare_fusion = pred[8,256,2048]{2,1,0:T(8,128)(4,1)S(1)} fusion(s32[8,256]{1,0:T(8,128)} %bitcast.124), kind=kLoop, calls=%fused_computation.3 | loop fusion | flops 4194304 | bytes 4202496 | tf_op jit(solution)/shard_map/eq | solution.py:159
  13.9 0.0 copy-start.2
  13.9 3.0 %slice_convert_fusion = bf16[4,256,2048]{2,1,0:T(8,128)(2,1)} fusion(pred[8,256,2048]{2,1,0:T(8,128)(4,1)S(1)} %iota_compare_fusion), kind=kLoop, calls=%fused_computation.12 | loop fusion | flops 2097152 | bytes 6291456 | tf_op jit(solution)/shard_map/slice | solution.py:161
  16.9 12.7 %fusion.12 = bf16[4,256,2048]{2,1,0:T(8,128)(2,1)} fusion(bf16[1,2048,2048]{2,1,0:T(8,128)(2,1)} %param.6, s32[8,256]{1,0:T(8,128)S(1)} %bitcast.125), kind=kOutput, calls=%fused_computation.16 | convolution fusion | flops 8596226048 | bytes 12591104 | tf_op jit(solution)/shard_map/hkm,mn->hkn/dot_general | solution.py:165
  29.6 0.1 stack_broadcast_in_dim_reshape.3
  29.7 0.0 collective-permute-done.1
  29.8 0.6 gather_fusion
  30.3 0.1 bitcast_select_fusion.1
  30.4 3.0 %collective-permute-start.5 = (bf16[4,1,16,512]{3,2,0,1:T(8,128)(2,1)S(1)}, bf16[4,1,16,512]{3,2,0,1:T(8,128)(2,1)S(1)}, u32[]{:S(2)}, u32[]{:S(2)}) collective-permute-start(bf16[4,1,16,512]{3,2,0,1:T(8,128)(2,1)S(1)} %bitcast_select_fusion.1), channel_id=1, source_target_pairs={{0,48},{8,56},{16,32},{24,40},{32,16},{40,24},{48,0},{56,8},{64,11... | collective-permute-start | bytes 196616 | tf_op jit(solution)/shard_map/ppermute | solution.py:75
  33.4 0.6 collective-permute-start.4
  34.1 0.5 collective-permute-start.3
  34.5 13.9 %fusion.9 = bf16[4,256,2048]{2,1,0:T(8,128)(2,1)} fusion(bf16[4,256,2048]{2,1,0:T(8,128)(2,1)} %slice_convert_fusion, bf16[1,2048,2048]{2,1,0:T(8,128)(2,1)} %param.6), kind=kOutput, calls=%fused_computation.15 | convolution fusion | flops 8592031744 | bytes 16777216 | tf_op jit(solution)/shard_map/hkm,mn->hkn/dot_general | solution.py:165
  48.4 0.0 collective-permute-done.5
  48.4 0.0 collective-permute-done.4
  48.4 0.6 gather_fusion.1
  49.0 0.1 bitcast_select_fusion
  49.1 0.1 collective-permute-start.6
  49.3 1.5 %collective-permute-done.6 = bf16[4,4,1,16,512]{4,3,1,0,2:T(8,128)(2,1)S(1)} collective-permute-done((bf16[4,4,1,16,512]{4,3,1,0,2:T(8,128)(2,1)S(1)}, bf16[4,4,1,16,512]{4,3,1,0,2:T(8,128)(2,1)S(1)}, u32[]{:S(2)}, u32[]{:S(2)}) %collective-permute-start.6) | collective-permute-done | bytes 262176 | tf_op jit(solution)/shard_map/ppermute | solution.py:75
  50.7 0.1 maximum_bitcast_fusion
  50.8 0.6 gather_fusion.2
  51.4 0.1 select_bitcast_fusion
  51.5 0.2 copy.11
  51.8 0.4 fusion.27
  52.2 3.2 %multiply_reduce_fusion = (f32[4,2048]{1,0:T(4,128)S(1)}, f32[4,64,2048]{2,1,0:T(8,128)S(1)}) fusion(bf16[256,8,64]{0,2,1:T(8,128)(2,1)S(1)} %fusion.27, bf16[4,256,2048]{2,1,0:T(8,128)(2,1)} %fusion.9), kind=kOutput, calls=%fused_computation.18 | convolution fusion | flops 269475840 | bytes 6586368 | tf_op jit(solution)/shard_map/khr,hkn->hrn/dot_general | solution.py:194
  55.5 0.0 copy-start.1
  55.5 1.3 %collective-permute-start.10 = (f32[4,2048]{1,0:T(4,128)S(1)}, f32[4,2048]{1,0:T(4,128)S(1)}, u32[]{:S(2)}, u32[]{:S(2)}) collective-permute-start(f32[4,2048]{1,0:T(4,128)S(1)} %get-tuple-element.20), channel_id=1, source_target_pairs={{0,1},{1,0},{2,3},{3,2},{4,5},{5,4},{6,7},{7,6},{8,9},{9,8},{10,11... | collective-permute-start | bytes 98312 | tf_op jit(solution)/shard_map/ppermute | solution.py:19
  56.8 2.3 %multiply_reduce_fusion.1 = (f32[4,2048]{1,0:T(4,128)S(1)}, f32[4,64,2048]{2,1,0:T(8,128)}) fusion(bf16[256,8,64]{0,2,1:T(8,128)(2,1)S(1)} %fusion.27, bf16[4,256,2048]{2,1,0:T(8,128)(2,1)S(1)} %copy-done.5), kind=kOutput, calls=%fused_computation.19 | convolution fusion | flops 269475840 | bytes 6586368 | tf_op jit(solution)/shard_map/khr,hkn->hrn/dot_general | solution.py:194
  59.0 0.8 collective-permute-start.7
  59.9 0.0 collective-permute-done.10
  59.9 0.6 collective-permute-start.11
  60.5 2.7 %collective-permute-done.7 = f32[4,2048]{1,0:T(4,128)S(1)} collective-permute-done((f32[4,2048]{1,0:T(4,128)S(1)}, f32[4,2048]{1,0:T(4,128)S(1)}, u32[]{:S(2)}, u32[]{:S(2)}) %collective-permute-start.7) | collective-permute-done | bytes 32800 | tf_op jit(solution)/shard_map/ppermute | solution.py:19
  63.2 0.7 collective-permute-start.8
  63.9 1.5 %collective-permute-done.11 = f32[4,2048]{1,0:T(4,128)S(1)} collective-permute-done((f32[4,2048]{1,0:T(4,128)S(1)}, f32[4,2048]{1,0:T(4,128)S(1)}, u32[]{:S(2)}, u32[]{:S(2)}) %collective-permute-start.11) | collective-permute-done | bytes 32800 | tf_op jit(solution)/shard_map/ppermute | solution.py:19
  65.4 1.1 %collective-permute-start.12 = (f32[4,2048]{1,0:T(4,128)S(1)}, f32[4,2048]{1,0:T(4,128)S(1)}, u32[]{:S(2)}, u32[]{:S(2)}) collective-permute-start(f32[4,2048]{1,0:T(4,128)S(1)} %add.158), channel_id=1, source_target_pairs={{0,4},{1,5},{2,6},{3,7},{4,0},{5,1},{6,2},{7,3},{8,12},{9,13},{10,... | collective-permute-start | bytes 98312 | tf_op jit(solution)/shard_map/ppermute | solution.py:19
  66.5 2.2 %collective-permute-done.8 = f32[4,2048]{1,0:T(4,128)S(1)} collective-permute-done((f32[4,2048]{1,0:T(4,128)S(1)}, f32[4,2048]{1,0:T(4,128)S(1)}, u32[]{:S(2)}, u32[]{:S(2)}) %collective-permute-start.8) | collective-permute-done | bytes 32800 | tf_op jit(solution)/shard_map/ppermute | solution.py:19
  68.7 1.1 %collective-permute-start.9 = (f32[4,2048]{1,0:T(4,128)S(1)}, f32[4,2048]{1,0:T(4,128)S(1)}, u32[]{:S(2)}, u32[]{:S(2)}) collective-permute-start(f32[4,2048]{1,0:T(4,128)S(1)} %add.155), channel_id=1, source_target_pairs={{0,4},{1,5},{2,6},{3,7},{4,0},{5,1},{6,2},{7,3},{8,12},{9,13},{10,... | collective-permute-start | bytes 98312 | tf_op jit(solution)/shard_map/ppermute | solution.py:19
  69.8 2.9 %collective-permute-done.9 = f32[4,2048]{1,0:T(4,128)S(1)} collective-permute-done((f32[4,2048]{1,0:T(4,128)S(1)}, f32[4,2048]{1,0:T(4,128)S(1)}, u32[]{:S(2)}, u32[]{:S(2)}) %collective-permute-start.9) | collective-permute-done | bytes 32800 | tf_op jit(solution)/shard_map/ppermute | solution.py:19
  72.8 0.7 multiply_bitcast_fusion
  73.4 6.1 %fusion.22 = f32[256,8,64]{0,2,1:T(8,128)S(1)} fusion(bf16[4,256,2048]{2,1,0:T(8,128)(2,1)} %fusion.9, bf16[4,256,2048]{2,1,0:T(8,128)(2,1)} %fusion.12, f32[4,64,2048]{2,1,0:T(8,128)S(1)} %get-tuple-element.21, f32[4,64,2048]{2,1,0:T(8,128)} %get-tuple-element.23, f32[8,2048]{1,0:T(8,128)S(1)} %get-tuple-element.10, f32[256,8]{0,1:T(8,128)S(1)} %bitcast.130), kind=kOutput, calls=%fused_computation.23 | convolution fusion | flops 544342016 | bytes 13180928 | tf_op jit(solution)/shard_map/hkn,hrn->khr/dot_general | solution.py:206
  79.5 0.1 fusion.28
  79.6 0.0 copy-start
  79.6 0.4 fusion.33
  80.0 0.4 convolution_add_fusion
  80.5 0.1 collective-permute-start.13
  80.6 1.9 %collective-permute-done.13 = f32[2,2,2,2,16,512]{5,4,3,2,1,0:T(8,128)S(1)} collective-permute-done((f32[2,2,2,2,16,512]{5,4,3,2,1,0:T(8,128)S(1)}, f32[2,2,2,2,16,512]{5,4,3,2,1,0:T(8,128)S(1)}, u32[]{:S(2)}, u32[]{:S(2)}) %collective-permute-start.13) | collective-permute-done | bytes 524320 | tf_op jit(solution)/shard_map/ppermute | solution.py:75
  82.5 0.1 bitcast_add_fusion
  82.7 3.3 %collective-permute-start.16 = (f32[2,2,16,512]{3,2,1,0:T(8,128)S(1)}, f32[2,2,16,512]{3,2,1,0:T(8,128)S(1)}, u32[]{:S(2)}, u32[]{:S(2)}) collective-permute-start(f32[2,2,16,512]{3,2,1,0:T(8,128)S(1)} %get-tuple-element.13), channel_id=1, source_target_pairs={{0,48},{8,56},{16,32},{24,40},{32,16},{40,24},{48,0},{56,8},{64,11... | collective-permute-start | bytes 393224 | tf_op jit(solution)/shard_map/ppermute | solution.py:75
  86.0 0.6 collective-permute-start.15
  86.6 0.5 collective-permute-start.14
  87.1 4.8 %collective-permute-done.16 = f32[2,2,16,512]{3,2,1,0:T(8,128)S(1)} collective-permute-done((f32[2,2,16,512]{3,2,1,0:T(8,128)S(1)}, f32[2,2,16,512]{3,2,1,0:T(8,128)S(1)}, u32[]{:S(2)}, u32[]{:S(2)}) %collective-permute-start.16) | collective-permute-done | bytes 131104 | tf_op jit(solution)/shard_map/ppermute | solution.py:75
  91.8 2.0 %collective-permute-done.15 = f32[2,2,16,512]{3,2,1,0:T(8,128)S(1)} collective-permute-done((f32[2,2,16,512]{3,2,1,0:T(8,128)S(1)}, f32[2,2,16,512]{3,2,1,0:T(8,128)S(1)}, u32[]{:S(2)}, u32[]{:S(2)}) %collective-permute-start.15) | collective-permute-done | bytes 131104 | tf_op jit(solution)/shard_map/ppermute | solution.py:75
  93.9 4.1 %collective-permute-start.19 = (f32[16,512]{1,0:T(8,128)S(1)}, f32[16,512]{1,0:T(8,128)S(1)}, u32[]{:S(2)}, u32[]{:S(2)}) collective-permute-start(f32[16,512]{1,0:T(8,128)S(1)} %get-tuple-element.18), channel_id=1, source_target_pairs={{0,192},{8,200},{16,208},{24,216},{32,224},{40,232},{48,240},{56,2... | collective-permute-start | bytes 98312 | tf_op jit(solution)/shard_map/ppermute | solution.py:75
  98.1 1.0 collective-permute-start.18
  99.1 1.5 %collective-permute-start.17 = (f32[16,512]{1,0:T(8,128)S(1)}, f32[16,512]{1,0:T(8,128)S(1)}, u32[]{:S(2)}, u32[]{:S(2)}) collective-permute-start(f32[16,512]{1,0:T(8,128)S(1)} %get-tuple-element.17), channel_id=1, source_target_pairs={{0,64},{8,72},{16,80},{24,88},{32,96},{40,104},{48,112},{56,120},{... | collective-permute-start | bytes 98312 | tf_op jit(solution)/shard_map/ppermute | solution.py:75
  100.5 0.0 collective-permute-done.19
  100.5 5.4 %collective-permute-done.18 = f32[16,512]{1,0:T(8,128)S(1)} collective-permute-done((f32[16,512]{1,0:T(8,128)S(1)}, f32[16,512]{1,0:T(8,128)S(1)}, u32[]{:S(2)}, u32[]{:S(2)}) %collective-permute-start.18) | collective-permute-done | bytes 32800 | tf_op jit(solution)/shard_map/ppermute | solution.py:75
  105.9 0.0 collective-permute-done.17
  105.9 0.1 mul.89
  106.0 0.6 sub.11
  (36 shorter events, 0.4 us)
Async XLA Ops:
  1.6 28.1 %collective-permute-start.2 = (bf16[1,16,512]{2,1,0:T(8,128)(2,1)S(1)}, bf16[1,16,512]{2,1,0:T(8,128)(2,1)S(1)}, u32[]{:S(2)}, u32[]{:S(2)}) collective-permute-start(bf16[1,16,512]{2,1,0:T(8,128)(2,1)S(1)} %broadcast_in_dim_reshape.4), channel_id=1, source_target_pairs={{0,192},{8,200},{16,208},{24,216},{32,224},{40,232},{48,240},{56,2... | collective-permute-start | bytes 49160 | tf_op jit(solution)/shard_map/ppermute | solution.py:75
  8.0 21.8 %collective-permute-start.1 = (bf16[1,16,512]{2,1,0:T(8,128)(2,1)S(1)}, bf16[1,16,512]{2,1,0:T(8,128)(2,1)S(1)}, u32[]{:S(2)}, u32[]{:S(2)}) collective-permute-start(bf16[1,16,512]{2,1,0:T(8,128)(2,1)S(1)} %broadcast_in_dim_reshape.4), channel_id=1, source_target_pairs={{0,128},{8,136},{16,144},{24,152},{32,160},{40,168},{48,176},{56,1... | collective-permute-start | bytes 49160 | tf_op jit(solution)/shard_map/ppermute | solution.py:75
  9.0 20.8 %collective-permute-start = (bf16[1,16,512]{2,1,0:T(8,128)(2,1)S(1)}, bf16[1,16,512]{2,1,0:T(8,128)(2,1)S(1)}, u32[]{:S(2)}, u32[]{:S(2)}) collective-permute-start(bf16[1,16,512]{2,1,0:T(8,128)(2,1)S(1)} %broadcast_in_dim_reshape.4), channel_id=1, source_target_pairs={{0,64},{8,72},{16,80},{24,88},{32,96},{40,104},{48,112},{56,120},{... | collective-permute-start | bytes 49160 | tf_op jit(solution)/shard_map/ppermute | solution.py:75
  13.9 3.1 %copy-start.2 = (s32[1,8,256]{2,1,0:T(8,128)S(1)}, s32[1,8,256]{2,1,0:T(8,128)}, u32[]{:S(2)}) copy-start(s32[1,8,256]{2,1,0:T(8,128)} %param.9) | copy-start | bytes 24580
  30.4 18.0 %collective-permute-start.5 = (bf16[4,1,16,512]{3,2,0,1:T(8,128)(2,1)S(1)}, bf16[4,1,16,512]{3,2,0,1:T(8,128)(2,1)S(1)}, u32[]{:S(2)}, u32[]{:S(2)}) collective-permute-start(bf16[4,1,16,512]{3,2,0,1:T(8,128)(2,1)S(1)} %bitcast_select_fusion.1), channel_id=1, source_target_pairs={{0,48},{8,56},{16,32},{24,40},{32,16},{40,24},{48,0},{56,8},{64,11... | collective-permute-start | bytes 196616 | tf_op jit(solution)/shard_map/ppermute | solution.py:75
  33.4 14.9 %collective-permute-start.4 = (bf16[4,1,16,512]{3,2,0,1:T(8,128)(2,1)S(1)}, bf16[4,1,16,512]{3,2,0,1:T(8,128)(2,1)S(1)}, u32[]{:S(2)}, u32[]{:S(2)}) collective-permute-start(bf16[4,1,16,512]{3,2,0,1:T(8,128)(2,1)S(1)} %bitcast_select_fusion.1), channel_id=1, source_target_pairs={{0,32},{8,40},{16,48},{24,56},{32,0},{40,8},{48,16},{56,24},{64,96... | collective-permute-start | bytes 196616 | tf_op jit(solution)/shard_map/ppermute | solution.py:75
  34.1 14.3 %collective-permute-start.3 = (bf16[4,1,16,512]{3,2,0,1:T(8,128)(2,1)S(1)}, bf16[4,1,16,512]{3,2,0,1:T(8,128)(2,1)S(1)}, u32[]{:S(2)}, u32[]{:S(2)}) collective-permute-start(bf16[4,1,16,512]{3,2,0,1:T(8,128)(2,1)S(1)} %bitcast_select_fusion.1), channel_id=1, source_target_pairs={{0,16},{8,24},{16,0},{24,8},{32,48},{40,56},{48,32},{56,40},{64,80... | collective-permute-start | bytes 196616 | tf_op jit(solution)/shard_map/ppermute | solution.py:75
  48.4 3.4 %copy-start.3 = (s32[1,256]{1,0:T(1,128)S(1)}, s32[1,256]{1,0:T(1,128)}, u32[]{:S(2)}) copy-start(s32[1,256]{1,0:T(1,128)} %param.10) | copy-start | bytes 3076
  48.4 3.4 %copy-start.4 = (f32[1,8,256]{2,1,0:T(8,128)S(1)}, f32[1,8,256]{2,1,0:T(8,128)}, u32[]{:S(2)}) copy-start(f32[1,8,256]{2,1,0:T(8,128)} %param.8) | copy-start | bytes 24580
  49.1 1.6 %collective-permute-start.6 = (bf16[4,4,1,16,512]{4,3,1,0,2:T(8,128)(2,1)S(1)}, bf16[4,4,1,16,512]{4,3,1,0,2:T(8,128)(2,1)S(1)}, u32[]{:S(2)}, u32[]{:S(2)}) collective-permute-start(bf16[4,4,1,16,512]{4,3,1,0,2:T(8,128)(2,1)S(1)} %bitcast_select_fusion), channel_id=1, source_target_pairs={{0,8},{8,0},{16,24},{24,16},{32,40},{40,32},{48,56},{56,48},{64,72... | collective-permute-start | bytes 786440 | tf_op jit(solution)/shard_map/ppermute | solution.py:75
  52.2 4.6 %copy-start.5 = (bf16[4,256,2048]{2,1,0:T(8,128)(2,1)S(1)}, bf16[4,256,2048]{2,1,0:T(8,128)(2,1)}, u32[]{:S(2)}) copy-start(bf16[4,256,2048]{2,1,0:T(8,128)(2,1)} %fusion.12) | copy-start | bytes 12582916
  55.5 17.3 %copy-start.1 = (f32[1,8,2048]{2,1,0:T(8,128)S(1)}, f32[1,8,2048]{2,1,0:T(8,128)}, u32[]{:S(2)}) copy-start(f32[1,8,2048]{2,1,0:T(8,128)} %param.7) | copy-start | bytes 196612
  55.5 4.4 %collective-permute-start.10 = (f32[4,2048]{1,0:T(4,128)S(1)}, f32[4,2048]{1,0:T(4,128)S(1)}, u32[]{:S(2)}, u32[]{:S(2)}) collective-permute-start(f32[4,2048]{1,0:T(4,128)S(1)} %get-tuple-element.20), channel_id=1, source_target_pairs={{0,1},{1,0},{2,3},{3,2},{4,5},{5,4},{6,7},{7,6},{8,9},{9,8},{10,11... | collective-permute-start | bytes 98312 | tf_op jit(solution)/shard_map/ppermute | solution.py:19
  59.0 4.1 %collective-permute-start.7 = (f32[4,2048]{1,0:T(4,128)S(1)}, f32[4,2048]{1,0:T(4,128)S(1)}, u32[]{:S(2)}, u32[]{:S(2)}) collective-permute-start(f32[4,2048]{1,0:T(4,128)S(1)} %get-tuple-element.22), channel_id=1, source_target_pairs={{0,1},{1,0},{2,3},{3,2},{4,5},{5,4},{6,7},{7,6},{8,9},{9,8},{10,11... | collective-permute-start | bytes 98312 | tf_op jit(solution)/shard_map/ppermute | solution.py:19
  59.9 5.5 %collective-permute-start.11 = (f32[4,2048]{1,0:T(4,128)S(1)}, f32[4,2048]{1,0:T(4,128)S(1)}, u32[]{:S(2)}, u32[]{:S(2)}) collective-permute-start(f32[4,2048]{1,0:T(4,128)S(1)} %add.157), channel_id=1, source_target_pairs={{0,2},{1,3},{2,0},{3,1},{4,6},{5,7},{6,4},{7,5},{8,10},{9,11},{10,... | collective-permute-start | bytes 98312 | tf_op jit(solution)/shard_map/ppermute | solution.py:19
  63.2 5.5 %collective-permute-start.8 = (f32[4,2048]{1,0:T(4,128)S(1)}, f32[4,2048]{1,0:T(4,128)S(1)}, u32[]{:S(2)}, u32[]{:S(2)}) collective-permute-start(f32[4,2048]{1,0:T(4,128)S(1)} %add.154), channel_id=1, source_target_pairs={{0,2},{1,3},{2,0},{3,1},{4,6},{5,7},{6,4},{7,5},{8,10},{9,11},{10,... | collective-permute-start | bytes 98312 | tf_op jit(solution)/shard_map/ppermute | solution.py:19
  65.4 4.4 %collective-permute-start.12 = (f32[4,2048]{1,0:T(4,128)S(1)}, f32[4,2048]{1,0:T(4,128)S(1)}, u32[]{:S(2)}, u32[]{:S(2)}) collective-permute-start(f32[4,2048]{1,0:T(4,128)S(1)} %add.158), channel_id=1, source_target_pairs={{0,4},{1,5},{2,6},{3,7},{4,0},{5,1},{6,2},{7,3},{8,12},{9,13},{10,... | collective-permute-start | bytes 98312 | tf_op jit(solution)/shard_map/ppermute | solution.py:19
  68.7 4.0 %collective-permute-start.9 = (f32[4,2048]{1,0:T(4,128)S(1)}, f32[4,2048]{1,0:T(4,128)S(1)}, u32[]{:S(2)}, u32[]{:S(2)}) collective-permute-start(f32[4,2048]{1,0:T(4,128)S(1)} %add.155), channel_id=1, source_target_pairs={{0,4},{1,5},{2,6},{3,7},{4,0},{5,1},{6,2},{7,3},{8,12},{9,13},{10,... | collective-permute-start | bytes 98312 | tf_op jit(solution)/shard_map/ppermute | solution.py:19
  79.6 26.4 %copy-start = (f32[16,8,64]{2,1,0:T(8,128)S(1)}, f32[16,8,64]{2,1,0:T(8,128)}, u32[]{:S(2)}) copy-start(f32[16,8,64]{2,1,0:T(8,128)} %param.11) | copy-start | bytes 98308
  80.5 2.0 %collective-permute-start.13 = (f32[2,2,2,2,16,512]{5,4,3,2,1,0:T(8,128)S(1)}, f32[2,2,2,2,16,512]{5,4,3,2,1,0:T(8,128)S(1)}, u32[]{:S(2)}, u32[]{:S(2)}) collective-permute-start(f32[2,2,2,2,16,512]{5,4,3,2,1,0:T(8,128)S(1)} %dynamic-slice_bitcast_fusion), channel_id=1, source_target_pairs={{0,8},{8,0},{16,24},{24,16},{32,40},{40,32},{48,56},{56,48},{64,72... | collective-permute-start | bytes 1572872 | tf_op jit(solution)/shard_map/ppermute | solution.py:75
  82.7 9.2 %collective-permute-start.16 = (f32[2,2,16,512]{3,2,1,0:T(8,128)S(1)}, f32[2,2,16,512]{3,2,1,0:T(8,128)S(1)}, u32[]{:S(2)}, u32[]{:S(2)}) collective-permute-start(f32[2,2,16,512]{3,2,1,0:T(8,128)S(1)} %get-tuple-element.13), channel_id=1, source_target_pairs={{0,48},{8,56},{16,32},{24,40},{32,16},{40,24},{48,0},{56,8},{64,11... | collective-permute-start | bytes 393224 | tf_op jit(solution)/shard_map/ppermute | solution.py:75
  86.0 7.9 %collective-permute-start.15 = (f32[2,2,16,512]{3,2,1,0:T(8,128)S(1)}, f32[2,2,16,512]{3,2,1,0:T(8,128)S(1)}, u32[]{:S(2)}, u32[]{:S(2)}) collective-permute-start(f32[2,2,16,512]{3,2,1,0:T(8,128)S(1)} %get-tuple-element.14), channel_id=1, source_target_pairs={{0,32},{8,40},{16,48},{24,56},{32,0},{40,8},{48,16},{56,24},{64,96... | collective-permute-start | bytes 393224 | tf_op jit(solution)/shard_map/ppermute | solution.py:75
  86.6 7.3 %collective-permute-start.14 = (f32[2,2,16,512]{3,2,1,0:T(8,128)S(1)}, f32[2,2,16,512]{3,2,1,0:T(8,128)S(1)}, u32[]{:S(2)}, u32[]{:S(2)}) collective-permute-start(f32[2,2,16,512]{3,2,1,0:T(8,128)S(1)} %get-tuple-element.12), channel_id=1, source_target_pairs={{0,16},{8,24},{16,0},{24,8},{32,48},{40,56},{48,32},{56,40},{64,80... | collective-permute-start | bytes 393224 | tf_op jit(solution)/shard_map/ppermute | solution.py:75
  93.9 6.6 %collective-permute-start.19 = (f32[16,512]{1,0:T(8,128)S(1)}, f32[16,512]{1,0:T(8,128)S(1)}, u32[]{:S(2)}, u32[]{:S(2)}) collective-permute-start(f32[16,512]{1,0:T(8,128)S(1)} %get-tuple-element.18), channel_id=1, source_target_pairs={{0,192},{8,200},{16,208},{24,216},{32,224},{40,232},{48,240},{56,2... | collective-permute-start | bytes 98312 | tf_op jit(solution)/shard_map/ppermute | solution.py:75
  98.1 7.8 %collective-permute-start.18 = (f32[16,512]{1,0:T(8,128)S(1)}, f32[16,512]{1,0:T(8,128)S(1)}, u32[]{:S(2)}, u32[]{:S(2)}) collective-permute-start(f32[16,512]{1,0:T(8,128)S(1)} %get-tuple-element.19), channel_id=1, source_target_pairs={{0,128},{8,136},{16,144},{24,152},{32,160},{40,168},{48,176},{56,1... | collective-permute-start | bytes 98312 | tf_op jit(solution)/shard_map/ppermute | solution.py:75
  99.1 6.8 %collective-permute-start.17 = (f32[16,512]{1,0:T(8,128)S(1)}, f32[16,512]{1,0:T(8,128)S(1)}, u32[]{:S(2)}, u32[]{:S(2)}) collective-permute-start(f32[16,512]{1,0:T(8,128)S(1)} %get-tuple-element.17), channel_id=1, source_target_pairs={{0,64},{8,72},{16,80},{24,88},{32,96},{40,104},{48,112},{56,120},{... | collective-permute-start | bytes 98312 | tf_op jit(solution)/shard_map/ppermute | solution.py:75

commit v9 on v5

--- a/solution.py
+++ b/solution.py
@@ -134,6 +134,9 @@
     return x
 
 
+CHUNKS = 2
+
+
 def _bit_groups(axis):
     rest = list(range(1, _bit_count(lax.axis_size(axis))))
     pairs = [tuple(rest[max(0, i - 1) : i + 1]) for i in range(len(rest) - 1, -1, -2)]
@@ -159,22 +162,31 @@
     power = ev_power[0].T
     weighted = (power[:, :, None] * looked).astype(jnp.bfloat16)
     node_hot = (ev_node[0][:, :, None] == lax.iota(jnp.int32, nodes)[None, None, :]).astype(jnp.bfloat16)
-    spread = jnp.einsum("khr,hkm->hrm", weighted, node_hot, preferred_element_type=jnp.float32)
+    sens = sensitivity[0]
+    span = hours // 2
+    early, late = slice(0, span), slice(span, hours)
+    rows = jnp.einsum("hkm,mn->hkn", node_hot[early], sens, preferred_element_type=jnp.float32)
+    rows = rows.astype(jnp.bfloat16)
+    volts_early = jnp.einsum("khr,hkn->hrn", weighted[:, early], rows, preferred_element_type=jnp.float32)
+    variance_early = sum_all(jnp.sum(volts_early * volts_early, axis=1), "factor")
+    spread = jnp.einsum("khr,hkm->hrm", weighted[:, late], node_hot[late], preferred_element_type=jnp.float32)
     spread_both = jnp.concatenate(_split_bf16(spread), axis=1)
-    sens = sensitivity[0]
     volts_both = jnp.einsum("hrm,mn->hrn", spread_both, sens, preferred_element_type=jnp.float32)
-    factor_volts = volts_both[:, :columns] + volts_both[:, columns:]
-    partial_sum = jnp.sum(factor_volts * factor_volts, axis=1)
-    variance = sum_all(partial_sum, "factor")[None]
+    volts_late = volts_both[:, :columns] + volts_both[:, columns:]
+    variance_late = sum_all(jnp.sum(volts_late * volts_late, axis=1), "factor")
+    factor_volts = jnp.concatenate([volts_early, volts_late], axis=0)
+    variance = jnp.concatenate([variance_early, variance_late], axis=0)[None]
     deviation = jnp.sqrt(variance + epsilon)
     margin = headroom - quantile * deviation
     violation = jnp.maximum(-margin, 0.0)
     var_grad = quantile * violation / deviation
     volt_grad = (2.0 * var_grad[0][:, None, :] * factor_volts).astype(jnp.bfloat16)
-    node_grads = jnp.einsum("hrn,mn->hrm", volt_grad, sens, preferred_element_type=jnp.float32)
+    picked_early = jnp.einsum("hkn,hrn->khr", rows, volt_grad[early], preferred_element_type=jnp.float32)
+    node_grads = jnp.einsum("hrn,mn->hrm", volt_grad[late], sens, preferred_element_type=jnp.float32)
     both = jnp.concatenate(_split_bf16(node_grads), axis=1)
-    picked_both = jnp.einsum("hkm,hrm->khr", node_hot, both, preferred_element_type=jnp.float32)
-    picked = picked_both[:, :, :columns] + picked_both[:, :, columns:]
+    picked_both = jnp.einsum("hkm,hrm->khr", node_hot[late], both, preferred_element_type=jnp.float32)
+    picked_late = picked_both[:, :, :columns] + picked_both[:, :, columns:]
+    picked = jnp.concatenate([picked_early, picked_late], axis=1)
     member_grads = (power[:, :, None] * picked).reshape(ev_count, hours * columns)
     grads_hi, grads_lo = _split_bf16(member_grads)
     summed = jnp.einsum("kg,kc->gc", matches, grads_hi, preferred_element_type=jnp.float32)

time: 104 us -> 108 us (1.038)
  waiting for transfers between devices: 33.9 us -> 27.9 us
  other arithmetic: 4.18 us -> 8.31 us
  starting transfers between devices: 27.2 us -> 30.7 us
  matrix products: 32.8 us -> 35.9 us
    dot_general x3 -> x7, matrix products: 19.8 us -> 28.1 us  [the longest x1 12.7 us: shards(): jnp.einsum('hkm,mn->hkn', node_hot[early], sens, preferred_element_type=j...]
    dot_general x1, matrix products: 12.1 us -> 6.96 us  [shards(): jnp.einsum('hrm,mn->hrn', spread_both, sens, preferred_element_type=jnp.f...]
    eq x0 -> x1, other arithmetic: none -> 4.71 us  [shards(): ev_node[0][:, :, None] == lax.iota(jnp.int32, nodes)[None, None, :]]
    ppermute x3 -> x6, starting transfers between devices: 3.12 us -> 6.57 us  [_exchange(): return lax.ppermute(x, axis, perm)]
    ppermute x3 -> x6, waiting for transfers between devices: 11.6 us -> 8.56 us  [_exchange(): return lax.ppermute(x, axis, perm)]
    ppermute x14, waiting for transfers between devices: 22.3 us -> 19.4 us  [_send_all(): out[j] = lax.ppermute(x_for(j), axis, [(i, i ^ m) for i in range(size)])]
    unnamed x12 -> x18, local copies, waits for them, and re-layouts: 2.17 us -> 1.23 us
  transfers between devices with their start and end apart: 17 -> 20, of which waited for: 11 -> 11; matrix products, arithmetic and copies ran while one was open for 0% -> 19% of each run, Pallas kernels for 0% -> 0%
where the time goes in v9:
time: 108 us; the launch traced here: 107 us
  matrix products  35.9 us (33%)
  starting transfers between devices  30.7 us (28%)
  waiting for transfers between devices  27.9 us (26%)
  other arithmetic  8.31 us (8%)
  local copies, waits for them, and re-layouts  3.55 us (3%)
    ppermute x14, starting transfers between devices, _send_all(): out[j] = lax.ppermute(x_for(j), axis, [(i, i ^ m) for i in range(size)])  24.1 us
    ppermute x14, waiting for transfers between devices, _send_all(): out[j] = lax.ppermute(x_for(j), axis, [(i, i ^ m) for i in range(size)])  19.4 us
    dot_general x1, matrix products, shards(): jnp.einsum('hkm,mn->hkn', node_hot[early], sens, preferred_element_type=j...  12.7 us
    ppermute x6, waiting for transfers between devices, _exchange(): return lax.ppermute(x, axis, perm)  8.56 us
    dot_general x1, matrix products, shards(): jnp.einsum('hrm,mn->hrn', spread_both, sens, preferred_element_type=jnp.f...  6.96 us
    ppermute x6, starting transfers between devices, _exchange(): return lax.ppermute(x, axis, perm)  6.57 us
    dot_general x1, matrix products, shards(): jnp.einsum('hrn,mn->hrm', volt_grad[late], sens, preferred_element_type=j...  5.96 us
    eq x1, other arithmetic, shards(): ev_node[0][:, :, None] == lax.iota(jnp.int32, nodes)[None, None, :]  4.71 us
  transfers between devices with their start and end apart: 20, of which 11 were waited for; matrix products, arithmetic and copies ran while one was open for 19% of the time, Pallas kernels for 0%

profile of v9, /device:TPU:4, one launch (start us, length us, event | category | flops | bytes accessed | tf_op | source)
XLA Modules:
  0.0 107.4 jit_solution(17367016997296787789)
XLA Ops:
  0.6 0.0 copy-start.3
  0.6 0.9 convert_element_type.32
  1.5 0.1 broadcast_in_dim_reshape.4
  1.6 6.4 %collective-permute-start.2 = (bf16[1,16,512]{2,1,0:T(8,128)(2,1)S(1)}, bf16[1,16,512]{2,1,0:T(8,128)(2,1)S(1)}, u32[]{:S(2)}, u32[]{:S(2)}) collective-permute-start(bf16[1,16,512]{2,1,0:T(8,128)(2,1)S(1)} %broadcast_in_dim_reshape.4), channel_id=1, source_target_pairs={{0,192},{8,200},{16,208},{24,216},{32,224},{40,232},{48,240},{56,2... | collective-permute-start | bytes 49160 | tf_op jit(solution)/shard_map/ppermute | solution.py:75
  8.0 1.0 collective-permute-start.1
  9.0 1.5 %collective-permute-start = (bf16[1,16,512]{2,1,0:T(8,128)(2,1)S(1)}, bf16[1,16,512]{2,1,0:T(8,128)(2,1)S(1)}, u32[]{:S(2)}, u32[]{:S(2)}) collective-permute-start(bf16[1,16,512]{2,1,0:T(8,128)(2,1)S(1)} %broadcast_in_dim_reshape.4), channel_id=1, source_target_pairs={{0,64},{8,72},{16,80},{24,88},{32,96},{40,104},{48,112},{56,120},{... | collective-permute-start | bytes 49160 | tf_op jit(solution)/shard_map/ppermute | solution.py:75
  10.5 4.7 %iota_compare_fusion = pred[8,256,2048]{2,1,0:T(32,128)(4,1)} fusion(s32[8,256]{1,0:T(8,128)} %bitcast.127), kind=kLoop, calls=%fused_computation.3 | loop fusion | flops 4194304 | bytes 4202496 | tf_op jit(solution)/shard_map/eq | solution.py:164
  15.2 12.7 %fusion.11 = bf16[4,256,2048]{2,1,0:T(8,128)(2,1)} fusion(bf16[1,2048,2048]{2,1,0:T(8,128)(2,1)} %param.6, s32[8,256]{1,0:T(8,128)S(1)} %bitcast.128), kind=kOutput, calls=%fused_computation.16 | convolution fusion | flops 8596226048 | bytes 12591104 | tf_op jit(solution)/shard_map/hkm,mn->hkn/dot_general | solution.py:168
  27.9 0.1 stack_broadcast_in_dim_reshape.3
  28.1 0.6 gather_fusion
  28.6 0.1 bitcast_select_fusion.2
  28.7 3.0 %collective-permute-start.5 = (bf16[4,1,16,512]{3,2,0,1:T(8,128)(2,1)S(1)}, bf16[4,1,16,512]{3,2,0,1:T(8,128)(2,1)S(1)}, u32[]{:S(2)}, u32[]{:S(2)}) collective-permute-start(bf16[4,1,16,512]{3,2,0,1:T(8,128)(2,1)S(1)} %bitcast_select_fusion.2), channel_id=1, source_target_pairs={{0,48},{8,56},{16,32},{24,40},{32,16},{40,24},{48,0},{56,8},{64,11... | collective-permute-start | bytes 196616 | tf_op jit(solution)/shard_map/ppermute | solution.py:75
  31.8 0.6 collective-permute-start.4
  32.4 0.5 collective-permute-start.3
  32.9 0.1 bitcast_select_fusion.3
  32.9 1.3 %collective-permute-done.5 = bf16[4,1,16,512]{3,2,0,1:T(8,128)(2,1)S(1)} collective-permute-done((bf16[4,1,16,512]{3,2,0,1:T(8,128)(2,1)S(1)}, bf16[4,1,16,512]{3,2,0,1:T(8,128)(2,1)S(1)}, u32[]{:S(2)}, u32[]{:S(2)}) %collective-permute-start.5) | collective-permute-done | bytes 65568 | tf_op jit(solution)/shard_map/ppermute | solution.py:75
  34.2 3.3 %collective-permute-done.4 = bf16[4,1,16,512]{3,2,0,1:T(8,128)(2,1)S(1)} collective-permute-done((bf16[4,1,16,512]{3,2,0,1:T(8,128)(2,1)S(1)}, bf16[4,1,16,512]{3,2,0,1:T(8,128)(2,1)S(1)}, u32[]{:S(2)}, u32[]{:S(2)}) %collective-permute-start.4) | collective-permute-done | bytes 65568 | tf_op jit(solution)/shard_map/ppermute | solution.py:75
  37.6 0.6 gather_fusion.1
  38.2 0.1 bitcast_select_fusion
  38.3 0.3 collective-permute-start.6
  38.6 0.1 fusion.35
  38.6 1.4 %collective-permute-done.6 = bf16[4,4,1,16,512]{4,3,1,0,2:T(8,128)(2,1)S(1)} collective-permute-done((bf16[4,4,1,16,512]{4,3,1,0,2:T(8,128)(2,1)S(1)}, bf16[4,4,1,16,512]{4,3,1,0,2:T(8,128)(2,1)S(1)}, u32[]{:S(2)}, u32[]{:S(2)}) %collective-permute-start.6) | collective-permute-done | bytes 262176 | tf_op jit(solution)/shard_map/ppermute | solution.py:75
  40.1 0.1 maximum_bitcast_fusion
  40.1 0.6 gather_fusion.2
  40.7 0.1 select_bitcast_fusion
  40.9 0.2 copy.11
  41.1 0.4 fusion.27
  41.5 2.9 %reduce-precision_convert_fusion.1 = (bf16[4,64,2048]{2,1,0:T(8,128)(2,1)S(1)}, bf16[4,64,2048]{2,1,0:T(8,128)(2,1)S(1)}) fusion(bf16[256,8,64]{0,2,1:T(8,128)(2,1)S(1)} %fusion.27, pred[8,256,2048]{2,1,0:T(32,128)(4,1)} %iota_compare_fusion), kind=kOutput, calls=%fused_computation.20 | convolution fusion | flops 270532608 | bytes 4456448 | tf_op jit(solution)/shard_map/khr,hkm->hrm/dot_general | solution.py:172
  44.4 7.0 %fusion.2 = f32[4,128,2048]{2,1,0:T(8,128)S(1)} fusion(bf16[1,2048,2048]{2,1,0:T(8,128)(2,1)} %param.6, bf16[4,64,2048]{2,1,0:T(8,128)(2,1)S(1)} %get-tuple-element.9, bf16[4,64,2048]{2,1,0:T(8,128)(2,1)S(1)} %get-tuple-element.8), kind=kOutput, calls=%fused_computation.6 | convolution fusion | flops 4299161600 | bytes 14680064 | tf_op jit(solution)/shard_map/hrm,mn->hrn/dot_general | solution.py:174
  51.4 0.5 multiply_reduce_fusion
  51.9 1.3 %collective-permute-start.10 = (f32[4,2048]{1,0:T(4,128)S(1)}, f32[4,2048]{1,0:T(4,128)S(1)}, u32[]{:S(2)}, u32[]{:S(2)}) collective-permute-start(f32[4,2048]{1,0:T(4,128)S(1)} %get-tuple-element.4), channel_id=1, source_target_pairs={{0,1},{1,0},{2,3},{3,2},{4,5},{5,4},{6,7},{7,6},{8,9},{9,8},{10,11... | collective-permute-start | bytes 98312 | tf_op jit(solution)/shard_map/ppermute | solution.py:19
  53.2 0.4 copy-done.6
  53.6 2.3 %multiply_reduce_fusion.1 = (f32[4,2048]{1,0:T(4,128)S(1)}, f32[4,64,2048]{2,1,0:T(8,128)}) fusion(bf16[256,8,64]{0,2,1:T(8,128)(2,1)S(1)} %fusion.27, bf16[4,256,2048]{2,1,0:T(8,128)(2,1)S(1)} %copy-done.6), kind=kOutput, calls=%fused_computation.31 | convolution fusion | flops 269475840 | bytes 6586368 | tf_op jit(solution)/shard_map/khr,hkn->hrn/dot_general | solution.py:170
  55.9 1.2 %collective-permute-start.7 = (f32[4,2048]{1,0:T(4,128)S(1)}, f32[4,2048]{1,0:T(4,128)S(1)}, u32[]{:S(2)}, u32[]{:S(2)}) collective-permute-start(f32[4,2048]{1,0:T(4,128)S(1)} %get-tuple-element.18), channel_id=1, source_target_pairs={{0,1},{1,0},{2,3},{3,2},{4,5},{5,4},{6,7},{7,6},{8,9},{9,8},{10,11... | collective-permute-start | bytes 98312 | tf_op jit(solution)/shard_map/ppermute | solution.py:19
  57.1 0.9 collective-permute-start.11
  58.0 2.1 %collective-permute-done.7 = f32[4,2048]{1,0:T(4,128)S(1)} collective-permute-done((f32[4,2048]{1,0:T(4,128)S(1)}, f32[4,2048]{1,0:T(4,128)S(1)}, u32[]{:S(2)}, u32[]{:S(2)}) %collective-permute-start.7) | collective-permute-done | bytes 32800 | tf_op jit(solution)/shard_map/ppermute | solution.py:19
  60.0 0.8 collective-permute-start.8
  60.8 1.8 %collective-permute-done.11 = f32[4,2048]{1,0:T(4,128)S(1)} collective-permute-done((f32[4,2048]{1,0:T(4,128)S(1)}, f32[4,2048]{1,0:T(4,128)S(1)}, u32[]{:S(2)}, u32[]{:S(2)}) %collective-permute-start.11) | collective-permute-done | bytes 32800 | tf_op jit(solution)/shard_map/ppermute | solution.py:19
  62.6 1.1 %collective-permute-start.12 = (f32[4,2048]{1,0:T(4,128)S(1)}, f32[4,2048]{1,0:T(4,128)S(1)}, u32[]{:S(2)}, u32[]{:S(2)}) collective-permute-start(f32[4,2048]{1,0:T(4,128)S(1)} %add.165), channel_id=1, source_target_pairs={{0,4},{1,5},{2,6},{3,7},{4,0},{5,1},{6,2},{7,3},{8,12},{9,13},{10,... | collective-permute-start | bytes 98312 | tf_op jit(solution)/shard_map/ppermute | solution.py:19
  63.7 1.8 %collective-permute-done.8 = f32[4,2048]{1,0:T(4,128)S(1)} collective-permute-done((f32[4,2048]{1,0:T(4,128)S(1)}, f32[4,2048]{1,0:T(4,128)S(1)}, u32[]{:S(2)}, u32[]{:S(2)}) %collective-permute-start.8) | collective-permute-done | bytes 32800 | tf_op jit(solution)/shard_map/ppermute | solution.py:19
  65.6 1.3 %collective-permute-start.9 = (f32[4,2048]{1,0:T(4,128)S(1)}, f32[4,2048]{1,0:T(4,128)S(1)}, u32[]{:S(2)}, u32[]{:S(2)}) collective-permute-start(f32[4,2048]{1,0:T(4,128)S(1)} %add.161), channel_id=1, source_target_pairs={{0,4},{1,5},{2,6},{3,7},{4,0},{5,1},{6,2},{7,3},{8,12},{9,13},{10,... | collective-permute-start | bytes 98312 | tf_op jit(solution)/shard_map/ppermute | solution.py:19
  66.9 2.9 %collective-permute-done.9 = f32[4,2048]{1,0:T(4,128)S(1)} collective-permute-done((f32[4,2048]{1,0:T(4,128)S(1)}, f32[4,2048]{1,0:T(4,128)S(1)}, u32[]{:S(2)}, u32[]{:S(2)}) %collective-permute-start.9) | collective-permute-done | bytes 32800 | tf_op jit(solution)/shard_map/ppermute | solution.py:19
  69.8 0.7 multiply_bitcast_fusion
  70.5 6.0 %reduce-precision_convert_fusion = (bf16[4,64,2048]{2,1,0:T(8,128)(2,1)S(1)}, bf16[4,64,2048]{2,1,0:T(8,128)(2,1)S(1)}) fusion(bf16[1,2048,2048]{2,1,0:T(8,128)(2,1)} %param.6, f32[4,64,2048]{2,1,0:T(8,128)S(1)} %get-tuple-element.5, f32[4,64,2048]{2,1,0:T(8,128)} %get-tuple-element.19, f32[8,2048]{1,0:T(8,128)S(1)} %get-tuple-element.2), kind=kOutput, calls=%fused_computation.18 | convolution fusion | flops 2152726528 | bytes 14745600 | tf_op jit(solution)/shard_map/hrn,mn->hrm/dot_general | solution.py:185
  76.5 1.4 %convolution_bitcast_fusion = f32[256,4,64]{0,2,1:T(8,128)S(1)} fusion(bf16[4,256,2048]{2,1,0:T(8,128)(2,1)S(1)} %copy-done.7, f32[4,64,2048]{2,1,0:T(8,128)S(1)} %get-tuple-element.5, f32[4,64,2048]{2,1,0:T(8,128)S(1)} %copy-done.8, f32[8,2048]{1,0:T(8,128)S(1)} %get-tuple-element.2), kind=kOutput, calls=%fused_computation.36 | convolution fusion | flops 271581184 | bytes 8716288 | tf_op jit(solution)/shard_map/hkn,hrn->khr/dot_general | solution.py:184
  77.9 0.8 copy-done
  78.7 2.4 %fusion.22 = f32[256,4,128]{0,2,1:T(8,128)S(1)} fusion(pred[8,256,2048]{2,1,0:T(32,128)(4,1)S(1)} %copy-done, bf16[4,64,2048]{2,1,0:T(8,128)(2,1)S(1)} %get-tuple-element.7, bf16[4,64,2048]{2,1,0:T(8,128)(2,1)S(1)} %get-tuple-element.6), kind=kOutput, calls=%fused_computation.33 | convolution fusion | flops 541065216 | bytes 4718592 | tf_op jit(solution)/shard_map/hkm,hrm->khr/dot_general | solution.py:187
  81.2 0.1 fusion.28
  81.3 0.4 fusion.33
  81.7 0.4 convolution_add_fusion
  82.2 0.1 collective-permute-start.13
  82.3 1.9 %collective-permute-done.13 = f32[2,2,2,2,16,512]{5,4,3,2,1,0:T(8,128)S(1)} collective-permute-done((f32[2,2,2,2,16,512]{5,4,3,2,1,0:T(8,128)S(1)}, f32[2,2,2,2,16,512]{5,4,3,2,1,0:T(8,128)S(1)}, u32[]{:S(2)}, u32[]{:S(2)}) %collective-permute-start.13) | collective-permute-done | bytes 524320 | tf_op jit(solution)/shard_map/ppermute | solution.py:75
  84.2 0.1 bitcast_add_fusion
  84.3 1.4 %collective-permute-start.16 = (f32[2,2,16,512]{3,2,1,0:T(8,128)S(1)}, f32[2,2,16,512]{3,2,1,0:T(8,128)S(1)}, u32[]{:S(2)}, u32[]{:S(2)}) collective-permute-start(f32[2,2,16,512]{3,2,1,0:T(8,128)S(1)} %get-tuple-element.11), channel_id=1, source_target_pairs={{0,48},{8,56},{16,32},{24,40},{32,16},{40,24},{48,0},{56,8},{64,11... | collective-permute-start | bytes 393224 | tf_op jit(solution)/shard_map/ppermute | solution.py:75
  85.7 0.9 collective-permute-start.15
  86.6 1.9 %collective-permute-start.14 = (f32[2,2,16,512]{3,2,1,0:T(8,128)S(1)}, f32[2,2,16,512]{3,2,1,0:T(8,128)S(1)}, u32[]{:S(2)}, u32[]{:S(2)}) collective-permute-start(f32[2,2,16,512]{3,2,1,0:T(8,128)S(1)} %get-tuple-element.10), channel_id=1, source_target_pairs={{0,16},{8,24},{16,0},{24,8},{32,48},{40,56},{48,32},{56,40},{64,80... | collective-permute-start | bytes 393224 | tf_op jit(solution)/shard_map/ppermute | solution.py:75
  88.5 5.5 %collective-permute-done.16 = f32[2,2,16,512]{3,2,1,0:T(8,128)S(1)} collective-permute-done((f32[2,2,16,512]{3,2,1,0:T(8,128)S(1)}, f32[2,2,16,512]{3,2,1,0:T(8,128)S(1)}, u32[]{:S(2)}, u32[]{:S(2)}) %collective-permute-start.16) | collective-permute-done | bytes 131104 | tf_op jit(solution)/shard_map/ppermute | solution.py:75
  94.0 0.6 collective-permute-done.14
  94.7 4.1 %collective-permute-start.19 = (f32[16,512]{1,0:T(8,128)S(1)}, f32[16,512]{1,0:T(8,128)S(1)}, u32[]{:S(2)}, u32[]{:S(2)}) collective-permute-start(f32[16,512]{1,0:T(8,128)S(1)} %get-tuple-element.16), channel_id=1, source_target_pairs={{0,192},{8,200},{16,208},{24,216},{32,224},{40,232},{48,240},{56,2... | collective-permute-start | bytes 98312 | tf_op jit(solution)/shard_map/ppermute | solution.py:75
  98.8 1.0 collective-permute-start.18
  99.8 1.5 %collective-permute-start.17 = (f32[16,512]{1,0:T(8,128)S(1)}, f32[16,512]{1,0:T(8,128)S(1)}, u32[]{:S(2)}, u32[]{:S(2)}) collective-permute-start(f32[16,512]{1,0:T(8,128)S(1)} %get-tuple-element.15), channel_id=1, source_target_pairs={{0,64},{8,72},{16,80},{24,88},{32,96},{40,104},{48,112},{56,120},{... | collective-permute-start | bytes 98312 | tf_op jit(solution)/shard_map/ppermute | solution.py:75
  101.3 5.4 %collective-permute-done.18 = f32[16,512]{1,0:T(8,128)S(1)} collective-permute-done((f32[16,512]{1,0:T(8,128)S(1)}, f32[16,512]{1,0:T(8,128)S(1)}, u32[]{:S(2)}, u32[]{:S(2)}) %collective-permute-start.18) | collective-permute-done | bytes 32800 | tf_op jit(solution)/shard_map/ppermute | solution.py:75
  106.6 0.1 mul.94
  106.7 0.6 sub.19
  (48 shorter events, 0.5 us)
Async XLA Ops:
  0.6 14.6 %copy-start.3 = (s32[1,8,256]{2,1,0:T(8,128)S(1)}, s32[1,8,256]{2,1,0:T(8,128)}, u32[]{:S(2)}) copy-start(s32[1,8,256]{2,1,0:T(8,128)} %param.9) | copy-start | bytes 24580
  1.6 26.5 %collective-permute-start.2 = (bf16[1,16,512]{2,1,0:T(8,128)(2,1)S(1)}, bf16[1,16,512]{2,1,0:T(8,128)(2,1)S(1)}, u32[]{:S(2)}, u32[]{:S(2)}) collective-permute-start(bf16[1,16,512]{2,1,0:T(8,128)(2,1)S(1)} %broadcast_in_dim_reshape.4), channel_id=1, source_target_pairs={{0,192},{8,200},{16,208},{24,216},{32,224},{40,232},{48,240},{56,2... | collective-permute-start | bytes 49160 | tf_op jit(solution)/shard_map/ppermute | solution.py:75
  8.0 20.1 %collective-permute-start.1 = (bf16[1,16,512]{2,1,0:T(8,128)(2,1)S(1)}, bf16[1,16,512]{2,1,0:T(8,128)(2,1)S(1)}, u32[]{:S(2)}, u32[]{:S(2)}) collective-permute-start(bf16[1,16,512]{2,1,0:T(8,128)(2,1)S(1)} %broadcast_in_dim_reshape.4), channel_id=1, source_target_pairs={{0,128},{8,136},{16,144},{24,152},{32,160},{40,168},{48,176},{56,1... | collective-permute-start | bytes 49160 | tf_op jit(solution)/shard_map/ppermute | solution.py:75
  9.0 19.1 %collective-permute-start = (bf16[1,16,512]{2,1,0:T(8,128)(2,1)S(1)}, bf16[1,16,512]{2,1,0:T(8,128)(2,1)S(1)}, u32[]{:S(2)}, u32[]{:S(2)}) collective-permute-start(bf16[1,16,512]{2,1,0:T(8,128)(2,1)S(1)} %broadcast_in_dim_reshape.4), channel_id=1, source_target_pairs={{0,64},{8,72},{16,80},{24,88},{32,96},{40,104},{48,112},{56,120},{... | collective-permute-start | bytes 49160 | tf_op jit(solution)/shard_map/ppermute | solution.py:75
  27.9 13.2 %copy-start.4 = (f32[1,8,256]{2,1,0:T(8,128)S(1)}, f32[1,8,256]{2,1,0:T(8,128)}, u32[]{:S(2)}) copy-start(f32[1,8,256]{2,1,0:T(8,128)} %param.8) | copy-start | bytes 24580
  27.9 13.2 %copy-start.5 = (s32[1,256]{1,0:T(1,128)S(1)}, s32[1,256]{1,0:T(1,128)}, u32[]{:S(2)}) copy-start(s32[1,256]{1,0:T(1,128)} %param.10) | copy-start | bytes 3076
  28.7 5.5 %collective-permute-start.5 = (bf16[4,1,16,512]{3,2,0,1:T(8,128)(2,1)S(1)}, bf16[4,1,16,512]{3,2,0,1:T(8,128)(2,1)S(1)}, u32[]{:S(2)}, u32[]{:S(2)}) collective-permute-start(bf16[4,1,16,512]{3,2,0,1:T(8,128)(2,1)S(1)} %bitcast_select_fusion.2), channel_id=1, source_target_pairs={{0,48},{8,56},{16,32},{24,40},{32,16},{40,24},{48,0},{56,8},{64,11... | collective-permute-start | bytes 196616 | tf_op jit(solution)/shard_map/ppermute | solution.py:75
  31.8 5.8 %collective-permute-start.4 = (bf16[4,1,16,512]{3,2,0,1:T(8,128)(2,1)S(1)}, bf16[4,1,16,512]{3,2,0,1:T(8,128)(2,1)S(1)}, u32[]{:S(2)}, u32[]{:S(2)}) collective-permute-start(bf16[4,1,16,512]{3,2,0,1:T(8,128)(2,1)S(1)} %bitcast_select_fusion.2), channel_id=1, source_target_pairs={{0,32},{8,40},{16,48},{24,56},{32,0},{40,8},{48,16},{56,24},{64,96... | collective-permute-start | bytes 196616 | tf_op jit(solution)/shard_map/ppermute | solution.py:75
  32.4 5.1 %collective-permute-start.3 = (bf16[4,1,16,512]{3,2,0,1:T(8,128)(2,1)S(1)}, bf16[4,1,16,512]{3,2,0,1:T(8,128)(2,1)S(1)}, u32[]{:S(2)}, u32[]{:S(2)}) collective-permute-start(bf16[4,1,16,512]{3,2,0,1:T(8,128)(2,1)S(1)} %bitcast_select_fusion.2), channel_id=1, source_target_pairs={{0,16},{8,24},{16,0},{24,8},{32,48},{40,56},{48,32},{56,40},{64,80... | collective-permute-start | bytes 196616 | tf_op jit(solution)/shard_map/ppermute | solution.py:75
  38.3 1.8 %collective-permute-start.6 = (bf16[4,4,1,16,512]{4,3,1,0,2:T(8,128)(2,1)S(1)}, bf16[4,4,1,16,512]{4,3,1,0,2:T(8,128)(2,1)S(1)}, u32[]{:S(2)}, u32[]{:S(2)}) collective-permute-start(bf16[4,4,1,16,512]{4,3,1,0,2:T(8,128)(2,1)S(1)} %bitcast_select_fusion), channel_id=1, source_target_pairs={{0,8},{8,0},{16,24},{24,16},{32,40},{40,32},{48,56},{56,48},{64,72... | collective-permute-start | bytes 786440 | tf_op jit(solution)/shard_map/ppermute | solution.py:75
  51.4 2.2 %copy-start.6 = (bf16[4,256,2048]{2,1,0:T(8,128)(2,1)S(1)}, bf16[4,256,2048]{2,1,0:T(8,128)(2,1)}, u32[]{:S(2)}) copy-start(bf16[4,256,2048]{2,1,0:T(8,128)(2,1)} %fusion.11) | copy-start | bytes 12582916
  51.9 17.9 %copy-start.2 = (f32[1,8,2048]{2,1,0:T(8,128)S(1)}, f32[1,8,2048]{2,1,0:T(8,128)}, u32[]{:S(2)}) copy-start(f32[1,8,2048]{2,1,0:T(8,128)} %param.7) | copy-start | bytes 196612
  51.9 5.2 %collective-permute-start.10 = (f32[4,2048]{1,0:T(4,128)S(1)}, f32[4,2048]{1,0:T(4,128)S(1)}, u32[]{:S(2)}, u32[]{:S(2)}) collective-permute-start(f32[4,2048]{1,0:T(4,128)S(1)} %get-tuple-element.4), channel_id=1, source_target_pairs={{0,1},{1,0},{2,3},{3,2},{4,5},{5,4},{6,7},{7,6},{8,9},{9,8},{10,11... | collective-permute-start | bytes 98312 | tf_op jit(solution)/shard_map/ppermute | solution.py:19
  55.9 4.2 %collective-permute-start.7 = (f32[4,2048]{1,0:T(4,128)S(1)}, f32[4,2048]{1,0:T(4,128)S(1)}, u32[]{:S(2)}, u32[]{:S(2)}) collective-permute-start(f32[4,2048]{1,0:T(4,128)S(1)} %get-tuple-element.18), channel_id=1, source_target_pairs={{0,1},{1,0},{2,3},{3,2},{4,5},{5,4},{6,7},{7,6},{8,9},{9,8},{10,11... | collective-permute-start | bytes 98312 | tf_op jit(solution)/shard_map/ppermute | solution.py:19
  57.1 5.5 %collective-permute-start.11 = (f32[4,2048]{1,0:T(4,128)S(1)}, f32[4,2048]{1,0:T(4,128)S(1)}, u32[]{:S(2)}, u32[]{:S(2)}) collective-permute-start(f32[4,2048]{1,0:T(4,128)S(1)} %add.164), channel_id=1, source_target_pairs={{0,2},{1,3},{2,0},{3,1},{4,6},{5,7},{6,4},{7,5},{8,10},{9,11},{10,... | collective-permute-start | bytes 98312 | tf_op jit(solution)/shard_map/ppermute | solution.py:19
  60.0 5.5 %collective-permute-start.8 = (f32[4,2048]{1,0:T(4,128)S(1)}, f32[4,2048]{1,0:T(4,128)S(1)}, u32[]{:S(2)}, u32[]{:S(2)}) collective-permute-start(f32[4,2048]{1,0:T(4,128)S(1)} %add.160), channel_id=1, source_target_pairs={{0,2},{1,3},{2,0},{3,1},{4,6},{5,7},{6,4},{7,5},{8,10},{9,11},{10,... | collective-permute-start | bytes 98312 | tf_op jit(solution)/shard_map/ppermute | solution.py:19
  62.6 4.3 %collective-permute-start.12 = (f32[4,2048]{1,0:T(4,128)S(1)}, f32[4,2048]{1,0:T(4,128)S(1)}, u32[]{:S(2)}, u32[]{:S(2)}) collective-permute-start(f32[4,2048]{1,0:T(4,128)S(1)} %add.165), channel_id=1, source_target_pairs={{0,4},{1,5},{2,6},{3,7},{4,0},{5,1},{6,2},{7,3},{8,12},{9,13},{10,... | collective-permute-start | bytes 98312 | tf_op jit(solution)/shard_map/ppermute | solution.py:19
  65.6 4.2 %collective-permute-start.9 = (f32[4,2048]{1,0:T(4,128)S(1)}, f32[4,2048]{1,0:T(4,128)S(1)}, u32[]{:S(2)}, u32[]{:S(2)}) collective-permute-start(f32[4,2048]{1,0:T(4,128)S(1)} %add.161), channel_id=1, source_target_pairs={{0,4},{1,5},{2,6},{3,7},{4,0},{5,1},{6,2},{7,3},{8,12},{9,13},{10,... | collective-permute-start | bytes 98312 | tf_op jit(solution)/shard_map/ppermute | solution.py:19
  70.5 6.0 %copy-start.7 = (bf16[4,256,2048]{2,1,0:T(8,128)(2,1)S(1)}, bf16[4,256,2048]{2,1,0:T(8,128)(2,1)}, u32[]{:S(2)}) copy-start(bf16[4,256,2048]{2,1,0:T(8,128)(2,1)} %fusion.11) | copy-start | bytes 12582916
  70.5 6.0 %copy-start.8 = (f32[4,64,2048]{2,1,0:T(8,128)S(1)}, f32[4,64,2048]{2,1,0:T(8,128)}, u32[]{:S(2)}) copy-start(f32[4,64,2048]{2,1,0:T(8,128)} %get-tuple-element.19) | copy-start | bytes 6291460
  76.5 2.2 %copy-start = (pred[8,256,2048]{2,1,0:T(32,128)(4,1)S(1)}, pred[8,256,2048]{2,1,0:T(32,128)(4,1)}, u32[]{:S(2)}) copy-start(pred[8,256,2048]{2,1,0:T(32,128)(4,1)} %iota_compare_fusion) | copy-start | bytes 12582916
  81.3 25.5 %copy-start.1 = (f32[16,8,64]{2,1,0:T(8,128)S(1)}, f32[16,8,64]{2,1,0:T(8,128)}, u32[]{:S(2)}) copy-start(f32[16,8,64]{2,1,0:T(8,128)} %param.11) | copy-start | bytes 98308
  82.2 2.0 %collective-permute-start.13 = (f32[2,2,2,2,16,512]{5,4,3,2,1,0:T(8,128)S(1)}, f32[2,2,2,2,16,512]{5,4,3,2,1,0:T(8,128)S(1)}, u32[]{:S(2)}, u32[]{:S(2)}) collective-permute-start(f32[2,2,2,2,16,512]{5,4,3,2,1,0:T(8,128)S(1)} %dynamic-slice_bitcast_fusion), channel_id=1, source_target_pairs={{0,8},{8,0},{16,24},{24,16},{32,40},{40,32},{48,56},{56,48},{64,72... | collective-permute-start | bytes 1572872 | tf_op jit(solution)/shard_map/ppermute | solution.py:75
  84.3 9.6 %collective-permute-start.16 = (f32[2,2,16,512]{3,2,1,0:T(8,128)S(1)}, f32[2,2,16,512]{3,2,1,0:T(8,128)S(1)}, u32[]{:S(2)}, u32[]{:S(2)}) collective-permute-start(f32[2,2,16,512]{3,2,1,0:T(8,128)S(1)} %get-tuple-element.11), channel_id=1, source_target_pairs={{0,48},{8,56},{16,32},{24,40},{32,16},{40,24},{48,0},{56,8},{64,11... | collective-permute-start | bytes 393224 | tf_op jit(solution)/shard_map/ppermute | solution.py:75
  85.7 8.3 %collective-permute-start.15 = (f32[2,2,16,512]{3,2,1,0:T(8,128)S(1)}, f32[2,2,16,512]{3,2,1,0:T(8,128)S(1)}, u32[]{:S(2)}, u32[]{:S(2)}) collective-permute-start(f32[2,2,16,512]{3,2,1,0:T(8,128)S(1)} %get-tuple-element.12), channel_id=1, source_target_pairs={{0,32},{8,40},{16,48},{24,56},{32,0},{40,8},{48,16},{56,24},{64,96... | collective-permute-start | bytes 393224 | tf_op jit(solution)/shard_map/ppermute | solution.py:75
  86.6 8.0 %collective-permute-start.14 = (f32[2,2,16,512]{3,2,1,0:T(8,128)S(1)}, f32[2,2,16,512]{3,2,1,0:T(8,128)S(1)}, u32[]{:S(2)}, u32[]{:S(2)}) collective-permute-start(f32[2,2,16,512]{3,2,1,0:T(8,128)S(1)} %get-tuple-element.10), channel_id=1, source_target_pairs={{0,16},{8,24},{16,0},{24,8},{32,48},{40,56},{48,32},{56,40},{64,80... | collective-permute-start | bytes 393224 | tf_op jit(solution)/shard_map/ppermute | solution.py:75
  94.7 6.6 %collective-permute-start.19 = (f32[16,512]{1,0:T(8,128)S(1)}, f32[16,512]{1,0:T(8,128)S(1)}, u32[]{:S(2)}, u32[]{:S(2)}) collective-permute-start(f32[16,512]{1,0:T(8,128)S(1)} %get-tuple-element.16), channel_id=1, source_target_pairs={{0,192},{8,200},{16,208},{24,216},{32,224},{40,232},{48,240},{56,2... | collective-permute-start | bytes 98312 | tf_op jit(solution)/shard_map/ppermute | solution.py:75
  98.8 7.8 %collective-permute-start.18 = (f32[16,512]{1,0:T(8,128)S(1)}, f32[16,512]{1,0:T(8,128)S(1)}, u32[]{:S(2)}, u32[]{:S(2)}) collective-permute-start(f32[16,512]{1,0:T(8,128)S(1)} %get-tuple-element.17), channel_id=1, source_target_pairs={{0,128},{8,136},{16,144},{24,152},{32,160},{40,168},{48,176},{56,1... | collective-permute-start | bytes 98312 | tf_op jit(solution)/shard_map/ppermute | solution.py:75
  99.8 6.8 %collective-permute-start.17 = (f32[16,512]{1,0:T(8,128)S(1)}, f32[16,512]{1,0:T(8,128)S(1)}, u32[]{:S(2)}, u32[]{:S(2)}) collective-permute-start(f32[16,512]{1,0:T(8,128)S(1)} %get-tuple-element.15), channel_id=1, source_target_pairs={{0,64},{8,72},{16,80},{24,88},{32,96},{40,104},{48,112},{56,120},{... | collective-permute-start | bytes 98312 | tf_op jit(solution)/shard_map/ppermute | solution.py:75

commit v10 on v7

--- a/solution.py
+++ b/solution.py
@@ -183,7 +183,8 @@
     violation = jnp.maximum(-margin, 0.0)
     var_grad = quantile * violation / deviation
     volt_grad = (2.0 * var_grad[0][:, None, :] * factor_volts).astype(jnp.bfloat16)
-    picked = jnp.einsum("hkn,hrn->khr", sens_rows, volt_grad, preferred_element_type=jnp.float32)
+    picked = jnp.einsum("hkn,hrn->hkr", sens_rows, volt_grad, preferred_element_type=jnp.float32)
+    picked = jnp.transpose(picked, (1, 0, 2))
     member_grads = (power[:, :, None] * picked).reshape(ev_count, hours * columns)
     grads_hi, grads_lo = _split_bf16(member_grads)
     summed = jnp.einsum("kg,kc->gc", matches, grads_hi, preferred_element_type=jnp.float32)

time: 101 us -> 101 us (level)
  no operation moved by 1% of the time
where the time goes in v10:
time: 101 us
  matrix products  36.1 us (36%)
  starting transfers between devices  29.7 us (29%)
  waiting for transfers between devices  28.7 us (28%)
  other arithmetic  3.05 us (3%)
  local copies, waits for them, and re-layouts  2.36 us (2%)
    ppermute x14, starting transfers between devices, _send_all(): out[j] = lax.ppermute(x_for(j), axis, [(i, i ^ m) for i in range(size)])  24.1 us
    dot_general x2, matrix products, shards(): jnp.einsum('hkm,mn->hkn', node_hot[at], sens, preferred_element_type=jnp....  23.3 us
    ppermute x14, waiting for transfers between devices, _send_all(): out[j] = lax.ppermute(x_for(j), axis, [(i, i ^ m) for i in range(size)])  19.3 us
    ppermute x6, waiting for transfers between devices, _exchange(): return lax.ppermute(x, axis, perm)  9.34 us
    dot_general x1, matrix products, shards(): jnp.einsum('hkn,hrn->hkr', sens_rows, volt_grad, preferred_element_type=j...  6.06 us
    ppermute x6, starting transfers between devices, _exchange(): return lax.ppermute(x, axis, perm)  5.56 us
    dot_general x2, matrix products, shards(): jnp.einsum('khr,hkn->hrn', weighted[:, at], rows, preferred_element_type=...  5.48 us
  transfers between devices with their start and end apart: 20, of which 11 were waited for; matrix products, arithmetic and copies ran while one was open for 26% of the time, Pallas kernels for 0%

profile of v10, /device:TPU:4, one launch (start us, length us, event | category | flops | bytes accessed | tf_op | source)
XLA Modules:
  0.0 100.8 jit_solution(12436768356669393252)
XLA Ops:
  0.6 0.8 convert_element_type.23
  1.5 0.1 broadcast_in_dim_reshape.4
  1.6 6.4 %collective-permute-start.2 = (bf16[1,16,512]{2,1,0:T(8,128)(2,1)S(1)}, bf16[1,16,512]{2,1,0:T(8,128)(2,1)S(1)}, u32[]{:S(2)}, u32[]{:S(2)}) collective-permute-start(bf16[1,16,512]{2,1,0:T(8,128)(2,1)S(1)} %broadcast_in_dim_reshape.4), channel_id=1, source_target_pairs={{0,192},{8,200},{16,208},{24,216},{32,224},{40,232},{48,240},{56,2... | collective-permute-start | bytes 49160 | tf_op jit(solution)/shard_map/ppermute | solution.py:75
  8.0 1.0 collective-permute-start.1
  9.0 1.5 %collective-permute-start = (bf16[1,16,512]{2,1,0:T(8,128)(2,1)S(1)}, bf16[1,16,512]{2,1,0:T(8,128)(2,1)S(1)}, u32[]{:S(2)}, u32[]{:S(2)}) collective-permute-start(bf16[1,16,512]{2,1,0:T(8,128)(2,1)S(1)} %broadcast_in_dim_reshape.4), channel_id=1, source_target_pairs={{0,64},{8,72},{16,80},{24,88},{32,96},{40,104},{48,112},{56,120},{... | collective-permute-start | bytes 49160 | tf_op jit(solution)/shard_map/ppermute | solution.py:75
  10.4 12.8 %fusion.14 = bf16[4,256,2048]{2,1,0:T(8,128)(2,1)} fusion(bf16[1,2048,2048]{2,1,0:T(8,128)(2,1)} %param.6, s32[8,256]{1,0:T(8,128)} %bitcast.128), kind=kOutput, calls=%fused_computation.17 | convolution fusion | flops 8596226048 | bytes 12591104 | tf_op jit(solution)/shard_map/hkm,mn->hkn/dot_general | solution.py:172
  23.2 10.5 %fusion.11 = bf16[4,256,2048]{2,1,0:T(8,128)(2,1)} fusion(bf16[1,2048,2048]{2,1,0:T(8,128)(2,1)S(1)} %copy-done.3, s32[8,256]{1,0:T(8,128)S(1)} %bitcast.129), kind=kOutput, calls=%fused_computation.16 | convolution fusion | flops 8596226048 | bytes 12591104 | tf_op jit(solution)/shard_map/hkm,mn->hkn/dot_general | solution.py:172
  33.8 0.1 stack_broadcast_in_dim_reshape.3
  33.9 0.0 collective-permute-done.1
  33.9 0.0 collective-permute-done
  34.0 0.6 gather_fusion
  34.5 0.1 bitcast_select_fusion.2
  34.6 3.0 %collective-permute-start.5 = (bf16[4,1,16,512]{3,2,0,1:T(8,128)(2,1)S(1)}, bf16[4,1,16,512]{3,2,0,1:T(8,128)(2,1)S(1)}, u32[]{:S(2)}, u32[]{:S(2)}) collective-permute-start(bf16[4,1,16,512]{3,2,0,1:T(8,128)(2,1)S(1)} %bitcast_select_fusion.2), channel_id=1, source_target_pairs={{0,48},{8,56},{16,32},{24,40},{32,16},{40,24},{48,0},{56,8},{64,11... | collective-permute-start | bytes 196616 | tf_op jit(solution)/shard_map/ppermute | solution.py:75
  37.6 0.6 collective-permute-start.4
  38.3 0.5 collective-permute-start.3
  38.7 0.1 bitcast_select_fusion.3
  38.8 1.3 %collective-permute-done.5 = bf16[4,1,16,512]{3,2,0,1:T(8,128)(2,1)S(1)} collective-permute-done((bf16[4,1,16,512]{3,2,0,1:T(8,128)(2,1)S(1)}, bf16[4,1,16,512]{3,2,0,1:T(8,128)(2,1)S(1)}, u32[]{:S(2)}, u32[]{:S(2)}) %collective-permute-start.5) | collective-permute-done | bytes 65568 | tf_op jit(solution)/shard_map/ppermute | solution.py:75
  40.1 3.3 %collective-permute-done.4 = bf16[4,1,16,512]{3,2,0,1:T(8,128)(2,1)S(1)} collective-permute-done((bf16[4,1,16,512]{3,2,0,1:T(8,128)(2,1)S(1)}, bf16[4,1,16,512]{3,2,0,1:T(8,128)(2,1)S(1)}, u32[]{:S(2)}, u32[]{:S(2)}) %collective-permute-start.4) | collective-permute-done | bytes 65568 | tf_op jit(solution)/shard_map/ppermute | solution.py:75
  43.4 0.6 gather_fusion.1
  44.0 0.1 bitcast_select_fusion
  44.1 0.3 collective-permute-start.6
  44.4 0.1 fusion.37
  44.5 1.4 %collective-permute-done.6 = bf16[4,4,1,16,512]{4,3,1,0,2:T(8,128)(2,1)S(1)} collective-permute-done((bf16[4,4,1,16,512]{4,3,1,0,2:T(8,128)(2,1)S(1)}, bf16[4,4,1,16,512]{4,3,1,0,2:T(8,128)(2,1)S(1)}, u32[]{:S(2)}, u32[]{:S(2)}) %collective-permute-start.6) | collective-permute-done | bytes 262176 | tf_op jit(solution)/shard_map/ppermute | solution.py:75
  45.9 0.1 maximum_bitcast_fusion
  46.0 0.6 gather_fusion.2
  46.6 0.1 select_bitcast_fusion
  46.7 0.2 copy.11
  47.0 0.4 fusion.29
  47.4 3.2 %multiply_reduce_fusion = (f32[4,2048]{1,0:T(4,128)S(1)}, f32[4,64,2048]{2,1,0:T(8,128)S(1)}) fusion(bf16[256,8,64]{0,2,1:T(8,128)(2,1)S(1)} %fusion.29, bf16[4,256,2048]{2,1,0:T(8,128)(2,1)} %fusion.14), kind=kOutput, calls=%fused_computation.19 | convolution fusion | flops 269475840 | bytes 6586368 | tf_op jit(solution)/shard_map/khr,hkn->hrn/dot_general | solution.py:174
  50.6 0.0 copy-start.1
  50.6 1.3 %collective-permute-start.10 = (f32[4,2048]{1,0:T(4,128)S(1)}, f32[4,2048]{1,0:T(4,128)S(1)}, u32[]{:S(2)}, u32[]{:S(2)}) collective-permute-start(f32[4,2048]{1,0:T(4,128)S(1)} %get-tuple-element.12), channel_id=1, source_target_pairs={{0,1},{1,0},{2,3},{3,2},{4,5},{5,4},{6,7},{7,6},{8,9},{9,8},{10,11... | collective-permute-start | bytes 98312 | tf_op jit(solution)/shard_map/ppermute | solution.py:19
  51.9 2.3 %multiply_reduce_fusion.1 = (f32[4,2048]{1,0:T(4,128)S(1)}, f32[4,64,2048]{2,1,0:T(8,128)}) fusion(bf16[256,8,64]{0,2,1:T(8,128)(2,1)S(1)} %fusion.29, bf16[4,256,2048]{2,1,0:T(8,128)(2,1)S(1)} %copy-done.6), kind=kOutput, calls=%fused_computation.20 | convolution fusion | flops 269475840 | bytes 6586368 | tf_op jit(solution)/shard_map/khr,hkn->hrn/dot_general | solution.py:174
  54.2 0.8 collective-permute-start.7
  55.0 0.6 collective-permute-start.11
  55.6 2.7 %collective-permute-done.7 = f32[4,2048]{1,0:T(4,128)S(1)} collective-permute-done((f32[4,2048]{1,0:T(4,128)S(1)}, f32[4,2048]{1,0:T(4,128)S(1)}, u32[]{:S(2)}, u32[]{:S(2)}) %collective-permute-start.7) | collective-permute-done | bytes 32800 | tf_op jit(solution)/shard_map/ppermute | solution.py:19
  58.3 0.6 collective-permute-start.8
  59.0 1.5 %collective-permute-done.11 = f32[4,2048]{1,0:T(4,128)S(1)} collective-permute-done((f32[4,2048]{1,0:T(4,128)S(1)}, f32[4,2048]{1,0:T(4,128)S(1)}, u32[]{:S(2)}, u32[]{:S(2)}) %collective-permute-start.11) | collective-permute-done | bytes 32800 | tf_op jit(solution)/shard_map/ppermute | solution.py:19
  60.5 1.1 %collective-permute-start.12 = (f32[4,2048]{1,0:T(4,128)S(1)}, f32[4,2048]{1,0:T(4,128)S(1)}, u32[]{:S(2)}, u32[]{:S(2)}) collective-permute-start(f32[4,2048]{1,0:T(4,128)S(1)} %add.158), channel_id=1, source_target_pairs={{0,4},{1,5},{2,6},{3,7},{4,0},{5,1},{6,2},{7,3},{8,12},{9,13},{10,... | collective-permute-start | bytes 98312 | tf_op jit(solution)/shard_map/ppermute | solution.py:19
  61.7 2.2 %collective-permute-done.8 = f32[4,2048]{1,0:T(4,128)S(1)} collective-permute-done((f32[4,2048]{1,0:T(4,128)S(1)}, f32[4,2048]{1,0:T(4,128)S(1)}, u32[]{:S(2)}, u32[]{:S(2)}) %collective-permute-start.8) | collective-permute-done | bytes 32800 | tf_op jit(solution)/shard_map/ppermute | solution.py:19
  63.9 1.1 %collective-permute-start.9 = (f32[4,2048]{1,0:T(4,128)S(1)}, f32[4,2048]{1,0:T(4,128)S(1)}, u32[]{:S(2)}, u32[]{:S(2)}) collective-permute-start(f32[4,2048]{1,0:T(4,128)S(1)} %add.155), channel_id=1, source_target_pairs={{0,4},{1,5},{2,6},{3,7},{4,0},{5,1},{6,2},{7,3},{8,12},{9,13},{10,... | collective-permute-start | bytes 98312 | tf_op jit(solution)/shard_map/ppermute | solution.py:19
  65.0 0.0 collective-permute-done.12
  65.0 2.9 %collective-permute-done.9 = f32[4,2048]{1,0:T(4,128)S(1)} collective-permute-done((f32[4,2048]{1,0:T(4,128)S(1)}, f32[4,2048]{1,0:T(4,128)S(1)}, u32[]{:S(2)}, u32[]{:S(2)}) %collective-permute-start.9) | collective-permute-done | bytes 32800 | tf_op jit(solution)/shard_map/ppermute | solution.py:19
  67.9 0.7 multiply_bitcast_fusion
  68.6 6.1 %fusion.24 = f32[256,8,64]{0,2,1:T(8,128)S(1)} fusion(f32[4,64,2048]{2,1,0:T(8,128)S(1)} %get-tuple-element.13, f32[4,64,2048]{2,1,0:T(8,128)} %get-tuple-element.15, f32[8,2048]{1,0:T(8,128)S(1)} %get-tuple-element.2, bf16[4,256,2048]{2,1,0:T(8,128)(2,1)} %fusion.14, bf16[4,256,2048]{2,1,0:T(8,128)(2,1)} %fusion.11, f32[256,8]{0,1:T(8,128)S(1)} %bitcast.131), kind=kOutput, calls=%fused_computation.24 | convolution fusion | flops 544342016 | bytes 13180928 | tf_op jit(solution)/shard_map/hkn,hrn->hkr/dot_general | solution.py:186
  74.6 0.1 fusion.30
  74.7 0.0 copy-start
  74.7 0.4 fusion.35
  75.2 0.4 convolution_add_fusion
  75.7 0.1 collective-permute-start.13
  75.8 1.9 %collective-permute-done.13 = f32[2,2,2,2,16,512]{5,4,3,2,1,0:T(8,128)S(1)} collective-permute-done((f32[2,2,2,2,16,512]{5,4,3,2,1,0:T(8,128)S(1)}, f32[2,2,2,2,16,512]{5,4,3,2,1,0:T(8,128)S(1)}, u32[]{:S(2)}, u32[]{:S(2)}) %collective-permute-start.13) | collective-permute-done | bytes 524320 | tf_op jit(solution)/shard_map/ppermute | solution.py:75
  77.7 0.1 bitcast_add_fusion
  77.8 1.4 %collective-permute-start.16 = (f32[2,2,16,512]{3,2,1,0:T(8,128)S(1)}, f32[2,2,16,512]{3,2,1,0:T(8,128)S(1)}, u32[]{:S(2)}, u32[]{:S(2)}) collective-permute-start(f32[2,2,16,512]{3,2,1,0:T(8,128)S(1)} %get-tuple-element.5), channel_id=1, source_target_pairs={{0,48},{8,56},{16,32},{24,40},{32,16},{40,24},{48,0},{56,8},{64,11... | collective-permute-start | bytes 393224 | tf_op jit(solution)/shard_map/ppermute | solution.py:75
  79.2 0.9 collective-permute-start.15
  80.1 1.9 %collective-permute-start.14 = (f32[2,2,16,512]{3,2,1,0:T(8,128)S(1)}, f32[2,2,16,512]{3,2,1,0:T(8,128)S(1)}, u32[]{:S(2)}, u32[]{:S(2)}) collective-permute-start(f32[2,2,16,512]{3,2,1,0:T(8,128)S(1)} %get-tuple-element.4), channel_id=1, source_target_pairs={{0,16},{8,24},{16,0},{24,8},{32,48},{40,56},{48,32},{56,40},{64,80... | collective-permute-start | bytes 393224 | tf_op jit(solution)/shard_map/ppermute | solution.py:75
  82.0 5.5 %collective-permute-done.16 = f32[2,2,16,512]{3,2,1,0:T(8,128)S(1)} collective-permute-done((f32[2,2,16,512]{3,2,1,0:T(8,128)S(1)}, f32[2,2,16,512]{3,2,1,0:T(8,128)S(1)}, u32[]{:S(2)}, u32[]{:S(2)}) %collective-permute-start.16) | collective-permute-done | bytes 131104 | tf_op jit(solution)/shard_map/ppermute | solution.py:75
  87.4 0.0 collective-permute-done.15
  87.4 0.6 collective-permute-done.14
  88.1 4.1 %collective-permute-start.19 = (f32[16,512]{1,0:T(8,128)S(1)}, f32[16,512]{1,0:T(8,128)S(1)}, u32[]{:S(2)}, u32[]{:S(2)}) collective-permute-start(f32[16,512]{1,0:T(8,128)S(1)} %get-tuple-element.10), channel_id=1, source_target_pairs={{0,192},{8,200},{16,208},{24,216},{32,224},{40,232},{48,240},{56,2... | collective-permute-start | bytes 98312 | tf_op jit(solution)/shard_map/ppermute | solution.py:75
  92.3 1.0 collective-permute-start.18
  93.2 1.5 %collective-permute-start.17 = (f32[16,512]{1,0:T(8,128)S(1)}, f32[16,512]{1,0:T(8,128)S(1)}, u32[]{:S(2)}, u32[]{:S(2)}) collective-permute-start(f32[16,512]{1,0:T(8,128)S(1)} %get-tuple-element.9), channel_id=1, source_target_pairs={{0,64},{8,72},{16,80},{24,88},{32,96},{40,104},{48,112},{56,120},{... | collective-permute-start | bytes 98312 | tf_op jit(solution)/shard_map/ppermute | solution.py:75
  94.7 0.0 collective-permute-done.19
  94.7 5.3 %collective-permute-done.18 = f32[16,512]{1,0:T(8,128)S(1)} collective-permute-done((f32[16,512]{1,0:T(8,128)S(1)}, f32[16,512]{1,0:T(8,128)S(1)}, u32[]{:S(2)}, u32[]{:S(2)}) %collective-permute-start.18) | collective-permute-done | bytes 32800 | tf_op jit(solution)/shard_map/ppermute | solution.py:75
  100.1 0.1 mul.89
  100.2 0.6 sub.11
  (38 shorter events, 0.4 us)
Async XLA Ops:
  1.6 32.3 %collective-permute-start.2 = (bf16[1,16,512]{2,1,0:T(8,128)(2,1)S(1)}, bf16[1,16,512]{2,1,0:T(8,128)(2,1)S(1)}, u32[]{:S(2)}, u32[]{:S(2)}) collective-permute-start(bf16[1,16,512]{2,1,0:T(8,128)(2,1)S(1)} %broadcast_in_dim_reshape.4), channel_id=1, source_target_pairs={{0,192},{8,200},{16,208},{24,216},{32,224},{40,232},{48,240},{56,2... | collective-permute-start | bytes 49160 | tf_op jit(solution)/shard_map/ppermute | solution.py:75
  8.0 26.0 %collective-permute-start.1 = (bf16[1,16,512]{2,1,0:T(8,128)(2,1)S(1)}, bf16[1,16,512]{2,1,0:T(8,128)(2,1)S(1)}, u32[]{:S(2)}, u32[]{:S(2)}) collective-permute-start(bf16[1,16,512]{2,1,0:T(8,128)(2,1)S(1)} %broadcast_in_dim_reshape.4), channel_id=1, source_target_pairs={{0,128},{8,136},{16,144},{24,152},{32,160},{40,168},{48,176},{56,1... | collective-permute-start | bytes 49160 | tf_op jit(solution)/shard_map/ppermute | solution.py:75
  9.0 25.0 %collective-permute-start = (bf16[1,16,512]{2,1,0:T(8,128)(2,1)S(1)}, bf16[1,16,512]{2,1,0:T(8,128)(2,1)S(1)}, u32[]{:S(2)}, u32[]{:S(2)}) collective-permute-start(bf16[1,16,512]{2,1,0:T(8,128)(2,1)S(1)} %broadcast_in_dim_reshape.4), channel_id=1, source_target_pairs={{0,64},{8,72},{16,80},{24,88},{32,96},{40,104},{48,112},{56,120},{... | collective-permute-start | bytes 49160 | tf_op jit(solution)/shard_map/ppermute | solution.py:75
  10.4 12.8 %copy-start.3 = (bf16[1,2048,2048]{2,1,0:T(8,128)(2,1)S(1)}, bf16[1,2048,2048]{2,1,0:T(8,128)(2,1)}, u32[]{:S(2)}) copy-start(bf16[1,2048,2048]{2,1,0:T(8,128)(2,1)} %param.6) | copy-start | bytes 25165828
  10.4 12.8 %copy-start.4 = (s32[1,8,256]{2,1,0:T(8,128)S(1)}, s32[1,8,256]{2,1,0:T(8,128)}, u32[]{:S(2)}) copy-start(s32[1,8,256]{2,1,0:T(8,128)} %param.9) | copy-start | bytes 24580
  33.7 13.2 %copy-start.2 = (s32[1,256]{1,0:T(1,128)S(1)}, s32[1,256]{1,0:T(1,128)}, u32[]{:S(2)}) copy-start(s32[1,256]{1,0:T(1,128)} %param.10) | copy-start | bytes 3076
  33.7 13.3 %copy-start.5 = (f32[1,8,256]{2,1,0:T(8,128)S(1)}, f32[1,8,256]{2,1,0:T(8,128)}, u32[]{:S(2)}) copy-start(f32[1,8,256]{2,1,0:T(8,128)} %param.8) | copy-start | bytes 24580
  34.6 5.5 %collective-permute-start.5 = (bf16[4,1,16,512]{3,2,0,1:T(8,128)(2,1)S(1)}, bf16[4,1,16,512]{3,2,0,1:T(8,128)(2,1)S(1)}, u32[]{:S(2)}, u32[]{:S(2)}) collective-permute-start(bf16[4,1,16,512]{3,2,0,1:T(8,128)(2,1)S(1)} %bitcast_select_fusion.2), channel_id=1, source_target_pairs={{0,48},{8,56},{16,32},{24,40},{32,16},{40,24},{48,0},{56,8},{64,11... | collective-permute-start | bytes 196616 | tf_op jit(solution)/shard_map/ppermute | solution.py:75
  37.6 5.8 %collective-permute-start.4 = (bf16[4,1,16,512]{3,2,0,1:T(8,128)(2,1)S(1)}, bf16[4,1,16,512]{3,2,0,1:T(8,128)(2,1)S(1)}, u32[]{:S(2)}, u32[]{:S(2)}) collective-permute-start(bf16[4,1,16,512]{3,2,0,1:T(8,128)(2,1)S(1)} %bitcast_select_fusion.2), channel_id=1, source_target_pairs={{0,32},{8,40},{16,48},{24,56},{32,0},{40,8},{48,16},{56,24},{64,96... | collective-permute-start | bytes 196616 | tf_op jit(solution)/shard_map/ppermute | solution.py:75
  38.3 5.1 %collective-permute-start.3 = (bf16[4,1,16,512]{3,2,0,1:T(8,128)(2,1)S(1)}, bf16[4,1,16,512]{3,2,0,1:T(8,128)(2,1)S(1)}, u32[]{:S(2)}, u32[]{:S(2)}) collective-permute-start(bf16[4,1,16,512]{3,2,0,1:T(8,128)(2,1)S(1)} %bitcast_select_fusion.2), channel_id=1, source_target_pairs={{0,16},{8,24},{16,0},{24,8},{32,48},{40,56},{48,32},{56,40},{64,80... | collective-permute-start | bytes 196616 | tf_op jit(solution)/shard_map/ppermute | solution.py:75
  44.1 1.8 %collective-permute-start.6 = (bf16[4,4,1,16,512]{4,3,1,0,2:T(8,128)(2,1)S(1)}, bf16[4,4,1,16,512]{4,3,1,0,2:T(8,128)(2,1)S(1)}, u32[]{:S(2)}, u32[]{:S(2)}) collective-permute-start(bf16[4,4,1,16,512]{4,3,1,0,2:T(8,128)(2,1)S(1)} %bitcast_select_fusion), channel_id=1, source_target_pairs={{0,8},{8,0},{16,24},{24,16},{32,40},{40,32},{48,56},{56,48},{64,72... | collective-permute-start | bytes 786440 | tf_op jit(solution)/shard_map/ppermute | solution.py:75
  47.4 4.5 %copy-start.6 = (bf16[4,256,2048]{2,1,0:T(8,128)(2,1)S(1)}, bf16[4,256,2048]{2,1,0:T(8,128)(2,1)}, u32[]{:S(2)}) copy-start(bf16[4,256,2048]{2,1,0:T(8,128)(2,1)} %fusion.11) | copy-start | bytes 12582916
  50.6 17.3 %copy-start.1 = (f32[1,8,2048]{2,1,0:T(8,128)S(1)}, f32[1,8,2048]{2,1,0:T(8,128)}, u32[]{:S(2)}) copy-start(f32[1,8,2048]{2,1,0:T(8,128)} %param.7) | copy-start | bytes 196612
  50.6 4.4 %collective-permute-start.10 = (f32[4,2048]{1,0:T(4,128)S(1)}, f32[4,2048]{1,0:T(4,128)S(1)}, u32[]{:S(2)}, u32[]{:S(2)}) collective-permute-start(f32[4,2048]{1,0:T(4,128)S(1)} %get-tuple-element.12), channel_id=1, source_target_pairs={{0,1},{1,0},{2,3},{3,2},{4,5},{5,4},{6,7},{7,6},{8,9},{9,8},{10,11... | collective-permute-start | bytes 98312 | tf_op jit(solution)/shard_map/ppermute | solution.py:19
  54.2 4.2 %collective-permute-start.7 = (f32[4,2048]{1,0:T(4,128)S(1)}, f32[4,2048]{1,0:T(4,128)S(1)}, u32[]{:S(2)}, u32[]{:S(2)}) collective-permute-start(f32[4,2048]{1,0:T(4,128)S(1)} %get-tuple-element.14), channel_id=1, source_target_pairs={{0,1},{1,0},{2,3},{3,2},{4,5},{5,4},{6,7},{7,6},{8,9},{9,8},{10,11... | collective-permute-start | bytes 98312 | tf_op jit(solution)/shard_map/ppermute | solution.py:19
  55.0 5.5 %collective-permute-start.11 = (f32[4,2048]{1,0:T(4,128)S(1)}, f32[4,2048]{1,0:T(4,128)S(1)}, u32[]{:S(2)}, u32[]{:S(2)}) collective-permute-start(f32[4,2048]{1,0:T(4,128)S(1)} %add.157), channel_id=1, source_target_pairs={{0,2},{1,3},{2,0},{3,1},{4,6},{5,7},{6,4},{7,5},{8,10},{9,11},{10,... | collective-permute-start | bytes 98312 | tf_op jit(solution)/shard_map/ppermute | solution.py:19
  58.3 5.5 %collective-permute-start.8 = (f32[4,2048]{1,0:T(4,128)S(1)}, f32[4,2048]{1,0:T(4,128)S(1)}, u32[]{:S(2)}, u32[]{:S(2)}) collective-permute-start(f32[4,2048]{1,0:T(4,128)S(1)} %add.154), channel_id=1, source_target_pairs={{0,2},{1,3},{2,0},{3,1},{4,6},{5,7},{6,4},{7,5},{8,10},{9,11},{10,... | collective-permute-start | bytes 98312 | tf_op jit(solution)/shard_map/ppermute | solution.py:19
  60.5 4.4 %collective-permute-start.12 = (f32[4,2048]{1,0:T(4,128)S(1)}, f32[4,2048]{1,0:T(4,128)S(1)}, u32[]{:S(2)}, u32[]{:S(2)}) collective-permute-start(f32[4,2048]{1,0:T(4,128)S(1)} %add.158), channel_id=1, source_target_pairs={{0,4},{1,5},{2,6},{3,7},{4,0},{5,1},{6,2},{7,3},{8,12},{9,13},{10,... | collective-permute-start | bytes 98312 | tf_op jit(solution)/shard_map/ppermute | solution.py:19
  63.9 4.0 %collective-permute-start.9 = (f32[4,2048]{1,0:T(4,128)S(1)}, f32[4,2048]{1,0:T(4,128)S(1)}, u32[]{:S(2)}, u32[]{:S(2)}) collective-permute-start(f32[4,2048]{1,0:T(4,128)S(1)} %add.155), channel_id=1, source_target_pairs={{0,4},{1,5},{2,6},{3,7},{4,0},{5,1},{6,2},{7,3},{8,12},{9,13},{10,... | collective-permute-start | bytes 98312 | tf_op jit(solution)/shard_map/ppermute | solution.py:19
  74.7 25.5 %copy-start = (f32[16,8,64]{2,1,0:T(8,128)S(1)}, f32[16,8,64]{2,1,0:T(8,128)}, u32[]{:S(2)}) copy-start(f32[16,8,64]{2,1,0:T(8,128)} %param.11) | copy-start | bytes 98308
  75.7 2.0 %collective-permute-start.13 = (f32[2,2,2,2,16,512]{5,4,3,2,1,0:T(8,128)S(1)}, f32[2,2,2,2,16,512]{5,4,3,2,1,0:T(8,128)S(1)}, u32[]{:S(2)}, u32[]{:S(2)}) collective-permute-start(f32[2,2,2,2,16,512]{5,4,3,2,1,0:T(8,128)S(1)} %dynamic-slice_bitcast_fusion), channel_id=1, source_target_pairs={{0,8},{8,0},{16,24},{24,16},{32,40},{40,32},{48,56},{56,48},{64,72... | collective-permute-start | bytes 1572872 | tf_op jit(solution)/shard_map/ppermute | solution.py:75
  77.8 9.6 %collective-permute-start.16 = (f32[2,2,16,512]{3,2,1,0:T(8,128)S(1)}, f32[2,2,16,512]{3,2,1,0:T(8,128)S(1)}, u32[]{:S(2)}, u32[]{:S(2)}) collective-permute-start(f32[2,2,16,512]{3,2,1,0:T(8,128)S(1)} %get-tuple-element.5), channel_id=1, source_target_pairs={{0,48},{8,56},{16,32},{24,40},{32,16},{40,24},{48,0},{56,8},{64,11... | collective-permute-start | bytes 393224 | tf_op jit(solution)/shard_map/ppermute | solution.py:75
  79.2 8.3 %collective-permute-start.15 = (f32[2,2,16,512]{3,2,1,0:T(8,128)S(1)}, f32[2,2,16,512]{3,2,1,0:T(8,128)S(1)}, u32[]{:S(2)}, u32[]{:S(2)}) collective-permute-start(f32[2,2,16,512]{3,2,1,0:T(8,128)S(1)} %get-tuple-element.6), channel_id=1, source_target_pairs={{0,32},{8,40},{16,48},{24,56},{32,0},{40,8},{48,16},{56,24},{64,96... | collective-permute-start | bytes 393224 | tf_op jit(solution)/shard_map/ppermute | solution.py:75
  80.1 8.0 %collective-permute-start.14 = (f32[2,2,16,512]{3,2,1,0:T(8,128)S(1)}, f32[2,2,16,512]{3,2,1,0:T(8,128)S(1)}, u32[]{:S(2)}, u32[]{:S(2)}) collective-permute-start(f32[2,2,16,512]{3,2,1,0:T(8,128)S(1)} %get-tuple-element.4), channel_id=1, source_target_pairs={{0,16},{8,24},{16,0},{24,8},{32,48},{40,56},{48,32},{56,40},{64,80... | collective-permute-start | bytes 393224 | tf_op jit(solution)/shard_map/ppermute | solution.py:75
  88.1 6.6 %collective-permute-start.19 = (f32[16,512]{1,0:T(8,128)S(1)}, f32[16,512]{1,0:T(8,128)S(1)}, u32[]{:S(2)}, u32[]{:S(2)}) collective-permute-start(f32[16,512]{1,0:T(8,128)S(1)} %get-tuple-element.10), channel_id=1, source_target_pairs={{0,192},{8,200},{16,208},{24,216},{32,224},{40,232},{48,240},{56,2... | collective-permute-start | bytes 98312 | tf_op jit(solution)/shard_map/ppermute | solution.py:75
  92.3 7.8 %collective-permute-start.18 = (f32[16,512]{1,0:T(8,128)S(1)}, f32[16,512]{1,0:T(8,128)S(1)}, u32[]{:S(2)}, u32[]{:S(2)}) collective-permute-start(f32[16,512]{1,0:T(8,128)S(1)} %get-tuple-element.11), channel_id=1, source_target_pairs={{0,128},{8,136},{16,144},{24,152},{32,160},{40,168},{48,176},{56,1... | collective-permute-start | bytes 98312 | tf_op jit(solution)/shard_map/ppermute | solution.py:75
  93.2 6.8 %collective-permute-start.17 = (f32[16,512]{1,0:T(8,128)S(1)}, f32[16,512]{1,0:T(8,128)S(1)}, u32[]{:S(2)}, u32[]{:S(2)}) collective-permute-start(f32[16,512]{1,0:T(8,128)S(1)} %get-tuple-element.9), channel_id=1, source_target_pairs={{0,64},{8,72},{16,80},{24,88},{32,96},{40,104},{48,112},{56,120},{... | collective-permute-start | bytes 98312 | tf_op jit(solution)/shard_map/ppermute | solution.py:75

commit v11 on v7

--- a/solution.py
+++ b/solution.py
@@ -141,6 +141,11 @@
     rest = list(range(1, _bit_count(lax.axis_size(axis))))
     pairs = [tuple(rest[max(0, i - 1) : i + 1]) for i in range(len(rest) - 1, -1, -2)]
     return pairs + [(0,)]
+
+
+def _scatter_groups(axis):
+    bits = list(range(_bit_count(lax.axis_size(axis))))
+    return [tuple(bits[i : i + 2]) for i in range(0, len(bits), 2)]
 
 
 def _split_bf16(x):
@@ -188,7 +193,7 @@
     grads_hi, grads_lo = _split_bf16(member_grads)
     summed = jnp.einsum("kg,kc->gc", matches, grads_hi, preferred_element_type=jnp.float32)
     summed = summed + jnp.einsum("kg,kc->gc", matches, grads_lo, preferred_element_type=jnp.float32)
-    reduced = scatter_groups(summed, "feeder", _bit_groups("feeder")[::-1])
+    reduced = scatter_groups(summed, "feeder", _scatter_groups("feeder"))
     new_loadings = loadings - step_size * reduced.reshape(reg_local, hours, columns)
     return (margin, new_loadings)
 

time: 101 us -> 109 us (1.079)
  waiting for transfers between devices: 28.7 us -> 34.2 us
  starting transfers between devices: 29.7 us -> 31.9 us
    ppermute x14, waiting for transfers between devices: 19.3 us -> 24.9 us  [_send_all(): out[j] = lax.ppermute(x_for(j), axis, [(i, i ^ m) for i in range(size)])]
    ppermute x14, starting transfers between devices: 24.1 us -> 26.3 us  [_send_all(): out[j] = lax.ppermute(x_for(j), axis, [(i, i ^ m) for i in range(size)])]
  transfers between devices with their start and end apart: 20 -> 20, of which waited for: 11 -> 12; matrix products, arithmetic and copies ran while one was open for 26% -> 24% of each run, Pallas kernels for 0% -> 0%
where the time goes in v11:
time: 109 us
  matrix products  36.1 us (33%)
  waiting for transfers between devices  34.2 us (31%)
  starting transfers between devices  31.9 us (29%)
  other arithmetic  3.02 us (3%)
  local copies, waits for them, and re-layouts  2.45 us (2%)
    ppermute x14, starting transfers between devices, _send_all(): out[j] = lax.ppermute(x_for(j), axis, [(i, i ^ m) for i in range(size)])  26.3 us
    ppermute x14, waiting for transfers between devices, _send_all(): out[j] = lax.ppermute(x_for(j), axis, [(i, i ^ m) for i in range(size)])  24.9 us
    dot_general x2, matrix products, shards(): jnp.einsum('hkm,mn->hkn', node_hot[at], sens, preferred_element_type=jnp....  23.3 us
    ppermute x6, waiting for transfers between devices, _exchange(): return lax.ppermute(x, axis, perm)  9.33 us
    dot_general x1, matrix products, shards(): jnp.einsum('hkn,hrn->khr', sens_rows, volt_grad, preferred_element_type=j...  6.06 us
    ppermute x6, starting transfers between devices, _exchange(): return lax.ppermute(x, axis, perm)  5.57 us
    dot_general x2, matrix products, shards(): jnp.einsum('khr,hkn->hrn', weighted[:, at], rows, preferred_element_type=...  5.47 us
  transfers between devices with their start and end apart: 20, of which 12 were waited for; matrix products, arithmetic and copies ran while one was open for 24% of the time, Pallas kernels for 0%

profile of v11, /device:TPU:4, one launch (start us, length us, event | category | flops | bytes accessed | tf_op | source)
XLA Modules:
  0.0 108.6 jit_solution(4764274063823139537)
XLA Ops:
  0.6 0.8 convert_element_type.23
  1.5 0.1 broadcast_in_dim_reshape.4
  1.6 6.4 %collective-permute-start.2 = (bf16[1,16,512]{2,1,0:T(8,128)(2,1)S(1)}, bf16[1,16,512]{2,1,0:T(8,128)(2,1)S(1)}, u32[]{:S(2)}, u32[]{:S(2)}) collective-permute-start(bf16[1,16,512]{2,1,0:T(8,128)(2,1)S(1)} %broadcast_in_dim_reshape.4), channel_id=1, source_target_pairs={{0,192},{8,200},{16,208},{24,216},{32,224},{40,232},{48,240},{56,2... | collective-permute-start | bytes 49160 | tf_op jit(solution)/shard_map/ppermute | solution.py:75
  8.0 1.0 collective-permute-start.1
  9.0 1.5 %collective-permute-start = (bf16[1,16,512]{2,1,0:T(8,128)(2,1)S(1)}, bf16[1,16,512]{2,1,0:T(8,128)(2,1)S(1)}, u32[]{:S(2)}, u32[]{:S(2)}) collective-permute-start(bf16[1,16,512]{2,1,0:T(8,128)(2,1)S(1)} %broadcast_in_dim_reshape.4), channel_id=1, source_target_pairs={{0,64},{8,72},{16,80},{24,88},{32,96},{40,104},{48,112},{56,120},{... | collective-permute-start | bytes 49160 | tf_op jit(solution)/shard_map/ppermute | solution.py:75
  10.4 12.8 %fusion.14 = bf16[4,256,2048]{2,1,0:T(8,128)(2,1)} fusion(bf16[1,2048,2048]{2,1,0:T(8,128)(2,1)} %param.6, s32[8,256]{1,0:T(8,128)} %bitcast.136), kind=kOutput, calls=%fused_computation.17 | convolution fusion | flops 8596226048 | bytes 12591104 | tf_op jit(solution)/shard_map/hkm,mn->hkn/dot_general | solution.py:177
  23.2 10.5 %fusion.11 = bf16[4,256,2048]{2,1,0:T(8,128)(2,1)} fusion(bf16[1,2048,2048]{2,1,0:T(8,128)(2,1)S(1)} %copy-done.3, s32[8,256]{1,0:T(8,128)S(1)} %bitcast.137), kind=kOutput, calls=%fused_computation.16 | convolution fusion | flops 8596226048 | bytes 12591104 | tf_op jit(solution)/shard_map/hkm,mn->hkn/dot_general | solution.py:177
  33.8 0.1 stack_broadcast_in_dim_reshape.3
  33.9 0.0 collective-permute-done.1
  33.9 0.0 collective-permute-done
  34.0 0.6 gather_fusion
  34.5 0.1 bitcast_select_fusion.2
  34.6 3.0 %collective-permute-start.5 = (bf16[4,1,16,512]{3,2,0,1:T(8,128)(2,1)S(1)}, bf16[4,1,16,512]{3,2,0,1:T(8,128)(2,1)S(1)}, u32[]{:S(2)}, u32[]{:S(2)}) collective-permute-start(bf16[4,1,16,512]{3,2,0,1:T(8,128)(2,1)S(1)} %bitcast_select_fusion.2), channel_id=1, source_target_pairs={{0,48},{8,56},{16,32},{24,40},{32,16},{40,24},{48,0},{56,8},{64,11... | collective-permute-start | bytes 196616 | tf_op jit(solution)/shard_map/ppermute | solution.py:75
  37.6 0.6 collective-permute-start.4
  38.3 0.5 collective-permute-start.3
  38.7 0.1 bitcast_select_fusion.3
  38.8 1.3 %collective-permute-done.5 = bf16[4,1,16,512]{3,2,0,1:T(8,128)(2,1)S(1)} collective-permute-done((bf16[4,1,16,512]{3,2,0,1:T(8,128)(2,1)S(1)}, bf16[4,1,16,512]{3,2,0,1:T(8,128)(2,1)S(1)}, u32[]{:S(2)}, u32[]{:S(2)}) %collective-permute-start.5) | collective-permute-done | bytes 65568 | tf_op jit(solution)/shard_map/ppermute | solution.py:75
  40.1 3.3 %collective-permute-done.4 = bf16[4,1,16,512]{3,2,0,1:T(8,128)(2,1)S(1)} collective-permute-done((bf16[4,1,16,512]{3,2,0,1:T(8,128)(2,1)S(1)}, bf16[4,1,16,512]{3,2,0,1:T(8,128)(2,1)S(1)}, u32[]{:S(2)}, u32[]{:S(2)}) %collective-permute-start.4) | collective-permute-done | bytes 65568 | tf_op jit(solution)/shard_map/ppermute | solution.py:75
  43.4 0.6 gather_fusion.1
  44.0 0.1 bitcast_select_fusion
  44.1 0.3 collective-permute-start.6
  44.4 0.1 fusion.40
  44.5 1.4 %collective-permute-done.6 = bf16[4,4,1,16,512]{4,3,1,0,2:T(8,128)(2,1)S(1)} collective-permute-done((bf16[4,4,1,16,512]{4,3,1,0,2:T(8,128)(2,1)S(1)}, bf16[4,4,1,16,512]{4,3,1,0,2:T(8,128)(2,1)S(1)}, u32[]{:S(2)}, u32[]{:S(2)}) %collective-permute-start.6) | collective-permute-done | bytes 262176 | tf_op jit(solution)/shard_map/ppermute | solution.py:75
  45.9 0.1 maximum_bitcast_fusion
  46.0 0.6 gather_fusion.2
  46.6 0.1 select_bitcast_fusion
  46.7 0.2 copy.15
  47.0 0.4 fusion.29
  47.4 3.2 %multiply_reduce_fusion = (f32[4,2048]{1,0:T(4,128)S(1)}, f32[4,64,2048]{2,1,0:T(8,128)S(1)}) fusion(bf16[256,8,64]{0,2,1:T(8,128)(2,1)S(1)} %fusion.29, bf16[4,256,2048]{2,1,0:T(8,128)(2,1)} %fusion.14), kind=kOutput, calls=%fused_computation.19 | convolution fusion | flops 269475840 | bytes 6586368 | tf_op jit(solution)/shard_map/khr,hkn->hrn/dot_general | solution.py:179
  50.6 0.0 copy-start.1
  50.6 1.3 %collective-permute-start.10 = (f32[4,2048]{1,0:T(4,128)S(1)}, f32[4,2048]{1,0:T(4,128)S(1)}, u32[]{:S(2)}, u32[]{:S(2)}) collective-permute-start(f32[4,2048]{1,0:T(4,128)S(1)} %get-tuple-element.13), channel_id=1, source_target_pairs={{0,1},{1,0},{2,3},{3,2},{4,5},{5,4},{6,7},{7,6},{8,9},{9,8},{10,11... | collective-permute-start | bytes 98312 | tf_op jit(solution)/shard_map/ppermute | solution.py:19
  51.9 2.3 %multiply_reduce_fusion.1 = (f32[4,2048]{1,0:T(4,128)S(1)}, f32[4,64,2048]{2,1,0:T(8,128)}) fusion(bf16[256,8,64]{0,2,1:T(8,128)(2,1)S(1)} %fusion.29, bf16[4,256,2048]{2,1,0:T(8,128)(2,1)S(1)} %copy-done.6), kind=kOutput, calls=%fused_computation.20 | convolution fusion | flops 269475840 | bytes 6586368 | tf_op jit(solution)/shard_map/khr,hkn->hrn/dot_general | solution.py:179
  54.2 0.8 collective-permute-start.7
  55.0 0.0 collective-permute-done.10
  55.0 0.6 collective-permute-start.11
  55.6 2.7 %collective-permute-done.7 = f32[4,2048]{1,0:T(4,128)S(1)} collective-permute-done((f32[4,2048]{1,0:T(4,128)S(1)}, f32[4,2048]{1,0:T(4,128)S(1)}, u32[]{:S(2)}, u32[]{:S(2)}) %collective-permute-start.7) | collective-permute-done | bytes 32800 | tf_op jit(solution)/shard_map/ppermute | solution.py:19
  58.3 0.7 collective-permute-start.8
  59.0 1.5 %collective-permute-done.11 = f32[4,2048]{1,0:T(4,128)S(1)} collective-permute-done((f32[4,2048]{1,0:T(4,128)S(1)}, f32[4,2048]{1,0:T(4,128)S(1)}, u32[]{:S(2)}, u32[]{:S(2)}) %collective-permute-start.11) | collective-permute-done | bytes 32800 | tf_op jit(solution)/shard_map/ppermute | solution.py:19
  60.5 1.1 %collective-permute-start.12 = (f32[4,2048]{1,0:T(4,128)S(1)}, f32[4,2048]{1,0:T(4,128)S(1)}, u32[]{:S(2)}, u32[]{:S(2)}) collective-permute-start(f32[4,2048]{1,0:T(4,128)S(1)} %add.162), channel_id=1, source_target_pairs={{0,4},{1,5},{2,6},{3,7},{4,0},{5,1},{6,2},{7,3},{8,12},{9,13},{10,... | collective-permute-start | bytes 98312 | tf_op jit(solution)/shard_map/ppermute | solution.py:19
  61.7 2.2 %collective-permute-done.8 = f32[4,2048]{1,0:T(4,128)S(1)} collective-permute-done((f32[4,2048]{1,0:T(4,128)S(1)}, f32[4,2048]{1,0:T(4,128)S(1)}, u32[]{:S(2)}, u32[]{:S(2)}) %collective-permute-start.8) | collective-permute-done | bytes 32800 | tf_op jit(solution)/shard_map/ppermute | solution.py:19
  63.9 1.1 %collective-permute-start.9 = (f32[4,2048]{1,0:T(4,128)S(1)}, f32[4,2048]{1,0:T(4,128)S(1)}, u32[]{:S(2)}, u32[]{:S(2)}) collective-permute-start(f32[4,2048]{1,0:T(4,128)S(1)} %add.159), channel_id=1, source_target_pairs={{0,4},{1,5},{2,6},{3,7},{4,0},{5,1},{6,2},{7,3},{8,12},{9,13},{10,... | collective-permute-start | bytes 98312 | tf_op jit(solution)/shard_map/ppermute | solution.py:19
  65.0 2.9 %collective-permute-done.9 = f32[4,2048]{1,0:T(4,128)S(1)} collective-permute-done((f32[4,2048]{1,0:T(4,128)S(1)}, f32[4,2048]{1,0:T(4,128)S(1)}, u32[]{:S(2)}, u32[]{:S(2)}) %collective-permute-start.9) | collective-permute-done | bytes 32800 | tf_op jit(solution)/shard_map/ppermute | solution.py:19
  67.9 0.7 multiply_bitcast_fusion
  68.6 6.1 %fusion.24 = f32[256,8,64]{0,2,1:T(8,128)S(1)} fusion(bf16[4,256,2048]{2,1,0:T(8,128)(2,1)} %fusion.14, bf16[4,256,2048]{2,1,0:T(8,128)(2,1)} %fusion.11, f32[4,64,2048]{2,1,0:T(8,128)S(1)} %get-tuple-element.14, f32[4,64,2048]{2,1,0:T(8,128)} %get-tuple-element.16, f32[8,2048]{1,0:T(8,128)S(1)} %get-tuple-element.2, f32[256,8]{0,1:T(8,128)S(1)} %bitcast.139), kind=kOutput, calls=%fused_computation.24 | convolution fusion | flops 544342016 | bytes 13180928 | tf_op jit(solution)/shard_map/hkn,hrn->khr/dot_general | solution.py:191
  74.6 0.1 fusion.30
  74.7 0.4 fusion.35
  75.1 0.0 copy-start
  75.2 0.4 convolution_add_fusion
  75.6 0.1 constant_dynamic-slice_fusion.3
  75.7 0.1 collective-permute-start.15
  75.9 0.2 collective-permute-start.14
  76.1 1.8 %collective-permute-start.13 = (f32[2,2,2,16,512]{4,3,0,2,1:T(8,128)S(1)}, f32[2,2,2,16,512]{4,3,0,2,1:T(8,128)S(1)}, u32[]{:S(2)}, u32[]{:S(2)}) collective-permute-start(f32[2,2,2,16,512]{4,3,0,2,1:T(8,128)S(1)} %bitcast.125), channel_id=1, source_target_pairs={{0,8},{8,0},{16,24},{24,16},{32,40},{40,32},{48,56},{56,48},{64,72... | collective-permute-start | bytes 786440 | tf_op jit(solution)/shard_map/ppermute | solution.py:75
  77.9 6.5 %collective-permute-done.15 = f32[2,2,2,16,512]{4,3,0,2,1:T(8,128)S(1)} collective-permute-done((f32[2,2,2,16,512]{4,3,0,2,1:T(8,128)S(1)}, f32[2,2,2,16,512]{4,3,0,2,1:T(8,128)S(1)}, u32[]{:S(2)}, u32[]{:S(2)}) %collective-permute-start.15) | collective-permute-done | bytes 262176 | tf_op jit(solution)/shard_map/ppermute | solution.py:75
  84.4 3.3 %collective-permute-done.14 = f32[2,2,2,16,512]{4,3,0,2,1:T(8,128)S(1)} collective-permute-done((f32[2,2,2,16,512]{4,3,0,2,1:T(8,128)S(1)}, f32[2,2,2,16,512]{4,3,0,2,1:T(8,128)S(1)}, u32[]{:S(2)}, u32[]{:S(2)}) %collective-permute-start.14) | collective-permute-done | bytes 262176 | tf_op jit(solution)/shard_map/ppermute | solution.py:75
  87.7 0.1 fusion.39
  87.8 3.9 %collective-permute-start.18 = (f32[2,16,512]{2,1,0:T(8,128)S(1)}, f32[2,16,512]{2,1,0:T(8,128)S(1)}, u32[]{:S(2)}, u32[]{:S(2)}) collective-permute-start(f32[2,16,512]{2,1,0:T(8,128)S(1)} %get-tuple-element.11), channel_id=1, source_target_pairs={{0,96},{8,104},{16,112},{24,120},{32,64},{40,72},{48,80},{56,88},{... | collective-permute-start | bytes 196616 | tf_op jit(solution)/shard_map/ppermute | solution.py:75
  91.7 1.5 %collective-permute-start.17 = (f32[2,16,512]{2,1,0:T(8,128)S(1)}, f32[2,16,512]{2,1,0:T(8,128)S(1)}, u32[]{:S(2)}, u32[]{:S(2)}) collective-permute-start(f32[2,16,512]{2,1,0:T(8,128)S(1)} %get-tuple-element.12), channel_id=1, source_target_pairs={{0,64},{8,72},{16,80},{24,88},{32,96},{40,104},{48,112},{56,120},{... | collective-permute-start | bytes 196616 | tf_op jit(solution)/shard_map/ppermute | solution.py:75
  93.2 0.6 collective-permute-start.16
  93.8 5.2 %collective-permute-done.18 = f32[2,16,512]{2,1,0:T(8,128)S(1)} collective-permute-done((f32[2,16,512]{2,1,0:T(8,128)S(1)}, f32[2,16,512]{2,1,0:T(8,128)S(1)}, u32[]{:S(2)}, u32[]{:S(2)}) %collective-permute-start.18) | collective-permute-done | bytes 65568 | tf_op jit(solution)/shard_map/ppermute | solution.py:75
  99.0 1.0 collective-permute-done.17
  100.0 5.0 %collective-permute-start.19 = (f32[16,512]{1,0:T(8,128)S(1)}, f32[16,512]{1,0:T(8,128)S(1)}, u32[]{:S(2)}, u32[]{:S(2)}) collective-permute-start(f32[16,512]{1,0:T(8,128)S(1)} %dynamic-slice_bitcast_fusion.3), channel_id=1, source_target_pairs={{0,128},{8,136},{16,144},{24,152},{32,160},{40,168},{48,176},{56,1... | collective-permute-start | bytes 98312 | tf_op jit(solution)/shard_map/ppermute | solution.py:75
  105.0 2.9 %collective-permute-done.19 = f32[16,512]{1,0:T(8,128)S(1)} collective-permute-done((f32[16,512]{1,0:T(8,128)S(1)}, f32[16,512]{1,0:T(8,128)S(1)}, u32[]{:S(2)}, u32[]{:S(2)}) %collective-permute-start.19) | collective-permute-done | bytes 32800 | tf_op jit(solution)/shard_map/ppermute | solution.py:75
  107.9 0.1 mul.95
  108.0 0.6 sub.11
  (41 shorter events, 0.4 us)
Async XLA Ops:
  1.6 32.3 %collective-permute-start.2 = (bf16[1,16,512]{2,1,0:T(8,128)(2,1)S(1)}, bf16[1,16,512]{2,1,0:T(8,128)(2,1)S(1)}, u32[]{:S(2)}, u32[]{:S(2)}) collective-permute-start(bf16[1,16,512]{2,1,0:T(8,128)(2,1)S(1)} %broadcast_in_dim_reshape.4), channel_id=1, source_target_pairs={{0,192},{8,200},{16,208},{24,216},{32,224},{40,232},{48,240},{56,2... | collective-permute-start | bytes 49160 | tf_op jit(solution)/shard_map/ppermute | solution.py:75
  8.0 26.0 %collective-permute-start.1 = (bf16[1,16,512]{2,1,0:T(8,128)(2,1)S(1)}, bf16[1,16,512]{2,1,0:T(8,128)(2,1)S(1)}, u32[]{:S(2)}, u32[]{:S(2)}) collective-permute-start(bf16[1,16,512]{2,1,0:T(8,128)(2,1)S(1)} %broadcast_in_dim_reshape.4), channel_id=1, source_target_pairs={{0,128},{8,136},{16,144},{24,152},{32,160},{40,168},{48,176},{56,1... | collective-permute-start | bytes 49160 | tf_op jit(solution)/shard_map/ppermute | solution.py:75
  9.0 25.0 %collective-permute-start = (bf16[1,16,512]{2,1,0:T(8,128)(2,1)S(1)}, bf16[1,16,512]{2,1,0:T(8,128)(2,1)S(1)}, u32[]{:S(2)}, u32[]{:S(2)}) collective-permute-start(bf16[1,16,512]{2,1,0:T(8,128)(2,1)S(1)} %broadcast_in_dim_reshape.4), channel_id=1, source_target_pairs={{0,64},{8,72},{16,80},{24,88},{32,96},{40,104},{48,112},{56,120},{... | collective-permute-start | bytes 49160 | tf_op jit(solution)/shard_map/ppermute | solution.py:75
  10.4 12.8 %copy-start.3 = (bf16[1,2048,2048]{2,1,0:T(8,128)(2,1)S(1)}, bf16[1,2048,2048]{2,1,0:T(8,128)(2,1)}, u32[]{:S(2)}) copy-start(bf16[1,2048,2048]{2,1,0:T(8,128)(2,1)} %param.6) | copy-start | bytes 25165828
  10.4 12.8 %copy-start.4 = (s32[1,8,256]{2,1,0:T(8,128)S(1)}, s32[1,8,256]{2,1,0:T(8,128)}, u32[]{:S(2)}) copy-start(s32[1,8,256]{2,1,0:T(8,128)} %param.9) | copy-start | bytes 24580
  33.7 13.2 %copy-start.2 = (s32[1,256]{1,0:T(1,128)S(1)}, s32[1,256]{1,0:T(1,128)}, u32[]{:S(2)}) copy-start(s32[1,256]{1,0:T(1,128)} %param.10) | copy-start | bytes 3076
  33.7 13.3 %copy-start.5 = (f32[1,8,256]{2,1,0:T(8,128)S(1)}, f32[1,8,256]{2,1,0:T(8,128)}, u32[]{:S(2)}) copy-start(f32[1,8,256]{2,1,0:T(8,128)} %param.8) | copy-start | bytes 24580
  34.6 5.5 %collective-permute-start.5 = (bf16[4,1,16,512]{3,2,0,1:T(8,128)(2,1)S(1)}, bf16[4,1,16,512]{3,2,0,1:T(8,128)(2,1)S(1)}, u32[]{:S(2)}, u32[]{:S(2)}) collective-permute-start(bf16[4,1,16,512]{3,2,0,1:T(8,128)(2,1)S(1)} %bitcast_select_fusion.2), channel_id=1, source_target_pairs={{0,48},{8,56},{16,32},{24,40},{32,16},{40,24},{48,0},{56,8},{64,11... | collective-permute-start | bytes 196616 | tf_op jit(solution)/shard_map/ppermute | solution.py:75
  37.6 5.8 %collective-permute-start.4 = (bf16[4,1,16,512]{3,2,0,1:T(8,128)(2,1)S(1)}, bf16[4,1,16,512]{3,2,0,1:T(8,128)(2,1)S(1)}, u32[]{:S(2)}, u32[]{:S(2)}) collective-permute-start(bf16[4,1,16,512]{3,2,0,1:T(8,128)(2,1)S(1)} %bitcast_select_fusion.2), channel_id=1, source_target_pairs={{0,32},{8,40},{16,48},{24,56},{32,0},{40,8},{48,16},{56,24},{64,96... | collective-permute-start | bytes 196616 | tf_op jit(solution)/shard_map/ppermute | solution.py:75
  38.3 5.1 %collective-permute-start.3 = (bf16[4,1,16,512]{3,2,0,1:T(8,128)(2,1)S(1)}, bf16[4,1,16,512]{3,2,0,1:T(8,128)(2,1)S(1)}, u32[]{:S(2)}, u32[]{:S(2)}) collective-permute-start(bf16[4,1,16,512]{3,2,0,1:T(8,128)(2,1)S(1)} %bitcast_select_fusion.2), channel_id=1, source_target_pairs={{0,16},{8,24},{16,0},{24,8},{32,48},{40,56},{48,32},{56,40},{64,80... | collective-permute-start | bytes 196616 | tf_op jit(solution)/shard_map/ppermute | solution.py:75
  44.1 1.8 %collective-permute-start.6 = (bf16[4,4,1,16,512]{4,3,1,0,2:T(8,128)(2,1)S(1)}, bf16[4,4,1,16,512]{4,3,1,0,2:T(8,128)(2,1)S(1)}, u32[]{:S(2)}, u32[]{:S(2)}) collective-permute-start(bf16[4,4,1,16,512]{4,3,1,0,2:T(8,128)(2,1)S(1)} %bitcast_select_fusion), channel_id=1, source_target_pairs={{0,8},{8,0},{16,24},{24,16},{32,40},{40,32},{48,56},{56,48},{64,72... | collective-permute-start | bytes 786440 | tf_op jit(solution)/shard_map/ppermute | solution.py:75
  47.4 4.5 %copy-start.6 = (bf16[4,256,2048]{2,1,0:T(8,128)(2,1)S(1)}, bf16[4,256,2048]{2,1,0:T(8,128)(2,1)}, u32[]{:S(2)}) copy-start(bf16[4,256,2048]{2,1,0:T(8,128)(2,1)} %fusion.11) | copy-start | bytes 12582916
  50.6 17.3 %copy-start.1 = (f32[1,8,2048]{2,1,0:T(8,128)S(1)}, f32[1,8,2048]{2,1,0:T(8,128)}, u32[]{:S(2)}) copy-start(f32[1,8,2048]{2,1,0:T(8,128)} %param.7) | copy-start | bytes 196612
  50.6 4.4 %collective-permute-start.10 = (f32[4,2048]{1,0:T(4,128)S(1)}, f32[4,2048]{1,0:T(4,128)S(1)}, u32[]{:S(2)}, u32[]{:S(2)}) collective-permute-start(f32[4,2048]{1,0:T(4,128)S(1)} %get-tuple-element.13), channel_id=1, source_target_pairs={{0,1},{1,0},{2,3},{3,2},{4,5},{5,4},{6,7},{7,6},{8,9},{9,8},{10,11... | collective-permute-start | bytes 98312 | tf_op jit(solution)/shard_map/ppermute | solution.py:19
  54.2 4.1 %collective-permute-start.7 = (f32[4,2048]{1,0:T(4,128)S(1)}, f32[4,2048]{1,0:T(4,128)S(1)}, u32[]{:S(2)}, u32[]{:S(2)}) collective-permute-start(f32[4,2048]{1,0:T(4,128)S(1)} %get-tuple-element.15), channel_id=1, source_target_pairs={{0,1},{1,0},{2,3},{3,2},{4,5},{5,4},{6,7},{7,6},{8,9},{9,8},{10,11... | collective-permute-start | bytes 98312 | tf_op jit(solution)/shard_map/ppermute | solution.py:19
  55.0 5.5 %collective-permute-start.11 = (f32[4,2048]{1,0:T(4,128)S(1)}, f32[4,2048]{1,0:T(4,128)S(1)}, u32[]{:S(2)}, u32[]{:S(2)}) collective-permute-start(f32[4,2048]{1,0:T(4,128)S(1)} %add.161), channel_id=1, source_target_pairs={{0,2},{1,3},{2,0},{3,1},{4,6},{5,7},{6,4},{7,5},{8,10},{9,11},{10,... | collective-permute-start | bytes 98312 | tf_op jit(solution)/shard_map/ppermute | solution.py:19
  58.3 5.5 %collective-permute-start.8 = (f32[4,2048]{1,0:T(4,128)S(1)}, f32[4,2048]{1,0:T(4,128)S(1)}, u32[]{:S(2)}, u32[]{:S(2)}) collective-permute-start(f32[4,2048]{1,0:T(4,128)S(1)} %add.158), channel_id=1, source_target_pairs={{0,2},{1,3},{2,0},{3,1},{4,6},{5,7},{6,4},{7,5},{8,10},{9,11},{10,... | collective-permute-start | bytes 98312 | tf_op jit(solution)/shard_map/ppermute | solution.py:19
  60.5 4.4 %collective-permute-start.12 = (f32[4,2048]{1,0:T(4,128)S(1)}, f32[4,2048]{1,0:T(4,128)S(1)}, u32[]{:S(2)}, u32[]{:S(2)}) collective-permute-start(f32[4,2048]{1,0:T(4,128)S(1)} %add.162), channel_id=1, source_target_pairs={{0,4},{1,5},{2,6},{3,7},{4,0},{5,1},{6,2},{7,3},{8,12},{9,13},{10,... | collective-permute-start | bytes 98312 | tf_op jit(solution)/shard_map/ppermute | solution.py:19
  63.9 4.0 %collective-permute-start.9 = (f32[4,2048]{1,0:T(4,128)S(1)}, f32[4,2048]{1,0:T(4,128)S(1)}, u32[]{:S(2)}, u32[]{:S(2)}) collective-permute-start(f32[4,2048]{1,0:T(4,128)S(1)} %add.159), channel_id=1, source_target_pairs={{0,4},{1,5},{2,6},{3,7},{4,0},{5,1},{6,2},{7,3},{8,12},{9,13},{10,... | collective-permute-start | bytes 98312 | tf_op jit(solution)/shard_map/ppermute | solution.py:19
  75.1 32.8 %copy-start = (f32[16,8,64]{2,1,0:T(8,128)S(1)}, f32[16,8,64]{2,1,0:T(8,128)}, u32[]{:S(2)}) copy-start(f32[16,8,64]{2,1,0:T(8,128)} %param.11) | copy-start | bytes 98308
  75.7 8.7 %collective-permute-start.15 = (f32[2,2,2,16,512]{4,3,0,2,1:T(8,128)S(1)}, f32[2,2,2,16,512]{4,3,0,2,1:T(8,128)S(1)}, u32[]{:S(2)}, u32[]{:S(2)}) collective-permute-start(f32[2,2,2,16,512]{4,3,0,2,1:T(8,128)S(1)} %bitcast.123), channel_id=1, source_target_pairs={{0,24},{8,16},{16,8},{24,0},{32,56},{40,48},{48,40},{56,32},{64,88... | collective-permute-start | bytes 786440 | tf_op jit(solution)/shard_map/ppermute | solution.py:75
  75.9 11.8 %collective-permute-start.14 = (f32[2,2,2,16,512]{4,3,0,2,1:T(8,128)S(1)}, f32[2,2,2,16,512]{4,3,0,2,1:T(8,128)S(1)}, u32[]{:S(2)}, u32[]{:S(2)}) collective-permute-start(f32[2,2,2,16,512]{4,3,0,2,1:T(8,128)S(1)} %bitcast.124), channel_id=1, source_target_pairs={{0,16},{8,24},{16,0},{24,8},{32,48},{40,56},{48,32},{56,40},{64,80... | collective-permute-start | bytes 786440 | tf_op jit(solution)/shard_map/ppermute | solution.py:75
  76.1 11.6 %collective-permute-start.13 = (f32[2,2,2,16,512]{4,3,0,2,1:T(8,128)S(1)}, f32[2,2,2,16,512]{4,3,0,2,1:T(8,128)S(1)}, u32[]{:S(2)}, u32[]{:S(2)}) collective-permute-start(f32[2,2,2,16,512]{4,3,0,2,1:T(8,128)S(1)} %bitcast.125), channel_id=1, source_target_pairs={{0,8},{8,0},{16,24},{24,16},{32,40},{40,32},{48,56},{56,48},{64,72... | collective-permute-start | bytes 786440 | tf_op jit(solution)/shard_map/ppermute | solution.py:75
  87.8 11.2 %collective-permute-start.18 = (f32[2,16,512]{2,1,0:T(8,128)S(1)}, f32[2,16,512]{2,1,0:T(8,128)S(1)}, u32[]{:S(2)}, u32[]{:S(2)}) collective-permute-start(f32[2,16,512]{2,1,0:T(8,128)S(1)} %get-tuple-element.11), channel_id=1, source_target_pairs={{0,96},{8,104},{16,112},{24,120},{32,64},{40,72},{48,80},{56,88},{... | collective-permute-start | bytes 196616 | tf_op jit(solution)/shard_map/ppermute | solution.py:75
  91.7 8.2 %collective-permute-start.17 = (f32[2,16,512]{2,1,0:T(8,128)S(1)}, f32[2,16,512]{2,1,0:T(8,128)S(1)}, u32[]{:S(2)}, u32[]{:S(2)}) collective-permute-start(f32[2,16,512]{2,1,0:T(8,128)S(1)} %get-tuple-element.12), channel_id=1, source_target_pairs={{0,64},{8,72},{16,80},{24,88},{32,96},{40,104},{48,112},{56,120},{... | collective-permute-start | bytes 196616 | tf_op jit(solution)/shard_map/ppermute | solution.py:75
  93.2 6.7 %collective-permute-start.16 = (f32[2,16,512]{2,1,0:T(8,128)S(1)}, f32[2,16,512]{2,1,0:T(8,128)S(1)}, u32[]{:S(2)}, u32[]{:S(2)}) collective-permute-start(f32[2,16,512]{2,1,0:T(8,128)S(1)} %get-tuple-element.10), channel_id=1, source_target_pairs={{0,32},{8,40},{16,48},{24,56},{32,0},{40,8},{48,16},{56,24},{64,96... | collective-permute-start | bytes 196616 | tf_op jit(solution)/shard_map/ppermute | solution.py:75
  100.0 7.9 %collective-permute-start.19 = (f32[16,512]{1,0:T(8,128)S(1)}, f32[16,512]{1,0:T(8,128)S(1)}, u32[]{:S(2)}, u32[]{:S(2)}) collective-permute-start(f32[16,512]{1,0:T(8,128)S(1)} %dynamic-slice_bitcast_fusion.3), channel_id=1, source_target_pairs={{0,128},{8,136},{16,144},{24,152},{32,160},{40,168},{48,176},{56,1... | collective-permute-start | bytes 98312 | tf_op jit(solution)/shard_map/ppermute | solution.py:75

commit v12 on v7

--- a/solution.py
+++ b/solution.py
@@ -134,7 +134,7 @@
     return x
 
 
-CHUNKS = 2
+CHUNKS = 1
 
 
 def _bit_groups(axis):

time: 101 us -> 101 us (level)
  starting transfers between devices: 29.7 us -> 27 us
  waiting for transfers between devices: 28.7 us -> 30.9 us
    ppermute x6 -> x3, starting transfers between devices: 5.56 us -> 3.08 us  [_exchange(): return lax.ppermute(x, axis, perm)]
    ppermute x6 -> x3, waiting for transfers between devices: 9.34 us -> 11.6 us  [_exchange(): return lax.ppermute(x, axis, perm)]
    dot_general x2 -> x1, matrix products: 5.48 us -> 7.16 us  [shards(): jnp.einsum('khr,hkn->hrn', weighted[:, at], rows, preferred_element_type=...]
    dot_general x2 -> x1, matrix products: 23.3 us -> 21.8 us  [shards(): jnp.einsum('hkm,mn->hkn', node_hot[at], sens, preferred_element_type=jnp....]
    dot_general x1, matrix products: 6.06 us -> 7.34 us  [shards(): jnp.einsum('hkn,hrn->khr', sens_rows, volt_grad, preferred_element_type=j...]
  transfers between devices with their start and end apart: 20 -> 17, of which waited for: 11 -> 10; matrix products, arithmetic and copies ran while one was open for 26% -> 22% of each run, Pallas kernels for 0% -> 0%
where the time goes in v12:
time: 101 us
  matrix products  37.1 us (37%)
  waiting for transfers between devices  30.9 us (31%)
  starting transfers between devices  27 us (27%)
  other arithmetic  2.99 us (3%)
  local copies, waits for them, and re-layouts  2.35 us (2%)
    ppermute x14, starting transfers between devices, _send_all(): out[j] = lax.ppermute(x_for(j), axis, [(i, i ^ m) for i in range(size)])  23.9 us
    dot_general x1, matrix products, shards(): jnp.einsum('hkm,mn->hkn', node_hot[at], sens, preferred_element_type=jnp....  21.8 us
    ppermute x14, waiting for transfers between devices, _send_all(): out[j] = lax.ppermute(x_for(j), axis, [(i, i ^ m) for i in range(size)])  19.4 us
    ppermute x3, waiting for transfers between devices, _exchange(): return lax.ppermute(x, axis, perm)  11.6 us
    dot_general x1, matrix products, shards(): jnp.einsum('hkn,hrn->khr', sens_rows, volt_grad, preferred_element_type=j...  7.34 us
    dot_general x1, matrix products, shards(): jnp.einsum('khr,hkn->hrn', weighted[:, at], rows, preferred_element_type=...  7.16 us
    ppermute x3, starting transfers between devices, _exchange(): return lax.ppermute(x, axis, perm)  3.08 us
  transfers between devices with their start and end apart: 17, of which 10 were waited for; matrix products, arithmetic and copies ran while one was open for 22% of the time, Pallas kernels for 0%

profile of v12, /device:TPU:4, one launch (start us, length us, event | category | flops | bytes accessed | tf_op | source)
XLA Modules:
  0.0 101.3 jit_solution(96294342943934261)
XLA Ops:
  0.6 0.8 convert_element_type.20
  1.5 0.1 broadcast_in_dim_reshape.4
  1.6 6.4 %collective-permute-start.2 = (bf16[1,16,512]{2,1,0:T(8,128)(2,1)S(1)}, bf16[1,16,512]{2,1,0:T(8,128)(2,1)S(1)}, u32[]{:S(2)}, u32[]{:S(2)}) collective-permute-start(bf16[1,16,512]{2,1,0:T(8,128)(2,1)S(1)} %broadcast_in_dim_reshape.4), channel_id=1, source_target_pairs={{0,192},{8,200},{16,208},{24,216},{32,224},{40,232},{48,240},{56,2... | collective-permute-start | bytes 49160 | tf_op jit(solution)/shard_map/ppermute | solution.py:75
  8.0 1.0 collective-permute-start.1
  9.0 1.5 %collective-permute-start = (bf16[1,16,512]{2,1,0:T(8,128)(2,1)S(1)}, bf16[1,16,512]{2,1,0:T(8,128)(2,1)S(1)}, u32[]{:S(2)}, u32[]{:S(2)}) collective-permute-start(bf16[1,16,512]{2,1,0:T(8,128)(2,1)S(1)} %broadcast_in_dim_reshape.4), channel_id=1, source_target_pairs={{0,64},{8,72},{16,80},{24,88},{32,96},{40,104},{48,112},{56,120},{... | collective-permute-start | bytes 49160 | tf_op jit(solution)/shard_map/ppermute | solution.py:75
  10.5 0.0 copy-start.2
  10.5 0.0 copy-start.3
  10.5 21.8 %fusion.3 = bf16[8,256,2048]{2,1,0:T(8,128)(2,1)} fusion(bf16[1,2048,2048]{2,1,0:T(8,128)(2,1)} %param.6, s32[8,256]{1,0:T(8,128)} %bitcast.132), kind=kOutput, calls=%fused_computation.7 | convolution fusion | flops 17188257792 | bytes 16785408 | tf_op jit(solution)/shard_map/hkm,mn->hkn/dot_general | solution.py:172
  32.3 0.1 stack_broadcast_in_dim_reshape.3
  32.4 0.0 collective-permute-done.2
  32.4 0.0 collective-permute-done.1
  32.4 0.0 collective-permute-done
  32.5 0.6 gather_fusion
  33.0 0.1 bitcast_select_fusion.2
  33.1 3.0 %collective-permute-start.5 = (bf16[4,1,16,512]{3,2,0,1:T(8,128)(2,1)S(1)}, bf16[4,1,16,512]{3,2,0,1:T(8,128)(2,1)S(1)}, u32[]{:S(2)}, u32[]{:S(2)}) collective-permute-start(bf16[4,1,16,512]{3,2,0,1:T(8,128)(2,1)S(1)} %bitcast_select_fusion.2), channel_id=1, source_target_pairs={{0,48},{8,56},{16,32},{24,40},{32,16},{40,24},{48,0},{56,8},{64,11... | collective-permute-start | bytes 196616 | tf_op jit(solution)/shard_map/ppermute | solution.py:75
  36.1 0.6 collective-permute-start.4
  36.8 0.4 collective-permute-start.3
  37.2 0.1 bitcast_select_fusion.3
  37.3 1.3 %collective-permute-done.5 = bf16[4,1,16,512]{3,2,0,1:T(8,128)(2,1)S(1)} collective-permute-done((bf16[4,1,16,512]{3,2,0,1:T(8,128)(2,1)S(1)}, bf16[4,1,16,512]{3,2,0,1:T(8,128)(2,1)S(1)}, u32[]{:S(2)}, u32[]{:S(2)}) %collective-permute-start.5) | collective-permute-done | bytes 65568 | tf_op jit(solution)/shard_map/ppermute | solution.py:75
  38.6 3.3 %collective-permute-done.4 = bf16[4,1,16,512]{3,2,0,1:T(8,128)(2,1)S(1)} collective-permute-done((bf16[4,1,16,512]{3,2,0,1:T(8,128)(2,1)S(1)}, bf16[4,1,16,512]{3,2,0,1:T(8,128)(2,1)S(1)}, u32[]{:S(2)}, u32[]{:S(2)}) %collective-permute-start.4) | collective-permute-done | bytes 65568 | tf_op jit(solution)/shard_map/ppermute | solution.py:75
  41.9 0.0 collective-permute-done.3
  41.9 0.6 gather_fusion.1
  42.5 0.1 bitcast_select_fusion
  42.6 0.1 collective-permute-start.6
  42.7 0.1 fusion.20
  42.8 1.4 %collective-permute-done.6 = bf16[4,4,1,16,512]{4,3,1,0,2:T(8,128)(2,1)S(1)} collective-permute-done((bf16[4,4,1,16,512]{4,3,1,0,2:T(8,128)(2,1)S(1)}, bf16[4,4,1,16,512]{4,3,1,0,2:T(8,128)(2,1)S(1)}, u32[]{:S(2)}, u32[]{:S(2)}) %collective-permute-start.6) | collective-permute-done | bytes 262176 | tf_op jit(solution)/shard_map/ppermute | solution.py:75
  44.2 0.1 maximum_bitcast_fusion
  44.3 0.6 gather_fusion.2
  44.9 0.0 copy-start.1
  44.9 0.1 select_bitcast_fusion
  45.1 0.2 copy.11
  45.3 0.0 copy-done.2
  45.3 0.0 copy-done.3
  45.3 7.2 %multiply_reduce_fusion = (f32[8,2048]{1,0:T(8,128)S(1)}, f32[8,64,2048]{2,1,0:T(8,128)}) fusion(bf16[8,256,2048]{2,1,0:T(8,128)(2,1)} %fusion.3, bf16[8,64,512]{2,1,0:T(8,128)(2,1)S(1)} %bitcast.114, s32[256]{0:T(256)S(1)} %bitcast.129, f32[256,8]{0,1:T(8,128)S(1)} %bitcast.124), kind=kOutput, calls=%fused_computation.9 | convolution fusion | flops 673562624 | bytes 13181952 | tf_op jit(solution)/shard_map/khr,hkn->hrn/dot_general | solution.py:174
  52.5 1.2 %collective-permute-start.7 = (f32[8,2048]{1,0:T(8,128)S(1)}, f32[8,2048]{1,0:T(8,128)S(1)}, u32[]{:S(2)}, u32[]{:S(2)}) collective-permute-start(f32[8,2048]{1,0:T(8,128)S(1)} %get-tuple-element.12), channel_id=1, source_target_pairs={{0,1},{1,0},{2,3},{3,2},{4,5},{5,4},{6,7},{7,6},{8,9},{9,8},{10,11... | collective-permute-start | bytes 196616 | tf_op jit(solution)/shard_map/ppermute | solution.py:19
  53.7 3.1 %collective-permute-done.7 = f32[8,2048]{1,0:T(8,128)S(1)} collective-permute-done((f32[8,2048]{1,0:T(8,128)S(1)}, f32[8,2048]{1,0:T(8,128)S(1)}, u32[]{:S(2)}, u32[]{:S(2)}) %collective-permute-start.7) | collective-permute-done | bytes 65568 | tf_op jit(solution)/shard_map/ppermute | solution.py:19
  56.7 0.6 collective-permute-start.8
  57.3 5.3 %collective-permute-done.8 = f32[8,2048]{1,0:T(8,128)S(1)} collective-permute-done((f32[8,2048]{1,0:T(8,128)S(1)}, f32[8,2048]{1,0:T(8,128)S(1)}, u32[]{:S(2)}, u32[]{:S(2)}) %collective-permute-start.8) | collective-permute-done | bytes 65568 | tf_op jit(solution)/shard_map/ppermute | solution.py:19
  62.6 1.3 %collective-permute-start.9 = (f32[8,2048]{1,0:T(8,128)S(1)}, f32[8,2048]{1,0:T(8,128)S(1)}, u32[]{:S(2)}, u32[]{:S(2)}) collective-permute-start(f32[8,2048]{1,0:T(8,128)S(1)} %add.135), channel_id=1, source_target_pairs={{0,4},{1,5},{2,6},{3,7},{4,0},{5,1},{6,2},{7,3},{8,12},{9,13},{10,... | collective-permute-start | bytes 196616 | tf_op jit(solution)/shard_map/ppermute | solution.py:19
  63.9 3.2 %collective-permute-done.9 = f32[8,2048]{1,0:T(8,128)S(1)} collective-permute-done((f32[8,2048]{1,0:T(8,128)S(1)}, f32[8,2048]{1,0:T(8,128)S(1)}, u32[]{:S(2)}, u32[]{:S(2)}) %collective-permute-start.9) | collective-permute-done | bytes 65568 | tf_op jit(solution)/shard_map/ppermute | solution.py:19
  67.1 0.0 copy-done.1
  67.1 0.7 fusion.29
  67.8 7.3 %fusion.9 = f32[256,8,64]{0,2,1:T(8,128)S(1)} fusion(bf16[8,256,2048]{2,1,0:T(8,128)(2,1)} %fusion.3, f32[8,64,2048]{2,1,0:T(8,128)} %get-tuple-element.13, f32[8,2048]{1,0:T(8,128)S(1)} %get-tuple-element.2, f32[256,8]{0,1:T(8,128)S(1)} %bitcast.125), kind=kOutput, calls=%fused_computation.14 | convolution fusion | flops 539099136 | bytes 13180928 | tf_op jit(solution)/shard_map/hkn,hrn->khr/dot_general | solution.py:186
  75.2 0.1 fusion.12
  75.2 0.4 fusion.18
  75.7 0.4 convolution_add_fusion
  76.2 0.1 collective-permute-start.10
  76.3 1.9 %collective-permute-done.10 = f32[2,2,2,2,16,512]{5,4,3,2,1,0:T(8,128)S(1)} collective-permute-done((f32[2,2,2,2,16,512]{5,4,3,2,1,0:T(8,128)S(1)}, f32[2,2,2,2,16,512]{5,4,3,2,1,0:T(8,128)S(1)}, u32[]{:S(2)}, u32[]{:S(2)}) %collective-permute-start.10) | collective-permute-done | bytes 524320 | tf_op jit(solution)/shard_map/ppermute | solution.py:75
  78.2 0.1 bitcast_add_fusion
  78.3 1.4 %collective-permute-start.13 = (f32[2,2,16,512]{3,2,1,0:T(8,128)S(1)}, f32[2,2,16,512]{3,2,1,0:T(8,128)S(1)}, u32[]{:S(2)}, u32[]{:S(2)}) collective-permute-start(f32[2,2,16,512]{3,2,1,0:T(8,128)S(1)} %get-tuple-element.5), channel_id=1, source_target_pairs={{0,48},{8,56},{16,32},{24,40},{32,16},{40,24},{48,0},{56,8},{64,11... | collective-permute-start | bytes 393224 | tf_op jit(solution)/shard_map/ppermute | solution.py:75
  79.7 0.9 collective-permute-start.12
  80.6 1.9 %collective-permute-start.11 = (f32[2,2,16,512]{3,2,1,0:T(8,128)S(1)}, f32[2,2,16,512]{3,2,1,0:T(8,128)S(1)}, u32[]{:S(2)}, u32[]{:S(2)}) collective-permute-start(f32[2,2,16,512]{3,2,1,0:T(8,128)S(1)} %get-tuple-element.4), channel_id=1, source_target_pairs={{0,16},{8,24},{16,0},{24,8},{32,48},{40,56},{48,32},{56,40},{64,80... | collective-permute-start | bytes 393224 | tf_op jit(solution)/shard_map/ppermute | solution.py:75
  82.5 5.5 %collective-permute-done.13 = f32[2,2,16,512]{3,2,1,0:T(8,128)S(1)} collective-permute-done((f32[2,2,16,512]{3,2,1,0:T(8,128)S(1)}, f32[2,2,16,512]{3,2,1,0:T(8,128)S(1)}, u32[]{:S(2)}, u32[]{:S(2)}) %collective-permute-start.13) | collective-permute-done | bytes 131104 | tf_op jit(solution)/shard_map/ppermute | solution.py:75
  88.0 0.0 collective-permute-done.12
  88.0 0.6 collective-permute-done.11
  88.6 4.1 %collective-permute-start.16 = (f32[16,512]{1,0:T(8,128)S(1)}, f32[16,512]{1,0:T(8,128)S(1)}, u32[]{:S(2)}, u32[]{:S(2)}) collective-permute-start(f32[16,512]{1,0:T(8,128)S(1)} %get-tuple-element.10), channel_id=1, source_target_pairs={{0,192},{8,200},{16,208},{24,216},{32,224},{40,232},{48,240},{56,2... | collective-permute-start | bytes 98312 | tf_op jit(solution)/shard_map/ppermute | solution.py:75
  92.8 1.0 collective-permute-start.15
  93.8 1.5 %collective-permute-start.14 = (f32[16,512]{1,0:T(8,128)S(1)}, f32[16,512]{1,0:T(8,128)S(1)}, u32[]{:S(2)}, u32[]{:S(2)}) collective-permute-start(f32[16,512]{1,0:T(8,128)S(1)} %get-tuple-element.9), channel_id=1, source_target_pairs={{0,64},{8,72},{16,80},{24,88},{32,96},{40,104},{48,112},{56,120},{... | collective-permute-start | bytes 98312 | tf_op jit(solution)/shard_map/ppermute | solution.py:75
  95.2 0.0 collective-permute-done.16
  95.2 5.4 %collective-permute-done.15 = f32[16,512]{1,0:T(8,128)S(1)} collective-permute-done((f32[16,512]{1,0:T(8,128)S(1)}, f32[16,512]{1,0:T(8,128)S(1)}, u32[]{:S(2)}, u32[]{:S(2)}) %collective-permute-start.15) | collective-permute-done | bytes 32800 | tf_op jit(solution)/shard_map/ppermute | solution.py:75
  100.6 0.0 collective-permute-done.14
  100.6 0.1 mul.81
  100.7 0.0 copy-done
  100.7 0.6 sub.11
  (19 shorter events, 0.3 us)
Async XLA Ops:
  1.6 30.8 %collective-permute-start.2 = (bf16[1,16,512]{2,1,0:T(8,128)(2,1)S(1)}, bf16[1,16,512]{2,1,0:T(8,128)(2,1)S(1)}, u32[]{:S(2)}, u32[]{:S(2)}) collective-permute-start(bf16[1,16,512]{2,1,0:T(8,128)(2,1)S(1)} %broadcast_in_dim_reshape.4), channel_id=1, source_target_pairs={{0,192},{8,200},{16,208},{24,216},{32,224},{40,232},{48,240},{56,2... | collective-permute-start | bytes 49160 | tf_op jit(solution)/shard_map/ppermute | solution.py:75
  8.0 24.5 %collective-permute-start.1 = (bf16[1,16,512]{2,1,0:T(8,128)(2,1)S(1)}, bf16[1,16,512]{2,1,0:T(8,128)(2,1)S(1)}, u32[]{:S(2)}, u32[]{:S(2)}) collective-permute-start(bf16[1,16,512]{2,1,0:T(8,128)(2,1)S(1)} %broadcast_in_dim_reshape.4), channel_id=1, source_target_pairs={{0,128},{8,136},{16,144},{24,152},{32,160},{40,168},{48,176},{56,1... | collective-permute-start | bytes 49160 | tf_op jit(solution)/shard_map/ppermute | solution.py:75
  9.0 23.5 %collective-permute-start = (bf16[1,16,512]{2,1,0:T(8,128)(2,1)S(1)}, bf16[1,16,512]{2,1,0:T(8,128)(2,1)S(1)}, u32[]{:S(2)}, u32[]{:S(2)}) collective-permute-start(bf16[1,16,512]{2,1,0:T(8,128)(2,1)S(1)} %broadcast_in_dim_reshape.4), channel_id=1, source_target_pairs={{0,64},{8,72},{16,80},{24,88},{32,96},{40,104},{48,112},{56,120},{... | collective-permute-start | bytes 49160 | tf_op jit(solution)/shard_map/ppermute | solution.py:75
  10.5 34.8 %copy-start.2 = (f32[1,8,256]{2,1,0:T(8,128)S(1)}, f32[1,8,256]{2,1,0:T(8,128)}, u32[]{:S(2)}) copy-start(f32[1,8,256]{2,1,0:T(8,128)} %param.8) | copy-start | bytes 24580
  10.5 34.8 %copy-start.3 = (s32[1,256]{1,0:T(1,128)S(1)}, s32[1,256]{1,0:T(1,128)}, u32[]{:S(2)}) copy-start(s32[1,256]{1,0:T(1,128)} %param.10) | copy-start | bytes 3076
  33.1 5.5 %collective-permute-start.5 = (bf16[4,1,16,512]{3,2,0,1:T(8,128)(2,1)S(1)}, bf16[4,1,16,512]{3,2,0,1:T(8,128)(2,1)S(1)}, u32[]{:S(2)}, u32[]{:S(2)}) collective-permute-start(bf16[4,1,16,512]{3,2,0,1:T(8,128)(2,1)S(1)} %bitcast_select_fusion.2), channel_id=1, source_target_pairs={{0,48},{8,56},{16,32},{24,40},{32,16},{40,24},{48,0},{56,8},{64,11... | collective-permute-start | bytes 196616 | tf_op jit(solution)/shard_map/ppermute | solution.py:75
  36.1 5.8 %collective-permute-start.4 = (bf16[4,1,16,512]{3,2,0,1:T(8,128)(2,1)S(1)}, bf16[4,1,16,512]{3,2,0,1:T(8,128)(2,1)S(1)}, u32[]{:S(2)}, u32[]{:S(2)}) collective-permute-start(bf16[4,1,16,512]{3,2,0,1:T(8,128)(2,1)S(1)} %bitcast_select_fusion.2), channel_id=1, source_target_pairs={{0,32},{8,40},{16,48},{24,56},{32,0},{40,8},{48,16},{56,24},{64,96... | collective-permute-start | bytes 196616 | tf_op jit(solution)/shard_map/ppermute | solution.py:75
  36.8 5.1 %collective-permute-start.3 = (bf16[4,1,16,512]{3,2,0,1:T(8,128)(2,1)S(1)}, bf16[4,1,16,512]{3,2,0,1:T(8,128)(2,1)S(1)}, u32[]{:S(2)}, u32[]{:S(2)}) collective-permute-start(bf16[4,1,16,512]{3,2,0,1:T(8,128)(2,1)S(1)} %bitcast_select_fusion.2), channel_id=1, source_target_pairs={{0,16},{8,24},{16,0},{24,8},{32,48},{40,56},{48,32},{56,40},{64,80... | collective-permute-start | bytes 196616 | tf_op jit(solution)/shard_map/ppermute | solution.py:75
  42.6 1.6 %collective-permute-start.6 = (bf16[4,4,1,16,512]{4,3,1,0,2:T(8,128)(2,1)S(1)}, bf16[4,4,1,16,512]{4,3,1,0,2:T(8,128)(2,1)S(1)}, u32[]{:S(2)}, u32[]{:S(2)}) collective-permute-start(bf16[4,4,1,16,512]{4,3,1,0,2:T(8,128)(2,1)S(1)} %bitcast_select_fusion), channel_id=1, source_target_pairs={{0,8},{8,0},{16,24},{24,16},{32,40},{40,32},{48,56},{56,48},{64,72... | collective-permute-start | bytes 786440 | tf_op jit(solution)/shard_map/ppermute | solution.py:75
  44.9 22.3 %copy-start.1 = (f32[1,8,2048]{2,1,0:T(8,128)S(1)}, f32[1,8,2048]{2,1,0:T(8,128)}, u32[]{:S(2)}) copy-start(f32[1,8,2048]{2,1,0:T(8,128)} %param.7) | copy-start | bytes 196612
  52.5 4.3 %collective-permute-start.7 = (f32[8,2048]{1,0:T(8,128)S(1)}, f32[8,2048]{1,0:T(8,128)S(1)}, u32[]{:S(2)}, u32[]{:S(2)}) collective-permute-start(f32[8,2048]{1,0:T(8,128)S(1)} %get-tuple-element.12), channel_id=1, source_target_pairs={{0,1},{1,0},{2,3},{3,2},{4,5},{5,4},{6,7},{7,6},{8,9},{9,8},{10,11... | collective-permute-start | bytes 196616 | tf_op jit(solution)/shard_map/ppermute | solution.py:19
  56.7 5.9 %collective-permute-start.8 = (f32[8,2048]{1,0:T(8,128)S(1)}, f32[8,2048]{1,0:T(8,128)S(1)}, u32[]{:S(2)}, u32[]{:S(2)}) collective-permute-start(f32[8,2048]{1,0:T(8,128)S(1)} %add.134), channel_id=1, source_target_pairs={{0,2},{1,3},{2,0},{3,1},{4,6},{5,7},{6,4},{7,5},{8,10},{9,11},{10,... | collective-permute-start | bytes 196616 | tf_op jit(solution)/shard_map/ppermute | solution.py:19
  62.6 4.5 %collective-permute-start.9 = (f32[8,2048]{1,0:T(8,128)S(1)}, f32[8,2048]{1,0:T(8,128)S(1)}, u32[]{:S(2)}, u32[]{:S(2)}) collective-permute-start(f32[8,2048]{1,0:T(8,128)S(1)} %add.135), channel_id=1, source_target_pairs={{0,4},{1,5},{2,6},{3,7},{4,0},{5,1},{6,2},{7,3},{8,12},{9,13},{10,... | collective-permute-start | bytes 196616 | tf_op jit(solution)/shard_map/ppermute | solution.py:19
  67.8 32.9 %copy-start = (f32[16,8,64]{2,1,0:T(8,128)S(1)}, f32[16,8,64]{2,1,0:T(8,128)}, u32[]{:S(2)}) copy-start(f32[16,8,64]{2,1,0:T(8,128)} %param.11) | copy-start | bytes 98308
  76.2 2.0 %collective-permute-start.10 = (f32[2,2,2,2,16,512]{5,4,3,2,1,0:T(8,128)S(1)}, f32[2,2,2,2,16,512]{5,4,3,2,1,0:T(8,128)S(1)}, u32[]{:S(2)}, u32[]{:S(2)}) collective-permute-start(f32[2,2,2,2,16,512]{5,4,3,2,1,0:T(8,128)S(1)} %dynamic-slice_bitcast_fusion), channel_id=1, source_target_pairs={{0,8},{8,0},{16,24},{24,16},{32,40},{40,32},{48,56},{56,48},{64,72... | collective-permute-start | bytes 1572872 | tf_op jit(solution)/shard_map/ppermute | solution.py:75
  78.3 9.6 %collective-permute-start.13 = (f32[2,2,16,512]{3,2,1,0:T(8,128)S(1)}, f32[2,2,16,512]{3,2,1,0:T(8,128)S(1)}, u32[]{:S(2)}, u32[]{:S(2)}) collective-permute-start(f32[2,2,16,512]{3,2,1,0:T(8,128)S(1)} %get-tuple-element.5), channel_id=1, source_target_pairs={{0,48},{8,56},{16,32},{24,40},{32,16},{40,24},{48,0},{56,8},{64,11... | collective-permute-start | bytes 393224 | tf_op jit(solution)/shard_map/ppermute | solution.py:75
  79.7 8.3 %collective-permute-start.12 = (f32[2,2,16,512]{3,2,1,0:T(8,128)S(1)}, f32[2,2,16,512]{3,2,1,0:T(8,128)S(1)}, u32[]{:S(2)}, u32[]{:S(2)}) collective-permute-start(f32[2,2,16,512]{3,2,1,0:T(8,128)S(1)} %get-tuple-element.6), channel_id=1, source_target_pairs={{0,32},{8,40},{16,48},{24,56},{32,0},{40,8},{48,16},{56,24},{64,96... | collective-permute-start | bytes 393224 | tf_op jit(solution)/shard_map/ppermute | solution.py:75
  80.6 8.0 %collective-permute-start.11 = (f32[2,2,16,512]{3,2,1,0:T(8,128)S(1)}, f32[2,2,16,512]{3,2,1,0:T(8,128)S(1)}, u32[]{:S(2)}, u32[]{:S(2)}) collective-permute-start(f32[2,2,16,512]{3,2,1,0:T(8,128)S(1)} %get-tuple-element.4), channel_id=1, source_target_pairs={{0,16},{8,24},{16,0},{24,8},{32,48},{40,56},{48,32},{56,40},{64,80... | collective-permute-start | bytes 393224 | tf_op jit(solution)/shard_map/ppermute | solution.py:75
  88.6 6.6 %collective-permute-start.16 = (f32[16,512]{1,0:T(8,128)S(1)}, f32[16,512]{1,0:T(8,128)S(1)}, u32[]{:S(2)}, u32[]{:S(2)}) collective-permute-start(f32[16,512]{1,0:T(8,128)S(1)} %get-tuple-element.10), channel_id=1, source_target_pairs={{0,192},{8,200},{16,208},{24,216},{32,224},{40,232},{48,240},{56,2... | collective-permute-start | bytes 98312 | tf_op jit(solution)/shard_map/ppermute | solution.py:75
  92.8 7.8 %collective-permute-start.15 = (f32[16,512]{1,0:T(8,128)S(1)}, f32[16,512]{1,0:T(8,128)S(1)}, u32[]{:S(2)}, u32[]{:S(2)}) collective-permute-start(f32[16,512]{1,0:T(8,128)S(1)} %get-tuple-element.11), channel_id=1, source_target_pairs={{0,128},{8,136},{16,144},{24,152},{32,160},{40,168},{48,176},{56,1... | collective-permute-start | bytes 98312 | tf_op jit(solution)/shard_map/ppermute | solution.py:75
  93.8 6.8 %collective-permute-start.14 = (f32[16,512]{1,0:T(8,128)S(1)}, f32[16,512]{1,0:T(8,128)S(1)}, u32[]{:S(2)}, u32[]{:S(2)}) collective-permute-start(f32[16,512]{1,0:T(8,128)S(1)} %get-tuple-element.9), channel_id=1, source_target_pairs={{0,64},{8,72},{16,80},{24,88},{32,96},{40,104},{48,112},{56,120},{... | collective-permute-start | bytes 98312 | tf_op jit(solution)/shard_map/ppermute | solution.py:75
